TPU v7x, 32 devices: a whole 2x2x4 slice. The times are simulated.
32 devices in a mesh: tile: 8 (over y, x, core), mem: 4 (over z).
Axes of the slice: x: 2, y: 2, z: 4, core: 2. Of those that a mesh axis runs over, the one named last changes fastest.
Arguments:
- control: bfloat16 [80, 1, 360, 720], P('mem', None, 'tile'), may hold values from -6 to 6
- perturb: bfloat16 [80, 1, 360, 720], P('mem', None, 'tile'), may hold values from -6 to 6
- lon_taps: bfloat16 [17], replicated, may hold values from 0.026367188 to 0.07910156
- lat_taps: bfloat16 [17], replicated, may hold values from 0.026367188 to 0.07910156
- innov: float32 [8, 8, 256], P('tile'), may hold values from -6 to 6
- inv_var: float32 [8, 8, 256], P('tile'), may hold values from 1 to 8
- cell_index: int32 [8, 8, 256], P('tile'), may hold values from 0 to 32399, as said below
- counts: int32 [8, 8], P('tile'), may hold values from 0 to 256, as said below
Outputs:
- gradient: float32 [80, 1, 360, 720], P('mem', None, 'tile')
Inputs may be any that keep to these rules, and one draw needn't show every extreme that they name: `cell_index`: an observation's cell within its owning tile, level * 45 * 720 + longitude within the tile * 720 + latitude; both ends are taken. `counts`: live slots per pair of tiles; some pair fills all 256 slots in every draw, and some owning tiles receive far more than others.
All inputs are finite; a program needn't handle non-finite values.
Results may differ from a plain program's by a relative error of at most 0.00066.
Values may be sent and summed in bfloat16 or wider, within the bound.
No kernel may reach another device: no remote copies, remote signals or barrier semaphores. Data moves between devices by JAX's collectives and lax.ppermute only.
A program may use at most 64 MiB of HBM per device.

v0:
```python
import math

import jax
import jax.numpy as jnp
from jax import lax
from jax.sharding import PartitionSpec as P


def extended_2(block, sides, width):
    for axis, dim in sides:
        count = lax.axis_size(axis)
        forward = [(i, i + 1) for i in range(count - 1)]
        forward.append((count - 1, 0))
        backward = [(target, source) for source, target in forward]
        low = lax.ppermute(
            lax.slice_in_dim(block, block.shape[dim] - width, None, axis=dim), axis, forward
        )
        high = lax.ppermute(lax.slice_in_dim(block, 0, width, axis=dim), axis, backward)
        block = jnp.concatenate([low, block, high], axis=dim)
    return block


def band_from(offsets, tap_weights):
    radius = tap_weights.shape[0] - 1
    taps = tap_weights.astype(jnp.float32)
    band = jnp.zeros(offsets.shape, jnp.float32)
    for offset in range(radius + 1):
        band = band + jnp.where(offsets == offset, taps[offset], 0.0)
    return band.astype(jnp.bfloat16)


def lon_band(tap_weights, lon_cells):
    radius = tap_weights.shape[0] - 1
    row_ids = lax.broadcasted_iota(jnp.int32, (lon_cells, lon_cells + 2 * radius), 0)
    col_ids = lax.broadcasted_iota(jnp.int32, (lon_cells, lon_cells + 2 * radius), 1)
    return band_from(jnp.abs(col_ids - row_ids - radius), tap_weights)


def lat_block_band(tap_weights, block_cells):
    radius = tap_weights.shape[0] - 1
    row_ids = lax.broadcasted_iota(jnp.int32, (block_cells + 2 * radius, block_cells), 0)
    col_ids = lax.broadcasted_iota(jnp.int32, (block_cells + 2 * radius, block_cells), 1)
    return band_from(jnp.abs(row_ids - radius - col_ids), tap_weights)


def localize(extended, band_lon, band_blocks, radius, block_cells):
    along = jnp.einsum(
        "ij,mljk->mlik", band_lon, extended, preferred_element_type=jnp.float32
    ).astype(jnp.bfloat16)
    members_here, levels, lon_cells, lat_cells = along.shape
    padded = jnp.pad(along, ((0, 0), (0, 0), (0, 0), (radius, radius)))
    block_count = lat_cells // block_cells
    windows = jnp.stack(
        [
            padded[:, :, :, block * block_cells : block * block_cells + block_cells + 2 * radius]
            for block in range(block_count)
        ],
        axis=3,
    )
    result = jnp.einsum("mlibk,kq->mlibq", windows, band_blocks, preferred_element_type=jnp.float32)
    return result.reshape(members_here, levels, lon_cells, lat_cells)


def pick_cells(field_rows, row_index, col_index, block_rows):
    row_count, col_count = field_rows.shape
    field_cols = field_rows.T

    def pick_one_block(indices):
        rows_here, cols_here = indices
        onehot_rows = (
            rows_here[:, None] == jnp.arange(row_count, dtype=jnp.int32)[None, :]
        ).astype(jnp.float32)
        onehot_cols = (
            cols_here[:, None] == jnp.arange(col_count, dtype=jnp.int32)[None, :]
        ).astype(jnp.float32)
        picked = jnp.dot(
            onehot_cols,
            field_cols,
            precision=lax.Precision.HIGHEST,
            preferred_element_type=jnp.float32,
        )
        return jnp.sum(picked * onehot_rows, axis=1)

    values = lax.map(
        pick_one_block, (row_index.reshape(-1, block_rows), col_index.reshape(-1, block_rows))
    )
    return values.reshape(-1)


def spread_cells(misfit, row_index, col_index, row_count, col_count, block_rows):

    def spread_one_block(total, items):
        rows_here, cols_here, values = items
        onehot_rows = (
            rows_here[:, None] == jnp.arange(row_count, dtype=jnp.int32)[None, :]
        ).astype(jnp.float32)
        onehot_cols = (
            cols_here[:, None] == jnp.arange(col_count, dtype=jnp.int32)[None, :]
        ).astype(jnp.float32)
        weighted = onehot_rows * values[:, None]
        return (
            total
            + jnp.dot(
                weighted.T,
                onehot_cols,
                precision=lax.Precision.HIGHEST,
                preferred_element_type=jnp.float32,
            ),
            None,
        )

    start = jnp.zeros((row_count, col_count), jnp.float32)
    items = (
        row_index.reshape(-1, block_rows),
        col_index.reshape(-1, block_rows),
        misfit.reshape(-1, block_rows),
    )
    total, _ = lax.scan(spread_one_block, start, items)
    return total


def local(control, perturb, lon_taps, lat_taps, innov, inv_var, cell_index, counts):
    members_here, levels, lon_cells, lat_cells = control.shape
    radius = lon_taps.shape[0] - 1
    block_cells = 144
    band_lon = lon_band(lon_taps, lon_cells)
    band_blocks = lat_block_band(lat_taps, block_cells)
    extended = extended_2(control, (("tile", 2),), radius)
    smoothed = localize(extended, band_lon, band_blocks, radius, block_cells)
    member_sum = jnp.sum(perturb.astype(jnp.float32) * smoothed, axis=0)
    slot_ids = lax.broadcasted_iota(jnp.int32, innov.shape, 2)
    is_live = slot_ids < counts[:, :, None]
    weights = jnp.where(is_live, inv_var, 0.0)
    received = (
        lax.all_to_all(innov, "tile", split_axis=1, concat_axis=0, tiled=True),
        lax.all_to_all(weights, "tile", split_axis=1, concat_axis=0, tiled=True),
        lax.all_to_all(cell_index, "tile", split_axis=1, concat_axis=0, tiled=True),
    )
    observed = received[0].reshape(-1)
    weight_recv = received[1].reshape(-1)
    cells_hit = received[2].reshape(-1)
    row_index = cells_hit // lat_cells
    col_index = cells_hit % lat_cells
    row_count = levels * lon_cells
    block_rows = math.gcd(observed.shape[0], 1024)
    increment = lax.psum(member_sum, "mem")
    at_cells = pick_cells(increment.reshape(row_count, lat_cells), row_index, col_index, block_rows)
    misfit = weight_recv * (at_cells - observed)
    spread = spread_cells(misfit, row_index, col_index, row_count, lat_cells, block_rows)
    spread = spread.reshape(levels, lon_cells, lat_cells)
    wide_pert = extended_2(perturb, (("tile", 2),), radius)
    wide_spread = extended_2(spread, (("tile", 1),), radius)
    wide_products = (wide_pert.astype(jnp.float32) * wide_spread[None]).astype(jnp.bfloat16)
    return control.astype(jnp.float32) + localize(
        wide_products, band_lon, band_blocks, radius, block_cells
    )


def solution(mesh):
    return jax.shard_map(
        local,
        mesh=mesh,
        in_specs=(
            P("mem", None, "tile", None),
            P("mem", None, "tile", None),
            P(),
            P(),
            P("tile", None, None),
            P("tile", None, None),
            P("tile", None, None),
            P("tile", None),
        ),
        out_specs=P("mem", None, "tile", None),
        check_vma=False,
    )
```

profile of v0, /device:TPU:0, one launch (start us, length us, event | category | flops | bytes accessed | tf_op | source)
XLA Modules:
  0.0 176.5 jit_solution(8008073635435257452)
XLA Ops:
  6.6 1.5 fusion.166
  8.1 0.5 collective-permute-start.2
  8.6 2.9 %collective-permute-start.3 = (bf16[20,1,16,720]{3,2,0,1:T(8,128)(2,1)S(1)}, bf16[20,1,16,720]{3,2,0,1:T(8,128)(2,1)}, u32[]{:S(2)}, u32[]{:S(2)}) collective-permute-start(bf16[20,1,16,720]{3,2,0,1:T(8,128)(2,1)S(1)} %get-tuple-element.116), channel_id=1, source_target_pairs={{4,0},{8,4},{12,8},{16,12},{20,16},{24,20},{28,24},{0,28},{5,1},{9... | collective-permute-start | bytes 1382408 | tf_op jit(solution)/shard_map/ppermute | solution.py:18
  11.6 1.3 copy.48
  12.9 3.5 %all-to-all-start = ((s32[1,8,256]{2,0,1:T(1,128)}), s32[1,8,256]{2,0,1:T(1,128)S(1)}, u32[]{:S(2)}, u32[]{:S(2)}) async-start(s32[1,8,256]{2,0,1:T(1,128)} %copy.48), calls=%async_computation | async-start | bytes 16384 | tf_op jit(solution)/shard_map/all_to_all | solution.py:137
  16.4 2.2 %fusion.167 = (bf16[20,1,16,720]{3,2,0,1:T(8,128)(2,1)}, bf16[20,1,16,720]{3,2,0,1:T(8,128)(2,1)S(1)}) fusion(bf16[20,1,45,720]{3,2,0,1:T(8,128)(2,1)} %bitcast.147), kind=kLoop, calls=%fused_computation.200 | loop fusion | bytes 1843200 | tf_op jit(solution)/shard_map/slice | solution.py:16
  18.5 0.5 collective-permute-start
  19.0 2.1 %collective-permute-start.1 = (bf16[20,1,16,720]{3,2,0,1:T(8,128)(2,1)S(1)}, bf16[20,1,16,720]{3,2,0,1:T(8,128)(2,1)}, u32[]{:S(2)}, u32[]{:S(2)}) collective-permute-start(bf16[20,1,16,720]{3,2,0,1:T(8,128)(2,1)S(1)} %get-tuple-element.118), channel_id=1, source_target_pairs={{4,0},{8,4},{12,8},{16,12},{20,16},{24,20},{28,24},{0,28},{5,1},{9... | collective-permute-start | bytes 1382408 | tf_op jit(solution)/shard_map/ppermute | solution.py:18
  21.2 0.7 compare_select_fusion
  21.9 0.7 fusion.170
  22.6 0.7 fusion.169
  23.3 0.6 copy.57
  23.9 1.0 all-to-all-done
  25.0 3.3 %all-to-all-start.1 = ((f32[1,8,256]{2,0,1:T(1,128)}), f32[1,8,256]{2,0,1:T(1,128)S(1)}, u32[]{:S(2)}, u32[]{:S(2)}) async-start(f32[1,8,256]{2,0,1:T(1,128)} %compare_select_fusion), calls=%async_computation.1 | async-start | bytes 16384 | tf_op jit(solution)/shard_map/all_to_all | solution.py:136
  28.3 0.1 remainder_reduce_fusion
  28.4 6.4 %all-to-all-done.1 = f32[1,8,256]{2,0,1:T(1,128)S(1)} async-done(((f32[1,8,256]{2,0,1:T(1,128)}), f32[1,8,256]{2,0,1:T(1,128)S(1)}, u32[]{:S(2)}, u32[]{:S(2)}) %all-to-all-start.1) | async-done | bytes 8224 | tf_op jit(solution)/shard_map/all_to_all | solution.py:136
  34.8 3.3 %all-to-all-start.2 = ((f32[1,8,256]{2,0,1:T(1,128)}), f32[1,8,256]{2,0,1:T(1,128)S(1)}, u32[]{:S(2)}, u32[]{:S(2)}) async-start(f32[1,8,256]{2,0,1:T(1,128)} %copy.57), calls=%async_computation.2 | async-start | bytes 16384 | tf_op jit(solution)/shard_map/all_to_all | solution.py:135
  38.3 4.5 %all-to-all-done.2 = f32[1,8,256]{2,0,1:T(1,128)S(1)} async-done(((f32[1,8,256]{2,0,1:T(1,128)}), f32[1,8,256]{2,0,1:T(1,128)S(1)}, u32[]{:S(2)}, u32[]{:S(2)}) %all-to-all-start.2) | async-done | bytes 8224 | tf_op jit(solution)/shard_map/all_to_all | solution.py:135
  42.8 12.1 %fusion.31 = bf16[20,1,45,720]{3,2,0,1:T(8,128)(2,1)S(1)} fusion(bf16[20,1,16,720]{3,2,0,1:T(8,128)(2,1)} %collective-permute-done.3, bf16[20,1,45,720]{3,2,0,1:T(8,128)(2,1)S(1)} %bitcast.146, bf16[20,1,16,720]{3,2,0,1:T(8,128)(2,1)} %collective-permute-done.2, f32[]{:T(128)} %bitcast.31, f32[]{:T(128)} %bitcast.30, f32[]{:T(128)} %bitcast.29, ...), kind=kOutput, calls=%fused_computation.44 | convolution fusion | flops 107279912 | bytes 3513668 | tf_op jit(solution)/shard_map/ij,mljk->mlik/dot_general | solution.py:47
  54.9 0.2 fusion.33
  55.1 0.2 fusion.44
  55.4 0.2 fusion.43
  55.6 0.2 fusion.35
  55.8 11.5 %fusion.25 = f32[20,45,5,144]{3,1,2,0:T(8,128)S(1)} fusion(f32[]{:T(128)} %bitcast.58, f32[]{:T(128)} %bitcast.57, f32[]{:T(128)} %bitcast.56, f32[]{:T(128)} %bitcast.55, f32[]{:T(128)} %bitcast.54, f32[]{:T(128)} %bitcast.53, f32[]{:T(128)} %bitcast.52, f32[]{:T(128)} %bitcast.51, f32[]{:T(128)} %bitcast.50, f32[]{:T(128)} %bitcast.49, f32[]{:T(128)} %bitcast.48, ...), kind=kOutput, calls=%fused_computation.38 | convolution fusion | flops 229439232 | bytes 4176772 | tf_op jit(solution)/shard_map/mlibk,kq->mlibq/dot_general | solution.py:60
  67.3 6.4 %copy.55 = f32[20,45,5,144]{3,2,1,0:T(8,128)} copy(f32[20,45,5,144]{3,1,2,0:T(8,128)S(1)} %fusion.25) | data formatting | bytes 5184000 | tf_op jit(solution)/shard_map/mlibk,kq->mlibq/dot_general | solution.py:60
  73.7 4.9 %reshape.136 = f32[20,1,45,720]{3,2,0,1:T(8,128)S(1)} reshape(f32[20,45,5,144]{3,2,1,0:T(8,128)} %copy.55) | data formatting | bytes 5184000 | tf_op jit(solution)/shard_map/reshape | solution.py:61
  78.6 2.4 %multiply_reduce_fusion = f32[45,720]{1,0:T(8,128)} fusion(f32[20,1,45,720]{3,2,0,1:T(8,128)S(1)} %reshape.136, bf16[20,1,45,720]{3,2,1,0:T(8,128)(2,1)} %param.13), kind=kLoop, calls=%fused_computation.22 | loop fusion | flops 1911600 | bytes 4017600 | tf_op jit(solution)/shard_map/reduce_sum | solution.py:130
  81.0 34.0 %all-reduce.4.cloned.1.call-done = f32[720,45]{0,1:T(8,128)} async-done(((f32[720,45]{0,1:T(8,128)}), f32[720,45]{0,1:T(8,128)}) %all-reduce.4.cloned.1.call-update) | async-done | bytes 129616 | tf_op jit(solution)/shard_map/psum | solution.py:146
  115.0 1.1 copy.56
  116.1 3.8 %while.21 = (s32[]{:T(128)}, f32[2,1024]{1,0:T(2,128)S(1)}, s32[2,1024]{1,0:T(2,128)S(1)}, s32[2,1024]{1,0:T(2,128)S(1)}, f32[720,45]{1,0:T(8,128)S(1)}, /*index=5*/s32[]{:T(128)}, s32[]{:T(128)}) while((s32[]{:T(128)}, f32[2,1024]{1,0:T(2,128)S(1)}, s32[2,1024]{1,0:T(2,128)S(1)}, s32[2,1024]{1,0:T(2,128)S(1)}, f32[720,45]{1,0:T(8,128)S(1)}, ...), condition=%wide.region_4.5_spmd, body=%wide.region_2.4_spmd.sunk | while | flops 399005696 | bytes 166549 | solution.py:84
  116.1 1.8 %fusion.179 = f32[1024]{0:T(1024)S(1)} fusion(f32[720,45]{1,0:T(8,128)S(1)} %get-tuple-element.245, s32[1024]{0:T(1024)S(1)} %bitcast.156, s32[1024]{0:T(1024)S(1)} %bitcast.157), kind=kOutput, calls=%fused_computation.4.clone.1 | convolution fusion | flops 399005696 | bytes 141888 | tf_op jit(solution)/shard_map/while/body/eval_jaxpr/dot_general | solution.py:76
  118.0 1.8 %fusion.179 = f32[1024]{0:T(1024)S(1)} fusion(f32[720,45]{1,0:T(8,128)S(1)} %get-tuple-element.245, s32[1024]{0:T(1024)S(1)} %bitcast.156, s32[1024]{0:T(1024)S(1)} %bitcast.157), kind=kOutput, calls=%fused_computation.4.clone.1 | convolution fusion | flops 399005696 | bytes 141888 | tf_op jit(solution)/shard_map/while/body/eval_jaxpr/dot_general | solution.py:76
  119.9 3.1 %while.22 = (s32[]{:T(128)}, f32[45,720]{1,0:T(8,128)S(1)}, s32[2,1024]{1,0:T(2,128)S(1)}, f32[2,1024]{1,0:T(2,128)S(1)}, s32[2,1024]{1,0:T(2,128)S(1)}, /*index=5*/s32[]{:T(128)}, s32[]{:T(128)}) while((s32[]{:T(128)}, f32[45,720]{1,0:T(8,128)S(1)}, s32[2,1024]{1,0:T(2,128)S(1)}, f32[2,1024]{1,0:T(2,128)S(1)}, ...), condition=%wide.region_6.7_spmd.clone, body=%wide.region_5.6_spmd.clone.sunk | while | flops 399025440 | bytes 296159 | solution.py:118
  120.0 1.5 fusion.181
  121.5 1.5 fusion.181
  123.1 0.1 collective-permute-start.4
  123.1 2.6 %collective-permute-start.5 = (f32[1,16,720]{2,1,0:T(8,128)S(1)}, f32[1,16,720]{2,1,0:T(8,128)S(1)}, u32[]{:S(2)}, u32[]{:S(2)}) collective-permute-start(f32[1,16,720]{2,1,0:T(8,128)S(1)} %get-tuple-element.120), channel_id=1, source_target_pairs={{4,0},{8,4},{12,8},{16,12},{20,16},{24,20},{28,24},{0,28},{5,1},{9... | collective-permute-start | bytes 138248 | tf_op jit(solution)/shard_map/ppermute | solution.py:18
  125.8 1.8 %collective-permute-done.4 = f32[1,16,720]{2,1,0:T(8,128)S(1)} collective-permute-done((f32[1,16,720]{2,1,0:T(8,128)S(1)}, f32[1,16,720]{2,1,0:T(8,128)S(1)}, u32[]{:S(2)}, u32[]{:S(2)}) %collective-permute-start.4) | collective-permute-done | bytes 46112 | tf_op jit(solution)/shard_map/ppermute | solution.py:15
  127.6 12.3 %fusion.30 = bf16[20,1,45,720]{3,2,0,1:T(8,128)(2,1)S(1)} fusion(bf16[20,16,720]{2,1,0:T(8,128)(2,1)} %bitcast.8, bf16[20,45,720]{2,1,0:T(8,128)(2,1)S(1)} %bitcast.148, bf16[20,16,720]{2,1,0:T(8,128)(2,1)} %bitcast.5, f32[77,720]{1,0:T(8,128)S(1)} %maximum_bitcast_fusion.6, f32[]{:T(128)} %bitcast.31, f32[]{:T(128)} %bitcast.30, f32[]{:T(128)} %bitcast.29, ...), kind=kOutput, calls=%fused_computation.43 | convolution fusion | flops 109497512 | bytes 3735428 | tf_op jit(solution)/shard_map/ij,mljk->mlik/dot_general | solution.py:47
  139.9 0.2 fusion.37
  140.1 0.2 fusion.41
  140.4 0.2 fusion.40
  140.6 0.2 fusion.39
  140.8 11.5 %fusion.23 = f32[20,45,5,144]{3,1,2,0:T(8,128)S(1)} fusion(f32[]{:T(128)} %bitcast.58, f32[]{:T(128)} %bitcast.57, f32[]{:T(128)} %bitcast.56, f32[]{:T(128)} %bitcast.55, f32[]{:T(128)} %bitcast.54, f32[]{:T(128)} %bitcast.53, f32[]{:T(128)} %bitcast.52, f32[]{:T(128)} %bitcast.51, f32[]{:T(128)} %bitcast.50, f32[]{:T(128)} %bitcast.49, f32[]{:T(128)} %bitcast.48, ...), kind=kOutput, calls=%fused_computation.36 | convolution fusion | flops 229439232 | bytes 4176772 | tf_op jit(solution)/shard_map/mlibk,kq->mlibq/dot_general | solution.py:60
  152.3 6.4 %copy.59 = f32[20,45,5,144]{3,2,1,0:T(8,128)} copy(f32[20,45,5,144]{3,1,2,0:T(8,128)S(1)} %fusion.23) | data formatting | bytes 5184000 | tf_op jit(solution)/shard_map/mlibk,kq->mlibq/dot_general | solution.py:60
  158.7 4.9 %reshape.141 = f32[20,1,45,720]{3,2,0,1:T(8,128)S(1)} reshape(f32[20,45,5,144]{3,2,1,0:T(8,128)} %copy.59) | data formatting | bytes 5184000 | tf_op jit(solution)/shard_map/reshape | solution.py:61
  163.6 1.7 convert_add_fusion
  165.3 4.4 %copy.60 = f32[20,1,45,720]{3,1,2,0:T(1,128)} copy(f32[20,1,45,720]{3,2,0,1:T(8,128)S(1)} %convert_add_fusion) | data formatting | bytes 5184000 | tf_op jit(solution)/shard_map/add | solution.py:154
  (48 shorter events, 0.6 us)
Async XLA Ops:
  6.5 36.3 %copy-start = (bf16[20,1,45,720]{3,2,1,0:T(8,128)(2,1)S(1)}, bf16[20,1,45,720]{3,2,1,0:T(8,128)(2,1)}, u32[]{:S(2)}) copy-start(bf16[20,1,45,720]{3,2,1,0:T(8,128)(2,1)} %param.12) | copy-start | bytes 3888004
  6.5 14.7 %copy-start.7 = (s32[1,8]{1,0:T(1,128)S(1)}, s32[1,8]{1,0:T(1,128)}, u32[]{:S(2)}) copy-start(s32[1,8]{1,0:T(1,128)} %param.19) | copy-start | bytes 100
  6.5 14.7 %copy-start.5 = (f32[1,8,256]{2,1,0:T(8,128)S(1)}, f32[1,8,256]{2,1,0:T(8,128)}, u32[]{:S(2)}) copy-start(f32[1,8,256]{2,1,0:T(8,128)} %param.17) | copy-start | bytes 24580
  6.5 15.3 %copy-start.3 = (bf16[17]{0:T(256)(128)(2,1)S(1)}, bf16[17]{0:T(256)(128)(2,1)}, u32[]{:S(2)}) copy-start(bf16[17]{0:T(256)(128)(2,1)} %param.14) | copy-start | bytes 106
  6.5 16.0 %copy-start.4 = (bf16[17]{0:T(256)(128)(2,1)S(1)}, bf16[17]{0:T(256)(128)(2,1)}, u32[]{:S(2)}) copy-start(bf16[17]{0:T(256)(128)(2,1)} %param.15) | copy-start | bytes 106
  6.5 16.8 %copy-start.6 = (f32[1,8,256]{2,1,0:T(8,128)S(1)}, f32[1,8,256]{2,1,0:T(8,128)}, u32[]{:S(2)}) copy-start(f32[1,8,256]{2,1,0:T(8,128)} %param.16) | copy-start | bytes 24580
  8.1 34.7 %collective-permute-start.2 = (bf16[20,1,16,720]{3,2,0,1:T(8,128)(2,1)S(1)}, bf16[20,1,16,720]{3,2,0,1:T(8,128)(2,1)}, u32[]{:S(2)}, u32[]{:S(2)}) collective-permute-start(bf16[20,1,16,720]{3,2,0,1:T(8,128)(2,1)S(1)} %get-tuple-element.115), channel_id=1, source_target_pairs={{0,4},{4,8},{8,12},{12,16},{16,20},{20,24},{24,28},{28,0},{1,5},{5... | collective-permute-start | bytes 1382408 | tf_op jit(solution)/shard_map/ppermute | solution.py:15
  8.6 34.2 %collective-permute-start.3 = (bf16[20,1,16,720]{3,2,0,1:T(8,128)(2,1)S(1)}, bf16[20,1,16,720]{3,2,0,1:T(8,128)(2,1)}, u32[]{:S(2)}, u32[]{:S(2)}) collective-permute-start(bf16[20,1,16,720]{3,2,0,1:T(8,128)(2,1)S(1)} %get-tuple-element.116), channel_id=1, source_target_pairs={{4,0},{8,4},{12,8},{16,12},{20,16},{24,20},{28,24},{0,28},{5,1},{9... | collective-permute-start | bytes 1382408 | tf_op jit(solution)/shard_map/ppermute | solution.py:18
  12.9 12.1 %all-to-all-start = ((s32[1,8,256]{2,0,1:T(1,128)}), s32[1,8,256]{2,0,1:T(1,128)S(1)}, u32[]{:S(2)}, u32[]{:S(2)}) async-start(s32[1,8,256]{2,0,1:T(1,128)} %copy.48), calls=%async_computation | async-start | bytes 16384 | tf_op jit(solution)/shard_map/all_to_all | solution.py:137
  18.5 109.0 %collective-permute-start = (bf16[20,1,16,720]{3,2,0,1:T(8,128)(2,1)}, bf16[20,1,16,720]{3,2,0,1:T(8,128)(2,1)}, u32[]{:S(2)}, u32[]{:S(2)}) collective-permute-start(bf16[20,1,16,720]{3,2,0,1:T(8,128)(2,1)} %get-tuple-element.117), channel_id=1, source_target_pairs={{0,4},{4,8},{8,12},{12,16},{16,20},{20,24},{24,28},{28,0},{1,5},{5... | collective-permute-start | bytes 1382408 | tf_op jit(solution)/shard_map/ppermute | solution.py:15
  19.0 108.5 %collective-permute-start.1 = (bf16[20,1,16,720]{3,2,0,1:T(8,128)(2,1)S(1)}, bf16[20,1,16,720]{3,2,0,1:T(8,128)(2,1)}, u32[]{:S(2)}, u32[]{:S(2)}) collective-permute-start(bf16[20,1,16,720]{3,2,0,1:T(8,128)(2,1)S(1)} %get-tuple-element.118), channel_id=1, source_target_pairs={{4,0},{8,4},{12,8},{16,12},{20,16},{24,20},{28,24},{0,28},{5,1},{9... | collective-permute-start | bytes 1382408 | tf_op jit(solution)/shard_map/ppermute | solution.py:18
  25.0 9.8 %all-to-all-start.1 = ((f32[1,8,256]{2,0,1:T(1,128)}), f32[1,8,256]{2,0,1:T(1,128)S(1)}, u32[]{:S(2)}, u32[]{:S(2)}) async-start(f32[1,8,256]{2,0,1:T(1,128)} %compare_select_fusion), calls=%async_computation.1 | async-start | bytes 16384 | tf_op jit(solution)/shard_map/all_to_all | solution.py:136
  34.8 8.0 %all-to-all-start.2 = ((f32[1,8,256]{2,0,1:T(1,128)}), f32[1,8,256]{2,0,1:T(1,128)S(1)}, u32[]{:S(2)}, u32[]{:S(2)}) async-start(f32[1,8,256]{2,0,1:T(1,128)} %copy.57), calls=%async_computation.2 | async-start | bytes 16384 | tf_op jit(solution)/shard_map/all_to_all | solution.py:135
  38.1 76.9 %all-reduce.4.cloned.1.call-start = ((), (), s32[]{:S(2)}) async-start(), calls=%async_computation.3 | async-start | bytes 294912 | tf_op jit(solution)/shard_map/psum | solution.py:146
  116.1 3.8 %copy-start.2 = (f32[45,720]{1,0:T(8,128)S(1)}, f32[45,720]{1,0:T(8,128)}, u32[]{:S(2)}) copy-start(f32[45,720]{1,0:T(8,128)} %custom-call) | copy-start | bytes 388804
  119.9 7.7 %copy-start.1 = (bf16[20,1,45,720]{3,2,1,0:T(8,128)(2,1)S(1)}, bf16[20,1,45,720]{3,2,1,0:T(8,128)(2,1)}, u32[]{:S(2)}) copy-start(bf16[20,1,45,720]{3,2,1,0:T(8,128)(2,1)} %param.13) | copy-start | bytes 3888004
  123.1 4.5 %collective-permute-start.4 = (f32[1,16,720]{2,1,0:T(8,128)S(1)}, f32[1,16,720]{2,1,0:T(8,128)S(1)}, u32[]{:S(2)}, u32[]{:S(2)}) collective-permute-start(f32[1,16,720]{2,1,0:T(8,128)S(1)} %get-tuple-element.119), channel_id=1, source_target_pairs={{0,4},{4,8},{8,12},{12,16},{16,20},{20,24},{24,28},{28,0},{1,5},{5... | collective-permute-start | bytes 138248 | tf_op jit(solution)/shard_map/ppermute | solution.py:15
  123.1 4.4 %collective-permute-start.5 = (f32[1,16,720]{2,1,0:T(8,128)S(1)}, f32[1,16,720]{2,1,0:T(8,128)S(1)}, u32[]{:S(2)}, u32[]{:S(2)}) collective-permute-start(f32[1,16,720]{2,1,0:T(8,128)S(1)} %get-tuple-element.120), channel_id=1, source_target_pairs={{4,0},{8,4},{12,8},{16,12},{20,16},{24,20},{28,24},{0,28},{5,1},{9... | collective-permute-start | bytes 138248 | tf_op jit(solution)/shard_map/ppermute | solution.py:18
Sparse Core Ops, SparseCore 0:
  81.1 33.8 all-reduce.3
where the time goes:
time: 178 us; the launch traced here: 176 us
  matrix products  54 us (30%)
  waiting for transfers between devices  47.7 us (27%)
  local copies, waits for them, and re-layouts  37 us (21%)
  starting transfers between devices  19 us (11%)
  between operations  13.8 us (8%)
  other arithmetic  4.94 us (3%)
    psum x1, waiting for transfers between devices, local(): increment = lax.psum(member_sum, 'mem')  34 us
    dot_general x2, matrix products, localize(): jnp.einsum('ij,mljk->mlik', band_lon, extended, preferred_element_type=jn...  24.4 us
    dot_general x2, matrix products, localize(): jnp.einsum('mlibk,kq->mlibq', windows, band_blocks, preferred_element_typ...  23 us
    dot_general x2, local copies, waits for them, and re-layouts, localize(): jnp.einsum('mlibk,kq->mlibq', windows, band_blocks, preferred_element_typ...  12.8 us
    reshape x2, local copies, waits for them, and re-layouts, localize(): return result.reshape(members_here, levels, lon_cells, lat_cells)  9.75 us
    ppermute x3, starting transfers between devices, extended_2(): lax.ppermute(lax.slice_in_dim(block, 0, width, axis=dim), axis, backward)  7.71 us
    all_to_all x1, waiting for transfers between devices, local(): lax.all_to_all(weights, 'tile', split_axis=1, concat_axis=0, tiled=True)  6.4 us
    all_to_all x1, waiting for transfers between devices, local(): lax.all_to_all(innov, 'tile', split_axis=1, concat_axis=0, tiled=True)  4.46 us
  transfers between devices with their start and end apart: 10, of which 5 were waited for; matrix products, arithmetic and copies ran while one was open for 30% of the time, Pallas kernels for 0%

commit v1 on v0

v1 whole, which is shorter than its diff:
```python
import math

import jax
import jax.numpy as jnp
from jax import lax
from jax.experimental import pallas as pl
from jax.experimental.pallas import tpu as pltpu
from jax.sharding import PartitionSpec as P


def halos(block, axis, dim, width):
    count = lax.axis_size(axis)
    forward = [(i, (i + 1) % count) for i in range(count)]
    backward = [((i + 1) % count, i) for i in range(count)]
    low = lax.ppermute(
        lax.slice_in_dim(block, block.shape[dim] - width, None, axis=dim), axis, forward
    )
    high = lax.ppermute(lax.slice_in_dim(block, 0, width, axis=dim), axis, backward)
    return low, high


def extend(block, low, high, dim, padded):
    pad_shape = list(block.shape)
    pad_shape[dim] = padded - block.shape[dim]
    parts = [block]
    if pad_shape[dim] > 0:
        parts.append(jnp.zeros(pad_shape, block.dtype))
    return jnp.concatenate(parts + [low, high], axis=dim)


def lon_band(tap_weights, lon_cells, padded):
    radius = tap_weights.shape[0] - 1
    taps = tap_weights.astype(jnp.float32)
    ext_cells = padded + 2 * radius
    rows = lax.broadcasted_iota(jnp.int32, (padded, ext_cells), 0)
    cols = lax.broadcasted_iota(jnp.int32, (padded, ext_cells), 1)
    source = jnp.where(
        cols < padded,
        cols,
        jnp.where(cols < padded + radius, cols - padded - radius, cols - padded - radius + lon_cells),
    )
    valid = (rows < lon_cells) & ((cols < lon_cells) | (cols >= padded))
    dist = jnp.abs(source - rows)
    band = jnp.where(valid & (dist <= radius), taps[jnp.minimum(dist, radius)], 0.0)
    return band.astype(jnp.bfloat16)


def lat_band(tap_weights, lat_cells):
    radius = tap_weights.shape[0] - 1
    taps = tap_weights.astype(jnp.float32)
    rows = lax.broadcasted_iota(jnp.int32, (lat_cells, lat_cells), 0)
    cols = lax.broadcasted_iota(jnp.int32, (lat_cells, lat_cells), 1)
    dist = jnp.abs(rows - cols)
    band = jnp.where(dist <= radius, taps[jnp.minimum(dist, radius)], 0.0)
    return band.astype(jnp.bfloat16)


def member_chunk(members):
    for size in (5, 4, 3, 2, 1):
        if members % size == 0:
            return size
    return 1


def forward_sum(ext_control, perturb, band_lon, band_lat):
    members, levels, ext_cells, lat_cells = ext_control.shape
    lon_cells = perturb.shape[2]
    padded = band_lon.shape[0]
    chunk = member_chunk(members)

    def kernel(ext_ref, pert_ref, blon_ref, blat_ref, out_ref, along_ref):
        step = pl.program_id(1)
        blon = blon_ref[...]
        for m in range(chunk):
            along = jnp.dot(blon, ext_ref[m], preferred_element_type=jnp.float32)
            along_ref[m * padded:(m + 1) * padded, :] = along.astype(jnp.bfloat16)
        smoothed = jnp.dot(along_ref[...], blat_ref[...], preferred_element_type=jnp.float32)
        total = pert_ref[0].astype(jnp.float32) * smoothed[0:lon_cells]
        for m in range(1, chunk):
            total = total + pert_ref[m].astype(jnp.float32) * smoothed[
                m * padded:m * padded + lon_cells
            ]

        @pl.when(step == 0)
        def _():
            out_ref[...] = total

        @pl.when(step > 0)
        def _():
            out_ref[...] = out_ref[...] + total

    return pl.pallas_call(
        kernel,
        grid=(levels, members // chunk),
        in_specs=[
            pl.BlockSpec((chunk, None, ext_cells, lat_cells), lambda l, g: (g, l, 0, 0)),
            pl.BlockSpec((chunk, None, lon_cells, lat_cells), lambda l, g: (g, l, 0, 0)),
            pl.BlockSpec(band_lon.shape, lambda l, g: (0, 0)),
            pl.BlockSpec(band_lat.shape, lambda l, g: (0, 0)),
        ],
        out_specs=pl.BlockSpec((None, lon_cells, lat_cells), lambda l, g: (l, 0, 0)),
        out_shape=jax.ShapeDtypeStruct((levels, lon_cells, lat_cells), jnp.float32),
        scratch_shapes=[pltpu.VMEM((chunk * padded, lat_cells), jnp.bfloat16)],
        compiler_params=pltpu.CompilerParams(dimension_semantics=("arbitrary", "arbitrary")),
    )(ext_control, perturb, band_lon, band_lat)


def backward_grad(ext_perturb, ext_spread, control, band_lon, band_lat):
    members, levels, ext_cells, lat_cells = ext_perturb.shape
    lon_cells = control.shape[2]
    padded = band_lon.shape[0]
    chunk = member_chunk(members)

    def kernel(pext_ref, spread_ref, ctrl_ref, blon_ref, blat_ref, out_ref, along_ref):
        blon = blon_ref[...]
        spread = spread_ref[...]
        for m in range(chunk):
            weighted = (pext_ref[m].astype(jnp.float32) * spread).astype(jnp.bfloat16)
            along = jnp.dot(blon, weighted, preferred_element_type=jnp.float32)
            along_ref[m * padded:(m + 1) * padded, :] = along.astype(jnp.bfloat16)
        smoothed = jnp.dot(along_ref[...], blat_ref[...], preferred_element_type=jnp.float32)
        for m in range(chunk):
            out_ref[m] = ctrl_ref[m].astype(jnp.float32) + smoothed[
                m * padded:m * padded + lon_cells
            ]

    return pl.pallas_call(
        kernel,
        grid=(levels, members // chunk),
        in_specs=[
            pl.BlockSpec((chunk, None, ext_cells, lat_cells), lambda l, g: (g, l, 0, 0)),
            pl.BlockSpec((None, ext_cells, lat_cells), lambda l, g: (l, 0, 0)),
            pl.BlockSpec((chunk, None, lon_cells, lat_cells), lambda l, g: (g, l, 0, 0)),
            pl.BlockSpec(band_lon.shape, lambda l, g: (0, 0)),
            pl.BlockSpec(band_lat.shape, lambda l, g: (0, 0)),
        ],
        out_specs=pl.BlockSpec((chunk, None, lon_cells, lat_cells), lambda l, g: (g, l, 0, 0)),
        out_shape=jax.ShapeDtypeStruct(control.shape, jnp.float32),
        scratch_shapes=[pltpu.VMEM((chunk * padded, lat_cells), jnp.bfloat16)],
        compiler_params=pltpu.CompilerParams(dimension_semantics=("parallel", "parallel")),
    )(ext_perturb, ext_spread, control, band_lon, band_lat)


def pick_cells(field_rows, row_index, col_index, block_rows):
    row_count, col_count = field_rows.shape
    field_cols = field_rows.T

    def pick_one_block(indices):
        rows_here, cols_here = indices
        onehot_rows = (
            rows_here[:, None] == jnp.arange(row_count, dtype=jnp.int32)[None, :]
        ).astype(jnp.float32)
        onehot_cols = (
            cols_here[:, None] == jnp.arange(col_count, dtype=jnp.int32)[None, :]
        ).astype(jnp.float32)
        picked = jnp.dot(
            onehot_cols,
            field_cols,
            precision=lax.Precision.HIGHEST,
            preferred_element_type=jnp.float32,
        )
        return jnp.sum(picked * onehot_rows, axis=1)

    values = lax.map(
        pick_one_block, (row_index.reshape(-1, block_rows), col_index.reshape(-1, block_rows))
    )
    return values.reshape(-1)


def spread_cells(misfit, row_index, col_index, row_count, col_count, block_rows):

    def spread_one_block(total, items):
        rows_here, cols_here, values = items
        onehot_rows = (
            rows_here[:, None] == jnp.arange(row_count, dtype=jnp.int32)[None, :]
        ).astype(jnp.float32)
        onehot_cols = (
            cols_here[:, None] == jnp.arange(col_count, dtype=jnp.int32)[None, :]
        ).astype(jnp.float32)
        weighted = onehot_rows * values[:, None]
        return (
            total
            + jnp.dot(
                weighted.T,
                onehot_cols,
                precision=lax.Precision.HIGHEST,
                preferred_element_type=jnp.float32,
            ),
            None,
        )

    start = jnp.zeros((row_count, col_count), jnp.float32)
    items = (
        row_index.reshape(-1, block_rows),
        col_index.reshape(-1, block_rows),
        misfit.reshape(-1, block_rows),
    )
    total, _ = lax.scan(spread_one_block, start, items)
    return total


def local(control, perturb, lon_taps, lat_taps, innov, inv_var, cell_index, counts):
    members_here, levels, lon_cells, lat_cells = control.shape
    radius = lon_taps.shape[0] - 1
    padded = -(-lon_cells // 16) * 16
    band_lon = lon_band(lon_taps, lon_cells, padded)
    band_lat = lat_band(lat_taps, lat_cells)

    slot_ids = lax.broadcasted_iota(jnp.int32, innov.shape, 2)
    weights = jnp.where(slot_ids < counts[:, :, None], inv_var, 0.0)
    lists = jnp.stack([innov, weights, cell_index.astype(jnp.float32)])
    received = lax.all_to_all(lists, "tile", split_axis=2, concat_axis=1, tiled=True)
    observed = received[0].reshape(-1)
    weight_recv = received[1].reshape(-1)
    cells_hit = received[2].reshape(-1).astype(jnp.int32)
    row_index = cells_hit // lat_cells
    col_index = cells_hit % lat_cells
    row_count = levels * lon_cells
    block_rows = math.gcd(observed.shape[0], 1024)

    c_low, c_high = halos(control, "tile", 2, radius)
    p_low, p_high = halos(perturb, "tile", 2, radius)
    ext_control = extend(control, c_low, c_high, 2, padded)
    member_sum = forward_sum(ext_control, perturb, band_lon, band_lat)
    partial = pick_cells(member_sum.reshape(row_count, lat_cells), row_index, col_index, block_rows)
    at_cells = lax.psum(partial, "mem")
    misfit = weight_recv * (at_cells - observed)
    spread = spread_cells(misfit, row_index, col_index, row_count, lat_cells, block_rows)
    spread = spread.reshape(levels, lon_cells, lat_cells)
    s_low, s_high = halos(spread, "tile", 1, radius)
    ext_spread = extend(spread, s_low, s_high, 1, padded)
    ext_perturb = extend(perturb, p_low, p_high, 2, padded)
    return backward_grad(ext_perturb, ext_spread, control, band_lon, band_lat)


def solution(mesh):
    return jax.shard_map(
        local,
        mesh=mesh,
        in_specs=(
            P("mem", None, "tile", None),
            P("mem", None, "tile", None),
            P(),
            P(),
            P("tile", None, None),
            P("tile", None, None),
            P("tile", None, None),
            P("tile", None),
        ),
        out_specs=P("mem", None, "tile", None),
        check_vma=False,
    )
```

time: 178 us -> 102 us (0.57)
  matrix products: 54 us -> 6.58 us
  waiting for transfers between devices: 47.7 us -> 4.81 us
  other arithmetic: 4.94 us -> 21.8 us
  between operations: 13.8 us -> 0.28 us
  blocking collectives: 0 us -> 12.1 us
  Pallas kernels: 0 us -> 11.2 us
  starting transfers between devices: 19 us -> 10.6 us
  local copies, waits for them, and re-layouts: 37 us -> 33.8 us
    dot_general x4 -> x0, matrix products: 47.4 us -> none  [the longest x2 24.4 us: localize(): jnp.einsum('ij,mljk->mlik', band_lon, extended, preferred_element_type=jn...]
    psum x1 -> x0, waiting for transfers between devices: 34 us -> none  [local(): increment = lax.psum(member_sum, 'mem')]
    gather x0 -> x3, local copies, waits for them, and re-layouts: none -> 22.5 us  [the longest x2 21.8 us: lon_band(): taps[jnp.minimum(dist, radius)]]
    convert_element_type x0 -> x3, other arithmetic: none -> 15.2 us  [the longest x1 14.6 us: lat_band(): return band.astype(jnp.bfloat16)]
    dot_general x2 -> x0, local copies, waits for them, and re-layouts: 12.8 us -> none  [localize(): jnp.einsum('mlibk,kq->mlibq', windows, band_blocks, preferred_element_typ...]
    psum x0 -> x1, blocking collectives: none -> 12.1 us  [local(): at_cells = lax.psum(partial, 'mem')]
    all_to_all x3 -> x1, waiting for transfers between devices: 11.9 us -> 0.01 us  [local(): lax.all_to_all(lists, 'tile', split_axis=2, concat_axis=1, tiled=True)]
    pallas_call x0 -> x2, Pallas kernels: none -> 11.2 us  [the longest x1 5.86 us: backward_grad(): pl.pallas_call(kernel, grid=(levels, members // chunk), in_specs=[pl.Bloc...]
  transfers between devices with their start and end apart: 10 -> 7, of which waited for: 5 -> 2; matrix products, arithmetic and copies ran while one was open for 30% -> 39% of each run, Pallas kernels for 0% -> 0%
where the time goes in v1:
time: 102 us; the launch traced here: 101 us
  local copies, waits for them, and re-layouts  33.8 us (33%)
  other arithmetic  21.8 us (21%)
  blocking collectives  12.1 us (12%)
  Pallas kernels  11.2 us (11%)
  starting transfers between devices  10.6 us (10%)
  matrix products  6.58 us (6%)
  waiting for transfers between devices  4.81 us (5%)
    gather x2, local copies, waits for them, and re-layouts, lon_band(): taps[jnp.minimum(dist, radius)]  21.8 us
    convert_element_type x1, other arithmetic, lat_band(): return band.astype(jnp.bfloat16)  14.6 us
    psum x1, blocking collectives, local(): at_cells = lax.psum(partial, 'mem')  12.1 us
    ppermute x3, starting transfers between devices, halos(): lax.ppermute(lax.slice_in_dim(block, 0, width, axis=dim), axis, backward)  6.67 us
    pallas_call x1, local copies, waits for them, and re-layouts, backward_grad(): pl.pallas_call(kernel, grid=(levels, members // chunk), in_specs=[pl.Bloc...  6.21 us
    pallas_call x1, Pallas kernels, backward_grad(): pl.pallas_call(kernel, grid=(levels, members // chunk), in_specs=[pl.Bloc...  5.86 us
    concatenate x2, other arithmetic, extend(): return jnp.concatenate(parts + [low, high], axis=dim)  5.61 us
    pallas_call x1, Pallas kernels, forward_sum(): pl.pallas_call(kernel, grid=(levels, members // chunk), in_specs=[pl.Bloc...  5.37 us
  transfers between devices with their start and end apart: 7, of which 2 were waited for; matrix products, arithmetic and copies ran while one was open for 39% of the time, Pallas kernels for 0%

profile of v1, /device:TPU:0, one launch (start us, length us, event | category | flops | bytes accessed | tf_op | source)
XLA Modules:
  0.0 101.4 jit_solution(9181925838361679418)
XLA Ops:
  0.0 0.0 copy-start
  0.0 0.0 copy-start.7
  0.0 0.0 copy-start.8
  0.0 2.4 %fusion.51 = (bf16[20,1,16,720]{3,2,1,0:T(8,128)(2,1)}, bf16[20,1,16,720]{3,2,1,0:T(8,128)(2,1)}) fusion(bf16[20,1,45,720]{3,2,1,0:T(8,128)(2,1)} %ctrl_ref.1), kind=kLoop, calls=%fused_computation.89 | loop fusion | bytes 1843200 | tf_op jit(solution)/shard_map/slice | solution.py:16
  2.5 3.4 %collective-permute-start.3 = (bf16[20,1,16,720]{3,2,1,0:T(8,128)(2,1)}, bf16[20,1,16,720]{3,2,1,0:T(8,128)(2,1)S(1)}, u32[]{:S(2)}, u32[]{:S(2)}) collective-permute-start(bf16[20,1,16,720]{3,2,1,0:T(8,128)(2,1)} %get-tuple-element.126), channel_id=1, source_target_pairs={{4,0},{8,4},{12,8},{16,12},{20,16},{24,20},{28,24},{0,28},{5,1},{9... | collective-permute-start | bytes 1382408 | tf_op jit(solution)/shard_map/ppermute | solution.py:18
  5.8 0.0 collective-permute-start.2
  5.8 1.1 %fusion.52 = (bf16[20,1,16,720]{3,2,1,0:T(8,128)(2,1)}, bf16[20,1,16,720]{3,2,1,0:T(8,128)(2,1)}) fusion(bf16[20,1,45,720]{3,2,1,0:T(8,128)(2,1)S(1)} %copy-done.2), kind=kLoop, calls=%fused_computation.90 | loop fusion | bytes 1843200 | tf_op jit(solution)/shard_map/slice | solution.py:16
  6.9 2.6 %collective-permute-start.1 = (bf16[20,1,16,720]{3,2,1,0:T(8,128)(2,1)}, bf16[20,1,16,720]{3,2,1,0:T(8,128)(2,1)}, u32[]{:S(2)}, u32[]{:S(2)}) collective-permute-start(bf16[20,1,16,720]{3,2,1,0:T(8,128)(2,1)} %get-tuple-element.128), channel_id=1, source_target_pairs={{4,0},{8,4},{12,8},{16,12},{20,16},{24,20},{28,24},{0,28},{5,1},{9... | collective-permute-start | bytes 1382408 | tf_op jit(solution)/shard_map/ppermute | solution.py:18
  9.6 0.0 collective-permute-start
  9.6 0.1 fusion.50
  9.7 0.6 pad_maximum_fusion.3
  10.3 3.9 %all-to-all-start = ((f32[3,1,8,256]{3,1,0,2:T(1,128)}), f32[3,1,8,256]{3,1,0,2:T(1,128)S(1)}, u32[]{:S(2)}, u32[]{:S(2)}) async-start(f32[3,1,8,256]{3,1,0,2:T(1,128)} %pad_maximum_fusion.3), calls=%async_computation | async-start | bytes 49152 | tf_op jit(solution)/shard_map/all_to_all | solution.py:212
  14.3 0.1 reshape.216
  14.4 0.0 copy-start.4
  14.4 0.0 copy-start.1
  14.4 21.7 %gather_fusion = bf16[3840]{0:T(1024)(128)(2,1)S(1)} fusion(bf16[17]{0:T(256)(128)(2,1)S(1)} %copy-done, s32[4096]{0:T(1024)S(1)} %pad_clamp_fusion), kind=kCustom, calls=%fused_computation | custom fusion | bytes 30720 | tf_op jit(solution)/shard_map/gather | solution.py:44
  36.1 0.1 reshape.215
  36.2 0.7 fusion.55
  36.9 14.6 %fusion.22.blat_ref = bf16[720,720]{1,0:T(8,128)(2,1)} fusion(bf16[]{:T(256)} %bitcast.27, bf16[]{:T(256)} %bitcast.28, bf16[]{:T(256)} %bitcast.29, bf16[]{:T(256)} %bitcast.30, bf16[]{:T(256)} %bitcast.31, bf16[]{:T(256)} %bitcast.33, bf16[]{:T(256)} %bitcast.32, bf16[]{:T(256)} %bitcast.8, bf16[]{:T(256)} %bitcast.10, bf16[]{:T(256)} %bitcast.12, ...), kind=kLoop, calls=%fused_computation.36 | loop fusion | flops 21772800 | bytes 1036834 | tf_op jit(solution)/shard_map/convert_element_type | solution.py:55
  51.5 0.7 select_convert_fusion.blon_ref
  52.2 0.1 pad.12.clone
  52.3 0.0 all-to-all-done
  52.3 0.1 remainder_reduce_fusion
  52.5 0.0 collective-permute-done.3
  52.5 0.0 collective-permute-done.2
  52.5 0.0 collective-permute-done.1
  52.5 0.0 collective-permute-done
  52.5 4.8 %pad_maximum_fusion.1 = (bf16[20,1,80,720]{3,2,1,0:T(8,128)(2,1)}, bf16[20,1,80,720]{3,2,1,0:T(8,128)(2,1)}) fusion(bf16[20,1,16,720]{3,2,1,0:T(8,128)(2,1)S(1)} %collective-permute-done.3, bf16[20,1,16,720]{3,2,1,0:T(8,128)(2,1)} %collective-permute-done.2, bf16[20,1,45,720]{3,2,1,0:T(8,128)(2,1)S(1)} %copy-done.1, bf16[80]{0:T(256)(128)(2,1)S(1)} %pad.12.clone, ...), kind=kLoop, calls=%fused_computation.24 | loop fusion | flops 17280000 | bytes 9043360 | tf_op jit(solution)/shard_map/concatenate | solution.py:28
  57.4 5.4 %shard_map.85 = f32[1,45,720]{2,1,0:T(8,128)} custom-call(bf16[20,1,80,720]{3,2,1,0:T(8,128)(2,1)} %get-tuple-element.152.ext_ref, bf16[20,1,45,720]{3,2,1,0:T(8,128)(2,1)} %pert_ref.1, bf16[48,80]{1,0:T(8,128)(2,1)} %select_convert_fusion.blon_ref, bf16[720,720]{1,0:T(8,128)(2,1)} %fusion.22.blat_ref), custom_call_target="tpu_custom_call" | custom-call | tf_op jit(solution)/shard_map/pallas_call | solution.py:92
  62.7 1.1 %copy.19 = f32[720,45]{1,0:T(8,128)S(1)} copy(f32[720,45]{0,1:T(8,128)} %bitcast.119) | data formatting | bytes 259200 | tf_op jit(solution)/shard_map/while | solution.py:164
  63.8 3.8 %while.21 = (s32[]{:T(128)}, f32[2,1024]{1,0:T(2,128)S(1)}, s32[2,1024]{1,0:T(2,128)S(1)}, s32[2,1024]{1,0:T(2,128)S(1)}, f32[720,45]{1,0:T(8,128)S(1)}, /*index=5*/s32[]{:T(128)}, s32[]{:T(128)}) while((s32[]{:T(128)}, f32[2,1024]{1,0:T(2,128)S(1)}, s32[2,1024]{1,0:T(2,128)S(1)}, s32[2,1024]{1,0:T(2,128)S(1)}, f32[720,45]{1,0:T(8,128)S(1)}, ...), condition=%wide.region_2.3_spmd, body=%wide.region_0.2_spmd.sunk | while | flops 399005696 | bytes 166557 | solution.py:164
  63.9 1.8 %fusion.62 = f32[1024]{0:T(1024)S(1)} fusion(f32[720,45]{1,0:T(8,128)S(1)} %get-tuple-element.248, s32[1024]{0:T(1024)S(1)} %bitcast.126, s32[1024]{0:T(1024)S(1)} %bitcast.127), kind=kOutput, calls=%fused_computation.5.clone.1 | convolution fusion | flops 399005696 | bytes 141888 | tf_op jit(solution)/shard_map/while/body/eval_jaxpr/dot_general | solution.py:156
  65.7 0.1 dynamic_update_slice.5
  65.8 1.8 %fusion.62 = f32[1024]{0:T(1024)S(1)} fusion(f32[720,45]{1,0:T(8,128)S(1)} %get-tuple-element.248, s32[1024]{0:T(1024)S(1)} %bitcast.126, s32[1024]{0:T(1024)S(1)} %bitcast.127), kind=kOutput, calls=%fused_computation.5.clone.1 | convolution fusion | flops 399005696 | bytes 141888 | tf_op jit(solution)/shard_map/while/body/eval_jaxpr/dot_general | solution.py:156
  67.6 0.1 dynamic_update_slice.5
  67.7 12.1 %psum.7 = f32[2048]{0:T(1024)S(1)} all-reduce(f32[2048]{0:T(1024)S(1)} %bitcast.128), channel_id=1, replica_groups=mesh['tile'=8,'mem'=4] {'mem'}, use_global_device_ids=true, to_apply=%region_3.4 | all-reduce | flops 2048 | bytes 16384 | tf_op jit(solution)/shard_map/psum | solution.py:226
  79.8 0.0 copy-done.3
  79.8 3.1 %while.22 = (s32[]{:T(128)}, f32[45,720]{1,0:T(8,128)S(1)}, s32[2,1024]{1,0:T(2,128)S(1)}, f32[2,1024]{1,0:T(2,128)S(1)}, s32[2,1024]{1,0:T(2,128)S(1)}, /*index=5*/s32[]{:T(128)}, s32[]{:T(128)}) while((s32[]{:T(128)}, f32[45,720]{1,0:T(8,128)S(1)}, s32[2,1024]{1,0:T(2,128)S(1)}, f32[2,1024]{1,0:T(2,128)S(1)}, ...), condition=%wide.region_5.6_spmd.clone, body=%wide.region_4.5_spmd.clone.sunk | while | flops 399025440 | bytes 296167 | solution.py:198
  79.9 1.5 %fusion.64 = f32[45,720]{1,0:T(8,128)S(1)} fusion(s32[1024]{0:T(1024)S(1)} %bitcast.124, f32[1024]{0:T(1024)S(1)} %bitcast.122, s32[1024]{0:T(1024)S(1)} %bitcast.125, f32[45,720]{1,0:T(8,128)S(1)} %get-tuple-element.259, pred[]{:T(512)S(6)} %compare.105), kind=kOutput, calls=%fused_computation.12.clone.1 | convolution fusion | flops 399025440 | bytes 271489 | tf_op jit(solution)/shard_map/while/body/eval_jaxpr/dot_general | solution.py:183
  81.4 1.5 %fusion.64 = f32[45,720]{1,0:T(8,128)S(1)} fusion(s32[1024]{0:T(1024)S(1)} %bitcast.124, f32[1024]{0:T(1024)S(1)} %bitcast.122, s32[1024]{0:T(1024)S(1)} %bitcast.125, f32[45,720]{1,0:T(8,128)S(1)} %get-tuple-element.259, pred[]{:T(512)S(6)} %compare.105), kind=kOutput, calls=%fused_computation.12.clone.1 | convolution fusion | flops 399025440 | bytes 271489 | tf_op jit(solution)/shard_map/while/body/eval_jaxpr/dot_general | solution.py:183
  83.0 0.7 collective-permute-start.5
  83.6 0.0 collective-permute-start.4
  83.6 0.1 pad.1.clone
  83.7 1.7 %collective-permute-done.5 = f32[1,16,720]{2,1,0:T(8,128)S(1)} collective-permute-done((f32[1,16,720]{2,1,0:T(8,128)S(1)}, f32[1,16,720]{2,1,0:T(8,128)S(1)}, u32[]{:S(2)}, u32[]{:S(2)}) %collective-permute-start.5) | collective-permute-done | bytes 46112 | tf_op jit(solution)/shard_map/ppermute | solution.py:18
  85.4 3.1 %collective-permute-done.4 = f32[1,16,720]{2,1,0:T(8,128)S(1)} collective-permute-done((f32[1,16,720]{2,1,0:T(8,128)S(1)}, f32[1,16,720]{2,1,0:T(8,128)S(1)}, u32[]{:S(2)}, u32[]{:S(2)}) %collective-permute-start.4) | collective-permute-done | bytes 46112 | tf_op jit(solution)/shard_map/ppermute | solution.py:15
  88.5 0.8 pad_maximum_fusion.2.spread_ref
  89.3 5.9 %shard_map.86 = f32[20,1,45,720]{3,2,1,0:T(8,128)} custom-call(bf16[20,1,80,720]{3,2,1,0:T(8,128)(2,1)} %get-tuple-element.153.pext_ref, f32[1,80,720]{2,1,0:T(8,128)} %pad_maximum_fusion.2.spread_ref, bf16[20,1,45,720]{3,2,1,0:T(8,128)(2,1)} %ctrl_ref.1, bf16[48,80]{1,0:T(8,128)(2,1)} %select_convert_fusion.blon_ref, bf16[720,720]{1,0:T(8,128)(2,1)} %fusion.22.blat_ref), custom_call_target="tpu_custom_call" | custom-call | tf_op jit(solution)/shard_map/pallas_call | solution.py:127
  95.2 6.2 %copy.20 = f32[20,1,45,720]{3,1,2,0:T(1,128)} copy(f32[20,1,45,720]{3,2,1,0:T(8,128)} %shard_map.86) | data formatting | bytes 5184000 | tf_op jit(solution)/shard_map/pallas_call | solution.py:127
  (40 shorter events, 0.3 us)
Async XLA Ops:
  0.0 14.4 %copy-start = (bf16[17]{0:T(256)(128)(2,1)S(1)}, bf16[17]{0:T(256)(128)(2,1)}, u32[]{:S(2)}) copy-start(bf16[17]{0:T(256)(128)(2,1)} %param.14) | copy-start | bytes 106
  0.0 5.8 %copy-start.2 = (bf16[20,1,45,720]{3,2,1,0:T(8,128)(2,1)S(1)}, bf16[20,1,45,720]{3,2,1,0:T(8,128)(2,1)}, u32[]{:S(2)}) copy-start(bf16[20,1,45,720]{3,2,1,0:T(8,128)(2,1)} %pert_ref.1) | copy-start | bytes 3888004
  0.0 9.6 %copy-start.5 = (s32[1,8,256]{2,1,0:T(8,128)S(1)}, s32[1,8,256]{2,1,0:T(8,128)}, u32[]{:S(2)}) copy-start(s32[1,8,256]{2,1,0:T(8,128)} %param.18) | copy-start | bytes 24580
  0.0 9.6 %copy-start.6 = (f32[1,8,256]{2,1,0:T(8,128)S(1)}, f32[1,8,256]{2,1,0:T(8,128)}, u32[]{:S(2)}) copy-start(f32[1,8,256]{2,1,0:T(8,128)} %param.16) | copy-start | bytes 24580
  0.0 9.6 %copy-start.7 = (f32[1,8,256]{2,1,0:T(8,128)S(1)}, f32[1,8,256]{2,1,0:T(8,128)}, u32[]{:S(2)}) copy-start(f32[1,8,256]{2,1,0:T(8,128)} %param.17) | copy-start | bytes 24580
  0.0 9.6 %copy-start.8 = (s32[1,8]{1,0:T(1,128)S(1)}, s32[1,8]{1,0:T(1,128)}, u32[]{:S(2)}) copy-start(s32[1,8]{1,0:T(1,128)} %param.19) | copy-start | bytes 100
  2.5 50.0 %collective-permute-start.3 = (bf16[20,1,16,720]{3,2,1,0:T(8,128)(2,1)}, bf16[20,1,16,720]{3,2,1,0:T(8,128)(2,1)S(1)}, u32[]{:S(2)}, u32[]{:S(2)}) collective-permute-start(bf16[20,1,16,720]{3,2,1,0:T(8,128)(2,1)} %get-tuple-element.126), channel_id=1, source_target_pairs={{4,0},{8,4},{12,8},{16,12},{20,16},{24,20},{28,24},{0,28},{5,1},{9... | collective-permute-start | bytes 1382408 | tf_op jit(solution)/shard_map/ppermute | solution.py:18
  5.8 46.7 %collective-permute-start.2 = (bf16[20,1,16,720]{3,2,1,0:T(8,128)(2,1)}, bf16[20,1,16,720]{3,2,1,0:T(8,128)(2,1)}, u32[]{:S(2)}, u32[]{:S(2)}) collective-permute-start(bf16[20,1,16,720]{3,2,1,0:T(8,128)(2,1)} %get-tuple-element.125), channel_id=1, source_target_pairs={{0,4},{4,8},{8,12},{12,16},{16,20},{20,24},{24,28},{28,0},{1,5},{5... | collective-permute-start | bytes 1382408 | tf_op jit(solution)/shard_map/ppermute | solution.py:15
  6.9 45.6 %collective-permute-start.1 = (bf16[20,1,16,720]{3,2,1,0:T(8,128)(2,1)}, bf16[20,1,16,720]{3,2,1,0:T(8,128)(2,1)}, u32[]{:S(2)}, u32[]{:S(2)}) collective-permute-start(bf16[20,1,16,720]{3,2,1,0:T(8,128)(2,1)} %get-tuple-element.128), channel_id=1, source_target_pairs={{4,0},{8,4},{12,8},{16,12},{20,16},{24,20},{28,24},{0,28},{5,1},{9... | collective-permute-start | bytes 1382408 | tf_op jit(solution)/shard_map/ppermute | solution.py:18
  9.6 43.0 %collective-permute-start = (bf16[20,1,16,720]{3,2,1,0:T(8,128)(2,1)}, bf16[20,1,16,720]{3,2,1,0:T(8,128)(2,1)}, u32[]{:S(2)}, u32[]{:S(2)}) collective-permute-start(bf16[20,1,16,720]{3,2,1,0:T(8,128)(2,1)} %get-tuple-element.127), channel_id=1, source_target_pairs={{0,4},{4,8},{8,12},{12,16},{16,20},{20,24},{24,28},{28,0},{1,5},{5... | collective-permute-start | bytes 1382408 | tf_op jit(solution)/shard_map/ppermute | solution.py:15
  10.3 42.0 %all-to-all-start = ((f32[3,1,8,256]{3,1,0,2:T(1,128)}), f32[3,1,8,256]{3,1,0,2:T(1,128)S(1)}, u32[]{:S(2)}, u32[]{:S(2)}) async-start(f32[3,1,8,256]{3,1,0,2:T(1,128)} %pad_maximum_fusion.3), calls=%async_computation | async-start | bytes 49152 | tf_op jit(solution)/shard_map/all_to_all | solution.py:212
  14.4 21.8 %copy-start.4 = (bf16[17]{0:T(256)(128)(2,1)S(1)}, bf16[17]{0:T(256)(128)(2,1)}, u32[]{:S(2)}) copy-start(bf16[17]{0:T(256)(128)(2,1)} %param.15) | copy-start | bytes 106
  14.4 38.1 %copy-start.1 = (bf16[20,1,45,720]{3,2,1,0:T(8,128)(2,1)S(1)}, bf16[20,1,45,720]{3,2,1,0:T(8,128)(2,1)}, u32[]{:S(2)}) copy-start(bf16[20,1,45,720]{3,2,1,0:T(8,128)(2,1)} %ctrl_ref.1) | copy-start | bytes 3888004
  63.8 16.0 %copy-start.3 = (f32[45,720]{1,0:T(8,128)S(1)}, f32[45,720]{1,0:T(8,128)}, u32[]{:S(2)}) copy-start(f32[45,720]{1,0:T(8,128)} %custom-call) | copy-start | bytes 388804
  83.0 2.4 %collective-permute-start.5 = (f32[1,16,720]{2,1,0:T(8,128)S(1)}, f32[1,16,720]{2,1,0:T(8,128)S(1)}, u32[]{:S(2)}, u32[]{:S(2)}) collective-permute-start(f32[1,16,720]{2,1,0:T(8,128)S(1)} %get-tuple-element.130), channel_id=1, source_target_pairs={{4,0},{8,4},{12,8},{16,12},{20,16},{24,20},{28,24},{0,28},{5,1},{9... | collective-permute-start | bytes 138248 | tf_op jit(solution)/shard_map/ppermute | solution.py:18
  83.6 4.9 %collective-permute-start.4 = (f32[1,16,720]{2,1,0:T(8,128)S(1)}, f32[1,16,720]{2,1,0:T(8,128)S(1)}, u32[]{:S(2)}, u32[]{:S(2)}) collective-permute-start(f32[1,16,720]{2,1,0:T(8,128)S(1)} %get-tuple-element.129), channel_id=1, source_target_pairs={{0,4},{4,8},{8,12},{12,16},{16,20},{20,24},{24,28},{28,0},{1,5},{5... | collective-permute-start | bytes 138248 | tf_op jit(solution)/shard_map/ppermute | solution.py:15

commit v2 on v1

--- a/solution.py
+++ b/solution.py
@@ -17,15 +17,6 @@
     )
     high = lax.ppermute(lax.slice_in_dim(block, 0, width, axis=dim), axis, backward)
     return low, high
-
-
-def extend(block, low, high, dim, padded):
-    pad_shape = list(block.shape)
-    pad_shape[dim] = padded - block.shape[dim]
-    parts = [block]
-    if pad_shape[dim] > 0:
-        parts.append(jnp.zeros(pad_shape, block.dtype))
-    return jnp.concatenate(parts + [low, high], axis=dim)
 
 
 def lon_band(tap_weights, lon_cells, padded):
@@ -41,7 +32,14 @@
     )
     valid = (rows < lon_cells) & ((cols < lon_cells) | (cols >= padded))
     dist = jnp.abs(source - rows)
-    band = jnp.where(valid & (dist <= radius), taps[jnp.minimum(dist, radius)], 0.0)
+    dist = jnp.where(valid, dist, radius + 1)
+    return band_from(dist, taps)
+
+
+def band_from(dist, taps):
+    band = jnp.zeros(dist.shape, jnp.float32)
+    for offset in range(taps.shape[0]):
+        band = jnp.where(dist == offset, taps[offset], band)
     return band.astype(jnp.bfloat16)
 
 
@@ -50,9 +48,7 @@
     taps = tap_weights.astype(jnp.float32)
     rows = lax.broadcasted_iota(jnp.int32, (lat_cells, lat_cells), 0)
     cols = lax.broadcasted_iota(jnp.int32, (lat_cells, lat_cells), 1)
-    dist = jnp.abs(rows - cols)
-    band = jnp.where(dist <= radius, taps[jnp.minimum(dist, radius)], 0.0)
-    return band.astype(jnp.bfloat16)
+    return band_from(jnp.abs(rows - cols), taps)
 
 
 def member_chunk(members):
@@ -62,17 +58,27 @@
     return 1
 
 
-def forward_sum(ext_control, perturb, band_lon, band_lat):
-    members, levels, ext_cells, lat_cells = ext_control.shape
-    lon_cells = perturb.shape[2]
-    padded = band_lon.shape[0]
+def fill_ext(ext_ref, local, low, high, lon_cells, padded):
+    radius = low.shape[0]
+    base = (lon_cells // 16) * 16
+    ext_ref[base:padded, :] = jnp.zeros((padded - base, ext_ref.shape[1]), ext_ref.dtype)
+    ext_ref[0:lon_cells, :] = local
+    ext_ref[padded:padded + radius, :] = low
+    ext_ref[padded + radius:padded + 2 * radius, :] = high
+
+
+def forward_sum(control, c_low, c_high, perturb, band_lon, band_lat):
+    members, levels, lon_cells, lat_cells = control.shape
+    radius = c_low.shape[2]
+    padded, ext_cells = band_lon.shape
     chunk = member_chunk(members)
 
-    def kernel(ext_ref, pert_ref, blon_ref, blat_ref, out_ref, along_ref):
+    def kernel(ctrl_ref, low_ref, high_ref, pert_ref, blon_ref, blat_ref, out_ref, ext_ref, along_ref):
         step = pl.program_id(1)
         blon = blon_ref[...]
         for m in range(chunk):
-            along = jnp.dot(blon, ext_ref[m], preferred_element_type=jnp.float32)
+            fill_ext(ext_ref, ctrl_ref[m], low_ref[m], high_ref[m], lon_cells, padded)
+            along = jnp.dot(blon, ext_ref[...], preferred_element_type=jnp.float32)
             along_ref[m * padded:(m + 1) * padded, :] = along.astype(jnp.bfloat16)
         smoothed = jnp.dot(along_ref[...], blat_ref[...], preferred_element_type=jnp.float32)
         total = pert_ref[0].astype(jnp.float32) * smoothed[0:lon_cells]
@@ -89,34 +95,51 @@
         def _():
             out_ref[...] = out_ref[...] + total
 
+    field = pl.BlockSpec((chunk, None, lon_cells, lat_cells), lambda l, g: (g, l, 0, 0))
+    halo = pl.BlockSpec((chunk, None, radius, lat_cells), lambda l, g: (g, l, 0, 0))
     return pl.pallas_call(
         kernel,
         grid=(levels, members // chunk),
         in_specs=[
-            pl.BlockSpec((chunk, None, ext_cells, lat_cells), lambda l, g: (g, l, 0, 0)),
-            pl.BlockSpec((chunk, None, lon_cells, lat_cells), lambda l, g: (g, l, 0, 0)),
+            field,
+            halo,
+            halo,
+            field,
             pl.BlockSpec(band_lon.shape, lambda l, g: (0, 0)),
             pl.BlockSpec(band_lat.shape, lambda l, g: (0, 0)),
         ],
         out_specs=pl.BlockSpec((None, lon_cells, lat_cells), lambda l, g: (l, 0, 0)),
         out_shape=jax.ShapeDtypeStruct((levels, lon_cells, lat_cells), jnp.float32),
-        scratch_shapes=[pltpu.VMEM((chunk * padded, lat_cells), jnp.bfloat16)],
+        scratch_shapes=[
+            pltpu.VMEM((ext_cells, lat_cells), jnp.bfloat16),
+            pltpu.VMEM((chunk * padded, lat_cells), jnp.bfloat16),
+        ],
         compiler_params=pltpu.CompilerParams(dimension_semantics=("arbitrary", "arbitrary")),
-    )(ext_control, perturb, band_lon, band_lat)
-
-
-def backward_grad(ext_perturb, ext_spread, control, band_lon, band_lat):
-    members, levels, ext_cells, lat_cells = ext_perturb.shape
-    lon_cells = control.shape[2]
-    padded = band_lon.shape[0]
+    )(control, c_low, c_high, perturb, band_lon, band_lat)
+
+
+def backward_grad(perturb, p_low, p_high, spread, s_low, s_high, control, band_lon, band_lat):
+    members, levels, lon_cells, lat_cells = control.shape
+    radius = p_low.shape[2]
+    padded, ext_cells = band_lon.shape
     chunk = member_chunk(members)
 
-    def kernel(pext_ref, spread_ref, ctrl_ref, blon_ref, blat_ref, out_ref, along_ref):
+    def kernel(pert_ref, plow_ref, phigh_ref, spread_ref, slow_ref, shigh_ref, ctrl_ref,
+               blon_ref, blat_ref, out_ref, ext_ref, along_ref):
         blon = blon_ref[...]
         spread = spread_ref[...]
+        s_lo = slow_ref[...]
+        s_hi = shigh_ref[...]
         for m in range(chunk):
-            weighted = (pext_ref[m].astype(jnp.float32) * spread).astype(jnp.bfloat16)
-            along = jnp.dot(blon, weighted, preferred_element_type=jnp.float32)
+            fill_ext(
+                ext_ref,
+                (pert_ref[m].astype(jnp.float32) * spread).astype(jnp.bfloat16),
+                (plow_ref[m].astype(jnp.float32) * s_lo).astype(jnp.bfloat16),
+                (phigh_ref[m].astype(jnp.float32) * s_hi).astype(jnp.bfloat16),
+                lon_cells,
+                padded,
+            )
+            along = jnp.dot(blon, ext_ref[...], preferred_element_type=jnp.float32)
             along_ref[m * padded:(m + 1) * padded, :] = along.astype(jnp.bfloat16)
         smoothed = jnp.dot(along_ref[...], blat_ref[...], preferred_element_type=jnp.float32)
         for m in range(chunk):
@@ -124,21 +147,33 @@
                 m * padded:m * padded + lon_cells
             ]
 
-    return pl.pallas_call(
+    field = pl.BlockSpec((chunk, None, lon_cells, lat_cells), lambda l, g: (g, l, 0, 0))
+    halo = pl.BlockSpec((chunk, None, radius, lat_cells), lambda l, g: (g, l, 0, 0))
+    level_field = pl.BlockSpec((None, lon_cells, lat_cells), lambda l, g: (l, 0, 0))
+    level_halo = pl.BlockSpec((None, radius, lat_cells), lambda l, g: (l, 0, 0))
+    out = pl.pallas_call(
         kernel,
         grid=(levels, members // chunk),
         in_specs=[
-            pl.BlockSpec((chunk, None, ext_cells, lat_cells), lambda l, g: (g, l, 0, 0)),
-            pl.BlockSpec((None, ext_cells, lat_cells), lambda l, g: (l, 0, 0)),
-            pl.BlockSpec((chunk, None, lon_cells, lat_cells), lambda l, g: (g, l, 0, 0)),
+            field,
+            halo,
+            halo,
+            level_field,
+            level_halo,
+            level_halo,
+            field,
             pl.BlockSpec(band_lon.shape, lambda l, g: (0, 0)),
             pl.BlockSpec(band_lat.shape, lambda l, g: (0, 0)),
         ],
-        out_specs=pl.BlockSpec((chunk, None, lon_cells, lat_cells), lambda l, g: (g, l, 0, 0)),
-        out_shape=jax.ShapeDtypeStruct(control.shape, jnp.float32),
-        scratch_shapes=[pltpu.VMEM((chunk * padded, lat_cells), jnp.bfloat16)],
-        compiler_params=pltpu.CompilerParams(dimension_semantics=("parallel", "parallel")),
-    )(ext_perturb, ext_spread, control, band_lon, band_lat)
+        out_specs=pl.BlockSpec((chunk, lon_cells, None, lat_cells), lambda l, g: (g, 0, l, 0)),
+        out_shape=jax.ShapeDtypeStruct((members, lon_cells, levels, lat_cells), jnp.float32),
+        scratch_shapes=[
+            pltpu.VMEM((ext_cells, lat_cells), jnp.bfloat16),
+            pltpu.VMEM((chunk * padded, lat_cells), jnp.bfloat16),
+        ],
+        compiler_params=pltpu.CompilerParams(dimension_semantics=("arbitrary", "arbitrary")),
+    )(perturb, p_low, p_high, spread, s_low, s_high, control, band_lon, band_lat)
+    return jnp.transpose(out, (0, 2, 1, 3))
 
 
 def pick_cells(field_rows, row_index, col_index, block_rows):
@@ -220,17 +255,16 @@
 
     c_low, c_high = halos(control, "tile", 2, radius)
     p_low, p_high = halos(perturb, "tile", 2, radius)
-    ext_control = extend(control, c_low, c_high, 2, padded)
-    member_sum = forward_sum(ext_control, perturb, band_lon, band_lat)
+    member_sum = forward_sum(control, c_low, c_high, perturb, band_lon, band_lat)
     partial = pick_cells(member_sum.reshape(row_count, lat_cells), row_index, col_index, block_rows)
     at_cells = lax.psum(partial, "mem")
     misfit = weight_recv * (at_cells - observed)
     spread = spread_cells(misfit, row_index, col_index, row_count, lat_cells, block_rows)
     spread = spread.reshape(levels, lon_cells, lat_cells)
     s_low, s_high = halos(spread, "tile", 1, radius)
-    ext_spread = extend(spread, s_low, s_high, 1, padded)
-    ext_perturb = extend(perturb, p_low, p_high, 2, padded)
-    return backward_grad(ext_perturb, ext_spread, control, band_lon, band_lat)
+    return backward_grad(
+        perturb, p_low, p_high, spread, s_low, s_high, control, band_lon, band_lat
+    )
 
 
 def solution(mesh):

time: 102 us -> 83.2 us (0.82)
  local copies, waits for them, and re-layouts: 33.8 us -> 8.25 us
  other arithmetic: 21.8 us -> 27.7 us
    gather x3 -> x0, local copies, waits for them, and re-layouts: 22.5 us -> none  [the longest x2 21.8 us: lon_band(): taps[jnp.minimum(dist, radius)]]
    convert_element_type x2, other arithmetic: 15.2 us -> 25.4 us  [band_from(): return band.astype(jnp.bfloat16)]
    pallas_call x1 -> x0, local copies, waits for them, and re-layouts: 6.21 us -> none  [backward_grad(): pl.pallas_call(kernel, grid=(levels, members // chunk), in_specs=[pl.Bloc...]
    concatenate x2 -> x0, other arithmetic: 5.61 us -> none  [extend(): return jnp.concatenate(parts + [low, high], axis=dim)]
    unnamed x19, local copies, waits for them, and re-layouts: 0.04 us -> 2.2 us
    all_to_all x1, starting transfers between devices: 3.9 us -> 5.2 us  [local(): lax.all_to_all(lists, 'tile', split_axis=2, concat_axis=1, tiled=True)]
    slice x3 -> x5, local copies, waits for them, and re-layouts: 3.52 us -> 3.92 us  [the longest x3 2.48 us: halos(): lax.slice_in_dim(block, 0, width, axis=dim)]
  transfers between devices with their start and end apart: 7 -> 7, of which waited for: 2 -> 2; matrix products, arithmetic and copies ran while one was open for 39% -> 45% of each run, Pallas kernels for 0% -> 7%
where the time goes in v2:
time: 83.2 us; the launch traced here: 82.4 us
  other arithmetic  27.7 us (33%)
  blocking collectives  12.1 us (15%)
  Pallas kernels  11.8 us (14%)
  starting transfers between devices  11.2 us (13%)
  local copies, waits for them, and re-layouts  8.25 us (10%)
  matrix products  6.57 us (8%)
  waiting for transfers between devices  4.39 us (5%)
    convert_element_type x2, other arithmetic, band_from(): return band.astype(jnp.bfloat16)  25.4 us
    psum x1, blocking collectives, local(): at_cells = lax.psum(partial, 'mem')  12.1 us
    pallas_call x1, Pallas kernels, backward_grad(): pl.pallas_call(kernel, grid=(levels, members // chunk), in_specs=[field,...  6.31 us
    ppermute x3, starting transfers between devices, halos(): lax.ppermute(lax.slice_in_dim(block, 0, width, axis=dim), axis, backward)  6.01 us
    pallas_call x1, Pallas kernels, forward_sum(): pl.pallas_call(kernel, grid=(levels, members // chunk), in_specs=[field,...  5.53 us
    all_to_all x1, starting transfers between devices, local(): lax.all_to_all(lists, 'tile', split_axis=2, concat_axis=1, tiled=True)  5.2 us
    dot_general x2, matrix products, pick_one_block(): jnp.dot(onehot_cols, field_cols, precision=lax.Precision.HIGHEST, preferr...  3.59 us
    dot_general x2, matrix products, spread_one_block(): jnp.dot(weighted.T, onehot_cols, precision=lax.Precision.HIGHEST, preferr...  2.98 us
  transfers between devices with their start and end apart: 7, of which 2 were waited for; matrix products, arithmetic and copies ran while one was open for 45% of the time, Pallas kernels for 7%

profile of v2, /device:TPU:0, one launch (start us, length us, event | category | flops | bytes accessed | tf_op | source)
XLA Modules:
  0.0 82.4 jit_solution(494797289047823143)
XLA Ops:
  0.0 0.8 stack.12
  0.8 0.7 convert_element_type.31
  1.5 0.8 fusion.46
  2.3 0.6 pad_maximum_fusion
  2.9 5.2 %all-to-all-start = ((f32[3,1,8,256]{3,1,0,2:T(1,128)}), f32[3,1,8,256]{3,1,0,2:T(1,128)S(1)}, u32[]{:S(2)}, u32[]{:S(2)}) async-start(f32[3,1,8,256]{3,1,0,2:T(1,128)} %pad_maximum_fusion), calls=%async_computation | async-start | bytes 49152 | tf_op jit(solution)/shard_map/all_to_all | solution.py:247
  8.1 2.3 %fusion.47 = (bf16[20,1,16,720]{3,2,1,0:T(8,128)(2,1)}, bf16[20,1,16,720]{3,2,1,0:T(8,128)(2,1)}) fusion(bf16[20,1,45,720]{3,2,1,0:T(8,128)(2,1)} %ctrl_ref.3), kind=kLoop, calls=%fused_computation.78 | loop fusion | bytes 1843200 | tf_op jit(solution)/shard_map/slice | solution.py:18
  10.5 2.6 %collective-permute-start.3 = (bf16[20,1,16,720]{3,2,1,0:T(8,128)(2,1)}, bf16[20,1,16,720]{3,2,1,0:T(8,128)(2,1)S(1)}, u32[]{:S(2)}, u32[]{:S(2)}) collective-permute-start(bf16[20,1,16,720]{3,2,1,0:T(8,128)(2,1)} %get-tuple-element.120), channel_id=1, source_target_pairs={{4,0},{8,4},{12,8},{16,12},{20,16},{24,20},{28,24},{0,28},{5,1},{9... | collective-permute-start | bytes 1382408 | tf_op jit(solution)/shard_map/ppermute | solution.py:18
  13.1 0.0 collective-permute-start.2
  13.1 0.0 copy-done
  13.1 0.1 fusion.48
  13.2 2.7 %collective-permute-start.1 = (bf16[20,1,16,720]{3,2,1,0:T(8,128)(2,1)S(1)}, bf16[20,1,16,720]{3,2,1,0:T(8,128)(2,1)S(1)}, u32[]{:S(2)}, u32[]{:S(2)}) collective-permute-start(bf16[20,1,16,720]{3,2,1,0:T(8,128)(2,1)S(1)} %get-tuple-element.122), channel_id=1, source_target_pairs={{4,0},{8,4},{12,8},{16,12},{20,16},{24,20},{28,24},{0,28},{5,1},{9... | collective-permute-start | bytes 1382408 | tf_op jit(solution)/shard_map/ppermute | solution.py:18
  15.9 0.0 collective-permute-start
  16.0 0.0 copy-done.5
  16.0 0.7 fusion.52
  16.7 0.0 copy-done.6
  16.7 0.7 fusion.51
  17.4 14.3 %select_convert_fusion.blat_ref = bf16[720,720]{1,0:T(8,128)(2,1)} fusion(bf16[]{:T(256)} %bitcast.40, bf16[]{:T(256)} %bitcast.39, bf16[]{:T(256)} %bitcast.38, bf16[]{:T(256)} %bitcast.37, bf16[]{:T(256)} %bitcast.36, bf16[]{:T(256)} %bitcast.35, bf16[]{:T(256)} %bitcast.34, bf16[]{:T(256)} %bitcast.33, bf16[]{:T(256)} %bitcast.32, bf16[]{:T(256)} %bitcast.31, ...), kind=kLoop, calls=%fused_computation.21 | loop fusion | flops 18662400 | bytes 1036834 | tf_op jit(solution)/shard_map/convert_element_type | solution.py:43
  31.8 11.1 %select_convert_fusion.1.blon_ref = bf16[48,80]{1,0:T(8,128)(2,1)} fusion(bf16[]{:T(256)} %bitcast.23, bf16[]{:T(256)} %bitcast.22, bf16[]{:T(256)} %bitcast.21, bf16[]{:T(256)} %bitcast.20, bf16[]{:T(256)} %bitcast.19, bf16[]{:T(256)} %bitcast.18, bf16[]{:T(256)} %bitcast.17, bf16[]{:T(256)} %bitcast.16, bf16[]{:T(256)} %bitcast.15, bf16[]{:T(256)} %bitcast.14, ...), kind=kLoop, calls=%fused_computation.43 | loop fusion | flops 153600 | bytes 8642 | tf_op jit(solution)/shard_map/convert_element_type | solution.py:43
  42.9 0.0 all-to-all-done
  42.9 0.1 remainder_reduce_fusion
  43.1 0.0 collective-permute-done.3.high_ref
  43.1 0.0 copy-start.3
  43.1 0.0 collective-permute-done.2.low_ref
  43.1 0.8 copy-done.3
  43.9 0.8 copy-done.4
  44.7 5.5 %shard_map.85 = f32[1,45,720]{2,1,0:T(8,128)} custom-call(bf16[20,1,45,720]{3,2,1,0:T(8,128)(2,1)} %ctrl_ref.3, bf16[20,1,16,720]{3,2,1,0:T(8,128)(2,1)} %copy-done.4, bf16[20,1,16,720]{3,2,1,0:T(8,128)(2,1)} %copy-done.3, bf16[20,1,45,720]{3,2,1,0:T(8,128)(2,1)} %pert_ref.3, bf16[48,80]{1,0:T(8,128)(2,1)} %select_convert_fusion.1.blon_ref, ...), custom_call_target="tpu_custom_call" | custom-call | tf_op jit(solution)/shard_map/pallas_call | solution.py:100
  50.2 1.1 %copy.15 = f32[720,45]{1,0:T(8,128)S(1)} copy(f32[720,45]{0,1:T(8,128)} %bitcast.71) | data formatting | bytes 259200 | tf_op jit(solution)/shard_map/while | solution.py:199
  51.3 3.8 %while.21 = (s32[]{:T(128)}, f32[2,1024]{1,0:T(2,128)S(1)}, s32[2,1024]{1,0:T(2,128)S(1)}, s32[2,1024]{1,0:T(2,128)S(1)}, f32[720,45]{1,0:T(8,128)S(1)}, /*index=5*/s32[]{:T(128)}, s32[]{:T(128)}) while((s32[]{:T(128)}, f32[2,1024]{1,0:T(2,128)S(1)}, s32[2,1024]{1,0:T(2,128)S(1)}, s32[2,1024]{1,0:T(2,128)S(1)}, f32[720,45]{1,0:T(8,128)S(1)}, ...), condition=%wide.region_2.3_spmd, body=%wide.region_0.2_spmd.sunk | while | flops 399005696 | bytes 166557 | solution.py:199
  51.3 1.8 %fusion.59 = f32[1024]{0:T(1024)S(1)} fusion(f32[720,45]{1,0:T(8,128)S(1)} %get-tuple-element.258, s32[1024]{0:T(1024)S(1)} %bitcast.78, s32[1024]{0:T(1024)S(1)} %bitcast.79), kind=kOutput, calls=%fused_computation.4.clone.1 | convolution fusion | flops 399005696 | bytes 141888 | tf_op jit(solution)/shard_map/while/body/eval_jaxpr/dot_general | solution.py:191
  53.1 0.1 dynamic_update_slice.5
  53.2 1.8 %fusion.59 = f32[1024]{0:T(1024)S(1)} fusion(f32[720,45]{1,0:T(8,128)S(1)} %get-tuple-element.258, s32[1024]{0:T(1024)S(1)} %bitcast.78, s32[1024]{0:T(1024)S(1)} %bitcast.79), kind=kOutput, calls=%fused_computation.4.clone.1 | convolution fusion | flops 399005696 | bytes 141888 | tf_op jit(solution)/shard_map/while/body/eval_jaxpr/dot_general | solution.py:191
  55.0 0.1 dynamic_update_slice.5
  55.1 12.1 %psum.7 = f32[2048]{0:T(1024)S(1)} all-reduce(f32[2048]{0:T(1024)S(1)} %bitcast.80), channel_id=1, replica_groups=mesh['tile'=8,'mem'=4] {'mem'}, use_global_device_ids=true, to_apply=%region_3.4 | all-reduce | flops 2048 | bytes 16384 | tf_op jit(solution)/shard_map/psum | solution.py:260
  67.3 3.1 %while.22 = (s32[]{:T(128)}, f32[45,720]{1,0:T(8,128)S(1)}, s32[2,1024]{1,0:T(2,128)S(1)}, f32[2,1024]{1,0:T(2,128)S(1)}, s32[2,1024]{1,0:T(2,128)S(1)}, /*index=5*/s32[]{:T(128)}, s32[]{:T(128)}) while((s32[]{:T(128)}, f32[45,720]{1,0:T(8,128)S(1)}, s32[2,1024]{1,0:T(2,128)S(1)}, f32[2,1024]{1,0:T(2,128)S(1)}, ...), condition=%wide.region_5.6_spmd.clone, body=%wide.region_4.5_spmd.clone.sunk | while | flops 399025440 | bytes 296167 | solution.py:233
  67.3 1.5 %fusion.61 = f32[45,720]{1,0:T(8,128)S(1)} fusion(s32[1024]{0:T(1024)S(1)} %bitcast.76, f32[1024]{0:T(1024)S(1)} %bitcast.74, s32[1024]{0:T(1024)S(1)} %bitcast.77, f32[45,720]{1,0:T(8,128)S(1)} %get-tuple-element.269, pred[]{:T(512)S(6)} %compare.3), kind=kOutput, calls=%fused_computation.11.clone.1 | convolution fusion | flops 399025440 | bytes 271489 | tf_op jit(solution)/shard_map/while/body/eval_jaxpr/dot_general | solution.py:218
  68.9 1.5 %fusion.61 = f32[45,720]{1,0:T(8,128)S(1)} fusion(s32[1024]{0:T(1024)S(1)} %bitcast.76, f32[1024]{0:T(1024)S(1)} %bitcast.74, s32[1024]{0:T(1024)S(1)} %bitcast.77, f32[45,720]{1,0:T(8,128)S(1)} %get-tuple-element.269, pred[]{:T(512)S(6)} %compare.3), kind=kOutput, calls=%fused_computation.11.clone.1 | convolution fusion | flops 399025440 | bytes 271489 | tf_op jit(solution)/shard_map/while/body/eval_jaxpr/dot_general | solution.py:218
  70.4 0.7 collective-permute-start.5
  71.1 0.0 collective-permute-start.4
  71.1 0.0 collective-permute-done.1.phigh_ref
  71.1 0.0 collective-permute-done.plow_ref
  71.1 0.0 copy-start.2
  71.1 1.7 %collective-permute-done.5.shigh_ref = f32[1,16,720]{2,1,0:T(8,128)S(1)} collective-permute-done((f32[1,16,720]{2,1,0:T(8,128)S(1)}, f32[1,16,720]{2,1,0:T(8,128)S(1)}, u32[]{:S(2)}, u32[]{:S(2)}) %collective-permute-start.5) | collective-permute-done | bytes 46112 | tf_op jit(solution)/shard_map/ppermute | solution.py:18
  72.8 2.7 %collective-permute-done.4.slow_ref = f32[1,16,720]{2,1,0:T(8,128)S(1)} collective-permute-done((f32[1,16,720]{2,1,0:T(8,128)S(1)}, f32[1,16,720]{2,1,0:T(8,128)S(1)}, u32[]{:S(2)}, u32[]{:S(2)}) %collective-permute-start.4) | collective-permute-done | bytes 46112 | tf_op jit(solution)/shard_map/ppermute | solution.py:15
  75.5 0.0 copy-done.1
  75.5 0.0 copy-done.2
  75.5 0.0 copy-done.7
  75.5 0.6 copy-done.8
  76.1 6.3 %shard_map.86 = f32[20,45,1,720]{3,2,1,0:T(1,128)} custom-call(bf16[20,1,45,720]{3,2,1,0:T(8,128)(2,1)} %pert_ref.3, bf16[20,1,16,720]{3,2,1,0:T(8,128)(2,1)} %copy-done.2, bf16[20,1,16,720]{3,2,1,0:T(8,128)(2,1)} %copy-done.1, f32[1,45,720]{2,1,0:T(8,128)S(1)} %bitcast.73, f32[1,16,720]{2,1,0:T(8,128)} %copy-done.8, f32[1,16,720]{2,1,0:T(8,128)} %copy-done.7, ...), custom_call_target="tpu_custom_call" | custom-call | tf_op jit(solution)/shard_map/pallas_call | solution.py:154
  (29 shorter events, 0.2 us)
Async XLA Ops:
  0.0 13.1 %copy-start = (bf16[20,1,45,720]{3,2,1,0:T(8,128)(2,1)S(1)}, bf16[20,1,45,720]{3,2,1,0:T(8,128)(2,1)}, u32[]{:S(2)}) copy-start(bf16[20,1,45,720]{3,2,1,0:T(8,128)(2,1)} %pert_ref.3) | copy-start | bytes 3888004
  2.9 39.9 %all-to-all-start = ((f32[3,1,8,256]{3,1,0,2:T(1,128)}), f32[3,1,8,256]{3,1,0,2:T(1,128)S(1)}, u32[]{:S(2)}, u32[]{:S(2)}) async-start(f32[3,1,8,256]{3,1,0,2:T(1,128)} %pad_maximum_fusion), calls=%async_computation | async-start | bytes 49152 | tf_op jit(solution)/shard_map/all_to_all | solution.py:247
  10.4 5.5 %copy-start.5 = (bf16[17]{0:T(256)(128)(2,1)S(1)}, bf16[17]{0:T(256)(128)(2,1)}, u32[]{:S(2)}) copy-start(bf16[17]{0:T(256)(128)(2,1)} %param.14) | copy-start | bytes 106
  10.4 6.3 %copy-start.6 = (bf16[17]{0:T(256)(128)(2,1)S(1)}, bf16[17]{0:T(256)(128)(2,1)}, u32[]{:S(2)}) copy-start(bf16[17]{0:T(256)(128)(2,1)} %param.15) | copy-start | bytes 106
  10.5 32.6 %collective-permute-start.3 = (bf16[20,1,16,720]{3,2,1,0:T(8,128)(2,1)}, bf16[20,1,16,720]{3,2,1,0:T(8,128)(2,1)S(1)}, u32[]{:S(2)}, u32[]{:S(2)}) collective-permute-start(bf16[20,1,16,720]{3,2,1,0:T(8,128)(2,1)} %get-tuple-element.120), channel_id=1, source_target_pairs={{4,0},{8,4},{12,8},{16,12},{20,16},{24,20},{28,24},{0,28},{5,1},{9... | collective-permute-start | bytes 1382408 | tf_op jit(solution)/shard_map/ppermute | solution.py:18
  13.1 30.0 %collective-permute-start.2 = (bf16[20,1,16,720]{3,2,1,0:T(8,128)(2,1)}, bf16[20,1,16,720]{3,2,1,0:T(8,128)(2,1)S(1)}, u32[]{:S(2)}, u32[]{:S(2)}) collective-permute-start(bf16[20,1,16,720]{3,2,1,0:T(8,128)(2,1)} %get-tuple-element.121), channel_id=1, source_target_pairs={{0,4},{4,8},{8,12},{12,16},{16,20},{20,24},{24,28},{28,0},{1,5},{5... | collective-permute-start | bytes 1382408 | tf_op jit(solution)/shard_map/ppermute | solution.py:15
  13.2 57.8 %collective-permute-start.1 = (bf16[20,1,16,720]{3,2,1,0:T(8,128)(2,1)S(1)}, bf16[20,1,16,720]{3,2,1,0:T(8,128)(2,1)S(1)}, u32[]{:S(2)}, u32[]{:S(2)}) collective-permute-start(bf16[20,1,16,720]{3,2,1,0:T(8,128)(2,1)S(1)} %get-tuple-element.122), channel_id=1, source_target_pairs={{4,0},{8,4},{12,8},{16,12},{20,16},{24,20},{28,24},{0,28},{5,1},{9... | collective-permute-start | bytes 1382408 | tf_op jit(solution)/shard_map/ppermute | solution.py:18
  15.9 55.1 %collective-permute-start = (bf16[20,1,16,720]{3,2,1,0:T(8,128)(2,1)S(1)}, bf16[20,1,16,720]{3,2,1,0:T(8,128)(2,1)S(1)}, u32[]{:S(2)}, u32[]{:S(2)}) collective-permute-start(bf16[20,1,16,720]{3,2,1,0:T(8,128)(2,1)S(1)} %get-tuple-element.123), channel_id=1, source_target_pairs={{0,4},{4,8},{8,12},{12,16},{16,20},{20,24},{24,28},{28,0},{1,5},{5... | collective-permute-start | bytes 1382408 | tf_op jit(solution)/shard_map/ppermute | solution.py:15
  43.1 0.8 copy-start.3
  43.9 0.8 copy-start.4
  70.4 2.4 %collective-permute-start.5 = (f32[1,16,720]{2,1,0:T(8,128)S(1)}, f32[1,16,720]{2,1,0:T(8,128)S(1)}, u32[]{:S(2)}, u32[]{:S(2)}) collective-permute-start(f32[1,16,720]{2,1,0:T(8,128)S(1)} %get-tuple-element.124), channel_id=1, source_target_pairs={{4,0},{8,4},{12,8},{16,12},{20,16},{24,20},{28,24},{0,28},{5,1},{9... | collective-permute-start | bytes 138248 | tf_op jit(solution)/shard_map/ppermute | solution.py:18
  71.1 4.4 %collective-permute-start.4 = (f32[1,16,720]{2,1,0:T(8,128)S(1)}, f32[1,16,720]{2,1,0:T(8,128)S(1)}, u32[]{:S(2)}, u32[]{:S(2)}) collective-permute-start(f32[1,16,720]{2,1,0:T(8,128)S(1)} %get-tuple-element.125), channel_id=1, source_target_pairs={{0,4},{4,8},{8,12},{12,16},{16,20},{20,24},{24,28},{28,0},{1,5},{5... | collective-permute-start | bytes 138248 | tf_op jit(solution)/shard_map/ppermute | solution.py:15
  71.1 4.4 %copy-start.1 = (bf16[20,1,16,720]{3,2,1,0:T(8,128)(2,1)}, bf16[20,1,16,720]{3,2,1,0:T(8,128)(2,1)S(1)}, u32[]{:S(2)}) copy-start(bf16[20,1,16,720]{3,2,1,0:T(8,128)(2,1)S(1)} %collective-permute-done.1.phigh_ref) | copy-start | bytes 1382404
  71.1 4.4 %copy-start.2 = (bf16[20,1,16,720]{3,2,1,0:T(8,128)(2,1)}, bf16[20,1,16,720]{3,2,1,0:T(8,128)(2,1)S(1)}, u32[]{:S(2)}) copy-start(bf16[20,1,16,720]{3,2,1,0:T(8,128)(2,1)S(1)} %collective-permute-done.plow_ref) | copy-start | bytes 1382404
  72.8 2.7 %copy-start.7 = (f32[1,16,720]{2,1,0:T(8,128)}, f32[1,16,720]{2,1,0:T(8,128)S(1)}, u32[]{:S(2)}) copy-start(f32[1,16,720]{2,1,0:T(8,128)S(1)} %collective-permute-done.5.shigh_ref) | copy-start | bytes 138244
  75.5 0.6 copy-start.8

commit v3 on v2

--- a/solution.py
+++ b/solution.py
@@ -19,36 +19,61 @@
     return low, high
 
 
-def lon_band(tap_weights, lon_cells, padded):
-    radius = tap_weights.shape[0] - 1
-    taps = tap_weights.astype(jnp.float32)
+def select_chain(dist, taps_ref):
+    band = jnp.zeros(dist.shape, jnp.float32)
+    for offset in range(taps_ref.shape[0]):
+        band = jnp.where(dist == offset, taps_ref[offset], band)
+    return band.astype(jnp.bfloat16)
+
+
+def build_bands(lon_taps, lat_taps, lon_cells, padded, lat_cells):
+    radius = lon_taps.shape[0] - 1
     ext_cells = padded + 2 * radius
-    rows = lax.broadcasted_iota(jnp.int32, (padded, ext_cells), 0)
-    cols = lax.broadcasted_iota(jnp.int32, (padded, ext_cells), 1)
-    source = jnp.where(
-        cols < padded,
-        cols,
-        jnp.where(cols < padded + radius, cols - padded - radius, cols - padded - radius + lon_cells),
-    )
-    valid = (rows < lon_cells) & ((cols < lon_cells) | (cols >= padded))
-    dist = jnp.abs(source - rows)
-    dist = jnp.where(valid, dist, radius + 1)
-    return band_from(dist, taps)
-
-
-def band_from(dist, taps):
-    band = jnp.zeros(dist.shape, jnp.float32)
-    for offset in range(taps.shape[0]):
-        band = jnp.where(dist == offset, taps[offset], band)
-    return band.astype(jnp.bfloat16)
-
-
-def lat_band(tap_weights, lat_cells):
-    radius = tap_weights.shape[0] - 1
-    taps = tap_weights.astype(jnp.float32)
-    rows = lax.broadcasted_iota(jnp.int32, (lat_cells, lat_cells), 0)
-    cols = lax.broadcasted_iota(jnp.int32, (lat_cells, lat_cells), 1)
-    return band_from(jnp.abs(rows - cols), taps)
+    tile = 128
+    tiles = -(-lat_cells // tile)
+
+    def kernel(lon_ref, lat_ref, blon_ref, blat_ref):
+        rows = lax.broadcasted_iota(jnp.int32, (padded, ext_cells), 0)
+        cols = lax.broadcasted_iota(jnp.int32, (padded, ext_cells), 1)
+        source = jnp.where(
+            cols < padded,
+            cols,
+            jnp.where(
+                cols < padded + radius,
+                cols - padded - radius,
+                cols - padded - radius + lon_cells,
+            ),
+        )
+        valid = (rows < lon_cells) & ((cols < lon_cells) | (cols >= padded))
+        dist = jnp.where(valid, jnp.abs(source - rows), radius + 1)
+        blon_ref[...] = select_chain(dist, lon_ref)
+
+        t_rows = lax.broadcasted_iota(jnp.int32, (tile, tile), 0)
+        t_cols = lax.broadcasted_iota(jnp.int32, (tile, tile), 1)
+        blocks = {
+            shift: select_chain(jnp.abs(t_rows - t_cols + shift * tile), lat_ref)
+            for shift in (-1, 0, 1)
+        }
+        blat_ref[...] = jnp.zeros(blat_ref.shape, blat_ref.dtype)
+        for a in range(tiles):
+            for b in (a - 1, a, a + 1):
+                if b < 0 or b >= tiles:
+                    continue
+                height = min(tile, lat_cells - a * tile)
+                width = min(tile, lat_cells - b * tile)
+                blat_ref[a * tile:a * tile + height, b * tile:b * tile + width] = blocks[a - b][
+                    :height, :width
+                ]
+
+    smem = pl.BlockSpec(memory_space=pltpu.SMEM)
+    return pl.pallas_call(
+        kernel,
+        in_specs=[smem, smem],
+        out_shape=(
+            jax.ShapeDtypeStruct((padded, ext_cells), jnp.bfloat16),
+            jax.ShapeDtypeStruct((lat_cells, lat_cells), jnp.bfloat16),
+        ),
+    )(lon_taps.astype(jnp.float32), lat_taps.astype(jnp.float32))
 
 
 def member_chunk(members):
@@ -238,8 +263,7 @@
     members_here, levels, lon_cells, lat_cells = control.shape
     radius = lon_taps.shape[0] - 1
     padded = -(-lon_cells // 16) * 16
-    band_lon = lon_band(lon_taps, lon_cells, padded)
-    band_lat = lat_band(lat_taps, lat_cells)
+    band_lon, band_lat = build_bands(lon_taps, lat_taps, lon_cells, padded, lat_cells)
 
     slot_ids = lax.broadcasted_iota(jnp.int32, innov.shape, 2)
     weights = jnp.where(slot_ids < counts[:, :, None], inv_var, 0.0)

time: 83.2 us -> 66.2 us (0.80)
  other arithmetic: 27.7 us -> 3.37 us
  waiting for transfers between devices: 4.39 us -> 12.4 us
  local copies, waits for them, and re-layouts: 8.25 us -> 6.04 us
  Pallas kernels: 11.8 us -> 13.8 us
    convert_element_type x2, other arithmetic: 25.4 us -> 1.11 us  [the longest x1 0.59 us: build_bands(): lat_taps.astype(jnp.float32)]
    ppermute x3, waiting for transfers between devices: 1.73 us -> 7.21 us  [halos(): lax.ppermute(lax.slice_in_dim(block, 0, width, axis=dim), axis, backward)]
    ppermute x3, waiting for transfers between devices: 2.67 us -> 5.21 us  [halos(): lax.ppermute(lax.slice_in_dim(block, block.shape[dim] - width, None, axis...]
    pallas_call x0 -> x1, Pallas kernels: none -> 1.96 us  [build_bands(): pl.pallas_call(kernel, in_specs=[smem, smem], out_shape=(jax.ShapeDtypeSt...]
    slice x2 -> x0, local copies, waits for them, and re-layouts: 1.44 us -> none  [band_from(): band = jnp.where(dist == offset, taps[offset], band)]
  transfers between devices with their start and end apart: 7 -> 7, of which waited for: 2 -> 4; matrix products, arithmetic and copies ran while one was open for 45% -> 18% of each run, Pallas kernels for 7% -> 11%
where the time goes in v3:
time: 66.2 us; the launch traced here: 65.7 us
  Pallas kernels  13.8 us (21%)
  waiting for transfers between devices  12.4 us (19%)
  blocking collectives  12.1 us (18%)
  starting transfers between devices  11.1 us (17%)
  matrix products  6.57 us (10%)
  local copies, waits for them, and re-layouts  6.04 us (9%)
  other arithmetic  3.37 us (5%)
    psum x1, blocking collectives, local(): at_cells = lax.psum(partial, 'mem')  12.1 us
    ppermute x3, waiting for transfers between devices, halos(): lax.ppermute(lax.slice_in_dim(block, 0, width, axis=dim), axis, backward)  7.21 us
    pallas_call x1, Pallas kernels, backward_grad(): pl.pallas_call(kernel, grid=(levels, members // chunk), in_specs=[field,...  6.31 us
    pallas_call x1, Pallas kernels, forward_sum(): pl.pallas_call(kernel, grid=(levels, members // chunk), in_specs=[field,...  5.55 us
    ppermute x3, starting transfers between devices, halos(): lax.ppermute(lax.slice_in_dim(block, 0, width, axis=dim), axis, backward)  5.39 us
    ppermute x3, waiting for transfers between devices, halos(): lax.ppermute(lax.slice_in_dim(block, block.shape[dim] - width, None, axis...  5.21 us
    all_to_all x1, starting transfers between devices, local(): lax.all_to_all(lists, 'tile', split_axis=2, concat_axis=1, tiled=True)  5.2 us
    dot_general x2, matrix products, pick_one_block(): jnp.dot(onehot_cols, field_cols, precision=lax.Precision.HIGHEST, preferr...  3.59 us
  transfers between devices with their start and end apart: 7, of which 4 were waited for; matrix products, arithmetic and copies ran while one was open for 18% of the time, Pallas kernels for 11%

profile of v3, /device:TPU:0, one launch (start us, length us, event | category | flops | bytes accessed | tf_op | source)
XLA Modules:
  0.0 65.7 jit_solution(11365378884673680230)
XLA Ops:
  0.0 0.0 copy-start
  0.0 0.8 %stack.12 = f32[1,1,8,256]{3,1,0,2:T(1,128)S(1)} reshape(f32[1,8,256]{2,1,0:T(8,128)} %param.16) | data formatting | bytes 16384 | tf_op jit(solution)/shard_map/stack | solution.py:270
  0.8 0.7 %convert_element_type.23 = f32[1,8,256]{2,1,0:T(8,128)S(1)} convert(s32[1,8,256]{2,1,0:T(8,128)} %param.18) | non-fusion elementwise | flops 2048 | bytes 16384 | tf_op jit(solution)/shard_map/convert_element_type | solution.py:270
  1.5 0.8 %fusion.12 = (f32[1,1,8,256]{3,1,0,2:T(1,128)S(1)}, f32[1,1,8,256]{3,1,0,2:T(1,128)S(1)}) fusion(f32[1,8,256]{2,1,0:T(8,128)} %param.17, s32[8]{0:T(128)} %bitcast.50, f32[1,8,256]{2,1,0:T(8,128)S(1)} %convert_element_type.23), kind=kLoop, calls=%fused_computation.26 | loop fusion | flops 4096 | bytes 32800 | tf_op jit(solution)/shard_map/stack | solution.py:270
  2.3 0.6 pad_maximum_fusion
  2.9 5.2 %all-to-all-start = ((f32[3,1,8,256]{3,1,0,2:T(1,128)}), f32[3,1,8,256]{3,1,0,2:T(1,128)S(1)}, u32[]{:S(2)}, u32[]{:S(2)}) async-start(f32[3,1,8,256]{3,1,0,2:T(1,128)} %pad_maximum_fusion), calls=%async_computation | async-start | bytes 49152 | tf_op jit(solution)/shard_map/all_to_all | solution.py:271
  8.1 2.4 %fusion.13 = (bf16[20,1,16,720]{3,2,1,0:T(8,128)(2,1)}, bf16[20,1,16,720]{3,2,1,0:T(8,128)(2,1)}) fusion(bf16[20,1,45,720]{3,2,1,0:T(8,128)(2,1)} %ctrl_ref.3), kind=kLoop, calls=%fused_computation.34 | loop fusion | bytes 1843200 | tf_op jit(solution)/shard_map/slice | solution.py:18
  10.5 2.6 %collective-permute-start.3 = (bf16[20,1,16,720]{3,2,1,0:T(8,128)(2,1)}, bf16[20,1,16,720]{3,2,1,0:T(8,128)(2,1)S(1)}, u32[]{:S(2)}, u32[]{:S(2)}) collective-permute-start(bf16[20,1,16,720]{3,2,1,0:T(8,128)(2,1)} %get-tuple-element.124), channel_id=1, source_target_pairs={{4,0},{8,4},{12,8},{16,12},{20,16},{24,20},{28,24},{0,28},{5,1},{9... | collective-permute-start | bytes 1382408 | tf_op jit(solution)/shard_map/ppermute | solution.py:18
  13.1 0.0 collective-permute-start.2
  13.1 0.0 copy-done
  13.1 0.1 fusion.14
  13.3 2.7 %collective-permute-start.1 = (bf16[20,1,16,720]{3,2,1,0:T(8,128)(2,1)S(1)}, bf16[20,1,16,720]{3,2,1,0:T(8,128)(2,1)S(1)}, u32[]{:S(2)}, u32[]{:S(2)}) collective-permute-start(bf16[20,1,16,720]{3,2,1,0:T(8,128)(2,1)S(1)} %get-tuple-element.126), channel_id=1, source_target_pairs={{4,0},{8,4},{12,8},{16,12},{20,16},{24,20},{28,24},{0,28},{5,1},{9... | collective-permute-start | bytes 1382408 | tf_op jit(solution)/shard_map/ppermute | solution.py:18
  16.0 0.0 collective-permute-start
  16.0 0.0 copy-done.7
  16.0 0.5 convert_element_type.21.lon_ref
  16.5 0.0 copy-done.8
  16.5 0.6 convert_element_type.22.lat_ref
  17.1 2.0 %shard_map.85 = (bf16[48,80]{1,0:T(8,128)(2,1)}, bf16[720,720]{1,0:T(8,128)(2,1)}) custom-call(f32[17]{0:T(128)} %convert_element_type.21.lon_ref, f32[17]{0:T(128)} %convert_element_type.22.lat_ref), custom_call_target="tpu_custom_call" | custom-call | tf_op jit(solution)/shard_map/pallas_call | solution.py:69
  19.1 0.0 all-to-all-done
  19.1 0.1 remainder_reduce_fusion
  19.3 5.8 %collective-permute-done.3.high_ref = bf16[20,1,16,720]{3,2,1,0:T(8,128)(2,1)S(1)} collective-permute-done((bf16[20,1,16,720]{3,2,1,0:T(8,128)(2,1)}, bf16[20,1,16,720]{3,2,1,0:T(8,128)(2,1)S(1)}, u32[]{:S(2)}, u32[]{:S(2)}) %collective-permute-start.3) | collective-permute-done | bytes 460832 | tf_op jit(solution)/shard_map/ppermute | solution.py:18
  25.1 2.7 %collective-permute-done.2.low_ref = bf16[20,1,16,720]{3,2,1,0:T(8,128)(2,1)S(1)} collective-permute-done((bf16[20,1,16,720]{3,2,1,0:T(8,128)(2,1)}, bf16[20,1,16,720]{3,2,1,0:T(8,128)(2,1)S(1)}, u32[]{:S(2)}, u32[]{:S(2)}) %collective-permute-start.2) | collective-permute-done | bytes 460832 | tf_op jit(solution)/shard_map/ppermute | solution.py:15
  27.8 0.0 copy-done.3
  27.8 0.8 %copy-done.4 = bf16[20,1,16,720]{3,2,1,0:T(8,128)(2,1)} copy-done((bf16[20,1,16,720]{3,2,1,0:T(8,128)(2,1)}, bf16[20,1,16,720]{3,2,1,0:T(8,128)(2,1)S(1)}, u32[]{:S(2)}) %copy-start.4) | copy-done | bytes 460824
  28.5 5.5 %shard_map.86 = f32[1,45,720]{2,1,0:T(8,128)} custom-call(bf16[20,1,45,720]{3,2,1,0:T(8,128)(2,1)} %ctrl_ref.3, bf16[20,1,16,720]{3,2,1,0:T(8,128)(2,1)} %copy-done.4, bf16[20,1,16,720]{3,2,1,0:T(8,128)(2,1)} %copy-done.3, bf16[20,1,45,720]{3,2,1,0:T(8,128)(2,1)} %pert_ref.3, bf16[48,80]{1,0:T(8,128)(2,1)} %get-tuple-element.61.blon_ref, ...), custom_call_target="tpu_custom_call" | custom-call | tf_op jit(solution)/shard_map/pallas_call | solution.py:125
  34.1 1.1 %copy.15 = f32[720,45]{1,0:T(8,128)S(1)} copy(f32[720,45]{0,1:T(8,128)} %bitcast.37) | data formatting | bytes 259200 | tf_op jit(solution)/shard_map/while | solution.py:224
  35.2 3.8 %while.21 = (s32[]{:T(128)}, f32[2,1024]{1,0:T(2,128)S(1)}, s32[2,1024]{1,0:T(2,128)S(1)}, s32[2,1024]{1,0:T(2,128)S(1)}, f32[720,45]{1,0:T(8,128)S(1)}, /*index=5*/s32[]{:T(128)}, s32[]{:T(128)}) while((s32[]{:T(128)}, f32[2,1024]{1,0:T(2,128)S(1)}, s32[2,1024]{1,0:T(2,128)S(1)}, s32[2,1024]{1,0:T(2,128)S(1)}, f32[720,45]{1,0:T(8,128)S(1)}, ...), condition=%wide.region_2.3_spmd, body=%wide.region_0.2_spmd.sunk | while | flops 399005696 | bytes 166557 | solution.py:224
  35.2 1.8 %fusion.23 = f32[1024]{0:T(1024)S(1)} fusion(f32[720,45]{1,0:T(8,128)S(1)} %get-tuple-element.224, s32[1024]{0:T(1024)S(1)} %bitcast.44, s32[1024]{0:T(1024)S(1)} %bitcast.45), kind=kOutput, calls=%fused_computation.4.clone.1 | convolution fusion | flops 399005696 | bytes 141888 | tf_op jit(solution)/shard_map/while/body/eval_jaxpr/dot_general | solution.py:216
  37.0 0.1 dynamic_update_slice.5
  37.1 1.8 %fusion.23 = f32[1024]{0:T(1024)S(1)} fusion(f32[720,45]{1,0:T(8,128)S(1)} %get-tuple-element.224, s32[1024]{0:T(1024)S(1)} %bitcast.44, s32[1024]{0:T(1024)S(1)} %bitcast.45), kind=kOutput, calls=%fused_computation.4.clone.1 | convolution fusion | flops 399005696 | bytes 141888 | tf_op jit(solution)/shard_map/while/body/eval_jaxpr/dot_general | solution.py:216
  38.9 0.1 dynamic_update_slice.5
  39.0 12.1 %psum.7 = f32[2048]{0:T(1024)S(1)} all-reduce(f32[2048]{0:T(1024)S(1)} %bitcast.46), channel_id=1, replica_groups=mesh['tile'=8,'mem'=4] {'mem'}, use_global_device_ids=true, to_apply=%region_3.4 | all-reduce | flops 2048 | bytes 16384 | tf_op jit(solution)/shard_map/psum | solution.py:284
  51.1 3.1 %while.22 = (s32[]{:T(128)}, f32[45,720]{1,0:T(8,128)S(1)}, s32[2,1024]{1,0:T(2,128)S(1)}, f32[2,1024]{1,0:T(2,128)S(1)}, s32[2,1024]{1,0:T(2,128)S(1)}, /*index=5*/s32[]{:T(128)}, s32[]{:T(128)}) while((s32[]{:T(128)}, f32[45,720]{1,0:T(8,128)S(1)}, s32[2,1024]{1,0:T(2,128)S(1)}, f32[2,1024]{1,0:T(2,128)S(1)}, ...), condition=%wide.region_5.6_spmd.clone, body=%wide.region_4.5_spmd.clone.sunk | while | flops 399025440 | bytes 296167 | solution.py:258
  51.2 1.5 %fusion.25 = f32[45,720]{1,0:T(8,128)S(1)} fusion(s32[1024]{0:T(1024)S(1)} %bitcast.42, f32[1024]{0:T(1024)S(1)} %bitcast.40, s32[1024]{0:T(1024)S(1)} %bitcast.43, f32[45,720]{1,0:T(8,128)S(1)} %get-tuple-element.235, pred[]{:T(512)S(6)} %compare.3), kind=kOutput, calls=%fused_computation.11.clone.1 | convolution fusion | flops 399025440 | bytes 271489 | tf_op jit(solution)/shard_map/while/body/eval_jaxpr/dot_general | solution.py:243
  52.7 1.5 %fusion.25 = f32[45,720]{1,0:T(8,128)S(1)} fusion(s32[1024]{0:T(1024)S(1)} %bitcast.42, f32[1024]{0:T(1024)S(1)} %bitcast.40, s32[1024]{0:T(1024)S(1)} %bitcast.43, f32[45,720]{1,0:T(8,128)S(1)} %get-tuple-element.235, pred[]{:T(512)S(6)} %compare.3), kind=kOutput, calls=%fused_computation.11.clone.1 | convolution fusion | flops 399025440 | bytes 271489 | tf_op jit(solution)/shard_map/while/body/eval_jaxpr/dot_general | solution.py:243
  54.3 0.1 collective-permute-start.5
  54.3 0.5 collective-permute-start.4
  54.8 0.0 collective-permute-done.1.phigh_ref
  54.8 0.0 collective-permute-done.plow_ref
  54.8 0.0 copy-start.2
  54.8 1.4 %collective-permute-done.5.shigh_ref = f32[1,16,720]{2,1,0:T(8,128)S(1)} collective-permute-done((f32[1,16,720]{2,1,0:T(8,128)S(1)}, f32[1,16,720]{2,1,0:T(8,128)S(1)}, u32[]{:S(2)}, u32[]{:S(2)}) %collective-permute-start.5) | collective-permute-done | bytes 46112 | tf_op jit(solution)/shard_map/ppermute | solution.py:18
  56.3 2.5 %collective-permute-done.4.slow_ref = f32[1,16,720]{2,1,0:T(8,128)S(1)} collective-permute-done((f32[1,16,720]{2,1,0:T(8,128)S(1)}, f32[1,16,720]{2,1,0:T(8,128)S(1)}, u32[]{:S(2)}, u32[]{:S(2)}) %collective-permute-start.4) | collective-permute-done | bytes 46112 | tf_op jit(solution)/shard_map/ppermute | solution.py:15
  58.8 0.0 copy-done.1
  58.8 0.0 copy-done.2
  58.8 0.0 copy-done.5
  58.8 0.0 copy-start.6
  58.8 0.6 copy-done.6
  59.4 6.3 %shard_map.87 = f32[20,45,1,720]{3,2,1,0:T(1,128)} custom-call(bf16[20,1,45,720]{3,2,1,0:T(8,128)(2,1)} %pert_ref.3, bf16[20,1,16,720]{3,2,1,0:T(8,128)(2,1)} %copy-done.2, bf16[20,1,16,720]{3,2,1,0:T(8,128)(2,1)} %copy-done.1, f32[1,45,720]{2,1,0:T(8,128)S(1)} %bitcast.39, f32[1,16,720]{2,1,0:T(8,128)} %copy-done.6, f32[1,16,720]{2,1,0:T(8,128)} %copy-done.5, ...), custom_call_target="tpu_custom_call" | custom-call | tf_op jit(solution)/shard_map/pallas_call | solution.py:179
  (24 shorter events, 0.2 us)
Async XLA Ops:
  0.0 13.1 %copy-start = (bf16[20,1,45,720]{3,2,1,0:T(8,128)(2,1)S(1)}, bf16[20,1,45,720]{3,2,1,0:T(8,128)(2,1)}, u32[]{:S(2)}) copy-start(bf16[20,1,45,720]{3,2,1,0:T(8,128)(2,1)} %pert_ref.3) | copy-start | bytes 3888004
  0.0 16.0 %copy-start.7 = (bf16[17]{0:T(256)(128)(2,1)S(1)}, bf16[17]{0:T(256)(128)(2,1)}, u32[]{:S(2)}) copy-start(bf16[17]{0:T(256)(128)(2,1)} %param.14) | copy-start | bytes 106
  0.0 16.5 %copy-start.8 = (bf16[17]{0:T(256)(128)(2,1)S(1)}, bf16[17]{0:T(256)(128)(2,1)}, u32[]{:S(2)}) copy-start(bf16[17]{0:T(256)(128)(2,1)} %param.15) | copy-start | bytes 106
  2.9 16.1 %all-to-all-start = ((f32[3,1,8,256]{3,1,0,2:T(1,128)}), f32[3,1,8,256]{3,1,0,2:T(1,128)S(1)}, u32[]{:S(2)}, u32[]{:S(2)}) async-start(f32[3,1,8,256]{3,1,0,2:T(1,128)} %pad_maximum_fusion), calls=%async_computation | async-start | bytes 49152 | tf_op jit(solution)/shard_map/all_to_all | solution.py:271
  10.5 14.6 %collective-permute-start.3 = (bf16[20,1,16,720]{3,2,1,0:T(8,128)(2,1)}, bf16[20,1,16,720]{3,2,1,0:T(8,128)(2,1)S(1)}, u32[]{:S(2)}, u32[]{:S(2)}) collective-permute-start(bf16[20,1,16,720]{3,2,1,0:T(8,128)(2,1)} %get-tuple-element.124), channel_id=1, source_target_pairs={{4,0},{8,4},{12,8},{16,12},{20,16},{24,20},{28,24},{0,28},{5,1},{9... | collective-permute-start | bytes 1382408 | tf_op jit(solution)/shard_map/ppermute | solution.py:18
  13.1 14.6 %collective-permute-start.2 = (bf16[20,1,16,720]{3,2,1,0:T(8,128)(2,1)}, bf16[20,1,16,720]{3,2,1,0:T(8,128)(2,1)S(1)}, u32[]{:S(2)}, u32[]{:S(2)}) collective-permute-start(bf16[20,1,16,720]{3,2,1,0:T(8,128)(2,1)} %get-tuple-element.125), channel_id=1, source_target_pairs={{0,4},{4,8},{8,12},{12,16},{16,20},{20,24},{24,28},{28,0},{1,5},{5... | collective-permute-start | bytes 1382408 | tf_op jit(solution)/shard_map/ppermute | solution.py:15
  13.3 41.5 %collective-permute-start.1 = (bf16[20,1,16,720]{3,2,1,0:T(8,128)(2,1)S(1)}, bf16[20,1,16,720]{3,2,1,0:T(8,128)(2,1)S(1)}, u32[]{:S(2)}, u32[]{:S(2)}) collective-permute-start(bf16[20,1,16,720]{3,2,1,0:T(8,128)(2,1)S(1)} %get-tuple-element.126), channel_id=1, source_target_pairs={{4,0},{8,4},{12,8},{16,12},{20,16},{24,20},{28,24},{0,28},{5,1},{9... | collective-permute-start | bytes 1382408 | tf_op jit(solution)/shard_map/ppermute | solution.py:18
  16.0 38.9 %collective-permute-start = (bf16[20,1,16,720]{3,2,1,0:T(8,128)(2,1)S(1)}, bf16[20,1,16,720]{3,2,1,0:T(8,128)(2,1)S(1)}, u32[]{:S(2)}, u32[]{:S(2)}) collective-permute-start(bf16[20,1,16,720]{3,2,1,0:T(8,128)(2,1)S(1)} %get-tuple-element.127), channel_id=1, source_target_pairs={{0,4},{4,8},{8,12},{12,16},{16,20},{20,24},{24,28},{28,0},{1,5},{5... | collective-permute-start | bytes 1382408 | tf_op jit(solution)/shard_map/ppermute | solution.py:15
  25.1 2.7 %copy-start.3 = (bf16[20,1,16,720]{3,2,1,0:T(8,128)(2,1)}, bf16[20,1,16,720]{3,2,1,0:T(8,128)(2,1)S(1)}, u32[]{:S(2)}) copy-start(bf16[20,1,16,720]{3,2,1,0:T(8,128)(2,1)S(1)} %collective-permute-done.3.high_ref) | copy-start | bytes 1382404
  27.8 0.8 %copy-start.4 = (bf16[20,1,16,720]{3,2,1,0:T(8,128)(2,1)}, bf16[20,1,16,720]{3,2,1,0:T(8,128)(2,1)S(1)}, u32[]{:S(2)}) copy-start(bf16[20,1,16,720]{3,2,1,0:T(8,128)(2,1)S(1)} %collective-permute-done.2.low_ref) | copy-start | bytes 1382404
  54.3 2.0 %collective-permute-start.5 = (f32[1,16,720]{2,1,0:T(8,128)S(1)}, f32[1,16,720]{2,1,0:T(8,128)S(1)}, u32[]{:S(2)}, u32[]{:S(2)}) collective-permute-start(f32[1,16,720]{2,1,0:T(8,128)S(1)} %get-tuple-element.128), channel_id=1, source_target_pairs={{4,0},{8,4},{12,8},{16,12},{20,16},{24,20},{28,24},{0,28},{5,1},{9... | collective-permute-start | bytes 138248 | tf_op jit(solution)/shard_map/ppermute | solution.py:18
  54.3 4.5 %collective-permute-start.4 = (f32[1,16,720]{2,1,0:T(8,128)S(1)}, f32[1,16,720]{2,1,0:T(8,128)S(1)}, u32[]{:S(2)}, u32[]{:S(2)}) collective-permute-start(f32[1,16,720]{2,1,0:T(8,128)S(1)} %get-tuple-element.129), channel_id=1, source_target_pairs={{0,4},{4,8},{8,12},{12,16},{16,20},{20,24},{24,28},{28,0},{1,5},{5... | collective-permute-start | bytes 138248 | tf_op jit(solution)/shard_map/ppermute | solution.py:15
  54.8 4.0 %copy-start.1 = (bf16[20,1,16,720]{3,2,1,0:T(8,128)(2,1)}, bf16[20,1,16,720]{3,2,1,0:T(8,128)(2,1)S(1)}, u32[]{:S(2)}) copy-start(bf16[20,1,16,720]{3,2,1,0:T(8,128)(2,1)S(1)} %collective-permute-done.1.phigh_ref) | copy-start | bytes 1382404
  54.8 4.0 %copy-start.2 = (bf16[20,1,16,720]{3,2,1,0:T(8,128)(2,1)}, bf16[20,1,16,720]{3,2,1,0:T(8,128)(2,1)S(1)}, u32[]{:S(2)}) copy-start(bf16[20,1,16,720]{3,2,1,0:T(8,128)(2,1)S(1)} %collective-permute-done.plow_ref) | copy-start | bytes 1382404
  56.3 2.5 %copy-start.5 = (f32[1,16,720]{2,1,0:T(8,128)}, f32[1,16,720]{2,1,0:T(8,128)S(1)}, u32[]{:S(2)}) copy-start(f32[1,16,720]{2,1,0:T(8,128)S(1)} %collective-permute-done.5.shigh_ref) | copy-start | bytes 138244
  58.8 0.6 copy-start.6

commit v4 on v3

--- a/solution.py
+++ b/solution.py
@@ -17,6 +17,16 @@
     )
     high = lax.ppermute(lax.slice_in_dim(block, 0, width, axis=dim), axis, backward)
     return low, high
+
+
+def sum_over(values, axis):
+    count = lax.axis_size(axis)
+    total = values
+    for shift in range(1, count):
+        total = total + lax.ppermute(
+            values, axis, [(i, (i + shift) % count) for i in range(count)]
+        )
+    return total
 
 
 def select_chain(dist, taps_ref):
@@ -278,10 +288,11 @@
     block_rows = math.gcd(observed.shape[0], 1024)
 
     c_low, c_high = halos(control, "tile", 2, radius)
-    p_low, p_high = halos(perturb, "tile", 2, radius)
+    late_perturb = lax.optimization_barrier((perturb, c_low, c_high))[0]
+    p_low, p_high = halos(late_perturb, "tile", 2, radius)
     member_sum = forward_sum(control, c_low, c_high, perturb, band_lon, band_lat)
     partial = pick_cells(member_sum.reshape(row_count, lat_cells), row_index, col_index, block_rows)
-    at_cells = lax.psum(partial, "mem")
+    at_cells = sum_over(partial, "mem")
     misfit = weight_recv * (at_cells - observed)
     spread = spread_cells(misfit, row_index, col_index, row_count, lat_cells, block_rows)
     spread = spread.reshape(levels, lon_cells, lat_cells)

time: 66.2 us -> 64 us (0.967)
  blocking collectives: 12.1 us -> 0 us
  waiting for transfers between devices: 12.4 us -> 18.4 us
  starting transfers between devices: 11.1 us -> 13.7 us
  other arithmetic: 3.37 us -> 4.63 us
    psum x1 -> x0, blocking collectives: 12.1 us -> none  [local(): at_cells = lax.psum(partial, 'mem')]
    ppermute x0 -> x3, starting transfers between devices: none -> 4.67 us  [sum_over(): lax.ppermute(values, axis, [(i, (i + shift) % count) for i in range(count)])]
    ppermute x0 -> x3, waiting for transfers between devices: none -> 4.07 us  [sum_over(): lax.ppermute(values, axis, [(i, (i + shift) % count) for i in range(count)])]
    ppermute x3, waiting for transfers between devices: 7.21 us -> 10.2 us  [halos(): lax.ppermute(lax.slice_in_dim(block, 0, width, axis=dim), axis, backward)]
    ppermute x3, starting transfers between devices: 5.39 us -> 2.84 us  [halos(): lax.ppermute(lax.slice_in_dim(block, 0, width, axis=dim), axis, backward)]
    ppermute x3, waiting for transfers between devices: 5.21 us -> 4.18 us  [halos(): lax.ppermute(lax.slice_in_dim(block, block.shape[dim] - width, None, axis...]
    unnamed x19 -> x15, local copies, waits for them, and re-layouts: 1.41 us -> 2.38 us
    slice x3, local copies, waits for them, and re-layouts: 2.5 us -> 1.56 us  [halos(): lax.slice_in_dim(block, 0, width, axis=dim)]
  transfers between devices with their start and end apart: 7 -> 10, of which waited for: 4 -> 6; matrix products, arithmetic and copies ran while one was open for 18% -> 11% of each run, Pallas kernels for 11% -> 3%
where the time goes in v4:
time: 64 us; the launch traced here: 63.4 us
  waiting for transfers between devices  18.4 us (29%)
  Pallas kernels  13.8 us (22%)
  starting transfers between devices  13.7 us (21%)
  matrix products  6.57 us (10%)
  local copies, waits for them, and re-layouts  6.07 us (9%)
  other arithmetic  4.63 us (7%)
    ppermute x3, waiting for transfers between devices, halos(): lax.ppermute(lax.slice_in_dim(block, 0, width, axis=dim), axis, backward)  10.2 us
    pallas_call x1, Pallas kernels, backward_grad(): pl.pallas_call(kernel, grid=(levels, members // chunk), in_specs=[field,...  6.31 us
    pallas_call x1, Pallas kernels, forward_sum(): pl.pallas_call(kernel, grid=(levels, members // chunk), in_specs=[field,...  5.54 us
    all_to_all x1, starting transfers between devices, local(): lax.all_to_all(lists, 'tile', split_axis=2, concat_axis=1, tiled=True)  5.2 us
    ppermute x3, starting transfers between devices, sum_over(): lax.ppermute(values, axis, [(i, (i + shift) % count) for i in range(count)])  4.67 us
    ppermute x3, waiting for transfers between devices, halos(): lax.ppermute(lax.slice_in_dim(block, block.shape[dim] - width, None, axis...  4.18 us
    ppermute x3, waiting for transfers between devices, sum_over(): lax.ppermute(values, axis, [(i, (i + shift) % count) for i in range(count)])  4.07 us
    dot_general x2, matrix products, pick_one_block(): jnp.dot(onehot_cols, field_cols, precision=lax.Precision.HIGHEST, preferr...  3.59 us
  transfers between devices with their start and end apart: 10, of which 6 were waited for; matrix products, arithmetic and copies ran while one was open for 11% of the time, Pallas kernels for 3%

profile of v4, /device:TPU:0, one launch (start us, length us, event | category | flops | bytes accessed | tf_op | source)
XLA Modules:
  0.0 63.4 jit_solution(6502280109691730881)
XLA Ops:
  0.0 0.7 %stack.12 = f32[1,1,8,256]{3,1,0,2:T(1,128)S(1)} reshape(f32[1,8,256]{2,1,0:T(8,128)} %param.16) | data formatting | bytes 16384 | tf_op jit(solution)/shard_map/stack | solution.py:280
  0.7 0.7 %convert_element_type.23 = f32[1,8,256]{2,1,0:T(8,128)S(1)} convert(s32[1,8,256]{2,1,0:T(8,128)} %param.18) | non-fusion elementwise | flops 2048 | bytes 16384 | tf_op jit(solution)/shard_map/convert_element_type | solution.py:280
  1.4 0.8 %fusion.12 = (f32[1,1,8,256]{3,1,0,2:T(1,128)S(1)}, f32[1,1,8,256]{3,1,0,2:T(1,128)S(1)}) fusion(f32[1,8,256]{2,1,0:T(8,128)} %param.17, s32[8]{0:T(128)} %bitcast.55, f32[1,8,256]{2,1,0:T(8,128)S(1)} %convert_element_type.23), kind=kLoop, calls=%fused_computation.26 | loop fusion | flops 4096 | bytes 32800 | tf_op jit(solution)/shard_map/stack | solution.py:280
  2.2 0.6 pad_maximum_fusion
  2.8 5.2 %all-to-all-start = ((f32[3,1,8,256]{3,1,0,2:T(1,128)}), f32[3,1,8,256]{3,1,0,2:T(1,128)S(1)}, u32[]{:S(2)}, u32[]{:S(2)}) async-start(f32[3,1,8,256]{3,1,0,2:T(1,128)} %pad_maximum_fusion), calls=%async_computation | async-start | bytes 49152 | tf_op jit(solution)/shard_map/all_to_all | solution.py:281
  8.0 1.4 %fusion.14 = (bf16[20,1,16,720]{3,2,1,0:T(8,128)(2,1)S(1)}, bf16[20,1,16,720]{3,2,1,0:T(8,128)(2,1)S(1)}) fusion(bf16[20,1,45,720]{3,2,1,0:T(8,128)(2,1)} %ctrl_ref.3), kind=kLoop, calls=%fused_computation.35 | loop fusion | bytes 1843200 | tf_op jit(solution)/shard_map/slice | solution.py:18
  9.4 2.7 %collective-permute-start.1 = (bf16[20,1,16,720]{3,2,1,0:T(8,128)(2,1)S(1)}, bf16[20,1,16,720]{3,2,1,0:T(8,128)(2,1)S(1)}, u32[]{:S(2)}, u32[]{:S(2)}) collective-permute-start(bf16[20,1,16,720]{3,2,1,0:T(8,128)(2,1)S(1)} %get-tuple-element.128), channel_id=1, source_target_pairs={{4,0},{8,4},{12,8},{16,12},{20,16},{24,20},{28,24},{0,28},{5,1},{9... | collective-permute-start | bytes 1382408 | tf_op jit(solution)/shard_map/ppermute | solution.py:18
  12.1 0.0 collective-permute-start
  12.1 1.2 %convert_element_type.21.lon_ref = f32[17]{0:T(128)} convert(bf16[17]{0:T(256)(128)(2,1)} %param.14) | non-fusion elementwise | flops 17 | bytes 102 | tf_op jit(solution)/shard_map/convert_element_type | solution.py:86
  13.3 1.2 %convert_element_type.22.lat_ref = f32[17]{0:T(128)} convert(bf16[17]{0:T(256)(128)(2,1)} %param.15) | non-fusion elementwise | flops 17 | bytes 102 | tf_op jit(solution)/shard_map/convert_element_type | solution.py:86
  14.5 2.0 %shard_map.85 = (bf16[48,80]{1,0:T(8,128)(2,1)}, bf16[720,720]{1,0:T(8,128)(2,1)}) custom-call(f32[17]{0:T(128)} %convert_element_type.21.lon_ref, f32[17]{0:T(128)} %convert_element_type.22.lat_ref), custom_call_target="tpu_custom_call" | custom-call | tf_op jit(solution)/shard_map/pallas_call | solution.py:79
  16.5 0.0 all-to-all-done
  16.5 0.1 remainder_reduce_fusion
  16.7 6.0 %collective-permute-done.1.high_ref = bf16[20,1,16,720]{3,2,1,0:T(8,128)(2,1)S(1)} collective-permute-done((bf16[20,1,16,720]{3,2,1,0:T(8,128)(2,1)S(1)}, bf16[20,1,16,720]{3,2,1,0:T(8,128)(2,1)S(1)}, u32[]{:S(2)}, u32[]{:S(2)}) %collective-permute-start.1) | collective-permute-done | bytes 460832 | tf_op jit(solution)/shard_map/ppermute | solution.py:18
  22.7 2.1 %collective-permute-done.low_ref = bf16[20,1,16,720]{3,2,1,0:T(8,128)(2,1)S(1)} collective-permute-done((bf16[20,1,16,720]{3,2,1,0:T(8,128)(2,1)S(1)}, bf16[20,1,16,720]{3,2,1,0:T(8,128)(2,1)S(1)}, u32[]{:S(2)}, u32[]{:S(2)}) %collective-permute-start) | collective-permute-done | bytes 460832 | tf_op jit(solution)/shard_map/ppermute | solution.py:15
  24.8 0.0 copy-done.3
  24.8 0.8 %copy-done.4 = bf16[20,1,16,720]{3,2,1,0:T(8,128)(2,1)} copy-done((bf16[20,1,16,720]{3,2,1,0:T(8,128)(2,1)}, bf16[20,1,16,720]{3,2,1,0:T(8,128)(2,1)S(1)}, u32[]{:S(2)}) %copy-start.4) | copy-done | bytes 460824
  25.5 5.5 %shard_map.86 = f32[1,45,720]{2,1,0:T(8,128)} custom-call(bf16[20,1,45,720]{3,2,1,0:T(8,128)(2,1)} %ctrl_ref.3, bf16[20,1,16,720]{3,2,1,0:T(8,128)(2,1)} %copy-done.4, bf16[20,1,16,720]{3,2,1,0:T(8,128)(2,1)} %copy-done.3, bf16[20,1,45,720]{3,2,1,0:T(8,128)(2,1)} %pert_ref.3, bf16[48,80]{1,0:T(8,128)(2,1)} %get-tuple-element.63.blon_ref, ...), custom_call_target="tpu_custom_call" | custom-call | tf_op jit(solution)/shard_map/pallas_call | solution.py:135
  31.1 1.2 %copy.15 = f32[720,45]{1,0:T(8,128)S(1)} copy(f32[720,45]{0,1:T(8,128)} %bitcast.39) | data formatting | bytes 259200 | tf_op jit(solution)/shard_map/while | solution.py:234
  32.3 3.8 %while.21 = (s32[]{:T(128)}, f32[2,1024]{1,0:T(2,128)S(1)}, s32[2,1024]{1,0:T(2,128)S(1)}, s32[2,1024]{1,0:T(2,128)S(1)}, f32[720,45]{1,0:T(8,128)S(1)}, /*index=5*/s32[]{:T(128)}, s32[]{:T(128)}) while((s32[]{:T(128)}, f32[2,1024]{1,0:T(2,128)S(1)}, s32[2,1024]{1,0:T(2,128)S(1)}, s32[2,1024]{1,0:T(2,128)S(1)}, f32[720,45]{1,0:T(8,128)S(1)}, ...), condition=%wide.region_2.3_spmd, body=%wide.region_0.2_spmd.sunk | while | flops 399005696 | bytes 166557 | solution.py:234
  32.3 1.8 %fusion.23 = f32[1024]{0:T(1024)S(1)} fusion(f32[720,45]{1,0:T(8,128)S(1)} %get-tuple-element.226, s32[1024]{0:T(1024)S(1)} %bitcast.46, s32[1024]{0:T(1024)S(1)} %bitcast.47), kind=kOutput, calls=%fused_computation.4.clone.1 | convolution fusion | flops 399005696 | bytes 141888 | tf_op jit(solution)/shard_map/while/body/eval_jaxpr/dot_general | solution.py:226
  34.1 0.1 dynamic_update_slice.5
  34.2 1.8 %fusion.23 = f32[1024]{0:T(1024)S(1)} fusion(f32[720,45]{1,0:T(8,128)S(1)} %get-tuple-element.226, s32[1024]{0:T(1024)S(1)} %bitcast.46, s32[1024]{0:T(1024)S(1)} %bitcast.47), kind=kOutput, calls=%fused_computation.4.clone.1 | convolution fusion | flops 399005696 | bytes 141888 | tf_op jit(solution)/shard_map/while/body/eval_jaxpr/dot_general | solution.py:226
  36.0 0.1 dynamic_update_slice.5
  36.1 2.6 %collective-permute-start.5 = (f32[2048]{0:T(1024)S(1)}, f32[2048]{0:T(1024)S(1)}, u32[]{:S(2)}, u32[]{:S(2)}) collective-permute-start(f32[2048]{0:T(1024)S(1)} %bitcast.52), channel_id=1, source_target_pairs={{0,2},{1,3},{2,0},{3,1},{4,6},{5,7},{6,4},{7,5},{8,10},{9,11},{10,... | collective-permute-start | bytes 24584 | tf_op jit(solution)/shard_map/ppermute | solution.py:26
  38.7 1.4 %collective-permute-start.6 = (f32[2048]{0:T(1024)S(1)}, f32[2048]{0:T(1024)S(1)}, u32[]{:S(2)}, u32[]{:S(2)}) collective-permute-start(f32[2048]{0:T(1024)S(1)} %bitcast.53), channel_id=1, source_target_pairs={{0,3},{1,0},{2,1},{3,2},{4,7},{5,4},{6,5},{7,6},{8,11},{9,8},{10,9... | collective-permute-start | bytes 24584 | tf_op jit(solution)/shard_map/ppermute | solution.py:26
  40.1 0.7 %collective-permute-start.4 = (f32[2048]{0:T(1024)S(1)}, f32[2048]{0:T(1024)S(1)}, u32[]{:S(2)}, u32[]{:S(2)}) collective-permute-start(f32[2048]{0:T(1024)S(1)} %bitcast.54), channel_id=1, source_target_pairs={{0,1},{1,2},{2,3},{3,0},{4,5},{5,6},{6,7},{7,4},{8,9},{9,10},{10,1... | collective-permute-start | bytes 24584 | tf_op jit(solution)/shard_map/ppermute | solution.py:26
  40.8 0.0 copy-done
  40.8 0.1 fusion.13
  40.9 0.1 collective-permute-start.3
  41.0 0.5 collective-permute-start.2
  41.5 0.0 collective-permute-done.5
  41.5 0.9 %collective-permute-done.6 = f32[2048]{0:T(1024)S(1)} collective-permute-done((f32[2048]{0:T(1024)S(1)}, f32[2048]{0:T(1024)S(1)}, u32[]{:S(2)}, u32[]{:S(2)}) %collective-permute-start.6) | collective-permute-done | bytes 8224 | tf_op jit(solution)/shard_map/ppermute | solution.py:26
  42.4 3.2 %collective-permute-done.4 = f32[2048]{0:T(1024)S(1)} collective-permute-done((f32[2048]{0:T(1024)S(1)}, f32[2048]{0:T(1024)S(1)}, u32[]{:S(2)}, u32[]{:S(2)}) %collective-permute-start.4) | collective-permute-done | bytes 8224 | tf_op jit(solution)/shard_map/ppermute | solution.py:26
  45.6 3.1 %while.22 = (s32[]{:T(128)}, f32[45,720]{1,0:T(8,128)S(1)}, s32[2,1024]{1,0:T(2,128)S(1)}, f32[2,1024]{1,0:T(2,128)S(1)}, s32[2,1024]{1,0:T(2,128)S(1)}, /*index=5*/s32[]{:T(128)}, s32[]{:T(128)}) while((s32[]{:T(128)}, f32[45,720]{1,0:T(8,128)S(1)}, s32[2,1024]{1,0:T(2,128)S(1)}, f32[2,1024]{1,0:T(2,128)S(1)}, ...), condition=%wide.region_4.5_spmd.clone, body=%wide.region_3.4_spmd.clone.sunk | while | flops 399025440 | bytes 296167 | solution.py:268
  45.6 1.5 %fusion.25 = f32[45,720]{1,0:T(8,128)S(1)} fusion(s32[1024]{0:T(1024)S(1)} %bitcast.44, f32[1024]{0:T(1024)S(1)} %bitcast.42, s32[1024]{0:T(1024)S(1)} %bitcast.45, f32[45,720]{1,0:T(8,128)S(1)} %get-tuple-element.237, pred[]{:T(512)S(6)} %compare.3), kind=kOutput, calls=%fused_computation.11.clone.1 | convolution fusion | flops 399025440 | bytes 271489 | tf_op jit(solution)/shard_map/while/body/eval_jaxpr/dot_general | solution.py:253
  47.2 1.5 %fusion.25 = f32[45,720]{1,0:T(8,128)S(1)} fusion(s32[1024]{0:T(1024)S(1)} %bitcast.44, f32[1024]{0:T(1024)S(1)} %bitcast.42, s32[1024]{0:T(1024)S(1)} %bitcast.45, f32[45,720]{1,0:T(8,128)S(1)} %get-tuple-element.237, pred[]{:T(512)S(6)} %compare.3), kind=kOutput, calls=%fused_computation.11.clone.1 | convolution fusion | flops 399025440 | bytes 271489 | tf_op jit(solution)/shard_map/while/body/eval_jaxpr/dot_general | solution.py:253
  48.7 0.1 collective-permute-start.8
  48.7 0.5 collective-permute-start.7
  49.2 4.2 %collective-permute-done.8.shigh_ref = f32[1,16,720]{2,1,0:T(8,128)S(1)} collective-permute-done((f32[1,16,720]{2,1,0:T(8,128)S(1)}, f32[1,16,720]{2,1,0:T(8,128)S(1)}, u32[]{:S(2)}, u32[]{:S(2)}) %collective-permute-start.8) | collective-permute-done | bytes 46112 | tf_op jit(solution)/shard_map/ppermute | solution.py:18
  53.4 2.1 %collective-permute-done.7.slow_ref = f32[1,16,720]{2,1,0:T(8,128)S(1)} collective-permute-done((f32[1,16,720]{2,1,0:T(8,128)S(1)}, f32[1,16,720]{2,1,0:T(8,128)S(1)}, u32[]{:S(2)}, u32[]{:S(2)}) %collective-permute-start.7) | collective-permute-done | bytes 46112 | tf_op jit(solution)/shard_map/ppermute | solution.py:15
  55.5 0.0 collective-permute-done.3.phigh_ref
  55.5 0.0 collective-permute-done.2.plow_ref
  55.5 0.0 copy-done.5
  55.5 0.6 copy-done.6
  56.1 0.2 copy-done.1
  56.3 0.8 %copy-done.2 = bf16[20,1,16,720]{3,2,1,0:T(8,128)(2,1)} copy-done((bf16[20,1,16,720]{3,2,1,0:T(8,128)(2,1)}, bf16[20,1,16,720]{3,2,1,0:T(8,128)(2,1)S(1)}, u32[]{:S(2)}) %copy-start.2) | copy-done | bytes 460824
  57.1 6.3 %shard_map.87 = f32[20,45,1,720]{3,2,1,0:T(1,128)} custom-call(bf16[20,1,45,720]{3,2,1,0:T(8,128)(2,1)} %pert_ref.3, bf16[20,1,16,720]{3,2,1,0:T(8,128)(2,1)} %copy-done.2, bf16[20,1,16,720]{3,2,1,0:T(8,128)(2,1)} %copy-done.1, f32[1,45,720]{2,1,0:T(8,128)S(1)} %bitcast.41, f32[1,16,720]{2,1,0:T(8,128)} %copy-done.6, f32[1,16,720]{2,1,0:T(8,128)} %copy-done.5, ...), custom_call_target="tpu_custom_call" | custom-call | tf_op jit(solution)/shard_map/pallas_call | solution.py:189
  (25 shorter events, 0.2 us)
Async XLA Ops:
  2.8 13.7 %all-to-all-start = ((f32[3,1,8,256]{3,1,0,2:T(1,128)}), f32[3,1,8,256]{3,1,0,2:T(1,128)S(1)}, u32[]{:S(2)}, u32[]{:S(2)}) async-start(f32[3,1,8,256]{3,1,0,2:T(1,128)} %pad_maximum_fusion), calls=%async_computation | async-start | bytes 49152 | tf_op jit(solution)/shard_map/all_to_all | solution.py:281
  9.4 13.2 %collective-permute-start.1 = (bf16[20,1,16,720]{3,2,1,0:T(8,128)(2,1)S(1)}, bf16[20,1,16,720]{3,2,1,0:T(8,128)(2,1)S(1)}, u32[]{:S(2)}, u32[]{:S(2)}) collective-permute-start(bf16[20,1,16,720]{3,2,1,0:T(8,128)(2,1)S(1)} %get-tuple-element.128), channel_id=1, source_target_pairs={{4,0},{8,4},{12,8},{16,12},{20,16},{24,20},{28,24},{0,28},{5,1},{9... | collective-permute-start | bytes 1382408 | tf_op jit(solution)/shard_map/ppermute | solution.py:18
  12.1 12.6 %collective-permute-start = (bf16[20,1,16,720]{3,2,1,0:T(8,128)(2,1)S(1)}, bf16[20,1,16,720]{3,2,1,0:T(8,128)(2,1)S(1)}, u32[]{:S(2)}, u32[]{:S(2)}) collective-permute-start(bf16[20,1,16,720]{3,2,1,0:T(8,128)(2,1)S(1)} %get-tuple-element.129), channel_id=1, source_target_pairs={{0,4},{4,8},{8,12},{12,16},{16,20},{20,24},{24,28},{28,0},{1,5},{5... | collective-permute-start | bytes 1382408 | tf_op jit(solution)/shard_map/ppermute | solution.py:15
  22.7 2.1 %copy-start.3 = (bf16[20,1,16,720]{3,2,1,0:T(8,128)(2,1)}, bf16[20,1,16,720]{3,2,1,0:T(8,128)(2,1)S(1)}, u32[]{:S(2)}) copy-start(bf16[20,1,16,720]{3,2,1,0:T(8,128)(2,1)S(1)} %collective-permute-done.1.high_ref) | copy-start | bytes 1382404
  24.8 0.8 %copy-start.4 = (bf16[20,1,16,720]{3,2,1,0:T(8,128)(2,1)}, bf16[20,1,16,720]{3,2,1,0:T(8,128)(2,1)S(1)}, u32[]{:S(2)}) copy-start(bf16[20,1,16,720]{3,2,1,0:T(8,128)(2,1)S(1)} %collective-permute-done.low_ref) | copy-start | bytes 1382404
  31.1 9.7 %copy-start = (bf16[20,1,45,720]{3,2,1,0:T(8,128)(2,1)S(1)}, bf16[20,1,45,720]{3,2,1,0:T(8,128)(2,1)}, u32[]{:S(2)}) copy-start(bf16[20,1,45,720]{3,2,1,0:T(8,128)(2,1)} %pert_ref.3) | copy-start | bytes 3888004
  36.1 5.4 %collective-permute-start.5 = (f32[2048]{0:T(1024)S(1)}, f32[2048]{0:T(1024)S(1)}, u32[]{:S(2)}, u32[]{:S(2)}) collective-permute-start(f32[2048]{0:T(1024)S(1)} %bitcast.52), channel_id=1, source_target_pairs={{0,2},{1,3},{2,0},{3,1},{4,6},{5,7},{6,4},{7,5},{8,10},{9,11},{10,... | collective-permute-start | bytes 24584 | tf_op jit(solution)/shard_map/ppermute | solution.py:26
  38.7 3.7 %collective-permute-start.6 = (f32[2048]{0:T(1024)S(1)}, f32[2048]{0:T(1024)S(1)}, u32[]{:S(2)}, u32[]{:S(2)}) collective-permute-start(f32[2048]{0:T(1024)S(1)} %bitcast.53), channel_id=1, source_target_pairs={{0,3},{1,0},{2,1},{3,2},{4,7},{5,4},{6,5},{7,6},{8,11},{9,8},{10,9... | collective-permute-start | bytes 24584 | tf_op jit(solution)/shard_map/ppermute | solution.py:26
  40.1 5.4 %collective-permute-start.4 = (f32[2048]{0:T(1024)S(1)}, f32[2048]{0:T(1024)S(1)}, u32[]{:S(2)}, u32[]{:S(2)}) collective-permute-start(f32[2048]{0:T(1024)S(1)} %bitcast.54), channel_id=1, source_target_pairs={{0,1},{1,2},{2,3},{3,0},{4,5},{5,6},{6,7},{7,4},{8,9},{9,10},{10,1... | collective-permute-start | bytes 24584 | tf_op jit(solution)/shard_map/ppermute | solution.py:26
  40.9 14.6 %collective-permute-start.3 = (bf16[20,1,16,720]{3,2,1,0:T(8,128)(2,1)S(1)}, bf16[20,1,16,720]{3,2,1,0:T(8,128)(2,1)S(1)}, u32[]{:S(2)}, u32[]{:S(2)}) collective-permute-start(bf16[20,1,16,720]{3,2,1,0:T(8,128)(2,1)S(1)} %get-tuple-element.126), channel_id=1, source_target_pairs={{4,0},{8,4},{12,8},{16,12},{20,16},{24,20},{28,24},{0,28},{5,1},{9... | collective-permute-start | bytes 1382408 | tf_op jit(solution)/shard_map/ppermute | solution.py:18
  41.0 14.5 %collective-permute-start.2 = (bf16[20,1,16,720]{3,2,1,0:T(8,128)(2,1)S(1)}, bf16[20,1,16,720]{3,2,1,0:T(8,128)(2,1)S(1)}, u32[]{:S(2)}, u32[]{:S(2)}) collective-permute-start(bf16[20,1,16,720]{3,2,1,0:T(8,128)(2,1)S(1)} %get-tuple-element.127), channel_id=1, source_target_pairs={{0,4},{4,8},{8,12},{12,16},{16,20},{20,24},{24,28},{28,0},{1,5},{5... | collective-permute-start | bytes 1382408 | tf_op jit(solution)/shard_map/ppermute | solution.py:15
  48.7 4.8 %collective-permute-start.8 = (f32[1,16,720]{2,1,0:T(8,128)S(1)}, f32[1,16,720]{2,1,0:T(8,128)S(1)}, u32[]{:S(2)}, u32[]{:S(2)}) collective-permute-start(f32[1,16,720]{2,1,0:T(8,128)S(1)} %get-tuple-element.130), channel_id=1, source_target_pairs={{4,0},{8,4},{12,8},{16,12},{20,16},{24,20},{28,24},{0,28},{5,1},{9... | collective-permute-start | bytes 138248 | tf_op jit(solution)/shard_map/ppermute | solution.py:18
  48.7 6.8 %collective-permute-start.7 = (f32[1,16,720]{2,1,0:T(8,128)S(1)}, f32[1,16,720]{2,1,0:T(8,128)S(1)}, u32[]{:S(2)}, u32[]{:S(2)}) collective-permute-start(f32[1,16,720]{2,1,0:T(8,128)S(1)} %get-tuple-element.131), channel_id=1, source_target_pairs={{0,4},{4,8},{8,12},{12,16},{16,20},{20,24},{24,28},{28,0},{1,5},{5... | collective-permute-start | bytes 138248 | tf_op jit(solution)/shard_map/ppermute | solution.py:15
  53.4 2.1 %copy-start.5 = (f32[1,16,720]{2,1,0:T(8,128)}, f32[1,16,720]{2,1,0:T(8,128)S(1)}, u32[]{:S(2)}) copy-start(f32[1,16,720]{2,1,0:T(8,128)S(1)} %collective-permute-done.8.shigh_ref) | copy-start | bytes 138244
  55.5 0.6 copy-start.6
  55.5 0.8 %copy-start.1 = (bf16[20,1,16,720]{3,2,1,0:T(8,128)(2,1)}, bf16[20,1,16,720]{3,2,1,0:T(8,128)(2,1)S(1)}, u32[]{:S(2)}) copy-start(bf16[20,1,16,720]{3,2,1,0:T(8,128)(2,1)S(1)} %collective-permute-done.3.phigh_ref) | copy-start | bytes 1382404
  56.3 0.8 %copy-start.2 = (bf16[20,1,16,720]{3,2,1,0:T(8,128)(2,1)}, bf16[20,1,16,720]{3,2,1,0:T(8,128)(2,1)S(1)}, u32[]{:S(2)}) copy-start(bf16[20,1,16,720]{3,2,1,0:T(8,128)(2,1)S(1)} %collective-permute-done.2.plow_ref) | copy-start | bytes 1382404

commit v5 on v4

--- a/solution.py
+++ b/solution.py
@@ -102,14 +102,42 @@
     ext_ref[padded + radius:padded + 2 * radius, :] = high
 
 
-def forward_sum(control, c_low, c_high, perturb, band_lon, band_lat):
+def split3(values):
+    hi = values.astype(jnp.bfloat16)
+    rest = values - hi.astype(jnp.float32)
+    mid = rest.astype(jnp.bfloat16)
+    lo = (rest - mid.astype(jnp.float32)).astype(jnp.bfloat16)
+    return hi, mid, lo
+
+
+def cell_onehots(cells, row_count, lat_cells):
+    rows = jnp.floor((cells + 0.5) / lat_cells)
+    cols = (cells - rows * lat_cells).astype(jnp.int32)
+    col_ids = lax.broadcasted_iota(jnp.int32, (lat_cells, cells.shape[1]), 0)
+    onehot_cols = jnp.where(col_ids == cols, 1.0, 0.0).astype(jnp.bfloat16)
+    row_ids = lax.broadcasted_iota(jnp.int32, (row_count, cells.shape[1]), 0)
+    return row_ids == rows.astype(jnp.int32), onehot_cols
+
+
+def obs_chunk(count):
+    for size in (2048, 1024, 512, 256, 128):
+        if count % size == 0:
+            return size
+    return count
+
+
+def forward_pick(control, c_low, c_high, perturb, band_lon, band_lat, cells):
     members, levels, lon_cells, lat_cells = control.shape
     radius = c_low.shape[2]
     padded, ext_cells = band_lon.shape
     chunk = member_chunk(members)
-
-    def kernel(ctrl_ref, low_ref, high_ref, pert_ref, blon_ref, blat_ref, out_ref, ext_ref, along_ref):
-        step = pl.program_id(1)
+    steps = members // chunk
+    count = cells.shape[1]
+    block = obs_chunk(count)
+
+    def kernel(ctrl_ref, low_ref, high_ref, pert_ref, blon_ref, blat_ref, cells_ref, out_ref,
+               ext_ref, along_ref, acc_ref):
+        step = pl.program_id(0)
         blon = blon_ref[...]
         for m in range(chunk):
             fill_ext(ext_ref, ctrl_ref[m], low_ref[m], high_ref[m], lon_cells, padded)
@@ -124,33 +152,85 @@
 
         @pl.when(step == 0)
         def _():
-            out_ref[...] = total
-
-        @pl.when(step > 0)
+            acc_ref[...] = jnp.zeros(acc_ref.shape, acc_ref.dtype)
+
+        acc_ref[0:lon_cells, :] = acc_ref[0:lon_cells, :] + total
+
+        @pl.when(step == steps - 1)
         def _():
-            out_ref[...] = out_ref[...] + total
-
-    field = pl.BlockSpec((chunk, None, lon_cells, lat_cells), lambda l, g: (g, l, 0, 0))
-    halo = pl.BlockSpec((chunk, None, radius, lat_cells), lambda l, g: (g, l, 0, 0))
+            pieces = split3(acc_ref[...])
+            for start in range(0, count, block):
+                onehot_rows, onehot_cols = cell_onehots(
+                    cells_ref[:, start:start + block], padded, lat_cells
+                )
+                at_rows = jnp.dot(pieces[0], onehot_cols, preferred_element_type=jnp.float32)
+                at_rows = at_rows + jnp.dot(
+                    pieces[1], onehot_cols, preferred_element_type=jnp.float32
+                )
+                at_rows = at_rows + jnp.dot(
+                    pieces[2], onehot_cols, preferred_element_type=jnp.float32
+                )
+                out_ref[:, start:start + block] = jnp.sum(
+                    jnp.where(onehot_rows, at_rows, 0.0), axis=0, keepdims=True
+                )
+
+    field = pl.BlockSpec((chunk, None, lon_cells, lat_cells), lambda g: (g, 0, 0, 0))
+    halo = pl.BlockSpec((chunk, None, radius, lat_cells), lambda g: (g, 0, 0, 0))
+    whole = lambda shape: pl.BlockSpec(shape, lambda g: (0,) * len(shape))
     return pl.pallas_call(
         kernel,
-        grid=(levels, members // chunk),
+        grid=(steps,),
         in_specs=[
             field,
             halo,
             halo,
             field,
-            pl.BlockSpec(band_lon.shape, lambda l, g: (0, 0)),
-            pl.BlockSpec(band_lat.shape, lambda l, g: (0, 0)),
+            whole(band_lon.shape),
+            whole(band_lat.shape),
+            whole(cells.shape),
         ],
-        out_specs=pl.BlockSpec((None, lon_cells, lat_cells), lambda l, g: (l, 0, 0)),
-        out_shape=jax.ShapeDtypeStruct((levels, lon_cells, lat_cells), jnp.float32),
+        out_specs=whole((1, count)),
+        out_shape=jax.ShapeDtypeStruct((1, count), jnp.float32),
         scratch_shapes=[
             pltpu.VMEM((ext_cells, lat_cells), jnp.bfloat16),
             pltpu.VMEM((chunk * padded, lat_cells), jnp.bfloat16),
+            pltpu.VMEM((padded, lat_cells), jnp.float32),
         ],
-        compiler_params=pltpu.CompilerParams(dimension_semantics=("arbitrary", "arbitrary")),
-    )(control, c_low, c_high, perturb, band_lon, band_lat)
+        compiler_params=pltpu.CompilerParams(dimension_semantics=("arbitrary",)),
+    )(control, c_low, c_high, perturb, band_lon, band_lat, cells)
+
+
+def spread_misfits(at_cells, lists, lon_cells, lat_cells, radius, padded):
+    count = lists.shape[1]
+    block = obs_chunk(count)
+
+    def kernel(at_ref, lists_ref, spread_ref, low_ref, high_ref):
+        misfit = lists_ref[1:2, :] * (at_ref[...] - lists_ref[0:1, :])
+        total = jnp.zeros((padded, lat_cells), jnp.float32)
+        for start in range(0, count, block):
+            onehot_rows, onehot_cols = cell_onehots(
+                lists_ref[2:3, start:start + block], padded, lat_cells
+            )
+            weighted = jnp.where(onehot_rows, misfit[:, start:start + block], 0.0)
+            for piece in split3(weighted):
+                total = total + lax.dot_general(
+                    piece,
+                    onehot_cols,
+                    (((1,), (1,)), ((), ())),
+                    preferred_element_type=jnp.float32,
+                )
+        spread_ref[...] = total[0:lon_cells]
+        low_ref[...] = total[lon_cells - radius:lon_cells]
+        high_ref[...] = total[0:radius]
+
+    return pl.pallas_call(
+        kernel,
+        out_shape=(
+            jax.ShapeDtypeStruct((lon_cells, lat_cells), jnp.float32),
+            jax.ShapeDtypeStruct((radius, lat_cells), jnp.float32),
+            jax.ShapeDtypeStruct((radius, lat_cells), jnp.float32),
+        ),
+    )(at_cells, lists)
 
 
 def backward_grad(perturb, p_low, p_high, spread, s_low, s_high, control, band_lon, band_lat):
@@ -211,64 +291,6 @@
     return jnp.transpose(out, (0, 2, 1, 3))
 
 
-def pick_cells(field_rows, row_index, col_index, block_rows):
-    row_count, col_count = field_rows.shape
-    field_cols = field_rows.T
-
-    def pick_one_block(indices):
-        rows_here, cols_here = indices
-        onehot_rows = (
-            rows_here[:, None] == jnp.arange(row_count, dtype=jnp.int32)[None, :]
-        ).astype(jnp.float32)
-        onehot_cols = (
-            cols_here[:, None] == jnp.arange(col_count, dtype=jnp.int32)[None, :]
-        ).astype(jnp.float32)
-        picked = jnp.dot(
-            onehot_cols,
-            field_cols,
-            precision=lax.Precision.HIGHEST,
-            preferred_element_type=jnp.float32,
-        )
-        return jnp.sum(picked * onehot_rows, axis=1)
-
-    values = lax.map(
-        pick_one_block, (row_index.reshape(-1, block_rows), col_index.reshape(-1, block_rows))
-    )
-    return values.reshape(-1)
-
-
-def spread_cells(misfit, row_index, col_index, row_count, col_count, block_rows):
-
-    def spread_one_block(total, items):
-        rows_here, cols_here, values = items
-        onehot_rows = (
-            rows_here[:, None] == jnp.arange(row_count, dtype=jnp.int32)[None, :]
-        ).astype(jnp.float32)
-        onehot_cols = (
-            cols_here[:, None] == jnp.arange(col_count, dtype=jnp.int32)[None, :]
-        ).astype(jnp.float32)
-        weighted = onehot_rows * values[:, None]
-        return (
-            total
-            + jnp.dot(
-                weighted.T,
-                onehot_cols,
-                precision=lax.Precision.HIGHEST,
-                preferred_element_type=jnp.float32,
-            ),
-            None,
-        )
-
-    start = jnp.zeros((row_count, col_count), jnp.float32)
-    items = (
-        row_index.reshape(-1, block_rows),
-        col_index.reshape(-1, block_rows),
-        misfit.reshape(-1, block_rows),
-    )
-    total, _ = lax.scan(spread_one_block, start, items)
-    return total
-
-
 def local(control, perturb, lon_taps, lat_taps, innov, inv_var, cell_index, counts):
     members_here, levels, lon_cells, lat_cells = control.shape
     radius = lon_taps.shape[0] - 1
@@ -279,26 +301,31 @@
     weights = jnp.where(slot_ids < counts[:, :, None], inv_var, 0.0)
     lists = jnp.stack([innov, weights, cell_index.astype(jnp.float32)])
     received = lax.all_to_all(lists, "tile", split_axis=2, concat_axis=1, tiled=True)
-    observed = received[0].reshape(-1)
-    weight_recv = received[1].reshape(-1)
-    cells_hit = received[2].reshape(-1).astype(jnp.int32)
-    row_index = cells_hit // lat_cells
-    col_index = cells_hit % lat_cells
-    row_count = levels * lon_cells
-    block_rows = math.gcd(observed.shape[0], 1024)
+    received = received.reshape(3, -1)
 
     c_low, c_high = halos(control, "tile", 2, radius)
     late_perturb = lax.optimization_barrier((perturb, c_low, c_high))[0]
     p_low, p_high = halos(late_perturb, "tile", 2, radius)
-    member_sum = forward_sum(control, c_low, c_high, perturb, band_lon, band_lat)
-    partial = pick_cells(member_sum.reshape(row_count, lat_cells), row_index, col_index, block_rows)
+    partial = forward_pick(
+        control, c_low, c_high, perturb, band_lon, band_lat, received[2:3]
+    )
     at_cells = sum_over(partial, "mem")
-    misfit = weight_recv * (at_cells - observed)
-    spread = spread_cells(misfit, row_index, col_index, row_count, lat_cells, block_rows)
-    spread = spread.reshape(levels, lon_cells, lat_cells)
-    s_low, s_high = halos(spread, "tile", 1, radius)
+    spread, low_send, high_send = spread_misfits(
+        at_cells, received, lon_cells, lat_cells, radius, padded
+    )
+    count = lax.axis_size("tile")
+    s_low = lax.ppermute(low_send, "tile", [(i, (i + 1) % count) for i in range(count)])
+    s_high = lax.ppermute(high_send, "tile", [((i + 1) % count, i) for i in range(count)])
     return backward_grad(
-        perturb, p_low, p_high, spread, s_low, s_high, control, band_lon, band_lat
+        perturb,
+        p_low,
+        p_high,
+        spread[None],
+        s_low[None],
+        s_high[None],
+        control,
+        band_lon,
+        band_lat,
     )
 
 

time: 64 us -> 54.2 us (0.85)
  waiting for transfers between devices: 18.4 us -> 11.6 us
  matrix products: 6.57 us -> 0 us
  Pallas kernels: 13.8 us -> 19.7 us
  other arithmetic: 4.63 us -> 2.44 us
  starting transfers between devices: 13.7 us -> 15.1 us
  local copies, waits for them, and re-layouts: 6.07 us -> 4.76 us
    ppermute x3 -> x2, waiting for transfers between devices: 10.2 us -> 0.01 us  [halos(): lax.ppermute(lax.slice_in_dim(block, 0, width, axis=dim), axis, backward)]
    dot_general x4 -> x0, matrix products: 6.57 us -> none  [the longest x2 3.59 us: pick_one_block(): jnp.dot(onehot_cols, field_cols, precision=lax.Precision.HIGHEST, preferr...]
    pallas_call x1 -> x2, Pallas kernels: 5.54 us -> 11.4 us  [the longest x1 7.43 us: forward_pick(): pl.pallas_call(kernel, grid=(steps,), in_specs=[field, halo, halo, field,...]
    all_to_all x1, waiting for transfers between devices: 0.01 us -> 5.13 us  [local(): lax.all_to_all(lists, 'tile', split_axis=2, concat_axis=1, tiled=True)]
    ppermute x3 -> x2, waiting for transfers between devices: 4.18 us -> 0.01 us  [halos(): lax.ppermute(lax.slice_in_dim(block, block.shape[dim] - width, None, axis...]
    ppermute x0 -> x2, starting transfers between devices: none -> 2.64 us  [the longest x1 2.64 us: local(): lax.ppermute(high_send, 'tile', [((i + 1) % count, i) for i in range(coun...]
    ppermute x0 -> x2, waiting for transfers between devices: none -> 2.48 us  [the longest x1 2.48 us: local(): lax.ppermute(low_send, 'tile', [(i, (i + 1) % count) for i in range(count)])]
    all_to_all x1, starting transfers between devices: 5.2 us -> 3.92 us  [local(): lax.all_to_all(lists, 'tile', split_axis=2, concat_axis=1, tiled=True)]
  transfers between devices with their start and end apart: 10 -> 10, of which waited for: 6 -> 4; matrix products, arithmetic and copies ran while one was open for 11% -> 7% of each run, Pallas kernels for 3% -> 11%
where the time goes in v5:
time: 54.2 us; the launch traced here: 53.8 us
  Pallas kernels  19.7 us (36%)
  starting transfers between devices  15.1 us (28%)
  waiting for transfers between devices  11.6 us (21%)
  local copies, waits for them, and re-layouts  4.76 us (9%)
  other arithmetic  2.44 us (5%)
    pallas_call x1, Pallas kernels, forward_pick(): pl.pallas_call(kernel, grid=(steps,), in_specs=[field, halo, halo, field,...  7.43 us
    pallas_call x1, Pallas kernels, backward_grad(): pl.pallas_call(kernel, grid=(levels, members // chunk), in_specs=[field,...  6.38 us
    all_to_all x1, waiting for transfers between devices, local(): lax.all_to_all(lists, 'tile', split_axis=2, concat_axis=1, tiled=True)  5.13 us
    ppermute x3, starting transfers between devices, sum_over(): lax.ppermute(values, axis, [(i, (i + shift) % count) for i in range(count)])  4.6 us
    ppermute x3, waiting for transfers between devices, sum_over(): lax.ppermute(values, axis, [(i, (i + shift) % count) for i in range(count)])  3.95 us
    pallas_call x1, Pallas kernels, spread_misfits(): pl.pallas_call(kernel, out_shape=(jax.ShapeDtypeStruct((lon_cells, lat_ce...  3.95 us
    all_to_all x1, starting transfers between devices, local(): lax.all_to_all(lists, 'tile', split_axis=2, concat_axis=1, tiled=True)  3.92 us
    ppermute x2, starting transfers between devices, halos(): lax.ppermute(lax.slice_in_dim(block, 0, width, axis=dim), axis, backward)  3.71 us
  transfers between devices with their start and end apart: 10, of which 4 were waited for; matrix products, arithmetic and copies ran while one was open for 7% of the time, Pallas kernels for 11%

profile of v5, /device:TPU:0, one launch (start us, length us, event | category | flops | bytes accessed | tf_op | source)
XLA Modules:
  0.0 53.8 jit_solution(848773113232821596)
XLA Ops:
  0.0 0.0 copy-start.13
  0.0 1.5 %fusion.2 = (bf16[20,1,16,720]{3,2,1,0:T(8,128)(2,1)S(1)}, bf16[20,1,16,720]{3,2,1,0:T(8,128)(2,1)S(1)}) fusion(bf16[20,1,45,720]{3,2,1,0:T(8,128)(2,1)} %ctrl_ref.3), kind=kLoop, calls=%fused_computation.7 | loop fusion | bytes 1843200 | tf_op jit(solution)/shard_map/slice | solution.py:18
  1.5 3.4 %collective-permute-start.1 = (bf16[20,1,16,720]{3,2,1,0:T(8,128)(2,1)S(1)}, bf16[20,1,16,720]{3,2,1,0:T(8,128)(2,1)S(1)}, u32[]{:S(2)}, u32[]{:S(2)}) collective-permute-start(bf16[20,1,16,720]{3,2,1,0:T(8,128)(2,1)S(1)} %get-tuple-element.19), channel_id=1, source_target_pairs={{4,0},{8,4},{12,8},{16,12},{20,16},{24,20},{28,24},{0,28},{5,1},{9... | collective-permute-start | bytes 1382408 | tf_op jit(solution)/shard_map/ppermute | solution.py:18
  4.9 0.0 collective-permute-start
  4.9 0.0 copy-done.8
  4.9 0.0 copy-done.9
  5.0 0.0 copy-done.11
  5.0 0.0 copy-done.10
  5.0 0.1 fusion
  5.1 0.6 %pad_maximum_fusion = f32[3,1,8,256]{3,1,0,2:T(1,128)} fusion(f32[1,1,8,256]{3,1,0,2:T(1,128)S(1)} %get-tuple-element.22, f32[1,1,8,256]{3,1,0,2:T(1,128)S(1)} %get-tuple-element.21, f32[1,1,8,256]{3,1,0,2:T(1,128)S(1)} %stack.12), kind=kLoop, calls=%fused_computation.1 | loop fusion | flops 12288 | bytes 49152 | tf_op jit(solution)/shard_map/stack | solution.py:302
  5.7 3.9 %all-to-all-start = ((f32[3,1,8,256]{3,1,0,2:T(1,128)}), f32[3,1,8,256]{3,1,0,2:T(1,128)S(1)}, u32[]{:S(2)}, u32[]{:S(2)}) async-start(f32[3,1,8,256]{3,1,0,2:T(1,128)} %pad_maximum_fusion), calls=%async_computation | async-start | bytes 49152 | tf_op jit(solution)/shard_map/all_to_all | solution.py:303
  9.6 0.0 copy-done.12
  9.6 0.5 convert_element_type.9.lon_ref
  10.1 0.0 copy-done.13
  10.1 0.6 %convert_element_type.10.lat_ref = f32[17]{0:T(128)} convert(bf16[17]{0:T(256)(128)(2,1)S(1)} %copy-done.13) | non-fusion elementwise | flops 17 | bytes 102 | tf_op jit(solution)/shard_map/convert_element_type | solution.py:86
  10.7 2.0 %shard_map.85 = (bf16[48,80]{1,0:T(8,128)(2,1)}, bf16[720,720]{1,0:T(8,128)(2,1)}) custom-call(f32[17]{0:T(128)} %convert_element_type.9.lon_ref, f32[17]{0:T(128)} %convert_element_type.10.lat_ref), custom_call_target="tpu_custom_call" | custom-call | tf_op jit(solution)/shard_map/pallas_call | solution.py:79
  12.7 5.1 %all-to-all-done = f32[3,1,8,256]{3,1,0,2:T(1,128)S(1)} async-done(((f32[3,1,8,256]{3,1,0,2:T(1,128)}), f32[3,1,8,256]{3,1,0,2:T(1,128)S(1)}, u32[]{:S(2)}, u32[]{:S(2)}) %all-to-all-start) | async-done | bytes 24608 | tf_op jit(solution)/shard_map/all_to_all | solution.py:303
  17.8 0.6 %copy.12 = f32[1,3,8,256]{3,1,2,0:T(4,128)} copy(f32[1,3,8,256]{3,2,1,0:T(8,128)S(1)} %bitcast.18) | data formatting | bytes 49152
  18.4 0.6 %slice.25 = f32[1,1,8,256]{3,1,0,2:T(1,128)} slice(f32[3,1,8,256]{3,1,0,2:T(1,128)S(1)} %all-to-all-done), slice={[2:3], [0:1], [0:8], [0:256]} | slice | bytes 16384 | tf_op jit(solution)/shard_map/slice | solution.py:310
  19.0 0.0 collective-permute-done.1.high_ref
  19.0 0.0 collective-permute-done.low_ref
  19.0 0.0 copy-start.4
  19.1 0.8 %copy-done.3 = bf16[20,1,16,720]{3,2,1,0:T(8,128)(2,1)} copy-done((bf16[20,1,16,720]{3,2,1,0:T(8,128)(2,1)}, bf16[20,1,16,720]{3,2,1,0:T(8,128)(2,1)S(1)}, u32[]{:S(2)}) %copy-start.3) | copy-done | bytes 460824
  19.8 0.1 copy-done.4
  20.0 7.4 %shard_map.86 = f32[1,2048]{1,0:T(1,128)} custom-call(bf16[20,1,45,720]{3,2,1,0:T(8,128)(2,1)} %ctrl_ref.3, bf16[20,1,16,720]{3,2,1,0:T(8,128)(2,1)} %copy-done.4, bf16[20,1,16,720]{3,2,1,0:T(8,128)(2,1)} %copy-done.3, bf16[20,1,45,720]{3,2,1,0:T(8,128)(2,1)} %pert_ref.3, bf16[48,80]{1,0:T(8,128)(2,1)} %get-tuple-element.12.blon_ref, ...), custom_call_target="tpu_custom_call" | custom-call | tf_op jit(solution)/shard_map/pallas_call | solution.py:180
  27.4 3.6 %collective-permute-start.6 = (f32[1,2048]{1,0:T(1,128)}, f32[1,2048]{1,0:T(1,128)S(1)}, u32[]{:S(2)}, u32[]{:S(2)}) collective-permute-start(f32[1,2048]{1,0:T(1,128)} %shard_map.86), channel_id=1, source_target_pairs={{0,3},{1,0},{2,1},{3,2},{4,7},{5,4},{6,5},{7,6},{8,11},{9,8},{10,9... | collective-permute-start | bytes 24584 | tf_op jit(solution)/shard_map/ppermute | solution.py:26
  31.0 0.0 collective-permute-start.5
  31.0 1.0 %collective-permute-start.4 = (f32[1,2048]{1,0:T(1,128)}, f32[1,2048]{1,0:T(1,128)S(1)}, u32[]{:S(2)}, u32[]{:S(2)}) collective-permute-start(f32[1,2048]{1,0:T(1,128)} %shard_map.86), channel_id=1, source_target_pairs={{0,1},{1,2},{2,3},{3,0},{4,5},{5,6},{6,7},{7,4},{8,9},{9,10},{10,1... | collective-permute-start | bytes 24584 | tf_op jit(solution)/shard_map/ppermute | solution.py:26
  32.0 0.1 fusion.1
  32.2 0.3 collective-permute-start.3
  32.5 0.3 collective-permute-start.2
  32.7 0.0 collective-permute-done.6
  32.7 3.0 %collective-permute-done.5 = f32[1,2048]{1,0:T(1,128)S(1)} collective-permute-done((f32[1,2048]{1,0:T(1,128)}, f32[1,2048]{1,0:T(1,128)S(1)}, u32[]{:S(2)}, u32[]{:S(2)}) %collective-permute-start.5) | collective-permute-done | bytes 8224 | tf_op jit(solution)/shard_map/ppermute | solution.py:26
  35.8 0.9 %collective-permute-done.4 = f32[1,2048]{1,0:T(1,128)S(1)} collective-permute-done((f32[1,2048]{1,0:T(1,128)}, f32[1,2048]{1,0:T(1,128)S(1)}, u32[]{:S(2)}, u32[]{:S(2)}) %collective-permute-start.4) | collective-permute-done | bytes 8224 | tf_op jit(solution)/shard_map/ppermute | solution.py:26
  36.7 0.6 %add_add_fusion.at_ref = f32[1,2048]{1,0:T(1,128)} fusion(f32[1,2048]{1,0:T(1,128)S(1)} %collective-permute-done.6, f32[1,2048]{1,0:T(1,128)S(1)} %collective-permute-done.5, f32[1,2048]{1,0:T(1,128)S(1)} %copy-done.7, f32[1,2048]{1,0:T(1,128)S(1)} %collective-permute-done.4), kind=kLoop, calls=%fused_computation.5 | loop fusion | flops 6144 | bytes 40960 | tf_op jit(solution)/shard_map/add | solution.py:26
  37.3 4.0 %shard_map.87 = (f32[45,720]{1,0:T(8,128)}, f32[16,720]{1,0:T(8,128)}, f32[16,720]{1,0:T(8,128)}) custom-call(f32[1,2048]{1,0:T(1,128)} %add_add_fusion.at_ref, f32[3,2048]{1,0:T(4,128)} %bitcast.17), custom_call_target="tpu_custom_call" | custom-call | tf_op jit(solution)/shard_map/pallas_call | solution.py:226
  41.2 0.0 collective-permute-start.7
  41.3 2.6 %collective-permute-start.8 = (f32[16,720]{1,0:T(8,128)}, f32[16,720]{1,0:T(8,128)S(1)}, u32[]{:S(2)}, u32[]{:S(2)}) collective-permute-start(f32[16,720]{1,0:T(8,128)} %get-tuple-element.16), channel_id=1, source_target_pairs={{4,0},{8,4},{12,8},{16,12},{20,16},{24,20},{28,24},{0,28},{5,1},{9... | collective-permute-start | bytes 138248 | tf_op jit(solution)/shard_map/ppermute | solution.py:318
  43.9 2.5 %collective-permute-done.7 = f32[16,720]{1,0:T(8,128)S(1)} collective-permute-done((f32[16,720]{1,0:T(8,128)}, f32[16,720]{1,0:T(8,128)S(1)}, u32[]{:S(2)}, u32[]{:S(2)}) %collective-permute-start.7) | collective-permute-done | bytes 46112 | tf_op jit(solution)/shard_map/ppermute | solution.py:317
  46.4 0.0 collective-permute-done.8
  46.4 0.0 collective-permute-done.3.phigh_ref
  46.4 0.0 copy-start.1
  46.4 0.0 collective-permute-done.2.plow_ref
  46.4 0.6 %copy-done.5 = f32[16,720]{1,0:T(8,128)} copy-done((f32[16,720]{1,0:T(8,128)}, f32[16,720]{1,0:T(8,128)S(1)}, u32[]{:S(2)}) %copy-start.5) | copy-done | bytes 46104
  47.0 0.0 copy-done.6
  47.0 0.2 copy-done.1
  47.2 0.2 copy-done.2
  47.4 6.4 %shard_map.88 = f32[20,45,1,720]{3,2,1,0:T(1,128)} custom-call(bf16[20,1,45,720]{3,2,1,0:T(8,128)(2,1)} %pert_ref.3, bf16[20,1,16,720]{3,2,1,0:T(8,128)(2,1)} %copy-done.2, bf16[20,1,16,720]{3,2,1,0:T(8,128)(2,1)} %copy-done.1, f32[1,45,720]{2,1,0:T(8,128)} %bitcast.16, f32[1,16,720]{2,1,0:T(8,128)} %bitcast.19, f32[1,16,720]{2,1,0:T(8,128)} %bitcast.20, ...), custom_call_target="tpu_custom_call" | custom-call | tf_op jit(solution)/shard_map/pallas_call | solution.py:269
  (16 shorter events, 0.0 us)
Async XLA Ops:
  0.0 4.9 %copy-start.8 = (f32[1,8,256]{2,1,0:T(8,128)S(1)}, f32[1,8,256]{2,1,0:T(8,128)}, u32[]{:S(2)}) copy-start(f32[1,8,256]{2,1,0:T(8,128)} %param.12) | copy-start | bytes 24580
  0.0 4.9 %copy-start.9 = (s32[1,8,256]{2,1,0:T(8,128)S(1)}, s32[1,8,256]{2,1,0:T(8,128)}, u32[]{:S(2)}) copy-start(s32[1,8,256]{2,1,0:T(8,128)} %param.14) | copy-start | bytes 24580
  0.0 5.0 %copy-start.11 = (s32[1,8]{1,0:T(1,128)S(1)}, s32[1,8]{1,0:T(1,128)}, u32[]{:S(2)}) copy-start(s32[1,8]{1,0:T(1,128)} %param.15) | copy-start | bytes 100
  0.0 5.0 %copy-start.10 = (f32[1,8,256]{2,1,0:T(8,128)S(1)}, f32[1,8,256]{2,1,0:T(8,128)}, u32[]{:S(2)}) copy-start(f32[1,8,256]{2,1,0:T(8,128)} %param.13) | copy-start | bytes 24580
  0.0 9.6 %copy-start.12 = (bf16[17]{0:T(256)(128)(2,1)S(1)}, bf16[17]{0:T(256)(128)(2,1)}, u32[]{:S(2)}) copy-start(bf16[17]{0:T(256)(128)(2,1)} %param.10) | copy-start | bytes 106
  0.0 10.1 %copy-start.13 = (bf16[17]{0:T(256)(128)(2,1)S(1)}, bf16[17]{0:T(256)(128)(2,1)}, u32[]{:S(2)}) copy-start(bf16[17]{0:T(256)(128)(2,1)} %param.11) | copy-start | bytes 106
  1.5 17.5 %collective-permute-start.1 = (bf16[20,1,16,720]{3,2,1,0:T(8,128)(2,1)S(1)}, bf16[20,1,16,720]{3,2,1,0:T(8,128)(2,1)S(1)}, u32[]{:S(2)}, u32[]{:S(2)}) collective-permute-start(bf16[20,1,16,720]{3,2,1,0:T(8,128)(2,1)S(1)} %get-tuple-element.19), channel_id=1, source_target_pairs={{4,0},{8,4},{12,8},{16,12},{20,16},{24,20},{28,24},{0,28},{5,1},{9... | collective-permute-start | bytes 1382408 | tf_op jit(solution)/shard_map/ppermute | solution.py:18
  4.9 14.1 %collective-permute-start = (bf16[20,1,16,720]{3,2,1,0:T(8,128)(2,1)S(1)}, bf16[20,1,16,720]{3,2,1,0:T(8,128)(2,1)S(1)}, u32[]{:S(2)}, u32[]{:S(2)}) collective-permute-start(bf16[20,1,16,720]{3,2,1,0:T(8,128)(2,1)S(1)} %get-tuple-element.20), channel_id=1, source_target_pairs={{0,4},{4,8},{8,12},{12,16},{16,20},{20,24},{24,28},{28,0},{1,5},{5... | collective-permute-start | bytes 1382408 | tf_op jit(solution)/shard_map/ppermute | solution.py:15
  5.7 12.1 %all-to-all-start = ((f32[3,1,8,256]{3,1,0,2:T(1,128)}), f32[3,1,8,256]{3,1,0,2:T(1,128)S(1)}, u32[]{:S(2)}, u32[]{:S(2)}) async-start(f32[3,1,8,256]{3,1,0,2:T(1,128)} %pad_maximum_fusion), calls=%async_computation | async-start | bytes 49152 | tf_op jit(solution)/shard_map/all_to_all | solution.py:303
  19.0 0.8 %copy-start.3 = (bf16[20,1,16,720]{3,2,1,0:T(8,128)(2,1)}, bf16[20,1,16,720]{3,2,1,0:T(8,128)(2,1)S(1)}, u32[]{:S(2)}) copy-start(bf16[20,1,16,720]{3,2,1,0:T(8,128)(2,1)S(1)} %collective-permute-done.1.high_ref) | copy-start | bytes 1382404
  19.0 0.9 %copy-start.4 = (bf16[20,1,16,720]{3,2,1,0:T(8,128)(2,1)}, bf16[20,1,16,720]{3,2,1,0:T(8,128)(2,1)S(1)}, u32[]{:S(2)}) copy-start(bf16[20,1,16,720]{3,2,1,0:T(8,128)(2,1)S(1)} %collective-permute-done.low_ref) | copy-start | bytes 1382404
  20.0 12.0 %copy-start = (bf16[20,1,45,720]{3,2,1,0:T(8,128)(2,1)S(1)}, bf16[20,1,45,720]{3,2,1,0:T(8,128)(2,1)}, u32[]{:S(2)}) copy-start(bf16[20,1,45,720]{3,2,1,0:T(8,128)(2,1)} %pert_ref.3) | copy-start | bytes 3888004
  27.4 9.3 %copy-start.7 = (f32[1,2048]{1,0:T(1,128)S(1)}, f32[1,2048]{1,0:T(1,128)}, u32[]{:S(2)}) copy-start(f32[1,2048]{1,0:T(1,128)} %shard_map.86) | copy-start | bytes 24580
  27.4 5.3 %collective-permute-start.6 = (f32[1,2048]{1,0:T(1,128)}, f32[1,2048]{1,0:T(1,128)S(1)}, u32[]{:S(2)}, u32[]{:S(2)}) collective-permute-start(f32[1,2048]{1,0:T(1,128)} %shard_map.86), channel_id=1, source_target_pairs={{0,3},{1,0},{2,1},{3,2},{4,7},{5,4},{6,5},{7,6},{8,11},{9,8},{10,9... | collective-permute-start | bytes 24584 | tf_op jit(solution)/shard_map/ppermute | solution.py:26
  31.0 4.8 %collective-permute-start.5 = (f32[1,2048]{1,0:T(1,128)}, f32[1,2048]{1,0:T(1,128)S(1)}, u32[]{:S(2)}, u32[]{:S(2)}) collective-permute-start(f32[1,2048]{1,0:T(1,128)} %shard_map.86), channel_id=1, source_target_pairs={{0,2},{1,3},{2,0},{3,1},{4,6},{5,7},{6,4},{7,5},{8,10},{9,11},{10,... | collective-permute-start | bytes 24584 | tf_op jit(solution)/shard_map/ppermute | solution.py:26
  31.0 5.7 %collective-permute-start.4 = (f32[1,2048]{1,0:T(1,128)}, f32[1,2048]{1,0:T(1,128)S(1)}, u32[]{:S(2)}, u32[]{:S(2)}) collective-permute-start(f32[1,2048]{1,0:T(1,128)} %shard_map.86), channel_id=1, source_target_pairs={{0,1},{1,2},{2,3},{3,0},{4,5},{5,6},{6,7},{7,4},{8,9},{9,10},{10,1... | collective-permute-start | bytes 24584 | tf_op jit(solution)/shard_map/ppermute | solution.py:26
  32.2 14.2 %collective-permute-start.3 = (bf16[20,1,16,720]{3,2,1,0:T(8,128)(2,1)S(1)}, bf16[20,1,16,720]{3,2,1,0:T(8,128)(2,1)S(1)}, u32[]{:S(2)}, u32[]{:S(2)}) collective-permute-start(bf16[20,1,16,720]{3,2,1,0:T(8,128)(2,1)S(1)} %get-tuple-element.17), channel_id=1, source_target_pairs={{4,0},{8,4},{12,8},{16,12},{20,16},{24,20},{28,24},{0,28},{5,1},{9... | collective-permute-start | bytes 1382408 | tf_op jit(solution)/shard_map/ppermute | solution.py:18
  32.5 13.9 %collective-permute-start.2 = (bf16[20,1,16,720]{3,2,1,0:T(8,128)(2,1)S(1)}, bf16[20,1,16,720]{3,2,1,0:T(8,128)(2,1)S(1)}, u32[]{:S(2)}, u32[]{:S(2)}) collective-permute-start(bf16[20,1,16,720]{3,2,1,0:T(8,128)(2,1)S(1)} %get-tuple-element.18), channel_id=1, source_target_pairs={{0,4},{4,8},{8,12},{12,16},{16,20},{20,24},{24,28},{28,0},{1,5},{5... | collective-permute-start | bytes 1382408 | tf_op jit(solution)/shard_map/ppermute | solution.py:15
  41.2 5.1 %collective-permute-start.7 = (f32[16,720]{1,0:T(8,128)}, f32[16,720]{1,0:T(8,128)S(1)}, u32[]{:S(2)}, u32[]{:S(2)}) collective-permute-start(f32[16,720]{1,0:T(8,128)} %get-tuple-element.15), channel_id=1, source_target_pairs={{0,4},{4,8},{8,12},{12,16},{16,20},{20,24},{24,28},{28,0},{1,5},{5... | collective-permute-start | bytes 138248 | tf_op jit(solution)/shard_map/ppermute | solution.py:317
  41.3 5.1 %collective-permute-start.8 = (f32[16,720]{1,0:T(8,128)}, f32[16,720]{1,0:T(8,128)S(1)}, u32[]{:S(2)}, u32[]{:S(2)}) collective-permute-start(f32[16,720]{1,0:T(8,128)} %get-tuple-element.16), channel_id=1, source_target_pairs={{4,0},{8,4},{12,8},{16,12},{20,16},{24,20},{28,24},{0,28},{5,1},{9... | collective-permute-start | bytes 138248 | tf_op jit(solution)/shard_map/ppermute | solution.py:318
  46.4 0.6 %copy-start.5 = (f32[16,720]{1,0:T(8,128)}, f32[16,720]{1,0:T(8,128)S(1)}, u32[]{:S(2)}) copy-start(f32[16,720]{1,0:T(8,128)S(1)} %collective-permute-done.7) | copy-start | bytes 138244
  46.4 0.6 %copy-start.6 = (f32[16,720]{1,0:T(8,128)}, f32[16,720]{1,0:T(8,128)S(1)}, u32[]{:S(2)}) copy-start(f32[16,720]{1,0:T(8,128)S(1)} %collective-permute-done.8) | copy-start | bytes 138244
  46.4 0.8 %copy-start.1 = (bf16[20,1,16,720]{3,2,1,0:T(8,128)(2,1)}, bf16[20,1,16,720]{3,2,1,0:T(8,128)(2,1)S(1)}, u32[]{:S(2)}) copy-start(bf16[20,1,16,720]{3,2,1,0:T(8,128)(2,1)S(1)} %collective-permute-done.3.phigh_ref) | copy-start | bytes 1382404
  46.4 1.0 %copy-start.2 = (bf16[20,1,16,720]{3,2,1,0:T(8,128)(2,1)}, bf16[20,1,16,720]{3,2,1,0:T(8,128)(2,1)S(1)}, u32[]{:S(2)}) copy-start(bf16[20,1,16,720]{3,2,1,0:T(8,128)(2,1)S(1)} %collective-permute-done.2.plow_ref) | copy-start | bytes 1382404

commit v6 on v5

--- a/solution.py
+++ b/solution.py
@@ -126,16 +126,14 @@
     return count
 
 
-def forward_pick(control, c_low, c_high, perturb, band_lon, band_lat, cells):
+def forward_sum(control, c_low, c_high, perturb, band_lon, band_lat):
     members, levels, lon_cells, lat_cells = control.shape
     radius = c_low.shape[2]
     padded, ext_cells = band_lon.shape
     chunk = member_chunk(members)
     steps = members // chunk
-    count = cells.shape[1]
-    block = obs_chunk(count)
-
-    def kernel(ctrl_ref, low_ref, high_ref, pert_ref, blon_ref, blat_ref, cells_ref, out_ref,
+
+    def kernel(ctrl_ref, low_ref, high_ref, pert_ref, blon_ref, blat_ref, out_ref,
                ext_ref, along_ref, acc_ref):
         step = pl.program_id(0)
         blon = blon_ref[...]
@@ -158,21 +156,7 @@
 
         @pl.when(step == steps - 1)
         def _():
-            pieces = split3(acc_ref[...])
-            for start in range(0, count, block):
-                onehot_rows, onehot_cols = cell_onehots(
-                    cells_ref[:, start:start + block], padded, lat_cells
-                )
-                at_rows = jnp.dot(pieces[0], onehot_cols, preferred_element_type=jnp.float32)
-                at_rows = at_rows + jnp.dot(
-                    pieces[1], onehot_cols, preferred_element_type=jnp.float32
-                )
-                at_rows = at_rows + jnp.dot(
-                    pieces[2], onehot_cols, preferred_element_type=jnp.float32
-                )
-                out_ref[:, start:start + block] = jnp.sum(
-                    jnp.where(onehot_rows, at_rows, 0.0), axis=0, keepdims=True
-                )
+            out_ref[...] = acc_ref[...]
 
     field = pl.BlockSpec((chunk, None, lon_cells, lat_cells), lambda g: (g, 0, 0, 0))
     halo = pl.BlockSpec((chunk, None, radius, lat_cells), lambda g: (g, 0, 0, 0))
@@ -187,38 +171,61 @@
             field,
             whole(band_lon.shape),
             whole(band_lat.shape),
-            whole(cells.shape),
         ],
-        out_specs=whole((1, count)),
-        out_shape=jax.ShapeDtypeStruct((1, count), jnp.float32),
+        out_specs=whole((padded, lat_cells)),
+        out_shape=jax.ShapeDtypeStruct((padded, lat_cells), jnp.float32),
         scratch_shapes=[
             pltpu.VMEM((ext_cells, lat_cells), jnp.bfloat16),
             pltpu.VMEM((chunk * padded, lat_cells), jnp.bfloat16),
             pltpu.VMEM((padded, lat_cells), jnp.float32),
         ],
         compiler_params=pltpu.CompilerParams(dimension_semantics=("arbitrary",)),
-    )(control, c_low, c_high, perturb, band_lon, band_lat, cells)
-
-
-def spread_misfits(at_cells, lists, lon_cells, lat_cells, radius, padded):
+    )(control, c_low, c_high, perturb, band_lon, band_lat)
+
+
+def pick_partials(field, cells):
+    padded, lat_cells = field.shape
+    count = cells.shape[1]
+    block = obs_chunk(count)
+
+    def kernel(field_ref, cells_ref, out_ref):
+        pieces = split3(field_ref[...])
+        for start in range(0, count, block):
+            onehot_rows, onehot_cols = cell_onehots(
+                cells_ref[:, start:start + block], padded, lat_cells
+            )
+            at_rows = jnp.dot(pieces[0], onehot_cols, preferred_element_type=jnp.float32)
+            at_rows = at_rows + jnp.dot(pieces[1], onehot_cols, preferred_element_type=jnp.float32)
+            at_rows = at_rows + jnp.dot(pieces[2], onehot_cols, preferred_element_type=jnp.float32)
+            out_ref[:, start:start + block] = jnp.sum(
+                jnp.where(onehot_rows, at_rows, 0.0), axis=0, keepdims=True
+            )
+
+    return pl.pallas_call(kernel, out_shape=jax.ShapeDtypeStruct((1, count), jnp.float32))(
+        field, cells
+    )
+
+
+def spread_misfits(at_cells, lists, cells_col, lon_cells, lat_cells, radius, padded):
     count = lists.shape[1]
     block = obs_chunk(count)
 
-    def kernel(at_ref, lists_ref, spread_ref, low_ref, high_ref):
+    def kernel(at_ref, lists_ref, col_ref, spread_ref, low_ref, high_ref):
         misfit = lists_ref[1:2, :] * (at_ref[...] - lists_ref[0:1, :])
+        cells = lists_ref[2:3, :]
+        rows = jnp.floor((cells + 0.5) / lat_cells).astype(jnp.int32)
         total = jnp.zeros((padded, lat_cells), jnp.float32)
         for start in range(0, count, block):
-            onehot_rows, onehot_cols = cell_onehots(
-                lists_ref[2:3, start:start + block], padded, lat_cells
+            row_ids = lax.broadcasted_iota(jnp.int32, (padded, block), 0)
+            weighted = jnp.where(
+                row_ids == rows[:, start:start + block], misfit[:, start:start + block], 0.0
             )
-            weighted = jnp.where(onehot_rows, misfit[:, start:start + block], 0.0)
+            col_ids = lax.broadcasted_iota(jnp.int32, (block, lat_cells), 1)
+            onehot_cols = jnp.where(
+                col_ids == col_ref[start:start + block, :], 1.0, 0.0
+            ).astype(jnp.bfloat16)
             for piece in split3(weighted):
-                total = total + lax.dot_general(
-                    piece,
-                    onehot_cols,
-                    (((1,), (1,)), ((), ())),
-                    preferred_element_type=jnp.float32,
-                )
+                total = total + jnp.dot(piece, onehot_cols, preferred_element_type=jnp.float32)
         spread_ref[...] = total[0:lon_cells]
         low_ref[...] = total[lon_cells - radius:lon_cells]
         high_ref[...] = total[0:radius]
@@ -230,7 +237,7 @@
             jax.ShapeDtypeStruct((radius, lat_cells), jnp.float32),
             jax.ShapeDtypeStruct((radius, lat_cells), jnp.float32),
         ),
-    )(at_cells, lists)
+    )(at_cells, lists, cells_col)
 
 
 def backward_grad(perturb, p_low, p_high, spread, s_low, s_high, control, band_lon, band_lat):
@@ -306,12 +313,13 @@
     c_low, c_high = halos(control, "tile", 2, radius)
     late_perturb = lax.optimization_barrier((perturb, c_low, c_high))[0]
     p_low, p_high = halos(late_perturb, "tile", 2, radius)
-    partial = forward_pick(
-        control, c_low, c_high, perturb, band_lon, band_lat, received[2:3]
-    )
+    field = forward_sum(control, c_low, c_high, perturb, band_lon, band_lat)
+    partial = pick_partials(field, received[2:3])
     at_cells = sum_over(partial, "mem")
+    cells_hit = received[2].astype(jnp.int32)
+    cells_col = (cells_hit % lat_cells)[:, None]
     spread, low_send, high_send = spread_misfits(
-        at_cells, received, lon_cells, lat_cells, radius, padded
+        at_cells, received, cells_col, lon_cells, lat_cells, radius, padded
     )
     count = lax.axis_size("tile")
     s_low = lax.ppermute(low_send, "tile", [(i, (i + 1) % count) for i in range(count)])

time: 54.2 us -> 61.4 us (1.13)
  other arithmetic: 2.44 us -> 4.91 us
  Pallas kernels: 19.7 us -> 21.4 us
  waiting for transfers between devices: 11.6 us -> 13.1 us
  local copies, waits for them, and re-layouts: 4.76 us -> 5.64 us
    all_to_all x1, waiting for transfers between devices: 5.13 us -> 0.01 us  [local(): lax.all_to_all(lists, 'tile', split_axis=2, concat_axis=1, tiled=True)]
    ppermute x2, waiting for transfers between devices: 0.01 us -> 4.74 us  [halos(): lax.ppermute(lax.slice_in_dim(block, 0, width, axis=dim), axis, backward)]
    ppermute x2, waiting for transfers between devices: 0.01 us -> 2.1 us  [halos(): lax.ppermute(lax.slice_in_dim(block, block.shape[dim] - width, None, axis...]
    pallas_call x1 -> x2, Pallas kernels: 7.43 us -> 9.07 us  [the longest x1 5.66 us: forward_sum(): pl.pallas_call(kernel, grid=(steps,), in_specs=[field, halo, halo, field,...]
    all_to_all x1, starting transfers between devices: 3.92 us -> 5.2 us  [local(): lax.all_to_all(lists, 'tile', split_axis=2, concat_axis=1, tiled=True)]
    select_n x0 -> x1, other arithmetic: none -> 1.14 us  [local(): cells_col = (cells_hit % lat_cells)[:, None]]
    ppermute x2, starting transfers between devices: 3.71 us -> 2.79 us  [halos(): lax.ppermute(lax.slice_in_dim(block, 0, width, axis=dim), axis, backward)]
    another operation x1, local copies, waits for them, and re-layouts: 0.01 us -> 0.73 us  [local(): lists = jnp.stack([innov, weights, cell_index.astype(jnp.float32)])]
  transfers between devices with their start and end apart: 10 -> 10, of which waited for: 4 -> 5; matrix products, arithmetic and copies ran while one was open for 7% -> 10% of each run, Pallas kernels for 11% -> 10%
where the time goes in v6:
time: 61.4 us; the launch traced here: 60.9 us
  Pallas kernels  21.4 us (35%)
  starting transfers between devices  15.7 us (26%)
  waiting for transfers between devices  13.1 us (21%)
  local copies, waits for them, and re-layouts  5.64 us (9%)
  other arithmetic  4.91 us (8%)
    pallas_call x1, Pallas kernels, backward_grad(): pl.pallas_call(kernel, grid=(levels, members // chunk), in_specs=[field,...  6.37 us
    pallas_call x1, Pallas kernels, forward_sum(): pl.pallas_call(kernel, grid=(steps,), in_specs=[field, halo, halo, field,...  5.66 us
    all_to_all x1, starting transfers between devices, local(): lax.all_to_all(lists, 'tile', split_axis=2, concat_axis=1, tiled=True)  5.2 us
    ppermute x2, waiting for transfers between devices, halos(): lax.ppermute(lax.slice_in_dim(block, 0, width, axis=dim), axis, backward)  4.74 us
    ppermute x3, starting transfers between devices, sum_over(): lax.ppermute(values, axis, [(i, (i + shift) % count) for i in range(count)])  4.62 us
    pallas_call x1, Pallas kernels, spread_misfits(): pl.pallas_call(kernel, out_shape=(jax.ShapeDtypeStruct((lon_cells, lat_ce...  4.01 us
    ppermute x3, waiting for transfers between devices, sum_over(): lax.ppermute(values, axis, [(i, (i + shift) % count) for i in range(count)])  3.94 us
    pallas_call x1, Pallas kernels, pick_partials(): pl.pallas_call(kernel, out_shape=jax.ShapeDtypeStruct((1, count), jnp.flo...  3.41 us
  transfers between devices with their start and end apart: 10, of which 5 were waited for; matrix products, arithmetic and copies ran while one was open for 10% of the time, Pallas kernels for 10%

profile of v6, /device:TPU:0, one launch (start us, length us, event | category | flops | bytes accessed | tf_op | source)
XLA Modules:
  0.0 60.9 jit_solution(10926216168454513801)
XLA Ops:
  0.0 0.7 %stack.12 = f32[1,1,8,256]{3,1,0,2:T(1,128)S(1)} reshape(f32[1,8,256]{2,1,0:T(8,128)} %param.12) | data formatting | bytes 16384 | tf_op jit(solution)/shard_map/stack | solution.py:309
  0.7 0.7 %convert_element_type.24 = f32[1,8,256]{2,1,0:T(8,128)S(1)} convert(s32[1,8,256]{2,1,0:T(8,128)} %param.14) | non-fusion elementwise | flops 2048 | bytes 16384 | tf_op jit(solution)/shard_map/convert_element_type | solution.py:309
  1.4 0.8 %fusion = (f32[1,1,8,256]{3,1,0,2:T(1,128)S(1)}, f32[1,1,8,256]{3,1,0,2:T(1,128)S(1)}) fusion(f32[1,8,256]{2,1,0:T(8,128)} %param.13, s32[8]{0:T(128)} %bitcast.24, f32[1,8,256]{2,1,0:T(8,128)S(1)} %convert_element_type.24), kind=kLoop, calls=%fused_computation.4 | loop fusion | flops 4096 | bytes 32800 | tf_op jit(solution)/shard_map/stack | solution.py:309
  2.2 0.6 %pad_maximum_fusion = f32[3,1,8,256]{3,1,0,2:T(1,128)} fusion(f32[1,1,8,256]{3,1,0,2:T(1,128)S(1)} %get-tuple-element.22, f32[1,1,8,256]{3,1,0,2:T(1,128)S(1)} %get-tuple-element.21, f32[1,1,8,256]{3,1,0,2:T(1,128)S(1)} %stack.12), kind=kLoop, calls=%fused_computation.2 | loop fusion | flops 12288 | bytes 49152 | tf_op jit(solution)/shard_map/stack | solution.py:309
  2.8 5.2 %all-to-all-start = ((f32[3,1,8,256]{3,1,0,2:T(1,128)}), f32[3,1,8,256]{3,1,0,2:T(1,128)S(1)}, u32[]{:S(2)}, u32[]{:S(2)}) async-start(f32[3,1,8,256]{3,1,0,2:T(1,128)} %pad_maximum_fusion), calls=%async_computation | async-start | bytes 49152 | tf_op jit(solution)/shard_map/all_to_all | solution.py:310
  8.0 1.4 %fusion.2 = (bf16[20,1,16,720]{3,2,1,0:T(8,128)(2,1)S(1)}, bf16[20,1,16,720]{3,2,1,0:T(8,128)(2,1)S(1)}) fusion(bf16[20,1,45,720]{3,2,1,0:T(8,128)(2,1)} %ctrl_ref.3), kind=kLoop, calls=%fused_computation.9 | loop fusion | bytes 1843200 | tf_op jit(solution)/shard_map/slice | solution.py:18
  9.5 2.7 %collective-permute-start.1 = (bf16[20,1,16,720]{3,2,1,0:T(8,128)(2,1)S(1)}, bf16[20,1,16,720]{3,2,1,0:T(8,128)(2,1)S(1)}, u32[]{:S(2)}, u32[]{:S(2)}) collective-permute-start(bf16[20,1,16,720]{3,2,1,0:T(8,128)(2,1)S(1)} %get-tuple-element.19), channel_id=1, source_target_pairs={{4,0},{8,4},{12,8},{16,12},{20,16},{24,20},{28,24},{0,28},{5,1},{9... | collective-permute-start | bytes 1382408 | tf_op jit(solution)/shard_map/ppermute | solution.py:18
  12.2 0.0 collective-permute-start
  12.2 0.0 copy-done.8
  12.2 0.5 convert_element_type.20.lon_ref
  12.7 0.0 copy-done.9
  12.7 0.5 convert_element_type.21.lat_ref
  13.2 2.0 %shard_map.85 = (bf16[48,80]{1,0:T(8,128)(2,1)}, bf16[720,720]{1,0:T(8,128)(2,1)}) custom-call(f32[17]{0:T(128)} %convert_element_type.20.lon_ref, f32[17]{0:T(128)} %convert_element_type.21.lat_ref), custom_call_target="tpu_custom_call" | custom-call | tf_op jit(solution)/shard_map/pallas_call | solution.py:79
  15.2 0.0 all-to-all-done
  15.2 0.6 %copy.20 = f32[1,3,8,256]{3,1,2,0:T(4,128)} copy(f32[1,3,8,256]{3,2,1,0:T(8,128)S(1)} %bitcast.19) | data formatting | bytes 49152
  15.8 0.4 copy.16
  16.2 0.6 slice.26
  16.8 1.1 %add_select_fusion.col_ref = s32[2048,1]{1,0:T(8,128)} fusion(s32[2048,1]{1,0:T(8,128)S(1)} %copy.16), kind=kLoop, calls=%fused_computation | loop fusion | flops 10240 | bytes 16384 | tf_op jit(solution)/shard_map/jit(remainder)/select_n | solution.py:320
  17.9 4.7 %collective-permute-done.1.high_ref = bf16[20,1,16,720]{3,2,1,0:T(8,128)(2,1)S(1)} collective-permute-done((bf16[20,1,16,720]{3,2,1,0:T(8,128)(2,1)S(1)}, bf16[20,1,16,720]{3,2,1,0:T(8,128)(2,1)S(1)}, u32[]{:S(2)}, u32[]{:S(2)}) %collective-permute-start.1) | collective-permute-done | bytes 460832 | tf_op jit(solution)/shard_map/ppermute | solution.py:18
  22.7 2.1 %collective-permute-done.low_ref = bf16[20,1,16,720]{3,2,1,0:T(8,128)(2,1)S(1)} collective-permute-done((bf16[20,1,16,720]{3,2,1,0:T(8,128)(2,1)S(1)}, bf16[20,1,16,720]{3,2,1,0:T(8,128)(2,1)S(1)}, u32[]{:S(2)}, u32[]{:S(2)}) %collective-permute-start) | collective-permute-done | bytes 460832 | tf_op jit(solution)/shard_map/ppermute | solution.py:15
  24.8 0.0 copy-done.3
  24.8 0.8 %copy-done.4 = bf16[20,1,16,720]{3,2,1,0:T(8,128)(2,1)} copy-done((bf16[20,1,16,720]{3,2,1,0:T(8,128)(2,1)}, bf16[20,1,16,720]{3,2,1,0:T(8,128)(2,1)S(1)}, u32[]{:S(2)}) %copy-start.4) | copy-done | bytes 460824
  25.6 5.7 %shard_map.86.field_ref = f32[48,720]{1,0:T(8,128)} custom-call(bf16[20,1,45,720]{3,2,1,0:T(8,128)(2,1)} %ctrl_ref.3, bf16[20,1,16,720]{3,2,1,0:T(8,128)(2,1)} %copy-done.4, bf16[20,1,16,720]{3,2,1,0:T(8,128)(2,1)} %copy-done.3, bf16[20,1,45,720]{3,2,1,0:T(8,128)(2,1)} %pert_ref.3, bf16[48,80]{1,0:T(8,128)(2,1)} %get-tuple-element.12.blon_ref, ...), custom_call_target="tpu_custom_call" | custom-call | tf_op jit(solution)/shard_map/pallas_call | solution.py:164
  31.2 3.4 %shard_map.87 = f32[1,2048]{1,0:T(1,128)} custom-call(f32[48,720]{1,0:T(8,128)} %shard_map.86.field_ref, f32[1,2048]{1,0:T(1,128)} %bitcast.23), custom_call_target="tpu_custom_call" | custom-call | tf_op jit(solution)/shard_map/pallas_call | solution.py:204
  34.6 3.6 %collective-permute-start.6 = (f32[1,2048]{1,0:T(1,128)}, f32[1,2048]{1,0:T(1,128)S(1)}, u32[]{:S(2)}, u32[]{:S(2)}) collective-permute-start(f32[1,2048]{1,0:T(1,128)} %shard_map.87), channel_id=1, source_target_pairs={{0,3},{1,0},{2,1},{3,2},{4,7},{5,4},{6,5},{7,6},{8,11},{9,8},{10,9... | collective-permute-start | bytes 24584 | tf_op jit(solution)/shard_map/ppermute | solution.py:26
  38.3 0.0 collective-permute-start.5
  38.3 1.0 %collective-permute-start.4 = (f32[1,2048]{1,0:T(1,128)}, f32[1,2048]{1,0:T(1,128)S(1)}, u32[]{:S(2)}, u32[]{:S(2)}) collective-permute-start(f32[1,2048]{1,0:T(1,128)} %shard_map.87), channel_id=1, source_target_pairs={{0,1},{1,2},{2,3},{3,0},{4,5},{5,6},{6,7},{7,4},{8,9},{9,10},{10,1... | collective-permute-start | bytes 24584 | tf_op jit(solution)/shard_map/ppermute | solution.py:26
  39.3 0.0 copy-done
  39.3 0.1 fusion.1
  39.4 0.1 collective-permute-start.3
  39.5 0.5 collective-permute-start.2
  40.0 0.0 collective-permute-done.6
  40.0 3.0 %collective-permute-done.5 = f32[1,2048]{1,0:T(1,128)S(1)} collective-permute-done((f32[1,2048]{1,0:T(1,128)}, f32[1,2048]{1,0:T(1,128)S(1)}, u32[]{:S(2)}, u32[]{:S(2)}) %collective-permute-start.5) | collective-permute-done | bytes 8224 | tf_op jit(solution)/shard_map/ppermute | solution.py:26
  43.0 0.9 %collective-permute-done.4 = f32[1,2048]{1,0:T(1,128)S(1)} collective-permute-done((f32[1,2048]{1,0:T(1,128)}, f32[1,2048]{1,0:T(1,128)S(1)}, u32[]{:S(2)}, u32[]{:S(2)}) %collective-permute-start.4) | collective-permute-done | bytes 8224 | tf_op jit(solution)/shard_map/ppermute | solution.py:26
  43.9 0.6 %add_add_fusion.at_ref = f32[1,2048]{1,0:T(1,128)} fusion(f32[1,2048]{1,0:T(1,128)S(1)} %collective-permute-done.6, f32[1,2048]{1,0:T(1,128)S(1)} %collective-permute-done.5, f32[1,2048]{1,0:T(1,128)S(1)} %copy-done.7, f32[1,2048]{1,0:T(1,128)S(1)} %collective-permute-done.4), kind=kLoop, calls=%fused_computation.7 | loop fusion | flops 6144 | bytes 40960 | tf_op jit(solution)/shard_map/add | solution.py:26
  44.5 4.0 %shard_map.88 = (f32[45,720]{1,0:T(8,128)}, f32[16,720]{1,0:T(8,128)}, f32[16,720]{1,0:T(8,128)}) custom-call(f32[1,2048]{1,0:T(1,128)} %add_add_fusion.at_ref, f32[3,2048]{1,0:T(4,128)} %bitcast.18, s32[2048,1]{1,0:T(8,128)} %add_select_fusion.col_ref), custom_call_target="tpu_custom_call" | custom-call | tf_op jit(solution)/shard_map/pallas_call | solution.py:233
  48.5 0.0 collective-permute-start.7
  48.5 2.6 %collective-permute-start.8 = (f32[16,720]{1,0:T(8,128)}, f32[16,720]{1,0:T(8,128)S(1)}, u32[]{:S(2)}, u32[]{:S(2)}) collective-permute-start(f32[16,720]{1,0:T(8,128)} %get-tuple-element.16), channel_id=1, source_target_pairs={{4,0},{8,4},{12,8},{16,12},{20,16},{24,20},{28,24},{0,28},{5,1},{9... | collective-permute-start | bytes 138248 | tf_op jit(solution)/shard_map/ppermute | solution.py:326
  51.2 2.3 %collective-permute-done.7 = f32[16,720]{1,0:T(8,128)S(1)} collective-permute-done((f32[16,720]{1,0:T(8,128)}, f32[16,720]{1,0:T(8,128)S(1)}, u32[]{:S(2)}, u32[]{:S(2)}) %collective-permute-start.7) | collective-permute-done | bytes 46112 | tf_op jit(solution)/shard_map/ppermute | solution.py:325
  53.5 0.0 collective-permute-done.8
  53.5 0.0 collective-permute-done.3.phigh_ref
  53.6 0.0 collective-permute-done.2.plow_ref
  53.6 0.0 copy-start.2
  53.6 0.6 copy-done.5
  54.1 0.0 copy-done.6
  54.2 0.2 copy-done.1
  54.4 0.2 copy-done.2
  54.5 6.4 %shard_map.89 = f32[20,45,1,720]{3,2,1,0:T(1,128)} custom-call(bf16[20,1,45,720]{3,2,1,0:T(8,128)(2,1)} %pert_ref.3, bf16[20,1,16,720]{3,2,1,0:T(8,128)(2,1)} %copy-done.2, bf16[20,1,16,720]{3,2,1,0:T(8,128)(2,1)} %copy-done.1, f32[1,45,720]{2,1,0:T(8,128)} %bitcast.17, f32[1,16,720]{2,1,0:T(8,128)} %bitcast.20, f32[1,16,720]{2,1,0:T(8,128)} %bitcast.21, ...), custom_call_target="tpu_custom_call" | custom-call | tf_op jit(solution)/shard_map/pallas_call | solution.py:276
  (12 shorter events, 0.1 us)
Async XLA Ops:
  0.0 12.2 %copy-start.8 = (bf16[17]{0:T(256)(128)(2,1)S(1)}, bf16[17]{0:T(256)(128)(2,1)}, u32[]{:S(2)}) copy-start(bf16[17]{0:T(256)(128)(2,1)} %param.10) | copy-start | bytes 106
  0.0 12.7 %copy-start.9 = (bf16[17]{0:T(256)(128)(2,1)S(1)}, bf16[17]{0:T(256)(128)(2,1)}, u32[]{:S(2)}) copy-start(bf16[17]{0:T(256)(128)(2,1)} %param.11) | copy-start | bytes 106
  2.8 12.3 %all-to-all-start = ((f32[3,1,8,256]{3,1,0,2:T(1,128)}), f32[3,1,8,256]{3,1,0,2:T(1,128)S(1)}, u32[]{:S(2)}, u32[]{:S(2)}) async-start(f32[3,1,8,256]{3,1,0,2:T(1,128)} %pad_maximum_fusion), calls=%async_computation | async-start | bytes 49152 | tf_op jit(solution)/shard_map/all_to_all | solution.py:310
  9.5 13.2 %collective-permute-start.1 = (bf16[20,1,16,720]{3,2,1,0:T(8,128)(2,1)S(1)}, bf16[20,1,16,720]{3,2,1,0:T(8,128)(2,1)S(1)}, u32[]{:S(2)}, u32[]{:S(2)}) collective-permute-start(bf16[20,1,16,720]{3,2,1,0:T(8,128)(2,1)S(1)} %get-tuple-element.19), channel_id=1, source_target_pairs={{4,0},{8,4},{12,8},{16,12},{20,16},{24,20},{28,24},{0,28},{5,1},{9... | collective-permute-start | bytes 1382408 | tf_op jit(solution)/shard_map/ppermute | solution.py:18
  12.2 12.6 %collective-permute-start = (bf16[20,1,16,720]{3,2,1,0:T(8,128)(2,1)S(1)}, bf16[20,1,16,720]{3,2,1,0:T(8,128)(2,1)S(1)}, u32[]{:S(2)}, u32[]{:S(2)}) collective-permute-start(bf16[20,1,16,720]{3,2,1,0:T(8,128)(2,1)S(1)} %get-tuple-element.20), channel_id=1, source_target_pairs={{0,4},{4,8},{8,12},{12,16},{16,20},{20,24},{24,28},{28,0},{1,5},{5... | collective-permute-start | bytes 1382408 | tf_op jit(solution)/shard_map/ppermute | solution.py:15
  22.7 2.1 %copy-start.3 = (bf16[20,1,16,720]{3,2,1,0:T(8,128)(2,1)}, bf16[20,1,16,720]{3,2,1,0:T(8,128)(2,1)S(1)}, u32[]{:S(2)}) copy-start(bf16[20,1,16,720]{3,2,1,0:T(8,128)(2,1)S(1)} %collective-permute-done.1.high_ref) | copy-start | bytes 1382404
  24.8 0.8 %copy-start.4 = (bf16[20,1,16,720]{3,2,1,0:T(8,128)(2,1)}, bf16[20,1,16,720]{3,2,1,0:T(8,128)(2,1)S(1)}, u32[]{:S(2)}) copy-start(bf16[20,1,16,720]{3,2,1,0:T(8,128)(2,1)S(1)} %collective-permute-done.low_ref) | copy-start | bytes 1382404
  25.6 13.7 %copy-start = (bf16[20,1,45,720]{3,2,1,0:T(8,128)(2,1)S(1)}, bf16[20,1,45,720]{3,2,1,0:T(8,128)(2,1)}, u32[]{:S(2)}) copy-start(bf16[20,1,45,720]{3,2,1,0:T(8,128)(2,1)} %pert_ref.3) | copy-start | bytes 3888004
  34.6 9.3 %copy-start.7 = (f32[1,2048]{1,0:T(1,128)S(1)}, f32[1,2048]{1,0:T(1,128)}, u32[]{:S(2)}) copy-start(f32[1,2048]{1,0:T(1,128)} %shard_map.87) | copy-start | bytes 24580
  34.6 5.3 %collective-permute-start.6 = (f32[1,2048]{1,0:T(1,128)}, f32[1,2048]{1,0:T(1,128)S(1)}, u32[]{:S(2)}, u32[]{:S(2)}) collective-permute-start(f32[1,2048]{1,0:T(1,128)} %shard_map.87), channel_id=1, source_target_pairs={{0,3},{1,0},{2,1},{3,2},{4,7},{5,4},{6,5},{7,6},{8,11},{9,8},{10,9... | collective-permute-start | bytes 24584 | tf_op jit(solution)/shard_map/ppermute | solution.py:26
  38.3 4.8 %collective-permute-start.5 = (f32[1,2048]{1,0:T(1,128)}, f32[1,2048]{1,0:T(1,128)S(1)}, u32[]{:S(2)}, u32[]{:S(2)}) collective-permute-start(f32[1,2048]{1,0:T(1,128)} %shard_map.87), channel_id=1, source_target_pairs={{0,2},{1,3},{2,0},{3,1},{4,6},{5,7},{6,4},{7,5},{8,10},{9,11},{10,... | collective-permute-start | bytes 24584 | tf_op jit(solution)/shard_map/ppermute | solution.py:26
  38.3 5.7 %collective-permute-start.4 = (f32[1,2048]{1,0:T(1,128)}, f32[1,2048]{1,0:T(1,128)S(1)}, u32[]{:S(2)}, u32[]{:S(2)}) collective-permute-start(f32[1,2048]{1,0:T(1,128)} %shard_map.87), channel_id=1, source_target_pairs={{0,1},{1,2},{2,3},{3,0},{4,5},{5,6},{6,7},{7,4},{8,9},{9,10},{10,1... | collective-permute-start | bytes 24584 | tf_op jit(solution)/shard_map/ppermute | solution.py:26
  39.4 14.1 %collective-permute-start.3 = (bf16[20,1,16,720]{3,2,1,0:T(8,128)(2,1)S(1)}, bf16[20,1,16,720]{3,2,1,0:T(8,128)(2,1)S(1)}, u32[]{:S(2)}, u32[]{:S(2)}) collective-permute-start(bf16[20,1,16,720]{3,2,1,0:T(8,128)(2,1)S(1)} %get-tuple-element.17), channel_id=1, source_target_pairs={{4,0},{8,4},{12,8},{16,12},{20,16},{24,20},{28,24},{0,28},{5,1},{9... | collective-permute-start | bytes 1382408 | tf_op jit(solution)/shard_map/ppermute | solution.py:18
  39.5 14.0 %collective-permute-start.2 = (bf16[20,1,16,720]{3,2,1,0:T(8,128)(2,1)S(1)}, bf16[20,1,16,720]{3,2,1,0:T(8,128)(2,1)S(1)}, u32[]{:S(2)}, u32[]{:S(2)}) collective-permute-start(bf16[20,1,16,720]{3,2,1,0:T(8,128)(2,1)S(1)} %get-tuple-element.18), channel_id=1, source_target_pairs={{0,4},{4,8},{8,12},{12,16},{16,20},{20,24},{24,28},{28,0},{1,5},{5... | collective-permute-start | bytes 1382408 | tf_op jit(solution)/shard_map/ppermute | solution.py:15
  48.5 5.0 %collective-permute-start.7 = (f32[16,720]{1,0:T(8,128)}, f32[16,720]{1,0:T(8,128)S(1)}, u32[]{:S(2)}, u32[]{:S(2)}) collective-permute-start(f32[16,720]{1,0:T(8,128)} %get-tuple-element.15), channel_id=1, source_target_pairs={{0,4},{4,8},{8,12},{12,16},{16,20},{20,24},{24,28},{28,0},{1,5},{5... | collective-permute-start | bytes 138248 | tf_op jit(solution)/shard_map/ppermute | solution.py:325
  48.5 5.0 %collective-permute-start.8 = (f32[16,720]{1,0:T(8,128)}, f32[16,720]{1,0:T(8,128)S(1)}, u32[]{:S(2)}, u32[]{:S(2)}) collective-permute-start(f32[16,720]{1,0:T(8,128)} %get-tuple-element.16), channel_id=1, source_target_pairs={{4,0},{8,4},{12,8},{16,12},{20,16},{24,20},{28,24},{0,28},{5,1},{9... | collective-permute-start | bytes 138248 | tf_op jit(solution)/shard_map/ppermute | solution.py:326
  53.5 0.6 %copy-start.5 = (f32[16,720]{1,0:T(8,128)}, f32[16,720]{1,0:T(8,128)S(1)}, u32[]{:S(2)}) copy-start(f32[16,720]{1,0:T(8,128)S(1)} %collective-permute-done.7) | copy-start | bytes 138244
  53.5 0.6 %copy-start.6 = (f32[16,720]{1,0:T(8,128)}, f32[16,720]{1,0:T(8,128)S(1)}, u32[]{:S(2)}) copy-start(f32[16,720]{1,0:T(8,128)S(1)} %collective-permute-done.8) | copy-start | bytes 138244
  53.5 0.8 %copy-start.1 = (bf16[20,1,16,720]{3,2,1,0:T(8,128)(2,1)}, bf16[20,1,16,720]{3,2,1,0:T(8,128)(2,1)S(1)}, u32[]{:S(2)}) copy-start(bf16[20,1,16,720]{3,2,1,0:T(8,128)(2,1)S(1)} %collective-permute-done.3.phigh_ref) | copy-start | bytes 1382404
  53.6 1.0 %copy-start.2 = (bf16[20,1,16,720]{3,2,1,0:T(8,128)(2,1)}, bf16[20,1,16,720]{3,2,1,0:T(8,128)(2,1)S(1)}, u32[]{:S(2)}) copy-start(bf16[20,1,16,720]{3,2,1,0:T(8,128)(2,1)S(1)} %collective-permute-done.2.plow_ref) | copy-start | bytes 1382404

commit v7 on v5

--- a/solution.py
+++ b/solution.py
@@ -110,20 +110,13 @@
     return hi, mid, lo
 
 
-def cell_onehots(cells, row_count, lat_cells):
+def cell_keys(cells, padded, lat_cells):
     rows = jnp.floor((cells + 0.5) / lat_cells)
     cols = (cells - rows * lat_cells).astype(jnp.int32)
-    col_ids = lax.broadcasted_iota(jnp.int32, (lat_cells, cells.shape[1]), 0)
-    onehot_cols = jnp.where(col_ids == cols, 1.0, 0.0).astype(jnp.bfloat16)
-    row_ids = lax.broadcasted_iota(jnp.int32, (row_count, cells.shape[1]), 0)
-    return row_ids == rows.astype(jnp.int32), onehot_cols
-
-
-def obs_chunk(count):
-    for size in (2048, 1024, 512, 256, 128):
-        if count % size == 0:
-            return size
-    return count
+    keys = (cols // 128) * padded + rows.astype(jnp.int32)
+    lane_ids = lax.broadcasted_iota(jnp.int32, (128, cells.shape[1]), 0)
+    onehot = jnp.where(lane_ids == cols % 128, 1.0, 0.0).astype(jnp.bfloat16)
+    return keys, onehot
 
 
 def forward_pick(control, c_low, c_high, perturb, band_lon, band_lat, cells):
@@ -132,11 +125,11 @@
     padded, ext_cells = band_lon.shape
     chunk = member_chunk(members)
     steps = members // chunk
-    count = cells.shape[1]
-    block = obs_chunk(count)
+    _, sources, slots = cells.shape
+    parts = -(-lat_cells // 128)
 
     def kernel(ctrl_ref, low_ref, high_ref, pert_ref, blon_ref, blat_ref, cells_ref, out_ref,
-               ext_ref, along_ref, acc_ref):
+               ext_ref, along_ref, acc_ref, fold_ref):
         step = pl.program_id(0)
         blon = blon_ref[...]
         for m in range(chunk):
@@ -158,20 +151,21 @@
 
         @pl.when(step == steps - 1)
         def _():
-            pieces = split3(acc_ref[...])
-            for start in range(0, count, block):
-                onehot_rows, onehot_cols = cell_onehots(
-                    cells_ref[:, start:start + block], padded, lat_cells
-                )
-                at_rows = jnp.dot(pieces[0], onehot_cols, preferred_element_type=jnp.float32)
-                at_rows = at_rows + jnp.dot(
-                    pieces[1], onehot_cols, preferred_element_type=jnp.float32
-                )
-                at_rows = at_rows + jnp.dot(
-                    pieces[2], onehot_cols, preferred_element_type=jnp.float32
-                )
-                out_ref[:, start:start + block] = jnp.sum(
-                    jnp.where(onehot_rows, at_rows, 0.0), axis=0, keepdims=True
+            fold_ref[...] = jnp.zeros(fold_ref.shape, fold_ref.dtype)
+            for part in range(parts):
+                width = min(128, lat_cells - part * 128)
+                fold_ref[part * padded:(part + 1) * padded, 0:width] = acc_ref[
+                    :, part * 128:part * 128 + width
+                ]
+            pieces = split3(fold_ref[...])
+            key_ids = lax.broadcasted_iota(jnp.int32, (parts * padded, slots), 0)
+            for row in range(sources):
+                keys, onehot = cell_keys(cells_ref[2, row:row + 1, :], padded, lat_cells)
+                at_keys = jnp.dot(pieces[0], onehot, preferred_element_type=jnp.float32)
+                at_keys = at_keys + jnp.dot(pieces[1], onehot, preferred_element_type=jnp.float32)
+                at_keys = at_keys + jnp.dot(pieces[2], onehot, preferred_element_type=jnp.float32)
+                out_ref[row:row + 1, :] = jnp.sum(
+                    jnp.where(key_ids == keys, at_keys, 0.0), axis=0, keepdims=True
                 )
 
     field = pl.BlockSpec((chunk, None, lon_cells, lat_cells), lambda g: (g, 0, 0, 0))
@@ -189,39 +183,46 @@
             whole(band_lat.shape),
             whole(cells.shape),
         ],
-        out_specs=whole((1, count)),
-        out_shape=jax.ShapeDtypeStruct((1, count), jnp.float32),
+        out_specs=whole((sources, slots)),
+        out_shape=jax.ShapeDtypeStruct((sources, slots), jnp.float32),
         scratch_shapes=[
             pltpu.VMEM((ext_cells, lat_cells), jnp.bfloat16),
             pltpu.VMEM((chunk * padded, lat_cells), jnp.bfloat16),
             pltpu.VMEM((padded, lat_cells), jnp.float32),
+            pltpu.VMEM((parts * padded, 128), jnp.float32),
         ],
         compiler_params=pltpu.CompilerParams(dimension_semantics=("arbitrary",)),
     )(control, c_low, c_high, perturb, band_lon, band_lat, cells)
 
 
 def spread_misfits(at_cells, lists, lon_cells, lat_cells, radius, padded):
-    count = lists.shape[1]
-    block = obs_chunk(count)
-
-    def kernel(at_ref, lists_ref, spread_ref, low_ref, high_ref):
-        misfit = lists_ref[1:2, :] * (at_ref[...] - lists_ref[0:1, :])
-        total = jnp.zeros((padded, lat_cells), jnp.float32)
-        for start in range(0, count, block):
-            onehot_rows, onehot_cols = cell_onehots(
-                lists_ref[2:3, start:start + block], padded, lat_cells
+    _, sources, slots = lists.shape
+    parts = -(-lat_cells // 128)
+
+    def kernel(at_ref, lists_ref, spread_ref, low_ref, high_ref, fold_ref):
+        key_ids = lax.broadcasted_iota(jnp.int32, (parts * padded, slots), 0)
+        folded = jnp.zeros((parts * padded, 128), jnp.float32)
+        for row in range(sources):
+            misfit = lists_ref[1, row:row + 1, :] * (
+                at_ref[row:row + 1, :] - lists_ref[0, row:row + 1, :]
             )
-            weighted = jnp.where(onehot_rows, misfit[:, start:start + block], 0.0)
-            for piece in split3(weighted):
-                total = total + lax.dot_general(
-                    piece,
-                    onehot_cols,
+            keys, onehot = cell_keys(lists_ref[2, row:row + 1, :], padded, lat_cells)
+            for piece in split3(misfit):
+                weighted = jnp.where(key_ids == keys, piece.astype(jnp.float32), 0.0)
+                folded = folded + lax.dot_general(
+                    weighted.astype(jnp.bfloat16),
+                    onehot,
                     (((1,), (1,)), ((), ())),
                     preferred_element_type=jnp.float32,
                 )
-        spread_ref[...] = total[0:lon_cells]
-        low_ref[...] = total[lon_cells - radius:lon_cells]
-        high_ref[...] = total[0:radius]
+        for part in range(parts):
+            width = min(128, lat_cells - part * 128)
+            fold_ref[:, part * 128:part * 128 + width] = folded[
+                part * padded:(part + 1) * padded, 0:width
+            ]
+        spread_ref[...] = fold_ref[0:lon_cells, :]
+        low_ref[...] = fold_ref[lon_cells - radius:lon_cells, :]
+        high_ref[...] = fold_ref[0:radius, :]
 
     return pl.pallas_call(
         kernel,
@@ -230,6 +231,7 @@
             jax.ShapeDtypeStruct((radius, lat_cells), jnp.float32),
             jax.ShapeDtypeStruct((radius, lat_cells), jnp.float32),
         ),
+        scratch_shapes=[pltpu.VMEM((padded, lat_cells), jnp.float32)],
     )(at_cells, lists)
 
 
@@ -299,15 +301,14 @@
 
     slot_ids = lax.broadcasted_iota(jnp.int32, innov.shape, 2)
     weights = jnp.where(slot_ids < counts[:, :, None], inv_var, 0.0)
-    lists = jnp.stack([innov, weights, cell_index.astype(jnp.float32)])
-    received = lax.all_to_all(lists, "tile", split_axis=2, concat_axis=1, tiled=True)
-    received = received.reshape(3, -1)
+    lists = jnp.concatenate([innov, weights, cell_index.astype(jnp.float32)])
+    received = lax.all_to_all(lists, "tile", split_axis=1, concat_axis=1, tiled=True)
 
     c_low, c_high = halos(control, "tile", 2, radius)
     late_perturb = lax.optimization_barrier((perturb, c_low, c_high))[0]
     p_low, p_high = halos(late_perturb, "tile", 2, radius)
     partial = forward_pick(
-        control, c_low, c_high, perturb, band_lon, band_lat, received[2:3]
+        control, c_low, c_high, perturb, band_lon, band_lat, received
     )
     at_cells = sum_over(partial, "mem")
     spread, low_send, high_send = spread_misfits(

time: 54.2 us -> 64.6 us (1.19)
  waiting for transfers between devices: 11.6 us -> 24.5 us
  Pallas kernels: 19.7 us -> 17.5 us
  local copies, waits for them, and re-layouts: 4.76 us -> 3.28 us
    ppermute x2, waiting for transfers between devices: 0.01 us -> 10.7 us  [halos(): lax.ppermute(lax.slice_in_dim(block, 0, width, axis=dim), axis, backward)]
    ppermute x2, waiting for transfers between devices: 0.01 us -> 1.93 us  [halos(): lax.ppermute(lax.slice_in_dim(block, block.shape[dim] - width, None, axis...]
    unnamed x29 -> x27, local copies, waits for them, and re-layouts: 2.55 us -> 1.01 us
    pallas_call x1, Pallas kernels: 3.95 us -> 2.56 us  [spread_misfits(): pl.pallas_call(kernel, out_shape=(jax.ShapeDtypeStruct((lon_cells, lat_ce...]
    pallas_call x1, Pallas kernels: 7.43 us -> 6.56 us  [forward_pick(): pl.pallas_call(kernel, grid=(steps,), in_specs=[field, halo, halo, field,...]
    another operation x2 -> x0, other arithmetic: 0.71 us -> none  [local(): lists = jnp.stack([innov, weights, cell_index.astype(jnp.float32)])]
    ppermute x3, waiting for transfers between devices: 3.95 us -> 4.65 us  [sum_over(): lax.ppermute(values, axis, [(i, (i + shift) % count) for i in range(count)])]
    add x1, other arithmetic: 0.61 us -> 1.3 us  [sum_over(): total + lax.ppermute(values, axis, [(i, (i + shift) % count) for i in ran...]
  transfers between devices with their start and end apart: 10 -> 10, of which waited for: 4 -> 8; matrix products, arithmetic and copies ran while one was open for 7% -> 6% of each run, Pallas kernels for 11% -> 17%
where the time goes in v7:
time: 64.6 us; the launch traced here: 64 us
  waiting for transfers between devices  24.5 us (38%)
  Pallas kernels  17.5 us (27%)
  starting transfers between devices  15.5 us (24%)
  local copies, waits for them, and re-layouts  3.28 us (5%)
  other arithmetic  3.07 us (5%)
    ppermute x2, waiting for transfers between devices, halos(): lax.ppermute(lax.slice_in_dim(block, 0, width, axis=dim), axis, backward)  10.7 us
    pallas_call x1, Pallas kernels, forward_pick(): pl.pallas_call(kernel, grid=(steps,), in_specs=[field, halo, halo, field,...  6.56 us
    pallas_call x1, Pallas kernels, backward_grad(): pl.pallas_call(kernel, grid=(levels, members // chunk), in_specs=[field,...  6.37 us
    all_to_all x1, waiting for transfers between devices, local(): lax.all_to_all(lists, 'tile', split_axis=1, concat_axis=1, tiled=True)  5.18 us
    ppermute x3, waiting for transfers between devices, sum_over(): lax.ppermute(values, axis, [(i, (i + shift) % count) for i in range(count)])  4.65 us
    ppermute x3, starting transfers between devices, sum_over(): lax.ppermute(values, axis, [(i, (i + shift) % count) for i in range(count)])  4.61 us
    ppermute x2, starting transfers between devices, halos(): lax.ppermute(lax.slice_in_dim(block, 0, width, axis=dim), axis, backward)  4.37 us
    all_to_all x1, starting transfers between devices, local(): lax.all_to_all(lists, 'tile', split_axis=1, concat_axis=1, tiled=True)  3.92 us
  transfers between devices with their start and end apart: 10, of which 8 were waited for; matrix products, arithmetic and copies ran while one was open for 6% of the time, Pallas kernels for 17%

profile of v7, /device:TPU:0, one launch (start us, length us, event | category | flops | bytes accessed | tf_op | source)
XLA Modules:
  0.0 64.0 jit_solution(12816387824569289411)
XLA Ops:
  0.0 1.5 %fusion.1 = (bf16[20,1,16,720]{3,2,1,0:T(8,128)(2,1)S(1)}, bf16[20,1,16,720]{3,2,1,0:T(8,128)(2,1)S(1)}) fusion(bf16[20,1,45,720]{3,2,1,0:T(8,128)(2,1)} %ctrl_ref.3), kind=kLoop, calls=%fused_computation.4 | loop fusion | bytes 1843200 | tf_op jit(solution)/shard_map/slice | solution.py:18
  1.5 0.0 copy-start.7
  1.5 0.0 copy-start.10
  1.5 0.0 copy-start.8
  1.6 0.0 copy-start.9
  1.6 0.0 copy-start.11
  1.6 0.0 copy-start.12
  1.6 3.4 %collective-permute-start.1 = (bf16[20,1,16,720]{3,2,1,0:T(8,128)(2,1)S(1)}, bf16[20,1,16,720]{3,2,1,0:T(8,128)(2,1)S(1)}, u32[]{:S(2)}, u32[]{:S(2)}) collective-permute-start(bf16[20,1,16,720]{3,2,1,0:T(8,128)(2,1)S(1)} %get-tuple-element.19), channel_id=1, source_target_pairs={{4,0},{8,4},{12,8},{16,12},{20,16},{24,20},{28,24},{0,28},{5,1},{9... | collective-permute-start | bytes 1382408 | tf_op jit(solution)/shard_map/ppermute | solution.py:18
  5.0 0.0 collective-permute-start
  5.0 10.7 %collective-permute-done.1.high_ref = bf16[20,1,16,720]{3,2,1,0:T(8,128)(2,1)S(1)} collective-permute-done((bf16[20,1,16,720]{3,2,1,0:T(8,128)(2,1)S(1)}, bf16[20,1,16,720]{3,2,1,0:T(8,128)(2,1)S(1)}, u32[]{:S(2)}, u32[]{:S(2)}) %collective-permute-start.1) | collective-permute-done | bytes 460832 | tf_op jit(solution)/shard_map/ppermute | solution.py:18
  15.7 1.9 %collective-permute-done.low_ref = bf16[20,1,16,720]{3,2,1,0:T(8,128)(2,1)S(1)} collective-permute-done((bf16[20,1,16,720]{3,2,1,0:T(8,128)(2,1)S(1)}, bf16[20,1,16,720]{3,2,1,0:T(8,128)(2,1)S(1)}, u32[]{:S(2)}, u32[]{:S(2)}) %collective-permute-start) | collective-permute-done | bytes 460832 | tf_op jit(solution)/shard_map/ppermute | solution.py:15
  17.6 0.0 copy-done
  17.7 0.1 fusion
  17.8 1.0 %collective-permute-start.3 = (bf16[20,1,16,720]{3,2,1,0:T(8,128)(2,1)S(1)}, bf16[20,1,16,720]{3,2,1,0:T(8,128)(2,1)S(1)}, u32[]{:S(2)}, u32[]{:S(2)}) collective-permute-start(bf16[20,1,16,720]{3,2,1,0:T(8,128)(2,1)S(1)} %get-tuple-element.17), channel_id=1, source_target_pairs={{4,0},{8,4},{12,8},{16,12},{20,16},{24,20},{28,24},{0,28},{5,1},{9... | collective-permute-start | bytes 1382408 | tf_op jit(solution)/shard_map/ppermute | solution.py:18
  18.8 0.0 collective-permute-start.2
  18.8 0.0 copy-done.7
  18.8 0.0 copy-done.10
  18.8 0.1 compare_select_fusion
  18.8 0.0 copy-done.8
  18.9 0.0 copy-done.9
  18.9 0.6 pad_maximum_fusion
  19.5 3.9 %all-to-all-start = ((f32[3,8,256]{2,0,1:T(4,128)}), f32[3,8,256]{2,0,1:T(4,128)S(1)}, u32[]{:S(2)}, u32[]{:S(2)}) async-start(f32[3,8,256]{2,0,1:T(4,128)} %pad_maximum_fusion), calls=%async_computation | async-start | bytes 65536 | tf_op jit(solution)/shard_map/all_to_all | solution.py:305
  23.5 0.0 copy-done.11
  23.5 0.5 convert_element_type.9.lon_ref
  24.0 0.5 convert_element_type.10.lat_ref
  24.5 2.0 %shard_map.85 = (bf16[48,80]{1,0:T(8,128)(2,1)}, bf16[720,720]{1,0:T(8,128)(2,1)}) custom-call(f32[17]{0:T(128)} %convert_element_type.9.lon_ref, f32[17]{0:T(128)} %convert_element_type.10.lat_ref), custom_call_target="tpu_custom_call" | custom-call | tf_op jit(solution)/shard_map/pallas_call | solution.py:79
  26.5 5.2 %all-to-all-done = f32[3,8,256]{2,0,1:T(4,128)S(1)} async-done(((f32[3,8,256]{2,0,1:T(4,128)}), f32[3,8,256]{2,0,1:T(4,128)S(1)}, u32[]{:S(2)}, u32[]{:S(2)}) %all-to-all-start) | async-done | bytes 24608 | tf_op jit(solution)/shard_map/all_to_all | solution.py:305
  31.7 0.6 copy.12.cells_ref.lists_ref
  32.3 6.6 %shard_map.86 = f32[8,256]{1,0:T(8,128)} custom-call(bf16[20,1,45,720]{3,2,1,0:T(8,128)(2,1)} %ctrl_ref.3, bf16[20,1,16,720]{3,2,1,0:T(8,128)(2,1)} %copy-done.4, bf16[20,1,16,720]{3,2,1,0:T(8,128)(2,1)} %copy-done.3, bf16[20,1,45,720]{3,2,1,0:T(8,128)(2,1)} %pert_ref.3, bf16[48,80]{1,0:T(8,128)(2,1)} %get-tuple-element.12.blon_ref, ...), custom_call_target="tpu_custom_call" | custom-call | tf_op jit(solution)/shard_map/pallas_call | solution.py:174
  38.8 3.6 %collective-permute-start.6 = (f32[8,256]{1,0:T(8,128)}, f32[8,256]{1,0:T(8,128)S(1)}, u32[]{:S(2)}, u32[]{:S(2)}) collective-permute-start(f32[8,256]{1,0:T(8,128)} %shard_map.86), channel_id=1, source_target_pairs={{0,3},{1,0},{2,1},{3,2},{4,7},{5,4},{6,5},{7,6},{8,11},{9,8},{10,9... | collective-permute-start | bytes 24584 | tf_op jit(solution)/shard_map/ppermute | solution.py:26
  42.4 0.0 collective-permute-start.5
  42.4 1.0 %collective-permute-start.4 = (f32[8,256]{1,0:T(8,128)}, f32[8,256]{1,0:T(8,128)S(1)}, u32[]{:S(2)}, u32[]{:S(2)}) collective-permute-start(f32[8,256]{1,0:T(8,128)} %shard_map.86), channel_id=1, source_target_pairs={{0,1},{1,2},{2,3},{3,0},{4,5},{5,6},{6,7},{7,4},{8,9},{9,10},{10,1... | collective-permute-start | bytes 24584 | tf_op jit(solution)/shard_map/ppermute | solution.py:26
  43.5 0.6 collective-permute-done.6
  44.0 3.2 %collective-permute-done.5 = f32[8,256]{1,0:T(8,128)S(1)} collective-permute-done((f32[8,256]{1,0:T(8,128)}, f32[8,256]{1,0:T(8,128)S(1)}, u32[]{:S(2)}, u32[]{:S(2)}) %collective-permute-start.5) | collective-permute-done | bytes 8224 | tf_op jit(solution)/shard_map/ppermute | solution.py:26
  47.2 0.9 %collective-permute-done.4 = f32[8,256]{1,0:T(8,128)S(1)} collective-permute-done((f32[8,256]{1,0:T(8,128)}, f32[8,256]{1,0:T(8,128)S(1)}, u32[]{:S(2)}, u32[]{:S(2)}) %collective-permute-start.4) | collective-permute-done | bytes 8224 | tf_op jit(solution)/shard_map/ppermute | solution.py:26
  48.1 1.3 %add_add_fusion.at_ref = f32[8,256]{1,0:T(8,128)} fusion(f32[8,256]{1,0:T(8,128)S(1)} %collective-permute-done.6, f32[8,256]{1,0:T(8,128)S(1)} %collective-permute-done.5, f32[8,256]{1,0:T(8,128)} %shard_map.86, f32[8,256]{1,0:T(8,128)S(1)} %collective-permute-done.4), kind=kLoop, calls=%fused_computation.2 | loop fusion | flops 6144 | bytes 40960 | tf_op jit(solution)/shard_map/add | solution.py:26
  49.4 2.6 %shard_map.87 = (f32[45,720]{1,0:T(8,128)}, f32[16,720]{1,0:T(8,128)}, f32[16,720]{1,0:T(8,128)}) custom-call(f32[8,256]{1,0:T(8,128)} %add_add_fusion.at_ref, f32[3,8,256]{2,1,0:T(8,128)} %copy.12.cells_ref.lists_ref), custom_call_target="tpu_custom_call" | custom-call | tf_op jit(solution)/shard_map/pallas_call | solution.py:227
  52.0 0.0 collective-permute-start.7
  52.0 2.6 %collective-permute-start.8 = (f32[16,720]{1,0:T(8,128)}, f32[16,720]{1,0:T(8,128)S(1)}, u32[]{:S(2)}, u32[]{:S(2)}) collective-permute-start(f32[16,720]{1,0:T(8,128)} %get-tuple-element.16), channel_id=1, source_target_pairs={{4,0},{8,4},{12,8},{16,12},{20,16},{24,20},{28,24},{0,28},{5,1},{9... | collective-permute-start | bytes 138248 | tf_op jit(solution)/shard_map/ppermute | solution.py:319
  54.6 2.0 %collective-permute-done.7 = f32[16,720]{1,0:T(8,128)S(1)} collective-permute-done((f32[16,720]{1,0:T(8,128)}, f32[16,720]{1,0:T(8,128)S(1)}, u32[]{:S(2)}, u32[]{:S(2)}) %collective-permute-start.7) | collective-permute-done | bytes 46112 | tf_op jit(solution)/shard_map/ppermute | solution.py:318
  56.6 0.1 collective-permute-done.8
  56.7 0.0 collective-permute-done.3.phigh_ref
  56.7 0.0 collective-permute-done.2.plow_ref
  56.7 0.5 copy-done.5
  57.2 0.1 copy-done.6
  57.3 0.2 copy-done.1
  57.5 0.2 copy-done.2
  57.6 6.4 %shard_map.88 = f32[20,45,1,720]{3,2,1,0:T(1,128)} custom-call(bf16[20,1,45,720]{3,2,1,0:T(8,128)(2,1)} %pert_ref.3, bf16[20,1,16,720]{3,2,1,0:T(8,128)(2,1)} %copy-done.2, bf16[20,1,16,720]{3,2,1,0:T(8,128)(2,1)} %copy-done.1, f32[1,45,720]{2,1,0:T(8,128)} %bitcast.5, f32[1,16,720]{2,1,0:T(8,128)} %bitcast.6, f32[1,16,720]{2,1,0:T(8,128)} %bitcast.7, ...), custom_call_target="tpu_custom_call" | custom-call | tf_op jit(solution)/shard_map/pallas_call | solution.py:271
  (13 shorter events, 0.0 us)
Async XLA Ops:
  0.0 17.7 %copy-start = (bf16[20,1,45,720]{3,2,1,0:T(8,128)(2,1)S(1)}, bf16[20,1,45,720]{3,2,1,0:T(8,128)(2,1)}, u32[]{:S(2)}) copy-start(bf16[20,1,45,720]{3,2,1,0:T(8,128)(2,1)} %pert_ref.3) | copy-start | bytes 3888004
  1.5 17.2 %copy-start.7 = (f32[1,8,256]{2,1,0:T(8,128)S(1)}, f32[1,8,256]{2,1,0:T(8,128)}, u32[]{:S(2)}) copy-start(f32[1,8,256]{2,1,0:T(8,128)} %param.13) | copy-start | bytes 24580
  1.5 17.2 %copy-start.10 = (s32[1,8]{1,0:T(1,128)S(1)}, s32[1,8]{1,0:T(1,128)}, u32[]{:S(2)}) copy-start(s32[1,8]{1,0:T(1,128)} %param.15) | copy-start | bytes 100
  1.5 17.3 %copy-start.8 = (f32[1,8,256]{2,1,0:T(8,128)S(1)}, f32[1,8,256]{2,1,0:T(8,128)}, u32[]{:S(2)}) copy-start(f32[1,8,256]{2,1,0:T(8,128)} %param.12) | copy-start | bytes 24580
  1.6 17.3 %copy-start.9 = (s32[1,8,256]{2,1,0:T(8,128)S(1)}, s32[1,8,256]{2,1,0:T(8,128)}, u32[]{:S(2)}) copy-start(s32[1,8,256]{2,1,0:T(8,128)} %param.14) | copy-start | bytes 24580
  1.6 21.9 %copy-start.11 = (bf16[17]{0:T(256)(128)(2,1)S(1)}, bf16[17]{0:T(256)(128)(2,1)}, u32[]{:S(2)}) copy-start(bf16[17]{0:T(256)(128)(2,1)} %param.10) | copy-start | bytes 106
  1.6 22.4 %copy-start.12 = (bf16[17]{0:T(256)(128)(2,1)S(1)}, bf16[17]{0:T(256)(128)(2,1)}, u32[]{:S(2)}) copy-start(bf16[17]{0:T(256)(128)(2,1)} %param.11) | copy-start | bytes 106
  1.6 14.1 %collective-permute-start.1 = (bf16[20,1,16,720]{3,2,1,0:T(8,128)(2,1)S(1)}, bf16[20,1,16,720]{3,2,1,0:T(8,128)(2,1)S(1)}, u32[]{:S(2)}, u32[]{:S(2)}) collective-permute-start(bf16[20,1,16,720]{3,2,1,0:T(8,128)(2,1)S(1)} %get-tuple-element.19), channel_id=1, source_target_pairs={{4,0},{8,4},{12,8},{16,12},{20,16},{24,20},{28,24},{0,28},{5,1},{9... | collective-permute-start | bytes 1382408 | tf_op jit(solution)/shard_map/ppermute | solution.py:18
  5.0 12.6 %collective-permute-start = (bf16[20,1,16,720]{3,2,1,0:T(8,128)(2,1)S(1)}, bf16[20,1,16,720]{3,2,1,0:T(8,128)(2,1)S(1)}, u32[]{:S(2)}, u32[]{:S(2)}) collective-permute-start(bf16[20,1,16,720]{3,2,1,0:T(8,128)(2,1)S(1)} %get-tuple-element.20), channel_id=1, source_target_pairs={{0,4},{4,8},{8,12},{12,16},{16,20},{20,24},{24,28},{28,0},{1,5},{5... | collective-permute-start | bytes 1382408 | tf_op jit(solution)/shard_map/ppermute | solution.py:15
  15.7 16.6 %copy-start.3 = (bf16[20,1,16,720]{3,2,1,0:T(8,128)(2,1)}, bf16[20,1,16,720]{3,2,1,0:T(8,128)(2,1)S(1)}, u32[]{:S(2)}) copy-start(bf16[20,1,16,720]{3,2,1,0:T(8,128)(2,1)S(1)} %collective-permute-done.1.high_ref) | copy-start | bytes 1382404
  17.7 14.6 %copy-start.4 = (bf16[20,1,16,720]{3,2,1,0:T(8,128)(2,1)}, bf16[20,1,16,720]{3,2,1,0:T(8,128)(2,1)S(1)}, u32[]{:S(2)}) copy-start(bf16[20,1,16,720]{3,2,1,0:T(8,128)(2,1)S(1)} %collective-permute-done.low_ref) | copy-start | bytes 1382404
  17.8 38.9 %collective-permute-start.3 = (bf16[20,1,16,720]{3,2,1,0:T(8,128)(2,1)S(1)}, bf16[20,1,16,720]{3,2,1,0:T(8,128)(2,1)S(1)}, u32[]{:S(2)}, u32[]{:S(2)}) collective-permute-start(bf16[20,1,16,720]{3,2,1,0:T(8,128)(2,1)S(1)} %get-tuple-element.17), channel_id=1, source_target_pairs={{4,0},{8,4},{12,8},{16,12},{20,16},{24,20},{28,24},{0,28},{5,1},{9... | collective-permute-start | bytes 1382408 | tf_op jit(solution)/shard_map/ppermute | solution.py:18
  18.8 37.9 %collective-permute-start.2 = (bf16[20,1,16,720]{3,2,1,0:T(8,128)(2,1)S(1)}, bf16[20,1,16,720]{3,2,1,0:T(8,128)(2,1)S(1)}, u32[]{:S(2)}, u32[]{:S(2)}) collective-permute-start(bf16[20,1,16,720]{3,2,1,0:T(8,128)(2,1)S(1)} %get-tuple-element.18), channel_id=1, source_target_pairs={{0,4},{4,8},{8,12},{12,16},{16,20},{20,24},{24,28},{28,0},{1,5},{5... | collective-permute-start | bytes 1382408 | tf_op jit(solution)/shard_map/ppermute | solution.py:15
  19.5 12.1 %all-to-all-start = ((f32[3,8,256]{2,0,1:T(4,128)}), f32[3,8,256]{2,0,1:T(4,128)S(1)}, u32[]{:S(2)}, u32[]{:S(2)}) async-start(f32[3,8,256]{2,0,1:T(4,128)} %pad_maximum_fusion), calls=%async_computation | async-start | bytes 65536 | tf_op jit(solution)/shard_map/all_to_all | solution.py:305
  38.8 5.2 %collective-permute-start.6 = (f32[8,256]{1,0:T(8,128)}, f32[8,256]{1,0:T(8,128)S(1)}, u32[]{:S(2)}, u32[]{:S(2)}) collective-permute-start(f32[8,256]{1,0:T(8,128)} %shard_map.86), channel_id=1, source_target_pairs={{0,3},{1,0},{2,1},{3,2},{4,7},{5,4},{6,5},{7,6},{8,11},{9,8},{10,9... | collective-permute-start | bytes 24584 | tf_op jit(solution)/shard_map/ppermute | solution.py:26
  42.4 4.8 %collective-permute-start.5 = (f32[8,256]{1,0:T(8,128)}, f32[8,256]{1,0:T(8,128)S(1)}, u32[]{:S(2)}, u32[]{:S(2)}) collective-permute-start(f32[8,256]{1,0:T(8,128)} %shard_map.86), channel_id=1, source_target_pairs={{0,2},{1,3},{2,0},{3,1},{4,6},{5,7},{6,4},{7,5},{8,10},{9,11},{10,... | collective-permute-start | bytes 24584 | tf_op jit(solution)/shard_map/ppermute | solution.py:26
  42.4 5.7 %collective-permute-start.4 = (f32[8,256]{1,0:T(8,128)}, f32[8,256]{1,0:T(8,128)S(1)}, u32[]{:S(2)}, u32[]{:S(2)}) collective-permute-start(f32[8,256]{1,0:T(8,128)} %shard_map.86), channel_id=1, source_target_pairs={{0,1},{1,2},{2,3},{3,0},{4,5},{5,6},{6,7},{7,4},{8,9},{9,10},{10,1... | collective-permute-start | bytes 24584 | tf_op jit(solution)/shard_map/ppermute | solution.py:26
  52.0 4.6 %collective-permute-start.7 = (f32[16,720]{1,0:T(8,128)}, f32[16,720]{1,0:T(8,128)S(1)}, u32[]{:S(2)}, u32[]{:S(2)}) collective-permute-start(f32[16,720]{1,0:T(8,128)} %get-tuple-element.15), channel_id=1, source_target_pairs={{0,4},{4,8},{8,12},{12,16},{16,20},{20,24},{24,28},{28,0},{1,5},{5... | collective-permute-start | bytes 138248 | tf_op jit(solution)/shard_map/ppermute | solution.py:318
  52.0 4.7 %collective-permute-start.8 = (f32[16,720]{1,0:T(8,128)}, f32[16,720]{1,0:T(8,128)S(1)}, u32[]{:S(2)}, u32[]{:S(2)}) collective-permute-start(f32[16,720]{1,0:T(8,128)} %get-tuple-element.16), channel_id=1, source_target_pairs={{4,0},{8,4},{12,8},{16,12},{20,16},{24,20},{28,24},{0,28},{5,1},{9... | collective-permute-start | bytes 138248 | tf_op jit(solution)/shard_map/ppermute | solution.py:319
  56.6 0.6 copy-start.5
  56.7 0.6 copy-start.6
  56.7 0.8 %copy-start.1 = (bf16[20,1,16,720]{3,2,1,0:T(8,128)(2,1)}, bf16[20,1,16,720]{3,2,1,0:T(8,128)(2,1)S(1)}, u32[]{:S(2)}) copy-start(bf16[20,1,16,720]{3,2,1,0:T(8,128)(2,1)S(1)} %collective-permute-done.3.phigh_ref) | copy-start | bytes 1382404
  56.7 1.0 %copy-start.2 = (bf16[20,1,16,720]{3,2,1,0:T(8,128)(2,1)}, bf16[20,1,16,720]{3,2,1,0:T(8,128)(2,1)S(1)}, u32[]{:S(2)}) copy-start(bf16[20,1,16,720]{3,2,1,0:T(8,128)(2,1)S(1)} %collective-permute-done.2.plow_ref) | copy-start | bytes 1382404

commit v8 on v7

--- a/solution.py
+++ b/solution.py
@@ -305,6 +305,7 @@
     received = lax.all_to_all(lists, "tile", split_axis=1, concat_axis=1, tiled=True)
 
     c_low, c_high = halos(control, "tile", 2, radius)
+    c_low, c_high, received = lax.optimization_barrier((c_low, c_high, received))
     late_perturb = lax.optimization_barrier((perturb, c_low, c_high))[0]
     p_low, p_high = halos(late_perturb, "tile", 2, radius)
     partial = forward_pick(

time: 64.6 us -> 55.3 us (0.86)
  waiting for transfers between devices: 24.5 us -> 6.88 us
  blocking collectives: 0 us -> 12.8 us
  starting transfers between devices: 15.5 us -> 11.8 us
    all_to_all x0 -> x1, blocking collectives: none -> 12.8 us  [local(): lax.all_to_all(lists, 'tile', split_axis=1, concat_axis=1, tiled=True)]
    ppermute x2, waiting for transfers between devices: 10.7 us -> 0.01 us  [halos(): lax.ppermute(lax.slice_in_dim(block, 0, width, axis=dim), axis, backward)]
    all_to_all x1 -> x0, waiting for transfers between devices: 5.18 us -> none  [local(): lax.all_to_all(lists, 'tile', split_axis=1, concat_axis=1, tiled=True)]
    all_to_all x1 -> x0, starting transfers between devices: 3.92 us -> none  [local(): lax.all_to_all(lists, 'tile', split_axis=1, concat_axis=1, tiled=True)]
    ppermute x2, waiting for transfers between devices: 1.93 us -> 0.01 us  [halos(): lax.ppermute(lax.slice_in_dim(block, block.shape[dim] - width, None, axis...]
  transfers between devices with their start and end apart: 10 -> 9, of which waited for: 8 -> 4; matrix products, arithmetic and copies ran while one was open for 6% -> 6% of each run, Pallas kernels for 17% -> 20%
where the time goes in v8:
time: 55.3 us; the launch traced here: 54.8 us
  Pallas kernels  17.5 us (32%)
  blocking collectives  12.8 us (23%)
  starting transfers between devices  11.8 us (21%)
  waiting for transfers between devices  6.88 us (12%)
  local copies, waits for them, and re-layouts  3.29 us (6%)
  other arithmetic  2.46 us (4%)
    all_to_all x1, blocking collectives, local(): lax.all_to_all(lists, 'tile', split_axis=1, concat_axis=1, tiled=True)  12.8 us
    pallas_call x1, Pallas kernels, forward_pick(): pl.pallas_call(kernel, grid=(steps,), in_specs=[field, halo, halo, field,...  6.56 us
    pallas_call x1, Pallas kernels, backward_grad(): pl.pallas_call(kernel, grid=(levels, members // chunk), in_specs=[field,...  6.38 us
    ppermute x3, waiting for transfers between devices, sum_over(): lax.ppermute(values, axis, [(i, (i + shift) % count) for i in range(count)])  4.65 us
    ppermute x3, starting transfers between devices, sum_over(): lax.ppermute(values, axis, [(i, (i + shift) % count) for i in range(count)])  4.62 us
    ppermute x2, starting transfers between devices, halos(): lax.ppermute(lax.slice_in_dim(block, 0, width, axis=dim), axis, backward)  4.52 us
    ppermute x1, starting transfers between devices, local(): lax.ppermute(high_send, 'tile', [((i + 1) % count, i) for i in range(coun...  2.64 us
    pallas_call x1, Pallas kernels, spread_misfits(): pl.pallas_call(kernel, out_shape=(jax.ShapeDtypeStruct((lon_cells, lat_ce...  2.56 us
  transfers between devices with their start and end apart: 9, of which 4 were waited for; matrix products, arithmetic and copies ran while one was open for 6% of the time, Pallas kernels for 20%

profile of v8, /device:TPU:0, one launch (start us, length us, event | category | flops | bytes accessed | tf_op | source)
XLA Modules:
  0.0 54.8 jit_solution(11836601665631814753)
XLA Ops:
  0.0 1.5 %fusion.1 = (bf16[20,1,16,720]{3,2,1,0:T(8,128)(2,1)S(1)}, bf16[20,1,16,720]{3,2,1,0:T(8,128)(2,1)S(1)}) fusion(bf16[20,1,45,720]{3,2,1,0:T(8,128)(2,1)} %ctrl_ref.3), kind=kLoop, calls=%fused_computation.4 | loop fusion | bytes 1843200 | tf_op jit(solution)/shard_map/slice | solution.py:18
  1.5 0.0 copy-start.11
  1.6 0.0 copy-start.12
  1.6 3.4 %collective-permute-start.1 = (bf16[20,1,16,720]{3,2,1,0:T(8,128)(2,1)S(1)}, bf16[20,1,16,720]{3,2,1,0:T(8,128)(2,1)S(1)}, u32[]{:S(2)}, u32[]{:S(2)}) collective-permute-start(bf16[20,1,16,720]{3,2,1,0:T(8,128)(2,1)S(1)} %get-tuple-element.25), channel_id=1, source_target_pairs={{4,0},{8,4},{12,8},{16,12},{20,16},{24,20},{28,24},{0,28},{5,1},{9... | collective-permute-start | bytes 1382408 | tf_op jit(solution)/shard_map/ppermute | solution.py:18
  5.0 0.0 collective-permute-start
  5.0 0.0 copy-done.7
  5.0 0.0 copy-done.8
  5.1 0.0 copy-done.10
  5.1 0.0 copy-done.9
  5.1 0.1 compare_select_fusion
  5.2 12.8 %all_to_all.5 = f32[3,8,256]{2,0,1:T(4,128)S(1)} all-to-all(f32[3,8,256]{2,0,1:T(4,128)S(1)} %pad_maximum_fusion), channel_id=1, replica_groups=mesh['tile'=8,'mem'=4] {'tile'}, dimensions={1} | all-to-all | bytes 49152 | tf_op jit(solution)/shard_map/all_to_all | solution.py:305
  18.0 0.0 collective-permute-done.1.high_ref
  18.0 0.0 collective-permute-done.low_ref
  18.0 0.0 copy-done
  18.0 0.0 copy-start.4
  18.0 0.1 fusion
  18.2 1.1 %collective-permute-start.3 = (bf16[20,1,16,720]{3,2,1,0:T(8,128)(2,1)S(1)}, bf16[20,1,16,720]{3,2,1,0:T(8,128)(2,1)S(1)}, u32[]{:S(2)}, u32[]{:S(2)}) collective-permute-start(bf16[20,1,16,720]{3,2,1,0:T(8,128)(2,1)S(1)} %get-tuple-element.23), channel_id=1, source_target_pairs={{4,0},{8,4},{12,8},{16,12},{20,16},{24,20},{28,24},{0,28},{5,1},{9... | collective-permute-start | bytes 1382408 | tf_op jit(solution)/shard_map/ppermute | solution.py:18
  19.3 0.0 collective-permute-start.2
  19.3 0.0 copy-done.11
  19.3 0.6 %convert_element_type.10.lon_ref = f32[17]{0:T(128)} convert(bf16[17]{0:T(256)(128)(2,1)S(1)} %copy-done.11) | non-fusion elementwise | flops 17 | bytes 102 | tf_op jit(solution)/shard_map/convert_element_type | solution.py:86
  19.8 0.0 copy-done.12
  19.8 0.5 convert_element_type.11.lat_ref
  20.3 2.0 %shard_map.85 = (bf16[48,80]{1,0:T(8,128)(2,1)}, bf16[720,720]{1,0:T(8,128)(2,1)}) custom-call(f32[17]{0:T(128)} %convert_element_type.10.lon_ref, f32[17]{0:T(128)} %convert_element_type.11.lat_ref), custom_call_target="tpu_custom_call" | custom-call | tf_op jit(solution)/shard_map/pallas_call | solution.py:79
  22.3 0.6 %copy.12.cells_ref.lists_ref = f32[3,8,256]{2,1,0:T(8,128)} copy(f32[3,8,256]{2,0,1:T(4,128)S(1)} %all_to_all.5) | data formatting | bytes 49152 | tf_op jit(solution)/shard_map/optimization_barrier | solution.py:308
  22.9 0.0 copy-done.3
  22.9 0.0 copy-done.4
  22.9 6.6 %shard_map.86 = f32[8,256]{1,0:T(8,128)} custom-call(bf16[20,1,45,720]{3,2,1,0:T(8,128)(2,1)} %ctrl_ref.3, bf16[20,1,16,720]{3,2,1,0:T(8,128)(2,1)} %copy-done.4, bf16[20,1,16,720]{3,2,1,0:T(8,128)(2,1)} %copy-done.3, bf16[20,1,45,720]{3,2,1,0:T(8,128)(2,1)} %pert_ref.3, bf16[48,80]{1,0:T(8,128)(2,1)} %get-tuple-element.17.blon_ref, ...), custom_call_target="tpu_custom_call" | custom-call | tf_op jit(solution)/shard_map/pallas_call | solution.py:174
  29.5 3.6 %collective-permute-start.6 = (f32[8,256]{1,0:T(8,128)}, f32[8,256]{1,0:T(8,128)S(1)}, u32[]{:S(2)}, u32[]{:S(2)}) collective-permute-start(f32[8,256]{1,0:T(8,128)} %shard_map.86), channel_id=1, source_target_pairs={{0,3},{1,0},{2,1},{3,2},{4,7},{5,4},{6,5},{7,6},{8,11},{9,8},{10,9... | collective-permute-start | bytes 24584 | tf_op jit(solution)/shard_map/ppermute | solution.py:26
  33.1 0.0 collective-permute-start.5
  33.1 1.0 %collective-permute-start.4 = (f32[8,256]{1,0:T(8,128)}, f32[8,256]{1,0:T(8,128)S(1)}, u32[]{:S(2)}, u32[]{:S(2)}) collective-permute-start(f32[8,256]{1,0:T(8,128)} %shard_map.86), channel_id=1, source_target_pairs={{0,1},{1,2},{2,3},{3,0},{4,5},{5,6},{6,7},{7,4},{8,9},{9,10},{10,1... | collective-permute-start | bytes 24584 | tf_op jit(solution)/shard_map/ppermute | solution.py:26
  34.1 0.6 %collective-permute-done.6 = f32[8,256]{1,0:T(8,128)S(1)} collective-permute-done((f32[8,256]{1,0:T(8,128)}, f32[8,256]{1,0:T(8,128)S(1)}, u32[]{:S(2)}, u32[]{:S(2)}) %collective-permute-start.6) | collective-permute-done | bytes 8224 | tf_op jit(solution)/shard_map/ppermute | solution.py:26
  34.6 3.2 %collective-permute-done.5 = f32[8,256]{1,0:T(8,128)S(1)} collective-permute-done((f32[8,256]{1,0:T(8,128)}, f32[8,256]{1,0:T(8,128)S(1)}, u32[]{:S(2)}, u32[]{:S(2)}) %collective-permute-start.5) | collective-permute-done | bytes 8224 | tf_op jit(solution)/shard_map/ppermute | solution.py:26
  37.8 0.9 %collective-permute-done.4 = f32[8,256]{1,0:T(8,128)S(1)} collective-permute-done((f32[8,256]{1,0:T(8,128)}, f32[8,256]{1,0:T(8,128)S(1)}, u32[]{:S(2)}, u32[]{:S(2)}) %collective-permute-start.4) | collective-permute-done | bytes 8224 | tf_op jit(solution)/shard_map/ppermute | solution.py:26
  38.7 1.3 %add_add_fusion.at_ref = f32[8,256]{1,0:T(8,128)} fusion(f32[8,256]{1,0:T(8,128)S(1)} %collective-permute-done.6, f32[8,256]{1,0:T(8,128)S(1)} %collective-permute-done.5, f32[8,256]{1,0:T(8,128)} %shard_map.86, f32[8,256]{1,0:T(8,128)S(1)} %collective-permute-done.4), kind=kLoop, calls=%fused_computation.2 | loop fusion | flops 6144 | bytes 40960 | tf_op jit(solution)/shard_map/add | solution.py:26
  40.0 2.6 %shard_map.87 = (f32[45,720]{1,0:T(8,128)}, f32[16,720]{1,0:T(8,128)}, f32[16,720]{1,0:T(8,128)}) custom-call(f32[8,256]{1,0:T(8,128)} %add_add_fusion.at_ref, f32[3,8,256]{2,1,0:T(8,128)} %copy.12.cells_ref.lists_ref), custom_call_target="tpu_custom_call" | custom-call | tf_op jit(solution)/shard_map/pallas_call | solution.py:227
  42.6 0.0 collective-permute-start.7
  42.6 2.6 %collective-permute-start.8 = (f32[16,720]{1,0:T(8,128)}, f32[16,720]{1,0:T(8,128)S(1)}, u32[]{:S(2)}, u32[]{:S(2)}) collective-permute-start(f32[16,720]{1,0:T(8,128)} %get-tuple-element.22), channel_id=1, source_target_pairs={{4,0},{8,4},{12,8},{16,12},{20,16},{24,20},{28,24},{0,28},{5,1},{9... | collective-permute-start | bytes 138248 | tf_op jit(solution)/shard_map/ppermute | solution.py:320
  45.2 2.2 %collective-permute-done.7 = f32[16,720]{1,0:T(8,128)S(1)} collective-permute-done((f32[16,720]{1,0:T(8,128)}, f32[16,720]{1,0:T(8,128)S(1)}, u32[]{:S(2)}, u32[]{:S(2)}) %collective-permute-start.7) | collective-permute-done | bytes 46112 | tf_op jit(solution)/shard_map/ppermute | solution.py:319
  47.5 0.0 collective-permute-done.8
  47.5 0.0 collective-permute-done.3.phigh_ref
  47.5 0.0 copy-start.1
  47.5 0.0 collective-permute-done.2.plow_ref
  47.5 0.0 copy-start.2
  47.5 0.6 %copy-done.5 = f32[16,720]{1,0:T(8,128)} copy-done((f32[16,720]{1,0:T(8,128)}, f32[16,720]{1,0:T(8,128)S(1)}, u32[]{:S(2)}) %copy-start.5) | copy-done | bytes 46104
  48.1 0.0 copy-done.6
  48.1 0.2 copy-done.1
  48.3 0.2 copy-done.2
  48.5 6.4 %shard_map.88 = f32[20,45,1,720]{3,2,1,0:T(1,128)} custom-call(bf16[20,1,45,720]{3,2,1,0:T(8,128)(2,1)} %pert_ref.3, bf16[20,1,16,720]{3,2,1,0:T(8,128)(2,1)} %copy-done.2, bf16[20,1,16,720]{3,2,1,0:T(8,128)(2,1)} %copy-done.1, f32[1,45,720]{2,1,0:T(8,128)} %bitcast.5, f32[1,16,720]{2,1,0:T(8,128)} %bitcast.6, f32[1,16,720]{2,1,0:T(8,128)} %bitcast.7, ...), custom_call_target="tpu_custom_call" | custom-call | tf_op jit(solution)/shard_map/pallas_call | solution.py:271
  (12 shorter events, 0.1 us)
Async XLA Ops:
  0.0 5.0 %copy-start.7 = (f32[1,8,256]{2,1,0:T(8,128)S(1)}, f32[1,8,256]{2,1,0:T(8,128)}, u32[]{:S(2)}) copy-start(f32[1,8,256]{2,1,0:T(8,128)} %param.12) | copy-start | bytes 24580
  0.0 5.0 %copy-start.8 = (s32[1,8,256]{2,1,0:T(8,128)S(1)}, s32[1,8,256]{2,1,0:T(8,128)}, u32[]{:S(2)}) copy-start(s32[1,8,256]{2,1,0:T(8,128)} %param.14) | copy-start | bytes 24580
  0.0 5.1 %copy-start.10 = (s32[1,8]{1,0:T(1,128)S(1)}, s32[1,8]{1,0:T(1,128)}, u32[]{:S(2)}) copy-start(s32[1,8]{1,0:T(1,128)} %param.15) | copy-start | bytes 100
  0.0 5.1 %copy-start.9 = (f32[1,8,256]{2,1,0:T(8,128)S(1)}, f32[1,8,256]{2,1,0:T(8,128)}, u32[]{:S(2)}) copy-start(f32[1,8,256]{2,1,0:T(8,128)} %param.13) | copy-start | bytes 24580
  0.0 18.0 %copy-start = (bf16[20,1,45,720]{3,2,1,0:T(8,128)(2,1)S(1)}, bf16[20,1,45,720]{3,2,1,0:T(8,128)(2,1)}, u32[]{:S(2)}) copy-start(bf16[20,1,45,720]{3,2,1,0:T(8,128)(2,1)} %pert_ref.3) | copy-start | bytes 3888004
  1.5 17.7 %copy-start.11 = (bf16[17]{0:T(256)(128)(2,1)S(1)}, bf16[17]{0:T(256)(128)(2,1)}, u32[]{:S(2)}) copy-start(bf16[17]{0:T(256)(128)(2,1)} %param.10) | copy-start | bytes 106
  1.6 18.3 %copy-start.12 = (bf16[17]{0:T(256)(128)(2,1)S(1)}, bf16[17]{0:T(256)(128)(2,1)}, u32[]{:S(2)}) copy-start(bf16[17]{0:T(256)(128)(2,1)} %param.11) | copy-start | bytes 106
  1.6 16.4 %collective-permute-start.1 = (bf16[20,1,16,720]{3,2,1,0:T(8,128)(2,1)S(1)}, bf16[20,1,16,720]{3,2,1,0:T(8,128)(2,1)S(1)}, u32[]{:S(2)}, u32[]{:S(2)}) collective-permute-start(bf16[20,1,16,720]{3,2,1,0:T(8,128)(2,1)S(1)} %get-tuple-element.25), channel_id=1, source_target_pairs={{4,0},{8,4},{12,8},{16,12},{20,16},{24,20},{28,24},{0,28},{5,1},{9... | collective-permute-start | bytes 1382408 | tf_op jit(solution)/shard_map/ppermute | solution.py:18
  5.0 13.0 %collective-permute-start = (bf16[20,1,16,720]{3,2,1,0:T(8,128)(2,1)S(1)}, bf16[20,1,16,720]{3,2,1,0:T(8,128)(2,1)S(1)}, u32[]{:S(2)}, u32[]{:S(2)}) collective-permute-start(bf16[20,1,16,720]{3,2,1,0:T(8,128)(2,1)S(1)} %get-tuple-element.26), channel_id=1, source_target_pairs={{0,4},{4,8},{8,12},{12,16},{16,20},{20,24},{24,28},{28,0},{1,5},{5... | collective-permute-start | bytes 1382408 | tf_op jit(solution)/shard_map/ppermute | solution.py:15
  18.0 4.9 %copy-start.3 = (bf16[20,1,16,720]{3,2,1,0:T(8,128)(2,1)}, bf16[20,1,16,720]{3,2,1,0:T(8,128)(2,1)S(1)}, u32[]{:S(2)}) copy-start(bf16[20,1,16,720]{3,2,1,0:T(8,128)(2,1)S(1)} %collective-permute-done.1.high_ref) | copy-start | bytes 1382404
  18.0 4.9 %copy-start.4 = (bf16[20,1,16,720]{3,2,1,0:T(8,128)(2,1)}, bf16[20,1,16,720]{3,2,1,0:T(8,128)(2,1)S(1)}, u32[]{:S(2)}) copy-start(bf16[20,1,16,720]{3,2,1,0:T(8,128)(2,1)S(1)} %collective-permute-done.low_ref) | copy-start | bytes 1382404
  18.2 29.3 %collective-permute-start.3 = (bf16[20,1,16,720]{3,2,1,0:T(8,128)(2,1)S(1)}, bf16[20,1,16,720]{3,2,1,0:T(8,128)(2,1)S(1)}, u32[]{:S(2)}, u32[]{:S(2)}) collective-permute-start(bf16[20,1,16,720]{3,2,1,0:T(8,128)(2,1)S(1)} %get-tuple-element.23), channel_id=1, source_target_pairs={{4,0},{8,4},{12,8},{16,12},{20,16},{24,20},{28,24},{0,28},{5,1},{9... | collective-permute-start | bytes 1382408 | tf_op jit(solution)/shard_map/ppermute | solution.py:18
  19.3 28.2 %collective-permute-start.2 = (bf16[20,1,16,720]{3,2,1,0:T(8,128)(2,1)S(1)}, bf16[20,1,16,720]{3,2,1,0:T(8,128)(2,1)S(1)}, u32[]{:S(2)}, u32[]{:S(2)}) collective-permute-start(bf16[20,1,16,720]{3,2,1,0:T(8,128)(2,1)S(1)} %get-tuple-element.24), channel_id=1, source_target_pairs={{0,4},{4,8},{8,12},{12,16},{16,20},{20,24},{24,28},{28,0},{1,5},{5... | collective-permute-start | bytes 1382408 | tf_op jit(solution)/shard_map/ppermute | solution.py:15
  29.5 5.2 %collective-permute-start.6 = (f32[8,256]{1,0:T(8,128)}, f32[8,256]{1,0:T(8,128)S(1)}, u32[]{:S(2)}, u32[]{:S(2)}) collective-permute-start(f32[8,256]{1,0:T(8,128)} %shard_map.86), channel_id=1, source_target_pairs={{0,3},{1,0},{2,1},{3,2},{4,7},{5,4},{6,5},{7,6},{8,11},{9,8},{10,9... | collective-permute-start | bytes 24584 | tf_op jit(solution)/shard_map/ppermute | solution.py:26
  33.1 4.8 %collective-permute-start.5 = (f32[8,256]{1,0:T(8,128)}, f32[8,256]{1,0:T(8,128)S(1)}, u32[]{:S(2)}, u32[]{:S(2)}) collective-permute-start(f32[8,256]{1,0:T(8,128)} %shard_map.86), channel_id=1, source_target_pairs={{0,2},{1,3},{2,0},{3,1},{4,6},{5,7},{6,4},{7,5},{8,10},{9,11},{10,... | collective-permute-start | bytes 24584 | tf_op jit(solution)/shard_map/ppermute | solution.py:26
  33.1 5.7 %collective-permute-start.4 = (f32[8,256]{1,0:T(8,128)}, f32[8,256]{1,0:T(8,128)S(1)}, u32[]{:S(2)}, u32[]{:S(2)}) collective-permute-start(f32[8,256]{1,0:T(8,128)} %shard_map.86), channel_id=1, source_target_pairs={{0,1},{1,2},{2,3},{3,0},{4,5},{5,6},{6,7},{7,4},{8,9},{9,10},{10,1... | collective-permute-start | bytes 24584 | tf_op jit(solution)/shard_map/ppermute | solution.py:26
  42.6 4.9 %collective-permute-start.7 = (f32[16,720]{1,0:T(8,128)}, f32[16,720]{1,0:T(8,128)S(1)}, u32[]{:S(2)}, u32[]{:S(2)}) collective-permute-start(f32[16,720]{1,0:T(8,128)} %get-tuple-element.21), channel_id=1, source_target_pairs={{0,4},{4,8},{8,12},{12,16},{16,20},{20,24},{24,28},{28,0},{1,5},{5... | collective-permute-start | bytes 138248 | tf_op jit(solution)/shard_map/ppermute | solution.py:319
  42.6 4.9 %collective-permute-start.8 = (f32[16,720]{1,0:T(8,128)}, f32[16,720]{1,0:T(8,128)S(1)}, u32[]{:S(2)}, u32[]{:S(2)}) collective-permute-start(f32[16,720]{1,0:T(8,128)} %get-tuple-element.22), channel_id=1, source_target_pairs={{4,0},{8,4},{12,8},{16,12},{20,16},{24,20},{28,24},{0,28},{5,1},{9... | collective-permute-start | bytes 138248 | tf_op jit(solution)/shard_map/ppermute | solution.py:320
  47.5 0.6 %copy-start.5 = (f32[16,720]{1,0:T(8,128)}, f32[16,720]{1,0:T(8,128)S(1)}, u32[]{:S(2)}) copy-start(f32[16,720]{1,0:T(8,128)S(1)} %collective-permute-done.7) | copy-start | bytes 138244
  47.5 0.6 %copy-start.6 = (f32[16,720]{1,0:T(8,128)}, f32[16,720]{1,0:T(8,128)S(1)}, u32[]{:S(2)}) copy-start(f32[16,720]{1,0:T(8,128)S(1)} %collective-permute-done.8) | copy-start | bytes 138244
  47.5 0.8 %copy-start.1 = (bf16[20,1,16,720]{3,2,1,0:T(8,128)(2,1)}, bf16[20,1,16,720]{3,2,1,0:T(8,128)(2,1)S(1)}, u32[]{:S(2)}) copy-start(bf16[20,1,16,720]{3,2,1,0:T(8,128)(2,1)S(1)} %collective-permute-done.3.phigh_ref) | copy-start | bytes 1382404
  47.5 1.0 %copy-start.2 = (bf16[20,1,16,720]{3,2,1,0:T(8,128)(2,1)}, bf16[20,1,16,720]{3,2,1,0:T(8,128)(2,1)S(1)}, u32[]{:S(2)}) copy-start(bf16[20,1,16,720]{3,2,1,0:T(8,128)(2,1)S(1)} %collective-permute-done.2.plow_ref) | copy-start | bytes 1382404

commit v9 on v8

--- a/solution.py
+++ b/solution.py
@@ -302,6 +302,7 @@
     slot_ids = lax.broadcasted_iota(jnp.int32, innov.shape, 2)
     weights = jnp.where(slot_ids < counts[:, :, None], inv_var, 0.0)
     lists = jnp.concatenate([innov, weights, cell_index.astype(jnp.float32)])
+    lists = lax.optimization_barrier((lists, band_lon, band_lat))[0]
     received = lax.all_to_all(lists, "tile", split_axis=1, concat_axis=1, tiled=True)
 
     c_low, c_high = halos(control, "tile", 2, radius)

time: 55.3 us -> 52.2 us (0.944)
  blocking collectives: 12.8 us -> 9.81 us
    all_to_all x1, blocking collectives: 12.8 us -> 9.81 us  [local(): lax.all_to_all(lists, 'tile', split_axis=1, concat_axis=1, tiled=True)]
  transfers between devices with their start and end apart: 9 -> 9, of which waited for: 4 -> 4; matrix products, arithmetic and copies ran while one was open for 6% -> 6% of each run, Pallas kernels for 20% -> 21%
where the time goes in v9:
time: 52.2 us; the launch traced here: 51.8 us
  Pallas kernels  17.5 us (34%)
  starting transfers between devices  11.8 us (23%)
  blocking collectives  9.81 us (19%)
  waiting for transfers between devices  6.87 us (13%)
  local copies, waits for them, and re-layouts  3.29 us (6%)
  other arithmetic  2.43 us (5%)
    all_to_all x1, blocking collectives, local(): lax.all_to_all(lists, 'tile', split_axis=1, concat_axis=1, tiled=True)  9.81 us
    pallas_call x1, Pallas kernels, forward_pick(): pl.pallas_call(kernel, grid=(steps,), in_specs=[field, halo, halo, field,...  6.55 us
    pallas_call x1, Pallas kernels, backward_grad(): pl.pallas_call(kernel, grid=(levels, members // chunk), in_specs=[field,...  6.37 us
    ppermute x3, waiting for transfers between devices, sum_over(): lax.ppermute(values, axis, [(i, (i + shift) % count) for i in range(count)])  4.65 us
    ppermute x3, starting transfers between devices, sum_over(): lax.ppermute(values, axis, [(i, (i + shift) % count) for i in range(count)])  4.62 us
    ppermute x2, starting transfers between devices, halos(): lax.ppermute(lax.slice_in_dim(block, 0, width, axis=dim), axis, backward)  4.52 us
    ppermute x1, starting transfers between devices, local(): lax.ppermute(high_send, 'tile', [((i + 1) % count, i) for i in range(coun...  2.64 us
    pallas_call x1, Pallas kernels, spread_misfits(): pl.pallas_call(kernel, out_shape=(jax.ShapeDtypeStruct((lon_cells, lat_ce...  2.56 us
  transfers between devices with their start and end apart: 9, of which 4 were waited for; matrix products, arithmetic and copies ran while one was open for 6% of the time, Pallas kernels for 21%

profile of v9, /device:TPU:0, one launch (start us, length us, event | category | flops | bytes accessed | tf_op | source)
XLA Modules:
  0.0 51.8 jit_solution(11594019918383705111)
XLA Ops:
  0.0 0.0 copy-start.9
  0.0 0.0 copy-start
  0.0 1.5 %fusion.1 = (bf16[20,1,16,720]{3,2,1,0:T(8,128)(2,1)S(1)}, bf16[20,1,16,720]{3,2,1,0:T(8,128)(2,1)S(1)}) fusion(bf16[20,1,45,720]{3,2,1,0:T(8,128)(2,1)} %ctrl_ref.3), kind=kLoop, calls=%fused_computation.4 | loop fusion | bytes 1843200 | tf_op jit(solution)/shard_map/slice | solution.py:18
  1.6 3.4 %collective-permute-start.1 = (bf16[20,1,16,720]{3,2,1,0:T(8,128)(2,1)S(1)}, bf16[20,1,16,720]{3,2,1,0:T(8,128)(2,1)S(1)}, u32[]{:S(2)}, u32[]{:S(2)}) collective-permute-start(bf16[20,1,16,720]{3,2,1,0:T(8,128)(2,1)S(1)} %get-tuple-element.27), channel_id=1, source_target_pairs={{4,0},{8,4},{12,8},{16,12},{20,16},{24,20},{28,24},{0,28},{5,1},{9... | collective-permute-start | bytes 1382408 | tf_op jit(solution)/shard_map/ppermute | solution.py:18
  5.0 0.0 collective-permute-start
  5.0 0.0 copy-done.11
  5.0 0.5 convert_element_type.10.lon_ref
  5.5 0.0 copy-done.12
  5.5 0.5 convert_element_type.11.lat_ref
  6.0 0.0 copy-done.7
  6.0 0.0 copy-done.8
  6.1 2.0 %shard_map.85 = (bf16[48,80]{1,0:T(8,128)(2,1)}, bf16[720,720]{1,0:T(8,128)(2,1)}) custom-call(f32[17]{0:T(128)} %convert_element_type.10.lon_ref, f32[17]{0:T(128)} %convert_element_type.11.lat_ref), custom_call_target="tpu_custom_call" | custom-call | tf_op jit(solution)/shard_map/pallas_call | solution.py:79
  8.1 0.0 copy-done.10
  8.1 0.0 copy-done.9
  8.1 0.1 compare_select_fusion
  8.2 9.8 %all_to_all.5 = f32[3,8,256]{2,0,1:T(4,128)S(1)} all-to-all(f32[3,8,256]{2,0,1:T(4,128)S(1)} %pad_maximum_fusion), channel_id=1, replica_groups=mesh['tile'=8,'mem'=4] {'tile'}, dimensions={1} | all-to-all | bytes 49152 | tf_op jit(solution)/shard_map/all_to_all | solution.py:306
  18.0 0.0 collective-permute-done.1.high_ref
  18.0 0.0 collective-permute-done.low_ref
  18.0 0.0 copy-done
  18.0 0.0 copy-start.4
  18.0 0.1 fusion
  18.2 1.1 %collective-permute-start.3 = (bf16[20,1,16,720]{3,2,1,0:T(8,128)(2,1)S(1)}, bf16[20,1,16,720]{3,2,1,0:T(8,128)(2,1)S(1)}, u32[]{:S(2)}, u32[]{:S(2)}) collective-permute-start(bf16[20,1,16,720]{3,2,1,0:T(8,128)(2,1)S(1)} %get-tuple-element.25), channel_id=1, source_target_pairs={{4,0},{8,4},{12,8},{16,12},{20,16},{24,20},{28,24},{0,28},{5,1},{9... | collective-permute-start | bytes 1382408 | tf_op jit(solution)/shard_map/ppermute | solution.py:18
  19.3 0.0 collective-permute-start.2
  19.3 0.6 %copy.12.cells_ref.lists_ref = f32[3,8,256]{2,1,0:T(8,128)} copy(f32[3,8,256]{2,0,1:T(4,128)S(1)} %all_to_all.5) | data formatting | bytes 49152 | tf_op jit(solution)/shard_map/optimization_barrier | solution.py:309
  19.9 0.0 copy-done.3
  19.9 0.0 copy-done.4
  19.9 6.6 %shard_map.86 = f32[8,256]{1,0:T(8,128)} custom-call(bf16[20,1,45,720]{3,2,1,0:T(8,128)(2,1)} %ctrl_ref.3, bf16[20,1,16,720]{3,2,1,0:T(8,128)(2,1)} %copy-done.4, bf16[20,1,16,720]{3,2,1,0:T(8,128)(2,1)} %copy-done.3, bf16[20,1,45,720]{3,2,1,0:T(8,128)(2,1)} %pert_ref.3, bf16[48,80]{1,0:T(8,128)(2,1)} %get-tuple-element.15.blon_ref, ...), custom_call_target="tpu_custom_call" | custom-call | tf_op jit(solution)/shard_map/pallas_call | solution.py:174
  26.4 3.6 %collective-permute-start.6 = (f32[8,256]{1,0:T(8,128)}, f32[8,256]{1,0:T(8,128)S(1)}, u32[]{:S(2)}, u32[]{:S(2)}) collective-permute-start(f32[8,256]{1,0:T(8,128)} %shard_map.86), channel_id=1, source_target_pairs={{0,3},{1,0},{2,1},{3,2},{4,7},{5,4},{6,5},{7,6},{8,11},{9,8},{10,9... | collective-permute-start | bytes 24584 | tf_op jit(solution)/shard_map/ppermute | solution.py:26
  30.0 0.0 collective-permute-start.5
  30.0 1.0 %collective-permute-start.4 = (f32[8,256]{1,0:T(8,128)}, f32[8,256]{1,0:T(8,128)S(1)}, u32[]{:S(2)}, u32[]{:S(2)}) collective-permute-start(f32[8,256]{1,0:T(8,128)} %shard_map.86), channel_id=1, source_target_pairs={{0,1},{1,2},{2,3},{3,0},{4,5},{5,6},{6,7},{7,4},{8,9},{9,10},{10,1... | collective-permute-start | bytes 24584 | tf_op jit(solution)/shard_map/ppermute | solution.py:26
  31.0 0.6 %collective-permute-done.6 = f32[8,256]{1,0:T(8,128)S(1)} collective-permute-done((f32[8,256]{1,0:T(8,128)}, f32[8,256]{1,0:T(8,128)S(1)}, u32[]{:S(2)}, u32[]{:S(2)}) %collective-permute-start.6) | collective-permute-done | bytes 8224 | tf_op jit(solution)/shard_map/ppermute | solution.py:26
  31.6 3.2 %collective-permute-done.5 = f32[8,256]{1,0:T(8,128)S(1)} collective-permute-done((f32[8,256]{1,0:T(8,128)}, f32[8,256]{1,0:T(8,128)S(1)}, u32[]{:S(2)}, u32[]{:S(2)}) %collective-permute-start.5) | collective-permute-done | bytes 8224 | tf_op jit(solution)/shard_map/ppermute | solution.py:26
  34.8 0.9 %collective-permute-done.4 = f32[8,256]{1,0:T(8,128)S(1)} collective-permute-done((f32[8,256]{1,0:T(8,128)}, f32[8,256]{1,0:T(8,128)S(1)}, u32[]{:S(2)}, u32[]{:S(2)}) %collective-permute-start.4) | collective-permute-done | bytes 8224 | tf_op jit(solution)/shard_map/ppermute | solution.py:26
  35.7 1.3 %add_add_fusion.at_ref = f32[8,256]{1,0:T(8,128)} fusion(f32[8,256]{1,0:T(8,128)S(1)} %collective-permute-done.6, f32[8,256]{1,0:T(8,128)S(1)} %collective-permute-done.5, f32[8,256]{1,0:T(8,128)} %shard_map.86, f32[8,256]{1,0:T(8,128)S(1)} %collective-permute-done.4), kind=kLoop, calls=%fused_computation.2 | loop fusion | flops 6144 | bytes 40960 | tf_op jit(solution)/shard_map/add | solution.py:26
  37.0 2.6 %shard_map.87 = (f32[45,720]{1,0:T(8,128)}, f32[16,720]{1,0:T(8,128)}, f32[16,720]{1,0:T(8,128)}) custom-call(f32[8,256]{1,0:T(8,128)} %add_add_fusion.at_ref, f32[3,8,256]{2,1,0:T(8,128)} %copy.12.cells_ref.lists_ref), custom_call_target="tpu_custom_call" | custom-call | tf_op jit(solution)/shard_map/pallas_call | solution.py:227
  39.5 0.0 collective-permute-start.7
  39.5 2.6 %collective-permute-start.8 = (f32[16,720]{1,0:T(8,128)}, f32[16,720]{1,0:T(8,128)S(1)}, u32[]{:S(2)}, u32[]{:S(2)}) collective-permute-start(f32[16,720]{1,0:T(8,128)} %get-tuple-element.24), channel_id=1, source_target_pairs={{4,0},{8,4},{12,8},{16,12},{20,16},{24,20},{28,24},{0,28},{5,1},{9... | collective-permute-start | bytes 138248 | tf_op jit(solution)/shard_map/ppermute | solution.py:321
  42.2 2.2 %collective-permute-done.7 = f32[16,720]{1,0:T(8,128)S(1)} collective-permute-done((f32[16,720]{1,0:T(8,128)}, f32[16,720]{1,0:T(8,128)S(1)}, u32[]{:S(2)}, u32[]{:S(2)}) %collective-permute-start.7) | collective-permute-done | bytes 46112 | tf_op jit(solution)/shard_map/ppermute | solution.py:320
  44.4 0.0 collective-permute-done.8
  44.4 0.0 collective-permute-done.3.phigh_ref
  44.4 0.0 copy-start.1
  44.4 0.0 collective-permute-done.2.plow_ref
  44.4 0.0 copy-start.2
  44.4 0.6 %copy-done.5 = f32[16,720]{1,0:T(8,128)} copy-done((f32[16,720]{1,0:T(8,128)}, f32[16,720]{1,0:T(8,128)S(1)}, u32[]{:S(2)}) %copy-start.5) | copy-done | bytes 46104
  45.0 0.0 copy-done.6
  45.0 0.2 copy-done.1
  45.2 0.2 copy-done.2
  45.4 6.4 %shard_map.88 = f32[20,45,1,720]{3,2,1,0:T(1,128)} custom-call(bf16[20,1,45,720]{3,2,1,0:T(8,128)(2,1)} %pert_ref.3, bf16[20,1,16,720]{3,2,1,0:T(8,128)(2,1)} %copy-done.2, bf16[20,1,16,720]{3,2,1,0:T(8,128)(2,1)} %copy-done.1, f32[1,45,720]{2,1,0:T(8,128)} %bitcast.5, f32[1,16,720]{2,1,0:T(8,128)} %bitcast.6, f32[1,16,720]{2,1,0:T(8,128)} %bitcast.7, ...), custom_call_target="tpu_custom_call" | custom-call | tf_op jit(solution)/shard_map/pallas_call | solution.py:271
  (12 shorter events, 0.1 us)
Async XLA Ops:
  0.0 5.0 %copy-start.11 = (bf16[17]{0:T(256)(128)(2,1)S(1)}, bf16[17]{0:T(256)(128)(2,1)}, u32[]{:S(2)}) copy-start(bf16[17]{0:T(256)(128)(2,1)} %param.10) | copy-start | bytes 106
  0.0 5.5 %copy-start.12 = (bf16[17]{0:T(256)(128)(2,1)S(1)}, bf16[17]{0:T(256)(128)(2,1)}, u32[]{:S(2)}) copy-start(bf16[17]{0:T(256)(128)(2,1)} %param.11) | copy-start | bytes 106
  0.0 6.0 %copy-start.7 = (f32[1,8,256]{2,1,0:T(8,128)S(1)}, f32[1,8,256]{2,1,0:T(8,128)}, u32[]{:S(2)}) copy-start(f32[1,8,256]{2,1,0:T(8,128)} %param.12) | copy-start | bytes 24580
  0.0 6.0 %copy-start.8 = (s32[1,8,256]{2,1,0:T(8,128)S(1)}, s32[1,8,256]{2,1,0:T(8,128)}, u32[]{:S(2)}) copy-start(s32[1,8,256]{2,1,0:T(8,128)} %param.14) | copy-start | bytes 24580
  0.0 8.1 %copy-start.10 = (s32[1,8]{1,0:T(1,128)S(1)}, s32[1,8]{1,0:T(1,128)}, u32[]{:S(2)}) copy-start(s32[1,8]{1,0:T(1,128)} %param.15) | copy-start | bytes 100
  0.0 8.1 %copy-start.9 = (f32[1,8,256]{2,1,0:T(8,128)S(1)}, f32[1,8,256]{2,1,0:T(8,128)}, u32[]{:S(2)}) copy-start(f32[1,8,256]{2,1,0:T(8,128)} %param.13) | copy-start | bytes 24580
  0.0 18.0 %copy-start = (bf16[20,1,45,720]{3,2,1,0:T(8,128)(2,1)S(1)}, bf16[20,1,45,720]{3,2,1,0:T(8,128)(2,1)}, u32[]{:S(2)}) copy-start(bf16[20,1,45,720]{3,2,1,0:T(8,128)(2,1)} %pert_ref.3) | copy-start | bytes 3888004
  1.6 16.4 %collective-permute-start.1 = (bf16[20,1,16,720]{3,2,1,0:T(8,128)(2,1)S(1)}, bf16[20,1,16,720]{3,2,1,0:T(8,128)(2,1)S(1)}, u32[]{:S(2)}, u32[]{:S(2)}) collective-permute-start(bf16[20,1,16,720]{3,2,1,0:T(8,128)(2,1)S(1)} %get-tuple-element.27), channel_id=1, source_target_pairs={{4,0},{8,4},{12,8},{16,12},{20,16},{24,20},{28,24},{0,28},{5,1},{9... | collective-permute-start | bytes 1382408 | tf_op jit(solution)/shard_map/ppermute | solution.py:18
  5.0 13.0 %collective-permute-start = (bf16[20,1,16,720]{3,2,1,0:T(8,128)(2,1)S(1)}, bf16[20,1,16,720]{3,2,1,0:T(8,128)(2,1)S(1)}, u32[]{:S(2)}, u32[]{:S(2)}) collective-permute-start(bf16[20,1,16,720]{3,2,1,0:T(8,128)(2,1)S(1)} %get-tuple-element.28), channel_id=1, source_target_pairs={{0,4},{4,8},{8,12},{12,16},{16,20},{20,24},{24,28},{28,0},{1,5},{5... | collective-permute-start | bytes 1382408 | tf_op jit(solution)/shard_map/ppermute | solution.py:15
  18.0 1.9 %copy-start.3 = (bf16[20,1,16,720]{3,2,1,0:T(8,128)(2,1)}, bf16[20,1,16,720]{3,2,1,0:T(8,128)(2,1)S(1)}, u32[]{:S(2)}) copy-start(bf16[20,1,16,720]{3,2,1,0:T(8,128)(2,1)S(1)} %collective-permute-done.1.high_ref) | copy-start | bytes 1382404
  18.0 1.9 %copy-start.4 = (bf16[20,1,16,720]{3,2,1,0:T(8,128)(2,1)}, bf16[20,1,16,720]{3,2,1,0:T(8,128)(2,1)S(1)}, u32[]{:S(2)}) copy-start(bf16[20,1,16,720]{3,2,1,0:T(8,128)(2,1)S(1)} %collective-permute-done.low_ref) | copy-start | bytes 1382404
  18.2 26.2 %collective-permute-start.3 = (bf16[20,1,16,720]{3,2,1,0:T(8,128)(2,1)S(1)}, bf16[20,1,16,720]{3,2,1,0:T(8,128)(2,1)S(1)}, u32[]{:S(2)}, u32[]{:S(2)}) collective-permute-start(bf16[20,1,16,720]{3,2,1,0:T(8,128)(2,1)S(1)} %get-tuple-element.25), channel_id=1, source_target_pairs={{4,0},{8,4},{12,8},{16,12},{20,16},{24,20},{28,24},{0,28},{5,1},{9... | collective-permute-start | bytes 1382408 | tf_op jit(solution)/shard_map/ppermute | solution.py:18
  19.3 25.2 %collective-permute-start.2 = (bf16[20,1,16,720]{3,2,1,0:T(8,128)(2,1)S(1)}, bf16[20,1,16,720]{3,2,1,0:T(8,128)(2,1)S(1)}, u32[]{:S(2)}, u32[]{:S(2)}) collective-permute-start(bf16[20,1,16,720]{3,2,1,0:T(8,128)(2,1)S(1)} %get-tuple-element.26), channel_id=1, source_target_pairs={{0,4},{4,8},{8,12},{12,16},{16,20},{20,24},{24,28},{28,0},{1,5},{5... | collective-permute-start | bytes 1382408 | tf_op jit(solution)/shard_map/ppermute | solution.py:15
  26.4 5.2 %collective-permute-start.6 = (f32[8,256]{1,0:T(8,128)}, f32[8,256]{1,0:T(8,128)S(1)}, u32[]{:S(2)}, u32[]{:S(2)}) collective-permute-start(f32[8,256]{1,0:T(8,128)} %shard_map.86), channel_id=1, source_target_pairs={{0,3},{1,0},{2,1},{3,2},{4,7},{5,4},{6,5},{7,6},{8,11},{9,8},{10,9... | collective-permute-start | bytes 24584 | tf_op jit(solution)/shard_map/ppermute | solution.py:26
  30.0 4.8 %collective-permute-start.5 = (f32[8,256]{1,0:T(8,128)}, f32[8,256]{1,0:T(8,128)S(1)}, u32[]{:S(2)}, u32[]{:S(2)}) collective-permute-start(f32[8,256]{1,0:T(8,128)} %shard_map.86), channel_id=1, source_target_pairs={{0,2},{1,3},{2,0},{3,1},{4,6},{5,7},{6,4},{7,5},{8,10},{9,11},{10,... | collective-permute-start | bytes 24584 | tf_op jit(solution)/shard_map/ppermute | solution.py:26
  30.0 5.7 %collective-permute-start.4 = (f32[8,256]{1,0:T(8,128)}, f32[8,256]{1,0:T(8,128)S(1)}, u32[]{:S(2)}, u32[]{:S(2)}) collective-permute-start(f32[8,256]{1,0:T(8,128)} %shard_map.86), channel_id=1, source_target_pairs={{0,1},{1,2},{2,3},{3,0},{4,5},{5,6},{6,7},{7,4},{8,9},{9,10},{10,1... | collective-permute-start | bytes 24584 | tf_op jit(solution)/shard_map/ppermute | solution.py:26
  39.5 4.9 %collective-permute-start.7 = (f32[16,720]{1,0:T(8,128)}, f32[16,720]{1,0:T(8,128)S(1)}, u32[]{:S(2)}, u32[]{:S(2)}) collective-permute-start(f32[16,720]{1,0:T(8,128)} %get-tuple-element.23), channel_id=1, source_target_pairs={{0,4},{4,8},{8,12},{12,16},{16,20},{20,24},{24,28},{28,0},{1,5},{5... | collective-permute-start | bytes 138248 | tf_op jit(solution)/shard_map/ppermute | solution.py:320
  39.5 4.9 %collective-permute-start.8 = (f32[16,720]{1,0:T(8,128)}, f32[16,720]{1,0:T(8,128)S(1)}, u32[]{:S(2)}, u32[]{:S(2)}) collective-permute-start(f32[16,720]{1,0:T(8,128)} %get-tuple-element.24), channel_id=1, source_target_pairs={{4,0},{8,4},{12,8},{16,12},{20,16},{24,20},{28,24},{0,28},{5,1},{9... | collective-permute-start | bytes 138248 | tf_op jit(solution)/shard_map/ppermute | solution.py:321
  44.4 0.6 %copy-start.5 = (f32[16,720]{1,0:T(8,128)}, f32[16,720]{1,0:T(8,128)S(1)}, u32[]{:S(2)}) copy-start(f32[16,720]{1,0:T(8,128)S(1)} %collective-permute-done.7) | copy-start | bytes 138244
  44.4 0.6 %copy-start.6 = (f32[16,720]{1,0:T(8,128)}, f32[16,720]{1,0:T(8,128)S(1)}, u32[]{:S(2)}) copy-start(f32[16,720]{1,0:T(8,128)S(1)} %collective-permute-done.8) | copy-start | bytes 138244
  44.4 0.8 %copy-start.1 = (bf16[20,1,16,720]{3,2,1,0:T(8,128)(2,1)}, bf16[20,1,16,720]{3,2,1,0:T(8,128)(2,1)S(1)}, u32[]{:S(2)}) copy-start(bf16[20,1,16,720]{3,2,1,0:T(8,128)(2,1)S(1)} %collective-permute-done.3.phigh_ref) | copy-start | bytes 1382404
  44.4 1.0 %copy-start.2 = (bf16[20,1,16,720]{3,2,1,0:T(8,128)(2,1)}, bf16[20,1,16,720]{3,2,1,0:T(8,128)(2,1)S(1)}, u32[]{:S(2)}) copy-start(bf16[20,1,16,720]{3,2,1,0:T(8,128)(2,1)S(1)} %collective-permute-done.2.plow_ref) | copy-start | bytes 1382404

commit v10 on v9

--- a/solution.py
+++ b/solution.py
@@ -19,14 +19,12 @@
     return low, high
 
 
-def sum_over(values, axis):
+def gather_over(values, axis):
     count = lax.axis_size(axis)
-    total = values
-    for shift in range(1, count):
-        total = total + lax.ppermute(
-            values, axis, [(i, (i + shift) % count) for i in range(count)]
-        )
-    return total
+    return [values] + [
+        lax.ppermute(values, axis, [(i, (i + shift) % count) for i in range(count)])
+        for shift in range(1, count)
+    ]
 
 
 def select_chain(dist, taps_ref):
@@ -195,16 +193,21 @@
     )(control, c_low, c_high, perturb, band_lon, band_lat, cells)
 
 
-def spread_misfits(at_cells, lists, lon_cells, lat_cells, radius, padded):
+def spread_misfits(partials, lists, lon_cells, lat_cells, radius, padded):
     _, sources, slots = lists.shape
     parts = -(-lat_cells // 128)
 
-    def kernel(at_ref, lists_ref, spread_ref, low_ref, high_ref, fold_ref):
+    def kernel(*refs):
+        part_refs = refs[:len(partials)]
+        lists_ref, spread_ref, low_ref, high_ref, fold_ref = refs[len(partials):]
+        at_cells = part_refs[0][...]
+        for ref in part_refs[1:]:
+            at_cells = at_cells + ref[...]
         key_ids = lax.broadcasted_iota(jnp.int32, (parts * padded, slots), 0)
         folded = jnp.zeros((parts * padded, 128), jnp.float32)
         for row in range(sources):
             misfit = lists_ref[1, row:row + 1, :] * (
-                at_ref[row:row + 1, :] - lists_ref[0, row:row + 1, :]
+                at_cells[row:row + 1, :] - lists_ref[0, row:row + 1, :]
             )
             keys, onehot = cell_keys(lists_ref[2, row:row + 1, :], padded, lat_cells)
             for piece in split3(misfit):
@@ -232,7 +235,7 @@
             jax.ShapeDtypeStruct((radius, lat_cells), jnp.float32),
         ),
         scratch_shapes=[pltpu.VMEM((padded, lat_cells), jnp.float32)],
-    )(at_cells, lists)
+    )(*partials, lists)
 
 
 def backward_grad(perturb, p_low, p_high, spread, s_low, s_high, control, band_lon, band_lat):
@@ -312,9 +315,9 @@
     partial = forward_pick(
         control, c_low, c_high, perturb, band_lon, band_lat, received
     )
-    at_cells = sum_over(partial, "mem")
+    partials = gather_over(partial, "mem")
     spread, low_send, high_send = spread_misfits(
-        at_cells, received, lon_cells, lat_cells, radius, padded
+        partials, received, lon_cells, lat_cells, radius, padded
     )
     count = lax.axis_size("tile")
     s_low = lax.ppermute(low_send, "tile", [(i, (i + 1) % count) for i in range(count)])

time: 52.2 us -> 51.5 us (0.987)
  other arithmetic: 2.43 us -> 1.2 us
  local copies, waits for them, and re-layouts: 3.29 us -> 3.91 us
    add x1 -> x0, other arithmetic: 1.3 us -> none  [sum_over(): total + lax.ppermute(values, axis, [(i, (i + shift) % count) for i in ran...]
    unnamed x27 -> x33, local copies, waits for them, and re-layouts: 1.01 us -> 1.63 us
  transfers between devices with their start and end apart: 9 -> 9, of which waited for: 4 -> 4; matrix products, arithmetic and copies ran while one was open for 6% -> 4% of each run, Pallas kernels for 21% -> 22%
where the time goes in v10:
time: 51.5 us; the launch traced here: 51.1 us
  Pallas kernels  17.5 us (34%)
  starting transfers between devices  11.8 us (23%)
  blocking collectives  9.75 us (19%)
  waiting for transfers between devices  6.79 us (13%)
  local copies, waits for them, and re-layouts  3.91 us (8%)
  other arithmetic  1.2 us (2%)
    all_to_all x1, blocking collectives, local(): lax.all_to_all(lists, 'tile', split_axis=1, concat_axis=1, tiled=True)  9.75 us
    pallas_call x1, Pallas kernels, forward_pick(): pl.pallas_call(kernel, grid=(steps,), in_specs=[field, halo, halo, field,...  6.56 us
    pallas_call x1, Pallas kernels, backward_grad(): pl.pallas_call(kernel, grid=(levels, members // chunk), in_specs=[field,...  6.37 us
    ppermute x3, waiting for transfers between devices, gather_over(): lax.ppermute(values, axis, [(i, (i + shift) % count) for i in range(count)])  4.65 us
    ppermute x3, starting transfers between devices, gather_over(): lax.ppermute(values, axis, [(i, (i + shift) % count) for i in range(count)])  4.61 us
    ppermute x2, starting transfers between devices, halos(): lax.ppermute(lax.slice_in_dim(block, 0, width, axis=dim), axis, backward)  4.52 us
    ppermute x1, starting transfers between devices, local(): lax.ppermute(high_send, 'tile', [((i + 1) % count, i) for i in range(coun...  2.64 us
    pallas_call x1, Pallas kernels, spread_misfits(): pl.pallas_call(kernel, out_shape=(jax.ShapeDtypeStruct((lon_cells, lat_ce...  2.61 us
  transfers between devices with their start and end apart: 9, of which 4 were waited for; matrix products, arithmetic and copies ran while one was open for 4% of the time, Pallas kernels for 22%

profile of v10, /device:TPU:0, one launch (start us, length us, event | category | flops | bytes accessed | tf_op | source)
XLA Modules:
  0.0 51.1 jit_solution(15009913523927668489)
XLA Ops:
  0.0 0.0 copy-start.12
  0.0 0.0 copy-start
  0.0 1.5 %fusion.1 = (bf16[20,1,16,720]{3,2,1,0:T(8,128)(2,1)S(1)}, bf16[20,1,16,720]{3,2,1,0:T(8,128)(2,1)S(1)}) fusion(bf16[20,1,45,720]{3,2,1,0:T(8,128)(2,1)} %ctrl_ref.3), kind=kLoop, calls=%fused_computation.3 | loop fusion | bytes 1843200 | tf_op jit(solution)/shard_map/slice | solution.py:18
  1.6 3.4 %collective-permute-start.1 = (bf16[20,1,16,720]{3,2,1,0:T(8,128)(2,1)S(1)}, bf16[20,1,16,720]{3,2,1,0:T(8,128)(2,1)S(1)}, u32[]{:S(2)}, u32[]{:S(2)}) collective-permute-start(bf16[20,1,16,720]{3,2,1,0:T(8,128)(2,1)S(1)} %get-tuple-element.27), channel_id=1, source_target_pairs={{4,0},{8,4},{12,8},{16,12},{20,16},{24,20},{28,24},{0,28},{5,1},{9... | collective-permute-start | bytes 1382408 | tf_op jit(solution)/shard_map/ppermute | solution.py:18
  5.0 0.0 collective-permute-start
  5.0 0.0 copy-done.14
  5.0 0.5 %convert_element_type.10.lon_ref = f32[17]{0:T(128)} convert(bf16[17]{0:T(256)(128)(2,1)S(1)} %copy-done.14) | non-fusion elementwise | flops 17 | bytes 102 | tf_op jit(solution)/shard_map/convert_element_type | solution.py:84
  5.5 0.0 copy-done.15
  5.5 0.6 %convert_element_type.11.lat_ref = f32[17]{0:T(128)} convert(bf16[17]{0:T(256)(128)(2,1)S(1)} %copy-done.15) | non-fusion elementwise | flops 17 | bytes 102 | tf_op jit(solution)/shard_map/convert_element_type | solution.py:84
  6.1 0.0 copy-done.10
  6.1 0.0 copy-done.11
  6.2 2.0 %shard_map.85 = (bf16[48,80]{1,0:T(8,128)(2,1)}, bf16[720,720]{1,0:T(8,128)(2,1)}) custom-call(f32[17]{0:T(128)} %convert_element_type.10.lon_ref, f32[17]{0:T(128)} %convert_element_type.11.lat_ref), custom_call_target="tpu_custom_call" | custom-call | tf_op jit(solution)/shard_map/pallas_call | solution.py:77
  8.1 0.0 copy-done.13
  8.1 0.0 copy-done.12
  8.1 0.1 compare_select_fusion
  8.2 9.7 %all_to_all.5 = f32[3,8,256]{2,0,1:T(4,128)S(1)} all-to-all(f32[3,8,256]{2,0,1:T(4,128)S(1)} %pad_maximum_fusion), channel_id=1, replica_groups=mesh['tile'=8,'mem'=4] {'tile'}, dimensions={1} | all-to-all | bytes 49152 | tf_op jit(solution)/shard_map/all_to_all | solution.py:309
  18.0 0.0 collective-permute-done.1.high_ref
  18.0 0.0 collective-permute-done.low_ref
  18.0 0.0 copy-done
  18.0 0.0 copy-start.4
  18.0 0.1 fusion
  18.2 1.1 %collective-permute-start.3 = (bf16[20,1,16,720]{3,2,1,0:T(8,128)(2,1)S(1)}, bf16[20,1,16,720]{3,2,1,0:T(8,128)(2,1)S(1)}, u32[]{:S(2)}, u32[]{:S(2)}) collective-permute-start(bf16[20,1,16,720]{3,2,1,0:T(8,128)(2,1)S(1)} %get-tuple-element.25), channel_id=1, source_target_pairs={{4,0},{8,4},{12,8},{16,12},{20,16},{24,20},{28,24},{0,28},{5,1},{9... | collective-permute-start | bytes 1382408 | tf_op jit(solution)/shard_map/ppermute | solution.py:18
  19.3 0.0 collective-permute-start.2
  19.3 0.6 %copy.12.cells_ref.refs_4_ = f32[3,8,256]{2,1,0:T(8,128)} copy(f32[3,8,256]{2,0,1:T(4,128)S(1)} %all_to_all.5) | data formatting | bytes 49152 | tf_op jit(solution)/shard_map/optimization_barrier | solution.py:312
  19.9 0.0 copy-done.3
  19.9 0.0 copy-done.4
  19.9 6.6 %shard_map.86.refs_0_ = f32[8,256]{1,0:T(8,128)} custom-call(bf16[20,1,45,720]{3,2,1,0:T(8,128)(2,1)} %ctrl_ref.3, bf16[20,1,16,720]{3,2,1,0:T(8,128)(2,1)} %copy-done.4, bf16[20,1,16,720]{3,2,1,0:T(8,128)(2,1)} %copy-done.3, bf16[20,1,45,720]{3,2,1,0:T(8,128)(2,1)} %pert_ref.3, bf16[48,80]{1,0:T(8,128)(2,1)} %get-tuple-element.15.blon_ref, ...), custom_call_target="tpu_custom_call" | custom-call | tf_op jit(solution)/shard_map/pallas_call | solution.py:172
  26.4 3.6 %collective-permute-start.6 = (f32[8,256]{1,0:T(8,128)}, f32[8,256]{1,0:T(8,128)S(1)}, u32[]{:S(2)}, u32[]{:S(2)}) collective-permute-start(f32[8,256]{1,0:T(8,128)} %shard_map.86.refs_0_), channel_id=1, source_target_pairs={{0,3},{1,0},{2,1},{3,2},{4,7},{5,4},{6,5},{7,6},{8,11},{9,8},{10,9... | collective-permute-start | bytes 24584 | tf_op jit(solution)/shard_map/ppermute | solution.py:25
  30.0 0.0 collective-permute-start.5
  30.0 1.0 %collective-permute-start.4 = (f32[8,256]{1,0:T(8,128)}, f32[8,256]{1,0:T(8,128)S(1)}, u32[]{:S(2)}, u32[]{:S(2)}) collective-permute-start(f32[8,256]{1,0:T(8,128)} %shard_map.86.refs_0_), channel_id=1, source_target_pairs={{0,1},{1,2},{2,3},{3,0},{4,5},{5,6},{6,7},{7,4},{8,9},{9,10},{10,1... | collective-permute-start | bytes 24584 | tf_op jit(solution)/shard_map/ppermute | solution.py:25
  31.0 0.6 %collective-permute-done.6.refs_3_ = f32[8,256]{1,0:T(8,128)S(1)} collective-permute-done((f32[8,256]{1,0:T(8,128)}, f32[8,256]{1,0:T(8,128)S(1)}, u32[]{:S(2)}, u32[]{:S(2)}) %collective-permute-start.6) | collective-permute-done | bytes 8224 | tf_op jit(solution)/shard_map/ppermute | solution.py:25
  31.6 3.2 %collective-permute-done.5.refs_2_ = f32[8,256]{1,0:T(8,128)S(1)} collective-permute-done((f32[8,256]{1,0:T(8,128)}, f32[8,256]{1,0:T(8,128)S(1)}, u32[]{:S(2)}, u32[]{:S(2)}) %collective-permute-start.5) | collective-permute-done | bytes 8224 | tf_op jit(solution)/shard_map/ppermute | solution.py:25
  34.8 0.9 %collective-permute-done.4.refs_1_ = f32[8,256]{1,0:T(8,128)S(1)} collective-permute-done((f32[8,256]{1,0:T(8,128)}, f32[8,256]{1,0:T(8,128)S(1)}, u32[]{:S(2)}, u32[]{:S(2)}) %collective-permute-start.4) | collective-permute-done | bytes 8224 | tf_op jit(solution)/shard_map/ppermute | solution.py:25
  35.7 0.0 copy-done.7
  35.7 0.0 copy-done.8
  35.7 0.6 %copy-done.9 = f32[8,256]{1,0:T(8,128)} copy-done((f32[8,256]{1,0:T(8,128)}, f32[8,256]{1,0:T(8,128)S(1)}, u32[]{:S(2)}) %copy-start.9) | copy-done | bytes 8216
  36.3 2.6 %shard_map.87 = (f32[45,720]{1,0:T(8,128)}, f32[16,720]{1,0:T(8,128)}, f32[16,720]{1,0:T(8,128)}) custom-call(f32[8,256]{1,0:T(8,128)} %shard_map.86.refs_0_, f32[8,256]{1,0:T(8,128)} %copy-done.9, f32[8,256]{1,0:T(8,128)} %copy-done.8, f32[8,256]{1,0:T(8,128)} %copy-done.7, f32[3,8,256]{2,1,0:T(8,128)} %copy.12.cells_ref.refs_4_), custom_call_target="tpu_custom_call" | custom-call | tf_op jit(solution)/shard_map/pallas_call | solution.py:230
  38.9 0.0 collective-permute-start.7
  38.9 2.6 %collective-permute-start.8 = (f32[16,720]{1,0:T(8,128)}, f32[16,720]{1,0:T(8,128)S(1)}, u32[]{:S(2)}, u32[]{:S(2)}) collective-permute-start(f32[16,720]{1,0:T(8,128)} %get-tuple-element.24), channel_id=1, source_target_pairs={{4,0},{8,4},{12,8},{16,12},{20,16},{24,20},{28,24},{0,28},{5,1},{9... | collective-permute-start | bytes 138248 | tf_op jit(solution)/shard_map/ppermute | solution.py:324
  41.6 2.1 %collective-permute-done.7 = f32[16,720]{1,0:T(8,128)S(1)} collective-permute-done((f32[16,720]{1,0:T(8,128)}, f32[16,720]{1,0:T(8,128)S(1)}, u32[]{:S(2)}, u32[]{:S(2)}) %collective-permute-start.7) | collective-permute-done | bytes 46112 | tf_op jit(solution)/shard_map/ppermute | solution.py:323
  43.7 0.0 collective-permute-done.8
  43.7 0.0 collective-permute-done.3.phigh_ref
  43.7 0.0 collective-permute-done.2.plow_ref
  43.7 0.6 %copy-done.5 = f32[16,720]{1,0:T(8,128)} copy-done((f32[16,720]{1,0:T(8,128)}, f32[16,720]{1,0:T(8,128)S(1)}, u32[]{:S(2)}) %copy-start.5) | copy-done | bytes 46104
  44.3 0.0 copy-done.6
  44.3 0.2 copy-done.1
  44.5 0.2 copy-done.2
  44.7 6.4 %shard_map.88 = f32[20,45,1,720]{3,2,1,0:T(1,128)} custom-call(bf16[20,1,45,720]{3,2,1,0:T(8,128)(2,1)} %pert_ref.3, bf16[20,1,16,720]{3,2,1,0:T(8,128)(2,1)} %copy-done.2, bf16[20,1,16,720]{3,2,1,0:T(8,128)(2,1)} %copy-done.1, f32[1,45,720]{2,1,0:T(8,128)} %bitcast.5, f32[1,16,720]{2,1,0:T(8,128)} %bitcast.6, f32[1,16,720]{2,1,0:T(8,128)} %bitcast.7, ...), custom_call_target="tpu_custom_call" | custom-call | tf_op jit(solution)/shard_map/pallas_call | solution.py:274
  (17 shorter events, 0.1 us)
Async XLA Ops:
  0.0 5.0 %copy-start.14 = (bf16[17]{0:T(256)(128)(2,1)S(1)}, bf16[17]{0:T(256)(128)(2,1)}, u32[]{:S(2)}) copy-start(bf16[17]{0:T(256)(128)(2,1)} %param.10) | copy-start | bytes 106
  0.0 5.5 %copy-start.15 = (bf16[17]{0:T(256)(128)(2,1)S(1)}, bf16[17]{0:T(256)(128)(2,1)}, u32[]{:S(2)}) copy-start(bf16[17]{0:T(256)(128)(2,1)} %param.11) | copy-start | bytes 106
  0.0 6.1 %copy-start.10 = (f32[1,8,256]{2,1,0:T(8,128)S(1)}, f32[1,8,256]{2,1,0:T(8,128)}, u32[]{:S(2)}) copy-start(f32[1,8,256]{2,1,0:T(8,128)} %param.12) | copy-start | bytes 24580
  0.0 6.1 %copy-start.11 = (s32[1,8,256]{2,1,0:T(8,128)S(1)}, s32[1,8,256]{2,1,0:T(8,128)}, u32[]{:S(2)}) copy-start(s32[1,8,256]{2,1,0:T(8,128)} %param.14) | copy-start | bytes 24580
  0.0 8.1 %copy-start.13 = (s32[1,8]{1,0:T(1,128)S(1)}, s32[1,8]{1,0:T(1,128)}, u32[]{:S(2)}) copy-start(s32[1,8]{1,0:T(1,128)} %param.15) | copy-start | bytes 100
  0.0 8.1 %copy-start.12 = (f32[1,8,256]{2,1,0:T(8,128)S(1)}, f32[1,8,256]{2,1,0:T(8,128)}, u32[]{:S(2)}) copy-start(f32[1,8,256]{2,1,0:T(8,128)} %param.13) | copy-start | bytes 24580
  0.0 18.0 %copy-start = (bf16[20,1,45,720]{3,2,1,0:T(8,128)(2,1)S(1)}, bf16[20,1,45,720]{3,2,1,0:T(8,128)(2,1)}, u32[]{:S(2)}) copy-start(bf16[20,1,45,720]{3,2,1,0:T(8,128)(2,1)} %pert_ref.3) | copy-start | bytes 3888004
  1.6 16.4 %collective-permute-start.1 = (bf16[20,1,16,720]{3,2,1,0:T(8,128)(2,1)S(1)}, bf16[20,1,16,720]{3,2,1,0:T(8,128)(2,1)S(1)}, u32[]{:S(2)}, u32[]{:S(2)}) collective-permute-start(bf16[20,1,16,720]{3,2,1,0:T(8,128)(2,1)S(1)} %get-tuple-element.27), channel_id=1, source_target_pairs={{4,0},{8,4},{12,8},{16,12},{20,16},{24,20},{28,24},{0,28},{5,1},{9... | collective-permute-start | bytes 1382408 | tf_op jit(solution)/shard_map/ppermute | solution.py:18
  5.0 13.0 %collective-permute-start = (bf16[20,1,16,720]{3,2,1,0:T(8,128)(2,1)S(1)}, bf16[20,1,16,720]{3,2,1,0:T(8,128)(2,1)S(1)}, u32[]{:S(2)}, u32[]{:S(2)}) collective-permute-start(bf16[20,1,16,720]{3,2,1,0:T(8,128)(2,1)S(1)} %get-tuple-element.28), channel_id=1, source_target_pairs={{0,4},{4,8},{8,12},{12,16},{16,20},{20,24},{24,28},{28,0},{1,5},{5... | collective-permute-start | bytes 1382408 | tf_op jit(solution)/shard_map/ppermute | solution.py:15
  18.0 1.9 %copy-start.3 = (bf16[20,1,16,720]{3,2,1,0:T(8,128)(2,1)}, bf16[20,1,16,720]{3,2,1,0:T(8,128)(2,1)S(1)}, u32[]{:S(2)}) copy-start(bf16[20,1,16,720]{3,2,1,0:T(8,128)(2,1)S(1)} %collective-permute-done.1.high_ref) | copy-start | bytes 1382404
  18.0 1.9 %copy-start.4 = (bf16[20,1,16,720]{3,2,1,0:T(8,128)(2,1)}, bf16[20,1,16,720]{3,2,1,0:T(8,128)(2,1)S(1)}, u32[]{:S(2)}) copy-start(bf16[20,1,16,720]{3,2,1,0:T(8,128)(2,1)S(1)} %collective-permute-done.low_ref) | copy-start | bytes 1382404
  18.2 25.5 %collective-permute-start.3 = (bf16[20,1,16,720]{3,2,1,0:T(8,128)(2,1)S(1)}, bf16[20,1,16,720]{3,2,1,0:T(8,128)(2,1)S(1)}, u32[]{:S(2)}, u32[]{:S(2)}) collective-permute-start(bf16[20,1,16,720]{3,2,1,0:T(8,128)(2,1)S(1)} %get-tuple-element.25), channel_id=1, source_target_pairs={{4,0},{8,4},{12,8},{16,12},{20,16},{24,20},{28,24},{0,28},{5,1},{9... | collective-permute-start | bytes 1382408 | tf_op jit(solution)/shard_map/ppermute | solution.py:18
  19.3 24.5 %collective-permute-start.2 = (bf16[20,1,16,720]{3,2,1,0:T(8,128)(2,1)S(1)}, bf16[20,1,16,720]{3,2,1,0:T(8,128)(2,1)S(1)}, u32[]{:S(2)}, u32[]{:S(2)}) collective-permute-start(bf16[20,1,16,720]{3,2,1,0:T(8,128)(2,1)S(1)} %get-tuple-element.26), channel_id=1, source_target_pairs={{0,4},{4,8},{8,12},{12,16},{16,20},{20,24},{24,28},{28,0},{1,5},{5... | collective-permute-start | bytes 1382408 | tf_op jit(solution)/shard_map/ppermute | solution.py:15
  26.4 5.2 %collective-permute-start.6 = (f32[8,256]{1,0:T(8,128)}, f32[8,256]{1,0:T(8,128)S(1)}, u32[]{:S(2)}, u32[]{:S(2)}) collective-permute-start(f32[8,256]{1,0:T(8,128)} %shard_map.86.refs_0_), channel_id=1, source_target_pairs={{0,3},{1,0},{2,1},{3,2},{4,7},{5,4},{6,5},{7,6},{8,11},{9,8},{10,9... | collective-permute-start | bytes 24584 | tf_op jit(solution)/shard_map/ppermute | solution.py:25
  30.0 4.8 %collective-permute-start.5 = (f32[8,256]{1,0:T(8,128)}, f32[8,256]{1,0:T(8,128)S(1)}, u32[]{:S(2)}, u32[]{:S(2)}) collective-permute-start(f32[8,256]{1,0:T(8,128)} %shard_map.86.refs_0_), channel_id=1, source_target_pairs={{0,2},{1,3},{2,0},{3,1},{4,6},{5,7},{6,4},{7,5},{8,10},{9,11},{10,... | collective-permute-start | bytes 24584 | tf_op jit(solution)/shard_map/ppermute | solution.py:25
  30.0 5.7 %collective-permute-start.4 = (f32[8,256]{1,0:T(8,128)}, f32[8,256]{1,0:T(8,128)S(1)}, u32[]{:S(2)}, u32[]{:S(2)}) collective-permute-start(f32[8,256]{1,0:T(8,128)} %shard_map.86.refs_0_), channel_id=1, source_target_pairs={{0,1},{1,2},{2,3},{3,0},{4,5},{5,6},{6,7},{7,4},{8,9},{9,10},{10,1... | collective-permute-start | bytes 24584 | tf_op jit(solution)/shard_map/ppermute | solution.py:25
  31.6 4.1 %copy-start.7 = (f32[8,256]{1,0:T(8,128)}, f32[8,256]{1,0:T(8,128)S(1)}, u32[]{:S(2)}) copy-start(f32[8,256]{1,0:T(8,128)S(1)} %collective-permute-done.6.refs_3_) | copy-start | bytes 24580
  34.8 0.9 %copy-start.8 = (f32[8,256]{1,0:T(8,128)}, f32[8,256]{1,0:T(8,128)S(1)}, u32[]{:S(2)}) copy-start(f32[8,256]{1,0:T(8,128)S(1)} %collective-permute-done.5.refs_2_) | copy-start | bytes 24580
  35.7 0.6 %copy-start.9 = (f32[8,256]{1,0:T(8,128)}, f32[8,256]{1,0:T(8,128)S(1)}, u32[]{:S(2)}) copy-start(f32[8,256]{1,0:T(8,128)S(1)} %collective-permute-done.4.refs_1_) | copy-start | bytes 24580
  38.9 4.8 %collective-permute-start.7 = (f32[16,720]{1,0:T(8,128)}, f32[16,720]{1,0:T(8,128)S(1)}, u32[]{:S(2)}, u32[]{:S(2)}) collective-permute-start(f32[16,720]{1,0:T(8,128)} %get-tuple-element.23), channel_id=1, source_target_pairs={{0,4},{4,8},{8,12},{12,16},{16,20},{20,24},{24,28},{28,0},{1,5},{5... | collective-permute-start | bytes 138248 | tf_op jit(solution)/shard_map/ppermute | solution.py:323
  38.9 4.8 %collective-permute-start.8 = (f32[16,720]{1,0:T(8,128)}, f32[16,720]{1,0:T(8,128)S(1)}, u32[]{:S(2)}, u32[]{:S(2)}) collective-permute-start(f32[16,720]{1,0:T(8,128)} %get-tuple-element.24), channel_id=1, source_target_pairs={{4,0},{8,4},{12,8},{16,12},{20,16},{24,20},{28,24},{0,28},{5,1},{9... | collective-permute-start | bytes 138248 | tf_op jit(solution)/shard_map/ppermute | solution.py:324
  43.7 0.6 %copy-start.5 = (f32[16,720]{1,0:T(8,128)}, f32[16,720]{1,0:T(8,128)S(1)}, u32[]{:S(2)}) copy-start(f32[16,720]{1,0:T(8,128)S(1)} %collective-permute-done.7) | copy-start | bytes 138244
  43.7 0.6 %copy-start.6 = (f32[16,720]{1,0:T(8,128)}, f32[16,720]{1,0:T(8,128)S(1)}, u32[]{:S(2)}) copy-start(f32[16,720]{1,0:T(8,128)S(1)} %collective-permute-done.8) | copy-start | bytes 138244
  43.7 0.8 %copy-start.1 = (bf16[20,1,16,720]{3,2,1,0:T(8,128)(2,1)}, bf16[20,1,16,720]{3,2,1,0:T(8,128)(2,1)S(1)}, u32[]{:S(2)}) copy-start(bf16[20,1,16,720]{3,2,1,0:T(8,128)(2,1)S(1)} %collective-permute-done.3.phigh_ref) | copy-start | bytes 1382404
  43.7 1.0 %copy-start.2 = (bf16[20,1,16,720]{3,2,1,0:T(8,128)(2,1)}, bf16[20,1,16,720]{3,2,1,0:T(8,128)(2,1)S(1)}, u32[]{:S(2)}) copy-start(bf16[20,1,16,720]{3,2,1,0:T(8,128)(2,1)S(1)} %collective-permute-done.2.plow_ref) | copy-start | bytes 1382404

commit v11 on v10

--- a/solution.py
+++ b/solution.py
@@ -17,6 +17,19 @@
     )
     high = lax.ppermute(lax.slice_in_dim(block, 0, width, axis=dim), axis, backward)
     return low, high
+
+
+def exchange(lists, axis):
+    count = lax.axis_size(axis)
+    rolled = jnp.roll(lists, -lax.axis_index(axis), axis=1)
+    rows = [rolled[:, 0:1]]
+    for shift in range(1, count):
+        rows.append(
+            lax.ppermute(
+                rolled[:, shift:shift + 1], axis, [(i, (i + shift) % count) for i in range(count)]
+            )
+        )
+    return jnp.concatenate(rows, axis=1)
 
 
 def gather_over(values, axis):
@@ -117,17 +130,24 @@
     return keys, onehot
 
 
-def forward_pick(control, c_low, c_high, perturb, band_lon, band_lat, cells):
-    members, levels, lon_cells, lat_cells = control.shape
+def forward_pick(control, c_low, c_high, perturb, band_lon, band_lat, prior, cells, first):
+    _, levels, lon_cells, lat_cells = control.shape
+    members = c_low.shape[0]
     radius = c_low.shape[2]
     padded, ext_cells = band_lon.shape
-    chunk = member_chunk(members)
+    chunk = member_chunk(math.gcd(members, first) if first else members)
     steps = members // chunk
-    _, sources, slots = cells.shape
+    base = first // chunk
     parts = -(-lat_cells // 128)
-
-    def kernel(ctrl_ref, low_ref, high_ref, pert_ref, blon_ref, blat_ref, cells_ref, out_ref,
-               ext_ref, along_ref, acc_ref, fold_ref):
+    if cells is not None:
+        _, sources, slots = cells.shape
+
+    def kernel(*refs):
+        ctrl_ref, low_ref, high_ref, pert_ref, blon_ref, blat_ref = refs[:6]
+        rest = list(refs[6:])
+        prior_ref = rest.pop(0) if prior is not None else None
+        cells_ref = rest.pop(0) if cells is not None else None
+        out_ref, ext_ref, along_ref, acc_ref, fold_ref = rest
         step = pl.program_id(0)
         blon = blon_ref[...]
         for m in range(chunk):
@@ -143,9 +163,19 @@
 
         @pl.when(step == 0)
         def _():
-            acc_ref[...] = jnp.zeros(acc_ref.shape, acc_ref.dtype)
+            if prior_ref is None:
+                acc_ref[...] = jnp.zeros(acc_ref.shape, acc_ref.dtype)
+            else:
+                acc_ref[...] = prior_ref[...]
 
         acc_ref[0:lon_cells, :] = acc_ref[0:lon_cells, :] + total
+
+        if cells_ref is None:
+            @pl.when(step == steps - 1)
+            def _():
+                out_ref[...] = acc_ref[...]
+
+            return
 
         @pl.when(step == steps - 1)
         def _():
@@ -166,9 +196,11 @@
                     jnp.where(key_ids == keys, at_keys, 0.0), axis=0, keepdims=True
                 )
 
-    field = pl.BlockSpec((chunk, None, lon_cells, lat_cells), lambda g: (g, 0, 0, 0))
+    field = pl.BlockSpec((chunk, None, lon_cells, lat_cells), lambda g: (g + base, 0, 0, 0))
     halo = pl.BlockSpec((chunk, None, radius, lat_cells), lambda g: (g, 0, 0, 0))
     whole = lambda shape: pl.BlockSpec(shape, lambda g: (0,) * len(shape))
+    extra = [a for a in (prior, cells) if a is not None]
+    out_shape = (sources, slots) if cells is not None else (padded, lat_cells)
     return pl.pallas_call(
         kernel,
         grid=(steps,),
@@ -179,10 +211,9 @@
             field,
             whole(band_lon.shape),
             whole(band_lat.shape),
-            whole(cells.shape),
-        ],
-        out_specs=whole((sources, slots)),
-        out_shape=jax.ShapeDtypeStruct((sources, slots), jnp.float32),
+        ] + [whole(a.shape) for a in extra],
+        out_specs=whole(out_shape),
+        out_shape=jax.ShapeDtypeStruct(out_shape, jnp.float32),
         scratch_shapes=[
             pltpu.VMEM((ext_cells, lat_cells), jnp.bfloat16),
             pltpu.VMEM((chunk * padded, lat_cells), jnp.bfloat16),
@@ -190,7 +221,7 @@
             pltpu.VMEM((parts * padded, 128), jnp.float32),
         ],
         compiler_params=pltpu.CompilerParams(dimension_semantics=("arbitrary",)),
-    )(control, c_low, c_high, perturb, band_lon, band_lat, cells)
+    )(control, c_low, c_high, perturb, band_lon, band_lat, *extra)
 
 
 def spread_misfits(partials, lists, lon_cells, lat_cells, radius, padded):
@@ -305,16 +336,24 @@
     slot_ids = lax.broadcasted_iota(jnp.int32, innov.shape, 2)
     weights = jnp.where(slot_ids < counts[:, :, None], inv_var, 0.0)
     lists = jnp.concatenate([innov, weights, cell_index.astype(jnp.float32)])
-    lists = lax.optimization_barrier((lists, band_lon, band_lat))[0]
-    received = lax.all_to_all(lists, "tile", split_axis=1, concat_axis=1, tiled=True)
-
-    c_low, c_high = halos(control, "tile", 2, radius)
-    c_low, c_high, received = lax.optimization_barrier((c_low, c_high, received))
-    late_perturb = lax.optimization_barrier((perturb, c_low, c_high))[0]
+    received = exchange(lists, "tile")
+
+    half = members_here // 2
+    a_low, a_high = halos(control[:half], "tile", 2, radius)
+    a_low, a_high, band_lon, band_lat = lax.optimization_barrier(
+        (a_low, a_high, band_lon, band_lat)
+    )
+    late_control = lax.optimization_barrier((control, a_low, a_high))[0]
+    b_low, b_high = halos(late_control[half:], "tile", 2, radius)
+    field = forward_pick(
+        control, a_low, a_high, perturb, band_lon, band_lat, None, None, 0
+    )
+    b_low, b_high, field, received = lax.optimization_barrier((b_low, b_high, field, received))
+    partial = forward_pick(
+        control, b_low, b_high, perturb, band_lon, band_lat, field, received, half
+    )
+    late_perturb = lax.optimization_barrier((perturb, partial))[0]
     p_low, p_high = halos(late_perturb, "tile", 2, radius)
-    partial = forward_pick(
-        control, c_low, c_high, perturb, band_lon, band_lat, received
-    )
     partials = gather_over(partial, "mem")
     spread, low_send, high_send = spread_misfits(
         partials, received, lon_cells, lat_cells, radius, padded

time: 51.5 us -> 63.9 us (1.24)
  blocking collectives: 9.75 us -> 0 us
  starting transfers between devices: 11.8 us -> 20.1 us
  waiting for transfers between devices: 6.79 us -> 13 us
  other arithmetic: 1.2 us -> 4.58 us
  local copies, waits for them, and re-layouts: 3.91 us -> 6.18 us
  Pallas kernels: 17.5 us -> 19.3 us
    all_to_all x1 -> x0, blocking collectives: 9.75 us -> none  [local(): lax.all_to_all(lists, 'tile', split_axis=1, concat_axis=1, tiled=True)]
    ppermute x0 -> x7, starting transfers between devices: none -> 6.85 us  [exchange(): lax.ppermute(rolled[:, shift:shift + 1], axis, [(i, (i + shift) % count)...]
    ppermute x0 -> x7, waiting for transfers between devices: none -> 5.71 us  [exchange(): lax.ppermute(rolled[:, shift:shift + 1], axis, [(i, (i + shift) % count)...]
    pallas_call x1 -> x2, Pallas kernels: 6.56 us -> 8.36 us  [forward_pick(): pl.pallas_call(kernel, grid=(steps,), in_specs=[field, halo, halo, field,...]
    unnamed x33 -> x26, local copies, waits for them, and re-layouts: 1.63 us -> 2.92 us
    ppermute x2 -> x3, starting transfers between devices: 4.52 us -> 5.52 us  [halos(): lax.ppermute(lax.slice_in_dim(block, 0, width, axis=dim), axis, backward)]
    slice x2 -> x3, local copies, waits for them, and re-layouts: 1.66 us -> 2.59 us  [halos(): lax.slice_in_dim(block, 0, width, axis=dim)]
    ppermute x2 -> x3, waiting for transfers between devices: 0.01 us -> 0.82 us  [halos(): lax.ppermute(lax.slice_in_dim(block, block.shape[dim] - width, None, axis...]
  transfers between devices with their start and end apart: 9 -> 18, of which waited for: 4 -> 10; matrix products, arithmetic and copies ran while one was open for 4% -> 8% of each run, Pallas kernels for 22% -> 13%
where the time goes in v11:
time: 63.9 us; the launch traced here: 63.3 us
  starting transfers between devices  20.1 us (31%)
  Pallas kernels  19.3 us (30%)
  waiting for transfers between devices  13 us (20%)
  local copies, waits for them, and re-layouts  6.18 us (10%)
  other arithmetic  4.58 us (7%)
    pallas_call x2, Pallas kernels, forward_pick(): pl.pallas_call(kernel, grid=(steps,), in_specs=[field, halo, halo, field,...  8.36 us
    ppermute x7, starting transfers between devices, exchange(): lax.ppermute(rolled[:, shift:shift + 1], axis, [(i, (i + shift) % count)...  6.85 us
    pallas_call x1, Pallas kernels, backward_grad(): pl.pallas_call(kernel, grid=(levels, members // chunk), in_specs=[field,...  6.37 us
    ppermute x7, waiting for transfers between devices, exchange(): lax.ppermute(rolled[:, shift:shift + 1], axis, [(i, (i + shift) % count)...  5.71 us
    ppermute x3, starting transfers between devices, halos(): lax.ppermute(lax.slice_in_dim(block, 0, width, axis=dim), axis, backward)  5.52 us
    ppermute x3, starting transfers between devices, gather_over(): lax.ppermute(values, axis, [(i, (i + shift) % count) for i in range(count)])  4.62 us
    ppermute x3, waiting for transfers between devices, gather_over(): lax.ppermute(values, axis, [(i, (i + shift) % count) for i in range(count)])  4.44 us
    unnamed x26, local copies, waits for them, and re-layouts  2.92 us
  transfers between devices with their start and end apart: 18, of which 10 were waited for; matrix products, arithmetic and copies ran while one was open for 8% of the time, Pallas kernels for 13%

profile of v11, /device:TPU:0, one launch (start us, length us, event | category | flops | bytes accessed | tf_op | source)
XLA Modules:
  0.0 63.3 jit_solution(3499941389899517801)
XLA Ops:
  0.0 1.2 %fusion.8 = (bf16[10,1,16,720]{3,2,1,0:T(8,128)(2,1)S(1)}, bf16[10,1,16,720]{3,2,1,0:T(8,128)(2,1)S(1)}) fusion(bf16[20,1,45,720]{3,2,1,0:T(8,128)(2,1)} %ctrl_ref.1), kind=kLoop, calls=%fused_computation.15 | loop fusion | bytes 921600 | tf_op jit(solution)/shard_map/slice | solution.py:18
  1.2 3.4 %collective-permute-start.1 = (bf16[10,1,16,720]{3,2,1,0:T(8,128)(2,1)S(1)}, bf16[10,1,16,720]{3,2,1,0:T(8,128)(2,1)S(1)}, u32[]{:S(2)}, u32[]{:S(2)}) collective-permute-start(bf16[10,1,16,720]{3,2,1,0:T(8,128)(2,1)S(1)} %get-tuple-element.39), channel_id=1, source_target_pairs={{4,0},{8,4},{12,8},{16,12},{20,16},{24,20},{28,24},{0,28},{5,1},{9... | collective-permute-start | bytes 691208 | tf_op jit(solution)/shard_map/ppermute | solution.py:18
  4.6 0.0 collective-permute-start
  4.6 1.2 %convert_element_type.9.lon_ref = f32[17]{0:T(128)} convert(bf16[17]{0:T(256)(128)(2,1)} %param.10) | non-fusion elementwise | flops 17 | bytes 102 | tf_op jit(solution)/shard_map/convert_element_type | solution.py:97
  5.8 1.2 %convert_element_type.10.lat_ref = f32[17]{0:T(128)} convert(bf16[17]{0:T(256)(128)(2,1)} %param.11) | non-fusion elementwise | flops 17 | bytes 102 | tf_op jit(solution)/shard_map/convert_element_type | solution.py:97
  7.0 0.7 %convert_element_type.11 = f32[1,8,256]{2,1,0:T(8,128)S(1)} convert(s32[1,8,256]{2,1,0:T(8,128)} %param.14) | non-fusion elementwise | flops 2048 | bytes 16384 | tf_op jit(solution)/shard_map/convert_element_type | solution.py:338
  7.7 1.9 %shard_map.85 = (bf16[48,80]{1,0:T(8,128)(2,1)}, bf16[720,720]{1,0:T(8,128)(2,1)}) custom-call(f32[17]{0:T(128)} %convert_element_type.9.lon_ref, f32[17]{0:T(128)} %convert_element_type.10.lat_ref), custom_call_target="tpu_custom_call" | custom-call | tf_op jit(solution)/shard_map/pallas_call | solution.py:90
  9.7 0.8 %fusion.5 = f32[1,8,256]{2,1,0:T(8,128)S(1)} fusion(f32[1,8,256]{2,1,0:T(8,128)} %param.13, s32[8]{0:T(128)} %bitcast.8), kind=kLoop, calls=%fused_computation.12 | loop fusion | flops 4096 | bytes 16416 | tf_op jit(solution)/shard_map/jit(_where)/select_n | solution.py:337
  10.4 0.7 %fusion.2 = f32[3,8,256]{2,1,0:T(8,128)S(1)} fusion(s32[]{:T(128)S(6)} %select_n.19, f32[1,8,256]{2,1,0:T(8,128)} %param.12, f32[1,8,256]{2,1,0:T(8,128)S(1)} %fusion.5, f32[1,8,256]{2,1,0:T(8,128)S(1)} %convert_element_type.11), kind=kLoop, calls=%fused_computation.8 | loop fusion | flops 30720 | bytes 49156 | tf_op jit(solution)/shard_map/jit(_roll_dynamic)/concatenate | solution.py:24
  11.2 0.8 %collective-permute-done.refs_1_ = bf16[10,1,16,720]{3,2,1,0:T(8,128)(2,1)S(1)} collective-permute-done((bf16[10,1,16,720]{3,2,1,0:T(8,128)(2,1)S(1)}, bf16[10,1,16,720]{3,2,1,0:T(8,128)(2,1)S(1)}, u32[]{:S(2)}, u32[]{:S(2)}) %collective-permute-start) | collective-permute-done | bytes 230432 | tf_op jit(solution)/shard_map/ppermute | solution.py:15
  12.0 1.3 %fusion.7 = (bf16[10,1,16,720]{3,2,1,0:T(8,128)(2,1)S(1)}, bf16[10,1,16,720]{3,2,1,0:T(8,128)(2,1)S(1)}) fusion(bf16[20,1,45,720]{3,2,1,0:T(8,128)(2,1)} %ctrl_ref.1), kind=kLoop, calls=%fused_computation.14 | loop fusion | bytes 921600 | tf_op jit(solution)/shard_map/slice | solution.py:18
  13.2 2.1 %collective-permute-start.3 = (bf16[10,1,16,720]{3,2,1,0:T(8,128)(2,1)S(1)}, bf16[10,1,16,720]{3,2,1,0:T(8,128)(2,1)S(1)}, u32[]{:S(2)}, u32[]{:S(2)}) collective-permute-start(bf16[10,1,16,720]{3,2,1,0:T(8,128)(2,1)S(1)} %get-tuple-element.37), channel_id=1, source_target_pairs={{4,0},{8,4},{12,8},{16,12},{20,16},{24,20},{28,24},{0,28},{5,1},{9... | collective-permute-start | bytes 691208 | tf_op jit(solution)/shard_map/ppermute | solution.py:18
  15.3 0.0 collective-permute-start.2
  15.3 2.7 %collective-permute-start.10 = (f32[3,1,256]{2,1,0:T(1,128)S(1)}, f32[3,1,256]{2,1,0:T(1,128)S(1)}, u32[]{:S(2)}, u32[]{:S(2)}) collective-permute-start(f32[3,1,256]{2,1,0:T(1,128)S(1)} %get-tuple-element.41), channel_id=1, source_target_pairs={{0,28},{4,0},{8,4},{12,8},{16,12},{20,16},{24,20},{28,24},{1,29},{... | collective-permute-start | bytes 9224 | tf_op jit(solution)/shard_map/ppermute | solution.py:28
  18.0 0.0 collective-permute-start.9
  18.0 0.3 collective-permute-start.8
  18.3 1.6 %collective-permute-done.10 = f32[3,1,256]{2,1,0:T(1,128)S(1)} collective-permute-done((f32[3,1,256]{2,1,0:T(1,128)S(1)}, f32[3,1,256]{2,1,0:T(1,128)S(1)}, u32[]{:S(2)}, u32[]{:S(2)}) %collective-permute-start.10) | collective-permute-done | bytes 3104 | tf_op jit(solution)/shard_map/ppermute | solution.py:28
  19.9 1.5 %collective-permute-start.7 = (f32[3,1,256]{2,1,0:T(1,128)S(1)}, f32[3,1,256]{2,1,0:T(1,128)S(1)}, u32[]{:S(2)}, u32[]{:S(2)}) collective-permute-start(f32[3,1,256]{2,1,0:T(1,128)S(1)} %get-tuple-element.44), channel_id=1, source_target_pairs={{0,16},{4,20},{8,24},{12,28},{16,0},{20,4},{24,8},{28,12},{1,17},{... | collective-permute-start | bytes 9224 | tf_op jit(solution)/shard_map/ppermute | solution.py:28
  21.4 0.2 collective-permute-done.9
  21.6 1.4 %collective-permute-start.6 = (f32[3,1,256]{2,1,0:T(1,128)S(1)}, f32[3,1,256]{2,1,0:T(1,128)S(1)}, u32[]{:S(2)}, u32[]{:S(2)}) collective-permute-start(f32[3,1,256]{2,1,0:T(1,128)S(1)} %get-tuple-element.45), channel_id=1, source_target_pairs={{0,12},{4,16},{8,20},{12,24},{16,28},{20,0},{24,4},{28,8},{1,13},{... | collective-permute-start | bytes 9224 | tf_op jit(solution)/shard_map/ppermute | solution.py:28
  23.0 0.9 %collective-permute-start.5 = (f32[3,1,256]{2,1,0:T(1,128)S(1)}, f32[3,1,256]{2,1,0:T(1,128)S(1)}, u32[]{:S(2)}, u32[]{:S(2)}) collective-permute-start(f32[3,1,256]{2,1,0:T(1,128)S(1)} %get-tuple-element.46), channel_id=1, source_target_pairs={{0,8},{4,12},{8,16},{12,20},{16,24},{20,28},{24,0},{28,4},{1,9},{5... | collective-permute-start | bytes 9224 | tf_op jit(solution)/shard_map/ppermute | solution.py:28
  24.0 0.0 collective-permute-done.7
  24.0 0.7 %collective-permute-done.6 = f32[3,1,256]{2,1,0:T(1,128)S(1)} collective-permute-done((f32[3,1,256]{2,1,0:T(1,128)S(1)}, f32[3,1,256]{2,1,0:T(1,128)S(1)}, u32[]{:S(2)}, u32[]{:S(2)}) %collective-permute-start.6) | collective-permute-done | bytes 3104 | tf_op jit(solution)/shard_map/ppermute | solution.py:28
  24.6 2.9 %collective-permute-done.5 = f32[3,1,256]{2,1,0:T(1,128)S(1)} collective-permute-done((f32[3,1,256]{2,1,0:T(1,128)S(1)}, f32[3,1,256]{2,1,0:T(1,128)S(1)}, u32[]{:S(2)}, u32[]{:S(2)}) %collective-permute-start.5) | collective-permute-done | bytes 3104 | tf_op jit(solution)/shard_map/ppermute | solution.py:28
  27.5 0.4 collective-permute-done.4
  27.9 0.7 %concatenate.12.refs_7_.refs_4_ = f32[3,8,256]{2,1,0:T(8,128)} concatenate(f32[3,1,256]{2,1,0:T(1,128)S(1)} %get-tuple-element.48, f32[3,1,256]{2,1,0:T(1,128)S(1)} %collective-permute-done.4, f32[3,1,256]{2,1,0:T(1,128)S(1)} %collective-permute-done.5, f32[3,1,256]{2,1,0:T(1,128)S(1)} %collective-permute-done.6, f32[3,1,256]{2,1,0:T(1,128)S(1)} %collective-permute-done.7, ...), dimensions={1} | concatenate | bytes 49152 | tf_op jit(solution)/shard_map/concatenate | solution.py:32
  28.5 3.7 %shard_map.86.refs_6_ = f32[48,720]{1,0:T(8,128)} custom-call(bf16[20,1,45,720]{3,2,1,0:T(8,128)(2,1)} %ctrl_ref.1, bf16[10,1,16,720]{3,2,1,0:T(8,128)(2,1)} %copy-done.4, bf16[10,1,16,720]{3,2,1,0:T(8,128)(2,1)} %copy-done.3, bf16[20,1,45,720]{3,2,1,0:T(8,128)(2,1)} %pert_ref.1, bf16[48,80]{1,0:T(8,128)(2,1)} %get-tuple-element.25.refs_4_.blon_ref, ...), custom_call_target="tpu_custom_call" | custom-call | tf_op jit(solution)/shard_map/pallas_call | solution.py:204
  32.2 0.7 %copy-done.5 = bf16[10,1,16,720]{3,2,1,0:T(8,128)(2,1)} copy-done((bf16[10,1,16,720]{3,2,1,0:T(8,128)(2,1)}, bf16[10,1,16,720]{3,2,1,0:T(8,128)(2,1)S(1)}, u32[]{:S(2)}) %copy-start.5) | copy-done | bytes 230424
  32.9 0.7 %copy-done.6 = bf16[10,1,16,720]{3,2,1,0:T(8,128)(2,1)} copy-done((bf16[10,1,16,720]{3,2,1,0:T(8,128)(2,1)}, bf16[10,1,16,720]{3,2,1,0:T(8,128)(2,1)S(1)}, u32[]{:S(2)}) %copy-start.6) | copy-done | bytes 230424
  33.6 4.7 %shard_map.87.refs_0_ = f32[8,256]{1,0:T(8,128)} custom-call(bf16[20,1,45,720]{3,2,1,0:T(8,128)(2,1)} %ctrl_ref.1, bf16[10,1,16,720]{3,2,1,0:T(8,128)(2,1)} %copy-done.6, bf16[10,1,16,720]{3,2,1,0:T(8,128)(2,1)} %copy-done.5, bf16[20,1,45,720]{3,2,1,0:T(8,128)(2,1)} %pert_ref.1, bf16[48,80]{1,0:T(8,128)(2,1)} %get-tuple-element.25.refs_4_.blon_ref, ...), custom_call_target="tpu_custom_call" | custom-call | tf_op jit(solution)/shard_map/pallas_call | solution.py:204
  38.3 0.1 fusion.6
  38.4 0.1 collective-permute-start.12
  38.5 0.5 collective-permute-start.11
  39.0 3.6 %collective-permute-start.15 = (f32[8,256]{1,0:T(8,128)S(1)}, f32[8,256]{1,0:T(8,128)S(1)}, u32[]{:S(2)}, u32[]{:S(2)}) collective-permute-start(f32[8,256]{1,0:T(8,128)S(1)} %copy-done.9), channel_id=1, source_target_pairs={{0,3},{1,0},{2,1},{3,2},{4,7},{5,4},{6,5},{7,6},{8,11},{9,8},{10,9... | collective-permute-start | bytes 24584 | tf_op jit(solution)/shard_map/ppermute | solution.py:38
  42.6 1.0 %collective-permute-start.13 = (f32[8,256]{1,0:T(8,128)S(1)}, f32[8,256]{1,0:T(8,128)S(1)}, u32[]{:S(2)}, u32[]{:S(2)}) collective-permute-start(f32[8,256]{1,0:T(8,128)S(1)} %copy-done.9), channel_id=1, source_target_pairs={{0,1},{1,2},{2,3},{3,0},{4,5},{5,6},{6,7},{7,4},{8,9},{9,10},{10,1... | collective-permute-start | bytes 24584 | tf_op jit(solution)/shard_map/ppermute | solution.py:38
  43.6 0.4 collective-permute-done.15.refs_3_
  44.0 3.2 %collective-permute-done.14.refs_2_ = f32[8,256]{1,0:T(8,128)S(1)} collective-permute-done((f32[8,256]{1,0:T(8,128)S(1)}, f32[8,256]{1,0:T(8,128)S(1)}, u32[]{:S(2)}, u32[]{:S(2)}) %collective-permute-start.14) | collective-permute-done | bytes 8224 | tf_op jit(solution)/shard_map/ppermute | solution.py:38
  47.2 0.9 %collective-permute-done.13.refs_1_ = f32[8,256]{1,0:T(8,128)S(1)} collective-permute-done((f32[8,256]{1,0:T(8,128)S(1)}, f32[8,256]{1,0:T(8,128)S(1)}, u32[]{:S(2)}, u32[]{:S(2)}) %collective-permute-start.13) | collective-permute-done | bytes 8224 | tf_op jit(solution)/shard_map/ppermute | solution.py:38
  48.1 0.6 copy-done.12
  48.7 2.6 %shard_map.88 = (f32[45,720]{1,0:T(8,128)}, f32[16,720]{1,0:T(8,128)}, f32[16,720]{1,0:T(8,128)}) custom-call(f32[8,256]{1,0:T(8,128)} %shard_map.87.refs_0_, f32[8,256]{1,0:T(8,128)} %copy-done.12, f32[8,256]{1,0:T(8,128)} %copy-done.11, f32[8,256]{1,0:T(8,128)} %copy-done.10, f32[3,8,256]{2,1,0:T(8,128)} %concatenate.12.refs_7_.refs_4_), custom_call_target="tpu_custom_call" | custom-call | tf_op jit(solution)/shard_map/pallas_call | solution.py:261
  51.3 2.6 %collective-permute-start.17 = (f32[16,720]{1,0:T(8,128)}, f32[16,720]{1,0:T(8,128)S(1)}, u32[]{:S(2)}, u32[]{:S(2)}) collective-permute-start(f32[16,720]{1,0:T(8,128)} %get-tuple-element.34), channel_id=1, source_target_pairs={{4,0},{8,4},{12,8},{16,12},{20,16},{24,20},{28,24},{0,28},{5,1},{9... | collective-permute-start | bytes 138248 | tf_op jit(solution)/shard_map/ppermute | solution.py:363
  53.9 2.0 %collective-permute-done.16 = f32[16,720]{1,0:T(8,128)S(1)} collective-permute-done((f32[16,720]{1,0:T(8,128)}, f32[16,720]{1,0:T(8,128)S(1)}, u32[]{:S(2)}, u32[]{:S(2)}) %collective-permute-start.16) | collective-permute-done | bytes 46112 | tf_op jit(solution)/shard_map/ppermute | solution.py:362
  56.0 0.0 collective-permute-done.17
  56.0 0.5 copy-done.7
  56.6 0.0 copy-done.8
  56.6 0.2 copy-done.1
  56.8 0.2 copy-done.2
  57.0 6.4 %shard_map.89 = f32[20,45,1,720]{3,2,1,0:T(1,128)} custom-call(bf16[20,1,45,720]{3,2,1,0:T(8,128)(2,1)} %pert_ref.1, bf16[20,1,16,720]{3,2,1,0:T(8,128)(2,1)} %copy-done.2, bf16[20,1,16,720]{3,2,1,0:T(8,128)(2,1)} %copy-done.1, f32[1,45,720]{2,1,0:T(8,128)} %bitcast.5, f32[1,16,720]{2,1,0:T(8,128)} %bitcast.6, f32[1,16,720]{2,1,0:T(8,128)} %bitcast.7, ...), custom_call_target="tpu_custom_call" | custom-call | tf_op jit(solution)/shard_map/pallas_call | solution.py:305
  (29 shorter events, 0.1 us)
Async XLA Ops:
  1.2 10.0 %collective-permute-start.1 = (bf16[10,1,16,720]{3,2,1,0:T(8,128)(2,1)S(1)}, bf16[10,1,16,720]{3,2,1,0:T(8,128)(2,1)S(1)}, u32[]{:S(2)}, u32[]{:S(2)}) collective-permute-start(bf16[10,1,16,720]{3,2,1,0:T(8,128)(2,1)S(1)} %get-tuple-element.39), channel_id=1, source_target_pairs={{4,0},{8,4},{12,8},{16,12},{20,16},{24,20},{28,24},{0,28},{5,1},{9... | collective-permute-start | bytes 691208 | tf_op jit(solution)/shard_map/ppermute | solution.py:18
  4.6 7.4 %collective-permute-start = (bf16[10,1,16,720]{3,2,1,0:T(8,128)(2,1)S(1)}, bf16[10,1,16,720]{3,2,1,0:T(8,128)(2,1)S(1)}, u32[]{:S(2)}, u32[]{:S(2)}) collective-permute-start(bf16[10,1,16,720]{3,2,1,0:T(8,128)(2,1)S(1)} %get-tuple-element.40), channel_id=1, source_target_pairs={{0,4},{4,8},{8,12},{12,16},{16,20},{20,24},{24,28},{28,0},{1,5},{5... | collective-permute-start | bytes 691208 | tf_op jit(solution)/shard_map/ppermute | solution.py:15
  11.2 17.4 %copy-start.3 = (bf16[10,1,16,720]{3,2,1,0:T(8,128)(2,1)}, bf16[10,1,16,720]{3,2,1,0:T(8,128)(2,1)S(1)}, u32[]{:S(2)}) copy-start(bf16[10,1,16,720]{3,2,1,0:T(8,128)(2,1)S(1)} %collective-permute-done.1.refs_2_) | copy-start | bytes 691204
  12.0 16.6 %copy-start.4 = (bf16[10,1,16,720]{3,2,1,0:T(8,128)(2,1)}, bf16[10,1,16,720]{3,2,1,0:T(8,128)(2,1)S(1)}, u32[]{:S(2)}) copy-start(bf16[10,1,16,720]{3,2,1,0:T(8,128)(2,1)S(1)} %collective-permute-done.refs_1_) | copy-start | bytes 691204
  13.2 19.0 %collective-permute-start.3 = (bf16[10,1,16,720]{3,2,1,0:T(8,128)(2,1)S(1)}, bf16[10,1,16,720]{3,2,1,0:T(8,128)(2,1)S(1)}, u32[]{:S(2)}, u32[]{:S(2)}) collective-permute-start(bf16[10,1,16,720]{3,2,1,0:T(8,128)(2,1)S(1)} %get-tuple-element.37), channel_id=1, source_target_pairs={{4,0},{8,4},{12,8},{16,12},{20,16},{24,20},{28,24},{0,28},{5,1},{9... | collective-permute-start | bytes 691208 | tf_op jit(solution)/shard_map/ppermute | solution.py:18
  15.3 16.9 %collective-permute-start.2 = (bf16[10,1,16,720]{3,2,1,0:T(8,128)(2,1)S(1)}, bf16[10,1,16,720]{3,2,1,0:T(8,128)(2,1)S(1)}, u32[]{:S(2)}, u32[]{:S(2)}) collective-permute-start(bf16[10,1,16,720]{3,2,1,0:T(8,128)(2,1)S(1)} %get-tuple-element.38), channel_id=1, source_target_pairs={{0,4},{4,8},{8,12},{12,16},{16,20},{20,24},{24,28},{28,0},{1,5},{5... | collective-permute-start | bytes 691208 | tf_op jit(solution)/shard_map/ppermute | solution.py:15
  15.3 4.6 %collective-permute-start.10 = (f32[3,1,256]{2,1,0:T(1,128)S(1)}, f32[3,1,256]{2,1,0:T(1,128)S(1)}, u32[]{:S(2)}, u32[]{:S(2)}) collective-permute-start(f32[3,1,256]{2,1,0:T(1,128)S(1)} %get-tuple-element.41), channel_id=1, source_target_pairs={{0,28},{4,0},{8,4},{12,8},{16,12},{20,16},{24,20},{28,24},{1,29},{... | collective-permute-start | bytes 9224 | tf_op jit(solution)/shard_map/ppermute | solution.py:28
  18.0 3.6 %collective-permute-start.9 = (f32[3,1,256]{2,1,0:T(1,128)S(1)}, f32[3,1,256]{2,1,0:T(1,128)S(1)}, u32[]{:S(2)}, u32[]{:S(2)}) collective-permute-start(f32[3,1,256]{2,1,0:T(1,128)S(1)} %get-tuple-element.42), channel_id=1, source_target_pairs={{0,24},{4,28},{8,0},{12,4},{16,8},{20,12},{24,16},{28,20},{1,25},{... | collective-permute-start | bytes 9224 | tf_op jit(solution)/shard_map/ppermute | solution.py:28
  18.0 5.0 %collective-permute-start.8 = (f32[3,1,256]{2,1,0:T(1,128)S(1)}, f32[3,1,256]{2,1,0:T(1,128)S(1)}, u32[]{:S(2)}, u32[]{:S(2)}) collective-permute-start(f32[3,1,256]{2,1,0:T(1,128)S(1)} %get-tuple-element.43), channel_id=1, source_target_pairs={{0,20},{4,24},{8,28},{12,0},{16,4},{20,8},{24,12},{28,16},{1,21},{... | collective-permute-start | bytes 9224 | tf_op jit(solution)/shard_map/ppermute | solution.py:28
  19.9 4.1 %collective-permute-start.7 = (f32[3,1,256]{2,1,0:T(1,128)S(1)}, f32[3,1,256]{2,1,0:T(1,128)S(1)}, u32[]{:S(2)}, u32[]{:S(2)}) collective-permute-start(f32[3,1,256]{2,1,0:T(1,128)S(1)} %get-tuple-element.44), channel_id=1, source_target_pairs={{0,16},{4,20},{8,24},{12,28},{16,0},{20,4},{24,8},{28,12},{1,17},{... | collective-permute-start | bytes 9224 | tf_op jit(solution)/shard_map/ppermute | solution.py:28
  21.6 3.0 %collective-permute-start.6 = (f32[3,1,256]{2,1,0:T(1,128)S(1)}, f32[3,1,256]{2,1,0:T(1,128)S(1)}, u32[]{:S(2)}, u32[]{:S(2)}) collective-permute-start(f32[3,1,256]{2,1,0:T(1,128)S(1)} %get-tuple-element.45), channel_id=1, source_target_pairs={{0,12},{4,16},{8,20},{12,24},{16,28},{20,0},{24,4},{28,8},{1,13},{... | collective-permute-start | bytes 9224 | tf_op jit(solution)/shard_map/ppermute | solution.py:28
  23.0 4.5 %collective-permute-start.5 = (f32[3,1,256]{2,1,0:T(1,128)S(1)}, f32[3,1,256]{2,1,0:T(1,128)S(1)}, u32[]{:S(2)}, u32[]{:S(2)}) collective-permute-start(f32[3,1,256]{2,1,0:T(1,128)S(1)} %get-tuple-element.46), channel_id=1, source_target_pairs={{0,8},{4,12},{8,16},{12,20},{16,24},{20,28},{24,0},{28,4},{1,9},{5... | collective-permute-start | bytes 9224 | tf_op jit(solution)/shard_map/ppermute | solution.py:28
  24.0 3.9 %collective-permute-start.4 = (f32[3,1,256]{2,1,0:T(1,128)S(1)}, f32[3,1,256]{2,1,0:T(1,128)S(1)}, u32[]{:S(2)}, u32[]{:S(2)}) collective-permute-start(f32[3,1,256]{2,1,0:T(1,128)S(1)} %get-tuple-element.47), channel_id=1, source_target_pairs={{0,4},{4,8},{8,12},{12,16},{16,20},{20,24},{24,28},{28,0},{1,5},{5... | collective-permute-start | bytes 9224 | tf_op jit(solution)/shard_map/ppermute | solution.py:28
  32.2 6.1 %copy-start = (bf16[20,1,45,720]{3,2,1,0:T(8,128)(2,1)S(1)}, bf16[20,1,45,720]{3,2,1,0:T(8,128)(2,1)}, u32[]{:S(2)}) copy-start(bf16[20,1,45,720]{3,2,1,0:T(8,128)(2,1)} %pert_ref.1) | copy-start | bytes 3888004
  32.2 0.7 %copy-start.5 = (bf16[10,1,16,720]{3,2,1,0:T(8,128)(2,1)}, bf16[10,1,16,720]{3,2,1,0:T(8,128)(2,1)S(1)}, u32[]{:S(2)}) copy-start(bf16[10,1,16,720]{3,2,1,0:T(8,128)(2,1)S(1)} %collective-permute-done.3.refs_2_) | copy-start | bytes 691204
  32.9 0.7 %copy-start.6 = (bf16[10,1,16,720]{3,2,1,0:T(8,128)(2,1)}, bf16[10,1,16,720]{3,2,1,0:T(8,128)(2,1)S(1)}, u32[]{:S(2)}) copy-start(bf16[10,1,16,720]{3,2,1,0:T(8,128)(2,1)S(1)} %collective-permute-done.2.refs_1_) | copy-start | bytes 691204
  38.3 0.7 %copy-start.9 = (f32[8,256]{1,0:T(8,128)S(1)}, f32[8,256]{1,0:T(8,128)}, u32[]{:S(2)}) copy-start(f32[8,256]{1,0:T(8,128)} %shard_map.87.refs_0_) | copy-start | bytes 24580
  38.4 17.6 %collective-permute-start.12 = (bf16[20,1,16,720]{3,2,1,0:T(8,128)(2,1)S(1)}, bf16[20,1,16,720]{3,2,1,0:T(8,128)(2,1)S(1)}, u32[]{:S(2)}, u32[]{:S(2)}) collective-permute-start(bf16[20,1,16,720]{3,2,1,0:T(8,128)(2,1)S(1)} %get-tuple-element.35), channel_id=1, source_target_pairs={{4,0},{8,4},{12,8},{16,12},{20,16},{24,20},{28,24},{0,28},{5,1},{9... | collective-permute-start | bytes 1382408 | tf_op jit(solution)/shard_map/ppermute | solution.py:18
  38.5 17.5 %collective-permute-start.11 = (bf16[20,1,16,720]{3,2,1,0:T(8,128)(2,1)S(1)}, bf16[20,1,16,720]{3,2,1,0:T(8,128)(2,1)S(1)}, u32[]{:S(2)}, u32[]{:S(2)}) collective-permute-start(bf16[20,1,16,720]{3,2,1,0:T(8,128)(2,1)S(1)} %get-tuple-element.36), channel_id=1, source_target_pairs={{0,4},{4,8},{8,12},{12,16},{16,20},{20,24},{24,28},{28,0},{1,5},{5... | collective-permute-start | bytes 1382408 | tf_op jit(solution)/shard_map/ppermute | solution.py:15
  39.0 5.0 %collective-permute-start.15 = (f32[8,256]{1,0:T(8,128)S(1)}, f32[8,256]{1,0:T(8,128)S(1)}, u32[]{:S(2)}, u32[]{:S(2)}) collective-permute-start(f32[8,256]{1,0:T(8,128)S(1)} %copy-done.9), channel_id=1, source_target_pairs={{0,3},{1,0},{2,1},{3,2},{4,7},{5,4},{6,5},{7,6},{8,11},{9,8},{10,9... | collective-permute-start | bytes 24584 | tf_op jit(solution)/shard_map/ppermute | solution.py:38
  42.6 4.5 %collective-permute-start.14 = (f32[8,256]{1,0:T(8,128)S(1)}, f32[8,256]{1,0:T(8,128)S(1)}, u32[]{:S(2)}, u32[]{:S(2)}) collective-permute-start(f32[8,256]{1,0:T(8,128)S(1)} %copy-done.9), channel_id=1, source_target_pairs={{0,2},{1,3},{2,0},{3,1},{4,6},{5,7},{6,4},{7,5},{8,10},{9,11},{10,... | collective-permute-start | bytes 24584 | tf_op jit(solution)/shard_map/ppermute | solution.py:38
  42.6 5.4 %collective-permute-start.13 = (f32[8,256]{1,0:T(8,128)S(1)}, f32[8,256]{1,0:T(8,128)S(1)}, u32[]{:S(2)}, u32[]{:S(2)}) collective-permute-start(f32[8,256]{1,0:T(8,128)S(1)} %copy-done.9), channel_id=1, source_target_pairs={{0,1},{1,2},{2,3},{3,0},{4,5},{5,6},{6,7},{7,4},{8,9},{9,10},{10,1... | collective-permute-start | bytes 24584 | tf_op jit(solution)/shard_map/ppermute | solution.py:38
  44.0 4.1 %copy-start.10 = (f32[8,256]{1,0:T(8,128)}, f32[8,256]{1,0:T(8,128)S(1)}, u32[]{:S(2)}) copy-start(f32[8,256]{1,0:T(8,128)S(1)} %collective-permute-done.15.refs_3_) | copy-start | bytes 24580
  47.2 0.9 %copy-start.11 = (f32[8,256]{1,0:T(8,128)}, f32[8,256]{1,0:T(8,128)S(1)}, u32[]{:S(2)}) copy-start(f32[8,256]{1,0:T(8,128)S(1)} %collective-permute-done.14.refs_2_) | copy-start | bytes 24580
  48.1 0.6 copy-start.12
  51.3 4.7 %collective-permute-start.16 = (f32[16,720]{1,0:T(8,128)}, f32[16,720]{1,0:T(8,128)S(1)}, u32[]{:S(2)}, u32[]{:S(2)}) collective-permute-start(f32[16,720]{1,0:T(8,128)} %get-tuple-element.33), channel_id=1, source_target_pairs={{0,4},{4,8},{8,12},{12,16},{16,20},{20,24},{24,28},{28,0},{1,5},{5... | collective-permute-start | bytes 138248 | tf_op jit(solution)/shard_map/ppermute | solution.py:362
  51.3 4.7 %collective-permute-start.17 = (f32[16,720]{1,0:T(8,128)}, f32[16,720]{1,0:T(8,128)S(1)}, u32[]{:S(2)}, u32[]{:S(2)}) collective-permute-start(f32[16,720]{1,0:T(8,128)} %get-tuple-element.34), channel_id=1, source_target_pairs={{4,0},{8,4},{12,8},{16,12},{20,16},{24,20},{28,24},{0,28},{5,1},{9... | collective-permute-start | bytes 138248 | tf_op jit(solution)/shard_map/ppermute | solution.py:363
  56.0 0.6 copy-start.7
  56.0 0.6 copy-start.8
  56.0 0.8 %copy-start.1 = (bf16[20,1,16,720]{3,2,1,0:T(8,128)(2,1)}, bf16[20,1,16,720]{3,2,1,0:T(8,128)(2,1)S(1)}, u32[]{:S(2)}) copy-start(bf16[20,1,16,720]{3,2,1,0:T(8,128)(2,1)S(1)} %collective-permute-done.12.phigh_ref) | copy-start | bytes 1382404
  56.0 0.9 %copy-start.2 = (bf16[20,1,16,720]{3,2,1,0:T(8,128)(2,1)}, bf16[20,1,16,720]{3,2,1,0:T(8,128)(2,1)S(1)}, u32[]{:S(2)}) copy-start(bf16[20,1,16,720]{3,2,1,0:T(8,128)(2,1)S(1)} %collective-permute-done.11.plow_ref) | copy-start | bytes 1382404

commit v12 on v10

--- a/solution.py
+++ b/solution.py
@@ -21,10 +21,17 @@
 
 def gather_over(values, axis):
     count = lax.axis_size(axis)
-    return [values] + [
-        lax.ppermute(values, axis, [(i, (i + shift) % count) for i in range(count)])
-        for shift in range(1, count)
-    ]
+    if count & (count - 1):
+        return [values] + [
+            lax.ppermute(values, axis, [(i, (i + shift) % count) for i in range(count)])
+            for shift in range(1, count)
+        ]
+    total = values
+    bit = 1
+    while bit < count:
+        total = total + lax.ppermute(total, axis, [(i, i ^ bit) for i in range(count)])
+        bit *= 2
+    return [total]
 
 
 def select_chain(dist, taps_ref):

time: 51.5 us -> 51.4 us (level)
  other arithmetic: 1.2 us -> 2.45 us
  local copies, waits for them, and re-layouts: 3.91 us -> 3.3 us
    add x0 -> x2, other arithmetic: none -> 1.29 us  [gather_over(): total + lax.ppermute(total, axis, [(i, i ^ bit) for i in range(count)])]
    unnamed x33 -> x27, local copies, waits for them, and re-layouts: 1.63 us -> 1.01 us
    ppermute x3 -> x2, starting transfers between devices: 4.61 us -> 4.16 us  [gather_over(): lax.ppermute(total, axis, [(i, i ^ bit) for i in range(count)])]
    ppermute x3 -> x2, waiting for transfers between devices: 4.65 us -> 4.25 us  [gather_over(): lax.ppermute(total, axis, [(i, i ^ bit) for i in range(count)])]
  transfers between devices with their start and end apart: 9 -> 8, of which waited for: 4 -> 3; matrix products, arithmetic and copies ran while one was open for 4% -> 6% of each run, Pallas kernels for 22% -> 22%
where the time goes in v12:
time: 51.4 us; the launch traced here: 50.9 us
  Pallas kernels  17.5 us (34%)
  starting transfers between devices  11.3 us (22%)
  blocking collectives  9.77 us (19%)
  waiting for transfers between devices  6.49 us (13%)
  local copies, waits for them, and re-layouts  3.3 us (6%)
  other arithmetic  2.45 us (5%)
    all_to_all x1, blocking collectives, local(): lax.all_to_all(lists, 'tile', split_axis=1, concat_axis=1, tiled=True)  9.77 us
    pallas_call x1, Pallas kernels, forward_pick(): pl.pallas_call(kernel, grid=(steps,), in_specs=[field, halo, halo, field,...  6.56 us
    pallas_call x1, Pallas kernels, backward_grad(): pl.pallas_call(kernel, grid=(levels, members // chunk), in_specs=[field,...  6.37 us
    ppermute x2, starting transfers between devices, halos(): lax.ppermute(lax.slice_in_dim(block, 0, width, axis=dim), axis, backward)  4.52 us
    ppermute x2, waiting for transfers between devices, gather_over(): lax.ppermute(total, axis, [(i, i ^ bit) for i in range(count)])  4.25 us
    ppermute x2, starting transfers between devices, gather_over(): lax.ppermute(total, axis, [(i, i ^ bit) for i in range(count)])  4.16 us
    ppermute x1, starting transfers between devices, local(): lax.ppermute(high_send, 'tile', [((i + 1) % count, i) for i in range(coun...  2.64 us
    pallas_call x1, Pallas kernels, spread_misfits(): pl.pallas_call(kernel, out_shape=(jax.ShapeDtypeStruct((lon_cells, lat_ce...  2.55 us
  transfers between devices with their start and end apart: 8, of which 3 were waited for; matrix products, arithmetic and copies ran while one was open for 6% of the time, Pallas kernels for 22%

profile of v12, /device:TPU:0, one launch (start us, length us, event | category | flops | bytes accessed | tf_op | source)
XLA Modules:
  0.0 50.9 jit_solution(13740266858068872120)
XLA Ops:
  0.0 0.0 copy-start.11
  0.0 0.0 copy-start.9
  0.0 0.0 copy-start
  0.0 1.5 %fusion.1 = (bf16[20,1,16,720]{3,2,1,0:T(8,128)(2,1)S(1)}, bf16[20,1,16,720]{3,2,1,0:T(8,128)(2,1)S(1)}) fusion(bf16[20,1,45,720]{3,2,1,0:T(8,128)(2,1)} %ctrl_ref.3), kind=kLoop, calls=%fused_computation.3 | loop fusion | bytes 1843200 | tf_op jit(solution)/shard_map/slice | solution.py:18
  1.6 3.4 %collective-permute-start.1 = (bf16[20,1,16,720]{3,2,1,0:T(8,128)(2,1)S(1)}, bf16[20,1,16,720]{3,2,1,0:T(8,128)(2,1)S(1)}, u32[]{:S(2)}, u32[]{:S(2)}) collective-permute-start(bf16[20,1,16,720]{3,2,1,0:T(8,128)(2,1)S(1)} %get-tuple-element.27), channel_id=1, source_target_pairs={{4,0},{8,4},{12,8},{16,12},{20,16},{24,20},{28,24},{0,28},{5,1},{9... | collective-permute-start | bytes 1382408 | tf_op jit(solution)/shard_map/ppermute | solution.py:18
  5.0 0.0 collective-permute-start
  5.0 0.0 copy-done.11
  5.0 0.5 %convert_element_type.10.lon_ref = f32[17]{0:T(128)} convert(bf16[17]{0:T(256)(128)(2,1)S(1)} %copy-done.11) | non-fusion elementwise | flops 17 | bytes 102 | tf_op jit(solution)/shard_map/convert_element_type | solution.py:91
  5.5 0.0 copy-done.12
  5.5 0.5 %convert_element_type.11.lat_ref = f32[17]{0:T(128)} convert(bf16[17]{0:T(256)(128)(2,1)S(1)} %copy-done.12) | non-fusion elementwise | flops 17 | bytes 102 | tf_op jit(solution)/shard_map/convert_element_type | solution.py:91
  6.1 0.0 copy-done.7
  6.1 0.0 copy-done.8
  6.1 2.0 %shard_map.85 = (bf16[48,80]{1,0:T(8,128)(2,1)}, bf16[720,720]{1,0:T(8,128)(2,1)}) custom-call(f32[17]{0:T(128)} %convert_element_type.10.lon_ref, f32[17]{0:T(128)} %convert_element_type.11.lat_ref), custom_call_target="tpu_custom_call" | custom-call | tf_op jit(solution)/shard_map/pallas_call | solution.py:84
  8.1 0.0 copy-done.10
  8.1 0.0 copy-done.9
  8.1 0.1 compare_select_fusion
  8.2 9.8 %all_to_all.5 = f32[3,8,256]{2,0,1:T(4,128)S(1)} all-to-all(f32[3,8,256]{2,0,1:T(4,128)S(1)} %pad_maximum_fusion), channel_id=1, replica_groups=mesh['tile'=8,'mem'=4] {'tile'}, dimensions={1} | all-to-all | bytes 49152 | tf_op jit(solution)/shard_map/all_to_all | solution.py:316
  18.0 0.0 collective-permute-done.1.high_ref
  18.0 0.0 collective-permute-done.low_ref
  18.0 0.0 copy-done
  18.0 0.0 copy-start.4
  18.0 0.1 fusion
  18.2 1.1 %collective-permute-start.3 = (bf16[20,1,16,720]{3,2,1,0:T(8,128)(2,1)S(1)}, bf16[20,1,16,720]{3,2,1,0:T(8,128)(2,1)S(1)}, u32[]{:S(2)}, u32[]{:S(2)}) collective-permute-start(bf16[20,1,16,720]{3,2,1,0:T(8,128)(2,1)S(1)} %get-tuple-element.25), channel_id=1, source_target_pairs={{4,0},{8,4},{12,8},{16,12},{20,16},{24,20},{28,24},{0,28},{5,1},{9... | collective-permute-start | bytes 1382408 | tf_op jit(solution)/shard_map/ppermute | solution.py:18
  19.3 0.0 collective-permute-start.2
  19.3 0.6 %copy.12.cells_ref.refs_1_ = f32[3,8,256]{2,1,0:T(8,128)} copy(f32[3,8,256]{2,0,1:T(4,128)S(1)} %all_to_all.5) | data formatting | bytes 49152 | tf_op jit(solution)/shard_map/optimization_barrier | solution.py:319
  19.9 0.0 copy-done.3
  19.9 0.0 copy-done.4
  19.9 6.6 %shard_map.86 = f32[8,256]{1,0:T(8,128)} custom-call(bf16[20,1,45,720]{3,2,1,0:T(8,128)(2,1)} %ctrl_ref.3, bf16[20,1,16,720]{3,2,1,0:T(8,128)(2,1)} %copy-done.4, bf16[20,1,16,720]{3,2,1,0:T(8,128)(2,1)} %copy-done.3, bf16[20,1,45,720]{3,2,1,0:T(8,128)(2,1)} %pert_ref.3, bf16[48,80]{1,0:T(8,128)(2,1)} %get-tuple-element.15.blon_ref, ...), custom_call_target="tpu_custom_call" | custom-call | tf_op jit(solution)/shard_map/pallas_call | solution.py:179
  26.4 1.6 %collective-permute-start.4 = (f32[8,256]{1,0:T(8,128)}, f32[8,256]{1,0:T(8,128)S(1)}, u32[]{:S(2)}, u32[]{:S(2)}) collective-permute-start(f32[8,256]{1,0:T(8,128)} %shard_map.86), channel_id=1, source_target_pairs={{0,1},{1,0},{2,3},{3,2},{4,5},{5,4},{6,7},{7,6},{8,9},{9,8},{10,11... | collective-permute-start | bytes 24584 | tf_op jit(solution)/shard_map/ppermute | solution.py:32
  28.0 2.3 %collective-permute-done.4 = f32[8,256]{1,0:T(8,128)S(1)} collective-permute-done((f32[8,256]{1,0:T(8,128)}, f32[8,256]{1,0:T(8,128)S(1)}, u32[]{:S(2)}, u32[]{:S(2)}) %collective-permute-start.4) | collective-permute-done | bytes 8224 | tf_op jit(solution)/shard_map/ppermute | solution.py:32
  30.3 0.7 %add.6 = f32[8,256]{1,0:T(8,128)S(1)} add(f32[8,256]{1,0:T(8,128)} %shard_map.86, f32[8,256]{1,0:T(8,128)S(1)} %collective-permute-done.4) | non-fusion elementwise | flops 2048 | bytes 24576 | tf_op jit(solution)/shard_map/add | solution.py:32
  31.0 2.6 %collective-permute-start.5 = (f32[8,256]{1,0:T(8,128)S(1)}, f32[8,256]{1,0:T(8,128)S(1)}, u32[]{:S(2)}, u32[]{:S(2)}) collective-permute-start(f32[8,256]{1,0:T(8,128)S(1)} %add.6), channel_id=1, source_target_pairs={{0,2},{1,3},{2,0},{3,1},{4,6},{5,7},{6,4},{7,5},{8,10},{9,11},{10,... | collective-permute-start | bytes 24584 | tf_op jit(solution)/shard_map/ppermute | solution.py:32
  33.6 2.0 %collective-permute-done.5 = f32[8,256]{1,0:T(8,128)S(1)} collective-permute-done((f32[8,256]{1,0:T(8,128)S(1)}, f32[8,256]{1,0:T(8,128)S(1)}, u32[]{:S(2)}, u32[]{:S(2)}) %collective-permute-start.5) | collective-permute-done | bytes 8224 | tf_op jit(solution)/shard_map/ppermute | solution.py:32
  35.6 0.6 %add.7.refs_0_ = f32[8,256]{1,0:T(8,128)} add(f32[8,256]{1,0:T(8,128)S(1)} %add.6, f32[8,256]{1,0:T(8,128)S(1)} %collective-permute-done.5) | non-fusion elementwise | flops 2048 | bytes 24576 | tf_op jit(solution)/shard_map/add | solution.py:32
  36.1 2.6 %shard_map.87 = (f32[45,720]{1,0:T(8,128)}, f32[16,720]{1,0:T(8,128)}, f32[16,720]{1,0:T(8,128)}) custom-call(f32[8,256]{1,0:T(8,128)} %add.7.refs_0_, f32[3,8,256]{2,1,0:T(8,128)} %copy.12.cells_ref.refs_1_), custom_call_target="tpu_custom_call" | custom-call | tf_op jit(solution)/shard_map/pallas_call | solution.py:237
  38.7 0.0 collective-permute-start.6
  38.7 2.6 %collective-permute-start.7 = (f32[16,720]{1,0:T(8,128)}, f32[16,720]{1,0:T(8,128)S(1)}, u32[]{:S(2)}, u32[]{:S(2)}) collective-permute-start(f32[16,720]{1,0:T(8,128)} %get-tuple-element.24), channel_id=1, source_target_pairs={{4,0},{8,4},{12,8},{16,12},{20,16},{24,20},{28,24},{0,28},{5,1},{9... | collective-permute-start | bytes 138248 | tf_op jit(solution)/shard_map/ppermute | solution.py:331
  41.3 2.2 %collective-permute-done.6 = f32[16,720]{1,0:T(8,128)S(1)} collective-permute-done((f32[16,720]{1,0:T(8,128)}, f32[16,720]{1,0:T(8,128)S(1)}, u32[]{:S(2)}, u32[]{:S(2)}) %collective-permute-start.6) | collective-permute-done | bytes 46112 | tf_op jit(solution)/shard_map/ppermute | solution.py:330
  43.6 0.0 collective-permute-done.7
  43.6 0.0 collective-permute-done.3.phigh_ref
  43.6 0.0 copy-start.1
  43.6 0.0 collective-permute-done.2.plow_ref
  43.6 0.0 copy-start.2
  43.6 0.6 %copy-done.5 = f32[16,720]{1,0:T(8,128)} copy-done((f32[16,720]{1,0:T(8,128)}, f32[16,720]{1,0:T(8,128)S(1)}, u32[]{:S(2)}) %copy-start.5) | copy-done | bytes 46104
  44.2 0.0 copy-done.6
  44.2 0.2 copy-done.1
  44.4 0.2 copy-done.2
  44.6 6.4 %shard_map.88 = f32[20,45,1,720]{3,2,1,0:T(1,128)} custom-call(bf16[20,1,45,720]{3,2,1,0:T(8,128)(2,1)} %pert_ref.3, bf16[20,1,16,720]{3,2,1,0:T(8,128)(2,1)} %copy-done.2, bf16[20,1,16,720]{3,2,1,0:T(8,128)(2,1)} %copy-done.1, f32[1,45,720]{2,1,0:T(8,128)} %bitcast.5, f32[1,16,720]{2,1,0:T(8,128)} %bitcast.6, f32[1,16,720]{2,1,0:T(8,128)} %bitcast.7, ...), custom_call_target="tpu_custom_call" | custom-call | tf_op jit(solution)/shard_map/pallas_call | solution.py:281
  (11 shorter events, 0.1 us)
Async XLA Ops:
  0.0 5.0 %copy-start.11 = (bf16[17]{0:T(256)(128)(2,1)S(1)}, bf16[17]{0:T(256)(128)(2,1)}, u32[]{:S(2)}) copy-start(bf16[17]{0:T(256)(128)(2,1)} %param.10) | copy-start | bytes 106
  0.0 5.5 %copy-start.12 = (bf16[17]{0:T(256)(128)(2,1)S(1)}, bf16[17]{0:T(256)(128)(2,1)}, u32[]{:S(2)}) copy-start(bf16[17]{0:T(256)(128)(2,1)} %param.11) | copy-start | bytes 106
  0.0 6.1 %copy-start.7 = (f32[1,8,256]{2,1,0:T(8,128)S(1)}, f32[1,8,256]{2,1,0:T(8,128)}, u32[]{:S(2)}) copy-start(f32[1,8,256]{2,1,0:T(8,128)} %param.12) | copy-start | bytes 24580
  0.0 6.1 %copy-start.8 = (s32[1,8,256]{2,1,0:T(8,128)S(1)}, s32[1,8,256]{2,1,0:T(8,128)}, u32[]{:S(2)}) copy-start(s32[1,8,256]{2,1,0:T(8,128)} %param.14) | copy-start | bytes 24580
  0.0 8.1 %copy-start.10 = (s32[1,8]{1,0:T(1,128)S(1)}, s32[1,8]{1,0:T(1,128)}, u32[]{:S(2)}) copy-start(s32[1,8]{1,0:T(1,128)} %param.15) | copy-start | bytes 100
  0.0 8.1 %copy-start.9 = (f32[1,8,256]{2,1,0:T(8,128)S(1)}, f32[1,8,256]{2,1,0:T(8,128)}, u32[]{:S(2)}) copy-start(f32[1,8,256]{2,1,0:T(8,128)} %param.13) | copy-start | bytes 24580
  0.0 18.0 %copy-start = (bf16[20,1,45,720]{3,2,1,0:T(8,128)(2,1)S(1)}, bf16[20,1,45,720]{3,2,1,0:T(8,128)(2,1)}, u32[]{:S(2)}) copy-start(bf16[20,1,45,720]{3,2,1,0:T(8,128)(2,1)} %pert_ref.3) | copy-start | bytes 3888004
  1.6 16.4 %collective-permute-start.1 = (bf16[20,1,16,720]{3,2,1,0:T(8,128)(2,1)S(1)}, bf16[20,1,16,720]{3,2,1,0:T(8,128)(2,1)S(1)}, u32[]{:S(2)}, u32[]{:S(2)}) collective-permute-start(bf16[20,1,16,720]{3,2,1,0:T(8,128)(2,1)S(1)} %get-tuple-element.27), channel_id=1, source_target_pairs={{4,0},{8,4},{12,8},{16,12},{20,16},{24,20},{28,24},{0,28},{5,1},{9... | collective-permute-start | bytes 1382408 | tf_op jit(solution)/shard_map/ppermute | solution.py:18
  5.0 13.0 %collective-permute-start = (bf16[20,1,16,720]{3,2,1,0:T(8,128)(2,1)S(1)}, bf16[20,1,16,720]{3,2,1,0:T(8,128)(2,1)S(1)}, u32[]{:S(2)}, u32[]{:S(2)}) collective-permute-start(bf16[20,1,16,720]{3,2,1,0:T(8,128)(2,1)S(1)} %get-tuple-element.28), channel_id=1, source_target_pairs={{0,4},{4,8},{8,12},{12,16},{16,20},{20,24},{24,28},{28,0},{1,5},{5... | collective-permute-start | bytes 1382408 | tf_op jit(solution)/shard_map/ppermute | solution.py:15
  18.0 1.9 %copy-start.3 = (bf16[20,1,16,720]{3,2,1,0:T(8,128)(2,1)}, bf16[20,1,16,720]{3,2,1,0:T(8,128)(2,1)S(1)}, u32[]{:S(2)}) copy-start(bf16[20,1,16,720]{3,2,1,0:T(8,128)(2,1)S(1)} %collective-permute-done.1.high_ref) | copy-start | bytes 1382404
  18.0 1.9 %copy-start.4 = (bf16[20,1,16,720]{3,2,1,0:T(8,128)(2,1)}, bf16[20,1,16,720]{3,2,1,0:T(8,128)(2,1)S(1)}, u32[]{:S(2)}) copy-start(bf16[20,1,16,720]{3,2,1,0:T(8,128)(2,1)S(1)} %collective-permute-done.low_ref) | copy-start | bytes 1382404
  18.2 25.4 %collective-permute-start.3 = (bf16[20,1,16,720]{3,2,1,0:T(8,128)(2,1)S(1)}, bf16[20,1,16,720]{3,2,1,0:T(8,128)(2,1)S(1)}, u32[]{:S(2)}, u32[]{:S(2)}) collective-permute-start(bf16[20,1,16,720]{3,2,1,0:T(8,128)(2,1)S(1)} %get-tuple-element.25), channel_id=1, source_target_pairs={{4,0},{8,4},{12,8},{16,12},{20,16},{24,20},{28,24},{0,28},{5,1},{9... | collective-permute-start | bytes 1382408 | tf_op jit(solution)/shard_map/ppermute | solution.py:18
  19.3 24.4 %collective-permute-start.2 = (bf16[20,1,16,720]{3,2,1,0:T(8,128)(2,1)S(1)}, bf16[20,1,16,720]{3,2,1,0:T(8,128)(2,1)S(1)}, u32[]{:S(2)}, u32[]{:S(2)}) collective-permute-start(bf16[20,1,16,720]{3,2,1,0:T(8,128)(2,1)S(1)} %get-tuple-element.26), channel_id=1, source_target_pairs={{0,4},{4,8},{8,12},{12,16},{16,20},{20,24},{24,28},{28,0},{1,5},{5... | collective-permute-start | bytes 1382408 | tf_op jit(solution)/shard_map/ppermute | solution.py:15
  26.4 3.9 %collective-permute-start.4 = (f32[8,256]{1,0:T(8,128)}, f32[8,256]{1,0:T(8,128)S(1)}, u32[]{:S(2)}, u32[]{:S(2)}) collective-permute-start(f32[8,256]{1,0:T(8,128)} %shard_map.86), channel_id=1, source_target_pairs={{0,1},{1,0},{2,3},{3,2},{4,5},{5,4},{6,7},{7,6},{8,9},{9,8},{10,11... | collective-permute-start | bytes 24584 | tf_op jit(solution)/shard_map/ppermute | solution.py:32
  31.0 4.5 %collective-permute-start.5 = (f32[8,256]{1,0:T(8,128)S(1)}, f32[8,256]{1,0:T(8,128)S(1)}, u32[]{:S(2)}, u32[]{:S(2)}) collective-permute-start(f32[8,256]{1,0:T(8,128)S(1)} %add.6), channel_id=1, source_target_pairs={{0,2},{1,3},{2,0},{3,1},{4,6},{5,7},{6,4},{7,5},{8,10},{9,11},{10,... | collective-permute-start | bytes 24584 | tf_op jit(solution)/shard_map/ppermute | solution.py:32
  38.7 4.9 %collective-permute-start.6 = (f32[16,720]{1,0:T(8,128)}, f32[16,720]{1,0:T(8,128)S(1)}, u32[]{:S(2)}, u32[]{:S(2)}) collective-permute-start(f32[16,720]{1,0:T(8,128)} %get-tuple-element.23), channel_id=1, source_target_pairs={{0,4},{4,8},{8,12},{12,16},{16,20},{20,24},{24,28},{28,0},{1,5},{5... | collective-permute-start | bytes 138248 | tf_op jit(solution)/shard_map/ppermute | solution.py:330
  38.7 4.9 %collective-permute-start.7 = (f32[16,720]{1,0:T(8,128)}, f32[16,720]{1,0:T(8,128)S(1)}, u32[]{:S(2)}, u32[]{:S(2)}) collective-permute-start(f32[16,720]{1,0:T(8,128)} %get-tuple-element.24), channel_id=1, source_target_pairs={{4,0},{8,4},{12,8},{16,12},{20,16},{24,20},{28,24},{0,28},{5,1},{9... | collective-permute-start | bytes 138248 | tf_op jit(solution)/shard_map/ppermute | solution.py:331
  43.6 0.6 %copy-start.5 = (f32[16,720]{1,0:T(8,128)}, f32[16,720]{1,0:T(8,128)S(1)}, u32[]{:S(2)}) copy-start(f32[16,720]{1,0:T(8,128)S(1)} %collective-permute-done.6) | copy-start | bytes 138244
  43.6 0.6 %copy-start.6 = (f32[16,720]{1,0:T(8,128)}, f32[16,720]{1,0:T(8,128)S(1)}, u32[]{:S(2)}) copy-start(f32[16,720]{1,0:T(8,128)S(1)} %collective-permute-done.7) | copy-start | bytes 138244
  43.6 0.8 %copy-start.1 = (bf16[20,1,16,720]{3,2,1,0:T(8,128)(2,1)}, bf16[20,1,16,720]{3,2,1,0:T(8,128)(2,1)S(1)}, u32[]{:S(2)}) copy-start(bf16[20,1,16,720]{3,2,1,0:T(8,128)(2,1)S(1)} %collective-permute-done.3.phigh_ref) | copy-start | bytes 1382404
  43.6 1.0 %copy-start.2 = (bf16[20,1,16,720]{3,2,1,0:T(8,128)(2,1)}, bf16[20,1,16,720]{3,2,1,0:T(8,128)(2,1)S(1)}, u32[]{:S(2)}) copy-start(bf16[20,1,16,720]{3,2,1,0:T(8,128)(2,1)S(1)} %collective-permute-done.2.plow_ref) | copy-start | bytes 1382404

commit v13 on v10

--- a/solution.py
+++ b/solution.py
@@ -91,6 +91,23 @@
     return 1
 
 
+def lat_conv(along_ref, blat_ref, radius):
+    lat_cells = blat_ref.shape[0]
+    blocks = []
+    for start in range(0, lat_cells, 256):
+        stop = min(lat_cells, start + 256)
+        low = max(0, (start - radius) // 128 * 128)
+        high = min(lat_cells, -(-(stop + radius) // 128) * 128)
+        blocks.append(
+            jnp.dot(
+                along_ref[:, low:high],
+                blat_ref[low:high, start:stop],
+                preferred_element_type=jnp.float32,
+            )
+        )
+    return jnp.concatenate(blocks, axis=1) if len(blocks) > 1 else blocks[0]
+
+
 def fill_ext(ext_ref, local, low, high, lon_cells, padded):
     radius = low.shape[0]
     base = (lon_cells // 16) * 16
@@ -134,7 +151,7 @@
             fill_ext(ext_ref, ctrl_ref[m], low_ref[m], high_ref[m], lon_cells, padded)
             along = jnp.dot(blon, ext_ref[...], preferred_element_type=jnp.float32)
             along_ref[m * padded:(m + 1) * padded, :] = along.astype(jnp.bfloat16)
-        smoothed = jnp.dot(along_ref[...], blat_ref[...], preferred_element_type=jnp.float32)
+        smoothed = lat_conv(along_ref, blat_ref, radius)
         total = pert_ref[0].astype(jnp.float32) * smoothed[0:lon_cells]
         for m in range(1, chunk):
             total = total + pert_ref[m].astype(jnp.float32) * smoothed[
@@ -261,7 +278,7 @@
             )
             along = jnp.dot(blon, ext_ref[...], preferred_element_type=jnp.float32)
             along_ref[m * padded:(m + 1) * padded, :] = along.astype(jnp.bfloat16)
-        smoothed = jnp.dot(along_ref[...], blat_ref[...], preferred_element_type=jnp.float32)
+        smoothed = lat_conv(along_ref, blat_ref, radius)
         for m in range(chunk):
             out_ref[m] = ctrl_ref[m].astype(jnp.float32) + smoothed[
                 m * padded:m * padded + lon_cells

time: 51.5 us -> 51.1 us (level)
  no operation moved by 1% of the time
where the time goes in v13:
time: 51.1 us; the launch traced here: 50.7 us
  Pallas kernels  17.1 us (33%)
  starting transfers between devices  11.8 us (23%)
  blocking collectives  9.75 us (19%)
  waiting for transfers between devices  6.89 us (13%)
  local copies, waits for them, and re-layouts  3.91 us (8%)
  other arithmetic  1.2 us (2%)
    all_to_all x1, blocking collectives, local(): lax.all_to_all(lists, 'tile', split_axis=1, concat_axis=1, tiled=True)  9.75 us
    pallas_call x1, Pallas kernels, forward_pick(): pl.pallas_call(kernel, grid=(steps,), in_specs=[field, halo, halo, field,...  6.33 us
    pallas_call x1, Pallas kernels, backward_grad(): pl.pallas_call(kernel, grid=(levels, members // chunk), in_specs=[field,...  6.15 us
    ppermute x3, waiting for transfers between devices, gather_over(): lax.ppermute(values, axis, [(i, (i + shift) % count) for i in range(count)])  4.65 us
    ppermute x3, starting transfers between devices, gather_over(): lax.ppermute(values, axis, [(i, (i + shift) % count) for i in range(count)])  4.61 us
    ppermute x2, starting transfers between devices, halos(): lax.ppermute(lax.slice_in_dim(block, 0, width, axis=dim), axis, backward)  4.52 us
    ppermute x1, starting transfers between devices, local(): lax.ppermute(high_send, 'tile', [((i + 1) % count, i) for i in range(coun...  2.64 us
    pallas_call x1, Pallas kernels, spread_misfits(): pl.pallas_call(kernel, out_shape=(jax.ShapeDtypeStruct((lon_cells, lat_ce...  2.61 us
  transfers between devices with their start and end apart: 9, of which 4 were waited for; matrix products, arithmetic and copies ran while one was open for 4% of the time, Pallas kernels for 22%

profile of v13, /device:TPU:0, one launch (start us, length us, event | category | flops | bytes accessed | tf_op | source)
XLA Modules:
  0.0 50.7 jit_solution(9781704943737597080)
XLA Ops:
  0.0 0.0 copy-start.12
  0.0 0.0 copy-start
  0.0 1.5 %fusion.1 = (bf16[20,1,16,720]{3,2,1,0:T(8,128)(2,1)S(1)}, bf16[20,1,16,720]{3,2,1,0:T(8,128)(2,1)S(1)}) fusion(bf16[20,1,45,720]{3,2,1,0:T(8,128)(2,1)} %ctrl_ref.3), kind=kLoop, calls=%fused_computation.3 | loop fusion | bytes 1843200 | tf_op jit(solution)/shard_map/slice | solution.py:18
  1.6 3.4 %collective-permute-start.1 = (bf16[20,1,16,720]{3,2,1,0:T(8,128)(2,1)S(1)}, bf16[20,1,16,720]{3,2,1,0:T(8,128)(2,1)S(1)}, u32[]{:S(2)}, u32[]{:S(2)}) collective-permute-start(bf16[20,1,16,720]{3,2,1,0:T(8,128)(2,1)S(1)} %get-tuple-element.27), channel_id=1, source_target_pairs={{4,0},{8,4},{12,8},{16,12},{20,16},{24,20},{28,24},{0,28},{5,1},{9... | collective-permute-start | bytes 1382408 | tf_op jit(solution)/shard_map/ppermute | solution.py:18
  5.0 0.0 collective-permute-start
  5.0 0.0 copy-done.14
  5.0 0.5 %convert_element_type.10.lon_ref = f32[17]{0:T(128)} convert(bf16[17]{0:T(256)(128)(2,1)S(1)} %copy-done.14) | non-fusion elementwise | flops 17 | bytes 102 | tf_op jit(solution)/shard_map/convert_element_type | solution.py:84
  5.5 0.0 copy-done.15
  5.5 0.6 %convert_element_type.11.lat_ref = f32[17]{0:T(128)} convert(bf16[17]{0:T(256)(128)(2,1)S(1)} %copy-done.15) | non-fusion elementwise | flops 17 | bytes 102 | tf_op jit(solution)/shard_map/convert_element_type | solution.py:84
  6.1 0.0 copy-done.10
  6.1 0.0 copy-done.11
  6.2 2.0 %shard_map.85 = (bf16[48,80]{1,0:T(8,128)(2,1)}, bf16[720,720]{1,0:T(8,128)(2,1)}) custom-call(f32[17]{0:T(128)} %convert_element_type.10.lon_ref, f32[17]{0:T(128)} %convert_element_type.11.lat_ref), custom_call_target="tpu_custom_call" | custom-call | tf_op jit(solution)/shard_map/pallas_call | solution.py:77
  8.1 0.0 copy-done.13
  8.1 0.0 copy-done.12
  8.1 0.1 compare_select_fusion
  8.2 9.7 %all_to_all.5 = f32[3,8,256]{2,0,1:T(4,128)S(1)} all-to-all(f32[3,8,256]{2,0,1:T(4,128)S(1)} %pad_maximum_fusion), channel_id=1, replica_groups=mesh['tile'=8,'mem'=4] {'tile'}, dimensions={1} | all-to-all | bytes 49152 | tf_op jit(solution)/shard_map/all_to_all | solution.py:326
  18.0 0.0 collective-permute-done.1.high_ref
  18.0 0.0 collective-permute-done.low_ref
  18.0 0.0 copy-done
  18.0 0.0 copy-start.4
  18.0 0.1 fusion
  18.2 1.1 %collective-permute-start.3 = (bf16[20,1,16,720]{3,2,1,0:T(8,128)(2,1)S(1)}, bf16[20,1,16,720]{3,2,1,0:T(8,128)(2,1)S(1)}, u32[]{:S(2)}, u32[]{:S(2)}) collective-permute-start(bf16[20,1,16,720]{3,2,1,0:T(8,128)(2,1)S(1)} %get-tuple-element.25), channel_id=1, source_target_pairs={{4,0},{8,4},{12,8},{16,12},{20,16},{24,20},{28,24},{0,28},{5,1},{9... | collective-permute-start | bytes 1382408 | tf_op jit(solution)/shard_map/ppermute | solution.py:18
  19.3 0.0 collective-permute-start.2
  19.3 0.6 %copy.12.cells_ref.refs_4_ = f32[3,8,256]{2,1,0:T(8,128)} copy(f32[3,8,256]{2,0,1:T(4,128)S(1)} %all_to_all.5) | data formatting | bytes 49152 | tf_op jit(solution)/shard_map/optimization_barrier | solution.py:329
  19.9 0.0 copy-done.3
  19.9 0.0 copy-done.4
  19.9 6.3 %shard_map.86.refs_0_ = f32[8,256]{1,0:T(8,128)} custom-call(bf16[20,1,45,720]{3,2,1,0:T(8,128)(2,1)} %ctrl_ref.3, bf16[20,1,16,720]{3,2,1,0:T(8,128)(2,1)} %copy-done.4, bf16[20,1,16,720]{3,2,1,0:T(8,128)(2,1)} %copy-done.3, bf16[20,1,45,720]{3,2,1,0:T(8,128)(2,1)} %pert_ref.3, bf16[48,80]{1,0:T(8,128)(2,1)} %get-tuple-element.15.blon_ref, ...), custom_call_target="tpu_custom_call" | custom-call | tf_op jit(solution)/shard_map/pallas_call | solution.py:189
  26.2 3.6 %collective-permute-start.6 = (f32[8,256]{1,0:T(8,128)}, f32[8,256]{1,0:T(8,128)S(1)}, u32[]{:S(2)}, u32[]{:S(2)}) collective-permute-start(f32[8,256]{1,0:T(8,128)} %shard_map.86.refs_0_), channel_id=1, source_target_pairs={{0,3},{1,0},{2,1},{3,2},{4,7},{5,4},{6,5},{7,6},{8,11},{9,8},{10,9... | collective-permute-start | bytes 24584 | tf_op jit(solution)/shard_map/ppermute | solution.py:25
  29.8 0.0 collective-permute-start.5
  29.8 1.0 %collective-permute-start.4 = (f32[8,256]{1,0:T(8,128)}, f32[8,256]{1,0:T(8,128)S(1)}, u32[]{:S(2)}, u32[]{:S(2)}) collective-permute-start(f32[8,256]{1,0:T(8,128)} %shard_map.86.refs_0_), channel_id=1, source_target_pairs={{0,1},{1,2},{2,3},{3,0},{4,5},{5,6},{6,7},{7,4},{8,9},{9,10},{10,1... | collective-permute-start | bytes 24584 | tf_op jit(solution)/shard_map/ppermute | solution.py:25
  30.8 0.6 %collective-permute-done.6.refs_3_ = f32[8,256]{1,0:T(8,128)S(1)} collective-permute-done((f32[8,256]{1,0:T(8,128)}, f32[8,256]{1,0:T(8,128)S(1)}, u32[]{:S(2)}, u32[]{:S(2)}) %collective-permute-start.6) | collective-permute-done | bytes 8224 | tf_op jit(solution)/shard_map/ppermute | solution.py:25
  31.4 3.2 %collective-permute-done.5.refs_2_ = f32[8,256]{1,0:T(8,128)S(1)} collective-permute-done((f32[8,256]{1,0:T(8,128)}, f32[8,256]{1,0:T(8,128)S(1)}, u32[]{:S(2)}, u32[]{:S(2)}) %collective-permute-start.5) | collective-permute-done | bytes 8224 | tf_op jit(solution)/shard_map/ppermute | solution.py:25
  34.6 0.9 %collective-permute-done.4.refs_1_ = f32[8,256]{1,0:T(8,128)S(1)} collective-permute-done((f32[8,256]{1,0:T(8,128)}, f32[8,256]{1,0:T(8,128)S(1)}, u32[]{:S(2)}, u32[]{:S(2)}) %collective-permute-start.4) | collective-permute-done | bytes 8224 | tf_op jit(solution)/shard_map/ppermute | solution.py:25
  35.5 0.0 copy-done.7
  35.5 0.6 %copy-done.9 = f32[8,256]{1,0:T(8,128)} copy-done((f32[8,256]{1,0:T(8,128)}, f32[8,256]{1,0:T(8,128)S(1)}, u32[]{:S(2)}) %copy-start.9) | copy-done | bytes 8216
  36.1 2.6 %shard_map.87 = (f32[45,720]{1,0:T(8,128)}, f32[16,720]{1,0:T(8,128)}, f32[16,720]{1,0:T(8,128)}) custom-call(f32[8,256]{1,0:T(8,128)} %shard_map.86.refs_0_, f32[8,256]{1,0:T(8,128)} %copy-done.9, f32[8,256]{1,0:T(8,128)} %copy-done.8, f32[8,256]{1,0:T(8,128)} %copy-done.7, f32[3,8,256]{2,1,0:T(8,128)} %copy.12.cells_ref.refs_4_), custom_call_target="tpu_custom_call" | custom-call | tf_op jit(solution)/shard_map/pallas_call | solution.py:247
  38.7 0.0 collective-permute-start.7
  38.7 2.6 %collective-permute-start.8 = (f32[16,720]{1,0:T(8,128)}, f32[16,720]{1,0:T(8,128)S(1)}, u32[]{:S(2)}, u32[]{:S(2)}) collective-permute-start(f32[16,720]{1,0:T(8,128)} %get-tuple-element.24), channel_id=1, source_target_pairs={{4,0},{8,4},{12,8},{16,12},{20,16},{24,20},{28,24},{0,28},{5,1},{9... | collective-permute-start | bytes 138248 | tf_op jit(solution)/shard_map/ppermute | solution.py:341
  41.3 2.2 %collective-permute-done.7 = f32[16,720]{1,0:T(8,128)S(1)} collective-permute-done((f32[16,720]{1,0:T(8,128)}, f32[16,720]{1,0:T(8,128)S(1)}, u32[]{:S(2)}, u32[]{:S(2)}) %collective-permute-start.7) | collective-permute-done | bytes 46112 | tf_op jit(solution)/shard_map/ppermute | solution.py:340
  43.6 0.0 collective-permute-done.8
  43.6 0.0 collective-permute-done.3.phigh_ref
  43.6 0.0 copy-start.1
  43.6 0.0 collective-permute-done.2.plow_ref
  43.6 0.6 %copy-done.5 = f32[16,720]{1,0:T(8,128)} copy-done((f32[16,720]{1,0:T(8,128)}, f32[16,720]{1,0:T(8,128)S(1)}, u32[]{:S(2)}) %copy-start.5) | copy-done | bytes 46104
  44.2 0.0 copy-done.6
  44.2 0.2 copy-done.1
  44.4 0.2 copy-done.2
  44.6 6.1 %shard_map.88 = f32[20,45,1,720]{3,2,1,0:T(1,128)} custom-call(bf16[20,1,45,720]{3,2,1,0:T(8,128)(2,1)} %pert_ref.3, bf16[20,1,16,720]{3,2,1,0:T(8,128)(2,1)} %copy-done.2, bf16[20,1,16,720]{3,2,1,0:T(8,128)(2,1)} %copy-done.1, f32[1,45,720]{2,1,0:T(8,128)} %bitcast.5, f32[1,16,720]{2,1,0:T(8,128)} %bitcast.6, f32[1,16,720]{2,1,0:T(8,128)} %bitcast.7, ...), custom_call_target="tpu_custom_call" | custom-call | tf_op jit(solution)/shard_map/pallas_call | solution.py:291
  (17 shorter events, 0.1 us)
Async XLA Ops:
  0.0 5.0 %copy-start.14 = (bf16[17]{0:T(256)(128)(2,1)S(1)}, bf16[17]{0:T(256)(128)(2,1)}, u32[]{:S(2)}) copy-start(bf16[17]{0:T(256)(128)(2,1)} %param.10) | copy-start | bytes 106
  0.0 5.5 %copy-start.15 = (bf16[17]{0:T(256)(128)(2,1)S(1)}, bf16[17]{0:T(256)(128)(2,1)}, u32[]{:S(2)}) copy-start(bf16[17]{0:T(256)(128)(2,1)} %param.11) | copy-start | bytes 106
  0.0 6.1 %copy-start.10 = (f32[1,8,256]{2,1,0:T(8,128)S(1)}, f32[1,8,256]{2,1,0:T(8,128)}, u32[]{:S(2)}) copy-start(f32[1,8,256]{2,1,0:T(8,128)} %param.12) | copy-start | bytes 24580
  0.0 6.1 %copy-start.11 = (s32[1,8,256]{2,1,0:T(8,128)S(1)}, s32[1,8,256]{2,1,0:T(8,128)}, u32[]{:S(2)}) copy-start(s32[1,8,256]{2,1,0:T(8,128)} %param.14) | copy-start | bytes 24580
  0.0 8.1 %copy-start.13 = (s32[1,8]{1,0:T(1,128)S(1)}, s32[1,8]{1,0:T(1,128)}, u32[]{:S(2)}) copy-start(s32[1,8]{1,0:T(1,128)} %param.15) | copy-start | bytes 100
  0.0 8.1 %copy-start.12 = (f32[1,8,256]{2,1,0:T(8,128)S(1)}, f32[1,8,256]{2,1,0:T(8,128)}, u32[]{:S(2)}) copy-start(f32[1,8,256]{2,1,0:T(8,128)} %param.13) | copy-start | bytes 24580
  0.0 18.0 %copy-start = (bf16[20,1,45,720]{3,2,1,0:T(8,128)(2,1)S(1)}, bf16[20,1,45,720]{3,2,1,0:T(8,128)(2,1)}, u32[]{:S(2)}) copy-start(bf16[20,1,45,720]{3,2,1,0:T(8,128)(2,1)} %pert_ref.3) | copy-start | bytes 3888004
  1.6 16.4 %collective-permute-start.1 = (bf16[20,1,16,720]{3,2,1,0:T(8,128)(2,1)S(1)}, bf16[20,1,16,720]{3,2,1,0:T(8,128)(2,1)S(1)}, u32[]{:S(2)}, u32[]{:S(2)}) collective-permute-start(bf16[20,1,16,720]{3,2,1,0:T(8,128)(2,1)S(1)} %get-tuple-element.27), channel_id=1, source_target_pairs={{4,0},{8,4},{12,8},{16,12},{20,16},{24,20},{28,24},{0,28},{5,1},{9... | collective-permute-start | bytes 1382408 | tf_op jit(solution)/shard_map/ppermute | solution.py:18
  5.0 13.0 %collective-permute-start = (bf16[20,1,16,720]{3,2,1,0:T(8,128)(2,1)S(1)}, bf16[20,1,16,720]{3,2,1,0:T(8,128)(2,1)S(1)}, u32[]{:S(2)}, u32[]{:S(2)}) collective-permute-start(bf16[20,1,16,720]{3,2,1,0:T(8,128)(2,1)S(1)} %get-tuple-element.28), channel_id=1, source_target_pairs={{0,4},{4,8},{8,12},{12,16},{16,20},{20,24},{24,28},{28,0},{1,5},{5... | collective-permute-start | bytes 1382408 | tf_op jit(solution)/shard_map/ppermute | solution.py:15
  18.0 1.9 %copy-start.3 = (bf16[20,1,16,720]{3,2,1,0:T(8,128)(2,1)}, bf16[20,1,16,720]{3,2,1,0:T(8,128)(2,1)S(1)}, u32[]{:S(2)}) copy-start(bf16[20,1,16,720]{3,2,1,0:T(8,128)(2,1)S(1)} %collective-permute-done.1.high_ref) | copy-start | bytes 1382404
  18.0 1.9 %copy-start.4 = (bf16[20,1,16,720]{3,2,1,0:T(8,128)(2,1)}, bf16[20,1,16,720]{3,2,1,0:T(8,128)(2,1)S(1)}, u32[]{:S(2)}) copy-start(bf16[20,1,16,720]{3,2,1,0:T(8,128)(2,1)S(1)} %collective-permute-done.low_ref) | copy-start | bytes 1382404
  18.2 25.4 %collective-permute-start.3 = (bf16[20,1,16,720]{3,2,1,0:T(8,128)(2,1)S(1)}, bf16[20,1,16,720]{3,2,1,0:T(8,128)(2,1)S(1)}, u32[]{:S(2)}, u32[]{:S(2)}) collective-permute-start(bf16[20,1,16,720]{3,2,1,0:T(8,128)(2,1)S(1)} %get-tuple-element.25), channel_id=1, source_target_pairs={{4,0},{8,4},{12,8},{16,12},{20,16},{24,20},{28,24},{0,28},{5,1},{9... | collective-permute-start | bytes 1382408 | tf_op jit(solution)/shard_map/ppermute | solution.py:18
  19.3 24.3 %collective-permute-start.2 = (bf16[20,1,16,720]{3,2,1,0:T(8,128)(2,1)S(1)}, bf16[20,1,16,720]{3,2,1,0:T(8,128)(2,1)S(1)}, u32[]{:S(2)}, u32[]{:S(2)}) collective-permute-start(bf16[20,1,16,720]{3,2,1,0:T(8,128)(2,1)S(1)} %get-tuple-element.26), channel_id=1, source_target_pairs={{0,4},{4,8},{8,12},{12,16},{16,20},{20,24},{24,28},{28,0},{1,5},{5... | collective-permute-start | bytes 1382408 | tf_op jit(solution)/shard_map/ppermute | solution.py:15
  26.2 5.2 %collective-permute-start.6 = (f32[8,256]{1,0:T(8,128)}, f32[8,256]{1,0:T(8,128)S(1)}, u32[]{:S(2)}, u32[]{:S(2)}) collective-permute-start(f32[8,256]{1,0:T(8,128)} %shard_map.86.refs_0_), channel_id=1, source_target_pairs={{0,3},{1,0},{2,1},{3,2},{4,7},{5,4},{6,5},{7,6},{8,11},{9,8},{10,9... | collective-permute-start | bytes 24584 | tf_op jit(solution)/shard_map/ppermute | solution.py:25
  29.8 4.8 %collective-permute-start.5 = (f32[8,256]{1,0:T(8,128)}, f32[8,256]{1,0:T(8,128)S(1)}, u32[]{:S(2)}, u32[]{:S(2)}) collective-permute-start(f32[8,256]{1,0:T(8,128)} %shard_map.86.refs_0_), channel_id=1, source_target_pairs={{0,2},{1,3},{2,0},{3,1},{4,6},{5,7},{6,4},{7,5},{8,10},{9,11},{10,... | collective-permute-start | bytes 24584 | tf_op jit(solution)/shard_map/ppermute | solution.py:25
  29.8 5.7 %collective-permute-start.4 = (f32[8,256]{1,0:T(8,128)}, f32[8,256]{1,0:T(8,128)S(1)}, u32[]{:S(2)}, u32[]{:S(2)}) collective-permute-start(f32[8,256]{1,0:T(8,128)} %shard_map.86.refs_0_), channel_id=1, source_target_pairs={{0,1},{1,2},{2,3},{3,0},{4,5},{5,6},{6,7},{7,4},{8,9},{9,10},{10,1... | collective-permute-start | bytes 24584 | tf_op jit(solution)/shard_map/ppermute | solution.py:25
  31.4 4.1 %copy-start.7 = (f32[8,256]{1,0:T(8,128)}, f32[8,256]{1,0:T(8,128)S(1)}, u32[]{:S(2)}) copy-start(f32[8,256]{1,0:T(8,128)S(1)} %collective-permute-done.6.refs_3_) | copy-start | bytes 24580
  34.6 0.9 %copy-start.8 = (f32[8,256]{1,0:T(8,128)}, f32[8,256]{1,0:T(8,128)S(1)}, u32[]{:S(2)}) copy-start(f32[8,256]{1,0:T(8,128)S(1)} %collective-permute-done.5.refs_2_) | copy-start | bytes 24580
  35.5 0.6 %copy-start.9 = (f32[8,256]{1,0:T(8,128)}, f32[8,256]{1,0:T(8,128)S(1)}, u32[]{:S(2)}) copy-start(f32[8,256]{1,0:T(8,128)S(1)} %collective-permute-done.4.refs_1_) | copy-start | bytes 24580
  38.7 4.9 %collective-permute-start.7 = (f32[16,720]{1,0:T(8,128)}, f32[16,720]{1,0:T(8,128)S(1)}, u32[]{:S(2)}, u32[]{:S(2)}) collective-permute-start(f32[16,720]{1,0:T(8,128)} %get-tuple-element.23), channel_id=1, source_target_pairs={{0,4},{4,8},{8,12},{12,16},{16,20},{20,24},{24,28},{28,0},{1,5},{5... | collective-permute-start | bytes 138248 | tf_op jit(solution)/shard_map/ppermute | solution.py:340
  38.7 4.9 %collective-permute-start.8 = (f32[16,720]{1,0:T(8,128)}, f32[16,720]{1,0:T(8,128)S(1)}, u32[]{:S(2)}, u32[]{:S(2)}) collective-permute-start(f32[16,720]{1,0:T(8,128)} %get-tuple-element.24), channel_id=1, source_target_pairs={{4,0},{8,4},{12,8},{16,12},{20,16},{24,20},{28,24},{0,28},{5,1},{9... | collective-permute-start | bytes 138248 | tf_op jit(solution)/shard_map/ppermute | solution.py:341
  43.5 0.6 %copy-start.5 = (f32[16,720]{1,0:T(8,128)}, f32[16,720]{1,0:T(8,128)S(1)}, u32[]{:S(2)}) copy-start(f32[16,720]{1,0:T(8,128)S(1)} %collective-permute-done.7) | copy-start | bytes 138244
  43.6 0.6 %copy-start.6 = (f32[16,720]{1,0:T(8,128)}, f32[16,720]{1,0:T(8,128)S(1)}, u32[]{:S(2)}) copy-start(f32[16,720]{1,0:T(8,128)S(1)} %collective-permute-done.8) | copy-start | bytes 138244
  43.6 0.8 %copy-start.1 = (bf16[20,1,16,720]{3,2,1,0:T(8,128)(2,1)}, bf16[20,1,16,720]{3,2,1,0:T(8,128)(2,1)S(1)}, u32[]{:S(2)}) copy-start(bf16[20,1,16,720]{3,2,1,0:T(8,128)(2,1)S(1)} %collective-permute-done.3.phigh_ref) | copy-start | bytes 1382404
  43.6 1.0 %copy-start.2 = (bf16[20,1,16,720]{3,2,1,0:T(8,128)(2,1)}, bf16[20,1,16,720]{3,2,1,0:T(8,128)(2,1)S(1)}, u32[]{:S(2)}) copy-start(bf16[20,1,16,720]{3,2,1,0:T(8,128)(2,1)S(1)} %collective-permute-done.2.plow_ref) | copy-start | bytes 1382404

commit v14 on v13

--- a/solution.py
+++ b/solution.py
@@ -85,7 +85,7 @@
 
 
 def member_chunk(members):
-    for size in (5, 4, 3, 2, 1):
+    for size in (10, 8, 5, 4, 3, 2, 1):
         if members % size == 0:
             return size
     return 1

time: 51.1 us -> 49.1 us (0.961)
  Pallas kernels: 17.1 us -> 15.3 us
    pallas_call x1, Pallas kernels: 6.33 us -> 5.31 us  [forward_pick(): pl.pallas_call(kernel, grid=(steps,), in_specs=[field, halo, halo, field,...]
    pallas_call x1, Pallas kernels: 6.15 us -> 5.4 us  [backward_grad(): pl.pallas_call(kernel, grid=(levels, members // chunk), in_specs=[field,...]
  transfers between devices with their start and end apart: 9 -> 9, of which waited for: 4 -> 4; matrix products, arithmetic and copies ran while one was open for 4% -> 4% of each run, Pallas kernels for 22% -> 20%
where the time goes in v14:
time: 49.1 us; the launch traced here: 48.8 us
  Pallas kernels  15.3 us (31%)
  starting transfers between devices  11.8 us (24%)
  blocking collectives  9.75 us (20%)
  waiting for transfers between devices  6.78 us (14%)
  local copies, waits for them, and re-layouts  3.91 us (8%)
  other arithmetic  1.2 us (2%)
    all_to_all x1, blocking collectives, local(): lax.all_to_all(lists, 'tile', split_axis=1, concat_axis=1, tiled=True)  9.75 us
    pallas_call x1, Pallas kernels, backward_grad(): pl.pallas_call(kernel, grid=(levels, members // chunk), in_specs=[field,...  5.4 us
    pallas_call x1, Pallas kernels, forward_pick(): pl.pallas_call(kernel, grid=(steps,), in_specs=[field, halo, halo, field,...  5.31 us
    ppermute x3, waiting for transfers between devices, gather_over(): lax.ppermute(values, axis, [(i, (i + shift) % count) for i in range(count)])  4.64 us
    ppermute x3, starting transfers between devices, gather_over(): lax.ppermute(values, axis, [(i, (i + shift) % count) for i in range(count)])  4.62 us
    ppermute x2, starting transfers between devices, halos(): lax.ppermute(lax.slice_in_dim(block, 0, width, axis=dim), axis, backward)  4.52 us
    ppermute x1, starting transfers between devices, local(): lax.ppermute(high_send, 'tile', [((i + 1) % count, i) for i in range(coun...  2.64 us
    pallas_call x1, Pallas kernels, spread_misfits(): pl.pallas_call(kernel, out_shape=(jax.ShapeDtypeStruct((lon_cells, lat_ce...  2.6 us
  transfers between devices with their start and end apart: 9, of which 4 were waited for; matrix products, arithmetic and copies ran while one was open for 4% of the time, Pallas kernels for 20%

profile of v14, /device:TPU:0, one launch (start us, length us, event | category | flops | bytes accessed | tf_op | source)
XLA Modules:
  0.0 48.8 jit_solution(4957182634271176678)
XLA Ops:
  0.0 0.0 copy-start.12
  0.0 0.0 copy-start
  0.0 1.5 %fusion.1 = (bf16[20,1,16,720]{3,2,1,0:T(8,128)(2,1)S(1)}, bf16[20,1,16,720]{3,2,1,0:T(8,128)(2,1)S(1)}) fusion(bf16[20,1,45,720]{3,2,1,0:T(8,128)(2,1)} %ctrl_ref.3), kind=kLoop, calls=%fused_computation.3 | loop fusion | bytes 1843200 | tf_op jit(solution)/shard_map/slice | solution.py:18
  1.6 3.4 %collective-permute-start.1 = (bf16[20,1,16,720]{3,2,1,0:T(8,128)(2,1)S(1)}, bf16[20,1,16,720]{3,2,1,0:T(8,128)(2,1)S(1)}, u32[]{:S(2)}, u32[]{:S(2)}) collective-permute-start(bf16[20,1,16,720]{3,2,1,0:T(8,128)(2,1)S(1)} %get-tuple-element.27), channel_id=1, source_target_pairs={{4,0},{8,4},{12,8},{16,12},{20,16},{24,20},{28,24},{0,28},{5,1},{9... | collective-permute-start | bytes 1382408 | tf_op jit(solution)/shard_map/ppermute | solution.py:18
  5.0 0.0 collective-permute-start
  5.0 0.0 copy-done.14
  5.0 0.5 %convert_element_type.10.lon_ref = f32[17]{0:T(128)} convert(bf16[17]{0:T(256)(128)(2,1)S(1)} %copy-done.14) | non-fusion elementwise | flops 17 | bytes 102 | tf_op jit(solution)/shard_map/convert_element_type | solution.py:84
  5.5 0.0 copy-done.15
  5.5 0.6 %convert_element_type.11.lat_ref = f32[17]{0:T(128)} convert(bf16[17]{0:T(256)(128)(2,1)S(1)} %copy-done.15) | non-fusion elementwise | flops 17 | bytes 102 | tf_op jit(solution)/shard_map/convert_element_type | solution.py:84
  6.1 0.0 copy-done.10
  6.1 0.0 copy-done.11
  6.2 2.0 %shard_map.85 = (bf16[48,80]{1,0:T(8,128)(2,1)}, bf16[720,720]{1,0:T(8,128)(2,1)}) custom-call(f32[17]{0:T(128)} %convert_element_type.10.lon_ref, f32[17]{0:T(128)} %convert_element_type.11.lat_ref), custom_call_target="tpu_custom_call" | custom-call | tf_op jit(solution)/shard_map/pallas_call | solution.py:77
  8.1 0.0 copy-done.13
  8.1 0.0 copy-done.12
  8.1 0.1 compare_select_fusion
  8.2 9.7 %all_to_all.5 = f32[3,8,256]{2,0,1:T(4,128)S(1)} all-to-all(f32[3,8,256]{2,0,1:T(4,128)S(1)} %pad_maximum_fusion), channel_id=1, replica_groups=mesh['tile'=8,'mem'=4] {'tile'}, dimensions={1} | all-to-all | bytes 49152 | tf_op jit(solution)/shard_map/all_to_all | solution.py:326
  18.0 0.0 collective-permute-done.1.high_ref
  18.0 0.0 collective-permute-done.low_ref
  18.0 0.0 copy-done
  18.0 0.0 copy-start.4
  18.0 0.1 fusion
  18.2 1.1 %collective-permute-start.3 = (bf16[20,1,16,720]{3,2,1,0:T(8,128)(2,1)S(1)}, bf16[20,1,16,720]{3,2,1,0:T(8,128)(2,1)S(1)}, u32[]{:S(2)}, u32[]{:S(2)}) collective-permute-start(bf16[20,1,16,720]{3,2,1,0:T(8,128)(2,1)S(1)} %get-tuple-element.25), channel_id=1, source_target_pairs={{4,0},{8,4},{12,8},{16,12},{20,16},{24,20},{28,24},{0,28},{5,1},{9... | collective-permute-start | bytes 1382408 | tf_op jit(solution)/shard_map/ppermute | solution.py:18
  19.3 0.0 collective-permute-start.2
  19.3 0.6 %copy.12.cells_ref.refs_4_ = f32[3,8,256]{2,1,0:T(8,128)} copy(f32[3,8,256]{2,0,1:T(4,128)S(1)} %all_to_all.5) | data formatting | bytes 49152 | tf_op jit(solution)/shard_map/optimization_barrier | solution.py:329
  19.9 0.0 copy-done.3
  19.9 0.0 copy-done.4
  19.9 5.3 %shard_map.86.refs_0_ = f32[8,256]{1,0:T(8,128)} custom-call(bf16[20,1,45,720]{3,2,1,0:T(8,128)(2,1)} %ctrl_ref.3, bf16[20,1,16,720]{3,2,1,0:T(8,128)(2,1)} %copy-done.4, bf16[20,1,16,720]{3,2,1,0:T(8,128)(2,1)} %copy-done.3, bf16[20,1,45,720]{3,2,1,0:T(8,128)(2,1)} %pert_ref.3, bf16[48,80]{1,0:T(8,128)(2,1)} %get-tuple-element.15.blon_ref, ...), custom_call_target="tpu_custom_call" | custom-call | tf_op jit(solution)/shard_map/pallas_call | solution.py:189
  25.2 3.6 %collective-permute-start.6 = (f32[8,256]{1,0:T(8,128)}, f32[8,256]{1,0:T(8,128)S(1)}, u32[]{:S(2)}, u32[]{:S(2)}) collective-permute-start(f32[8,256]{1,0:T(8,128)} %shard_map.86.refs_0_), channel_id=1, source_target_pairs={{0,3},{1,0},{2,1},{3,2},{4,7},{5,4},{6,5},{7,6},{8,11},{9,8},{10,9... | collective-permute-start | bytes 24584 | tf_op jit(solution)/shard_map/ppermute | solution.py:25
  28.8 0.0 collective-permute-start.5
  28.8 1.0 %collective-permute-start.4 = (f32[8,256]{1,0:T(8,128)}, f32[8,256]{1,0:T(8,128)S(1)}, u32[]{:S(2)}, u32[]{:S(2)}) collective-permute-start(f32[8,256]{1,0:T(8,128)} %shard_map.86.refs_0_), channel_id=1, source_target_pairs={{0,1},{1,2},{2,3},{3,0},{4,5},{5,6},{6,7},{7,4},{8,9},{9,10},{10,1... | collective-permute-start | bytes 24584 | tf_op jit(solution)/shard_map/ppermute | solution.py:25
  29.8 0.6 %collective-permute-done.6.refs_3_ = f32[8,256]{1,0:T(8,128)S(1)} collective-permute-done((f32[8,256]{1,0:T(8,128)}, f32[8,256]{1,0:T(8,128)S(1)}, u32[]{:S(2)}, u32[]{:S(2)}) %collective-permute-start.6) | collective-permute-done | bytes 8224 | tf_op jit(solution)/shard_map/ppermute | solution.py:25
  30.4 3.2 %collective-permute-done.5.refs_2_ = f32[8,256]{1,0:T(8,128)S(1)} collective-permute-done((f32[8,256]{1,0:T(8,128)}, f32[8,256]{1,0:T(8,128)S(1)}, u32[]{:S(2)}, u32[]{:S(2)}) %collective-permute-start.5) | collective-permute-done | bytes 8224 | tf_op jit(solution)/shard_map/ppermute | solution.py:25
  33.6 0.9 %collective-permute-done.4.refs_1_ = f32[8,256]{1,0:T(8,128)S(1)} collective-permute-done((f32[8,256]{1,0:T(8,128)}, f32[8,256]{1,0:T(8,128)S(1)}, u32[]{:S(2)}, u32[]{:S(2)}) %collective-permute-start.4) | collective-permute-done | bytes 8224 | tf_op jit(solution)/shard_map/ppermute | solution.py:25
  34.5 0.0 copy-done.7
  34.5 0.0 copy-done.8
  34.5 0.6 %copy-done.9 = f32[8,256]{1,0:T(8,128)} copy-done((f32[8,256]{1,0:T(8,128)}, f32[8,256]{1,0:T(8,128)S(1)}, u32[]{:S(2)}) %copy-start.9) | copy-done | bytes 8216
  35.1 2.6 %shard_map.87 = (f32[45,720]{1,0:T(8,128)}, f32[16,720]{1,0:T(8,128)}, f32[16,720]{1,0:T(8,128)}) custom-call(f32[8,256]{1,0:T(8,128)} %shard_map.86.refs_0_, f32[8,256]{1,0:T(8,128)} %copy-done.9, f32[8,256]{1,0:T(8,128)} %copy-done.8, f32[8,256]{1,0:T(8,128)} %copy-done.7, f32[3,8,256]{2,1,0:T(8,128)} %copy.12.cells_ref.refs_4_), custom_call_target="tpu_custom_call" | custom-call | tf_op jit(solution)/shard_map/pallas_call | solution.py:247
  37.7 0.0 collective-permute-start.7
  37.7 2.6 %collective-permute-start.8 = (f32[16,720]{1,0:T(8,128)}, f32[16,720]{1,0:T(8,128)S(1)}, u32[]{:S(2)}, u32[]{:S(2)}) collective-permute-start(f32[16,720]{1,0:T(8,128)} %get-tuple-element.24), channel_id=1, source_target_pairs={{4,0},{8,4},{12,8},{16,12},{20,16},{24,20},{28,24},{0,28},{5,1},{9... | collective-permute-start | bytes 138248 | tf_op jit(solution)/shard_map/ppermute | solution.py:341
  40.3 2.1 %collective-permute-done.7 = f32[16,720]{1,0:T(8,128)S(1)} collective-permute-done((f32[16,720]{1,0:T(8,128)}, f32[16,720]{1,0:T(8,128)S(1)}, u32[]{:S(2)}, u32[]{:S(2)}) %collective-permute-start.7) | collective-permute-done | bytes 46112 | tf_op jit(solution)/shard_map/ppermute | solution.py:340
  42.4 0.0 collective-permute-done.8
  42.4 0.0 collective-permute-done.3.phigh_ref
  42.4 0.0 collective-permute-done.2.plow_ref
  42.5 0.6 %copy-done.5 = f32[16,720]{1,0:T(8,128)} copy-done((f32[16,720]{1,0:T(8,128)}, f32[16,720]{1,0:T(8,128)S(1)}, u32[]{:S(2)}) %copy-start.5) | copy-done | bytes 46104
  43.0 0.0 copy-done.6
  43.1 0.2 copy-done.1
  43.2 0.2 copy-done.2
  43.4 5.4 %shard_map.88 = f32[20,45,1,720]{3,2,1,0:T(1,128)} custom-call(bf16[20,1,45,720]{3,2,1,0:T(8,128)(2,1)} %pert_ref.3, bf16[20,1,16,720]{3,2,1,0:T(8,128)(2,1)} %copy-done.2, bf16[20,1,16,720]{3,2,1,0:T(8,128)(2,1)} %copy-done.1, f32[1,45,720]{2,1,0:T(8,128)} %bitcast.5, f32[1,16,720]{2,1,0:T(8,128)} %bitcast.6, f32[1,16,720]{2,1,0:T(8,128)} %bitcast.7, ...), custom_call_target="tpu_custom_call" | custom-call | tf_op jit(solution)/shard_map/pallas_call | solution.py:291
  (17 shorter events, 0.1 us)
Async XLA Ops:
  0.0 5.0 %copy-start.14 = (bf16[17]{0:T(256)(128)(2,1)S(1)}, bf16[17]{0:T(256)(128)(2,1)}, u32[]{:S(2)}) copy-start(bf16[17]{0:T(256)(128)(2,1)} %param.10) | copy-start | bytes 106
  0.0 5.5 %copy-start.15 = (bf16[17]{0:T(256)(128)(2,1)S(1)}, bf16[17]{0:T(256)(128)(2,1)}, u32[]{:S(2)}) copy-start(bf16[17]{0:T(256)(128)(2,1)} %param.11) | copy-start | bytes 106
  0.0 6.1 %copy-start.10 = (f32[1,8,256]{2,1,0:T(8,128)S(1)}, f32[1,8,256]{2,1,0:T(8,128)}, u32[]{:S(2)}) copy-start(f32[1,8,256]{2,1,0:T(8,128)} %param.12) | copy-start | bytes 24580
  0.0 6.1 %copy-start.11 = (s32[1,8,256]{2,1,0:T(8,128)S(1)}, s32[1,8,256]{2,1,0:T(8,128)}, u32[]{:S(2)}) copy-start(s32[1,8,256]{2,1,0:T(8,128)} %param.14) | copy-start | bytes 24580
  0.0 8.1 %copy-start.13 = (s32[1,8]{1,0:T(1,128)S(1)}, s32[1,8]{1,0:T(1,128)}, u32[]{:S(2)}) copy-start(s32[1,8]{1,0:T(1,128)} %param.15) | copy-start | bytes 100
  0.0 8.1 %copy-start.12 = (f32[1,8,256]{2,1,0:T(8,128)S(1)}, f32[1,8,256]{2,1,0:T(8,128)}, u32[]{:S(2)}) copy-start(f32[1,8,256]{2,1,0:T(8,128)} %param.13) | copy-start | bytes 24580
  0.0 18.0 %copy-start = (bf16[20,1,45,720]{3,2,1,0:T(8,128)(2,1)S(1)}, bf16[20,1,45,720]{3,2,1,0:T(8,128)(2,1)}, u32[]{:S(2)}) copy-start(bf16[20,1,45,720]{3,2,1,0:T(8,128)(2,1)} %pert_ref.3) | copy-start | bytes 3888004
  1.6 16.4 %collective-permute-start.1 = (bf16[20,1,16,720]{3,2,1,0:T(8,128)(2,1)S(1)}, bf16[20,1,16,720]{3,2,1,0:T(8,128)(2,1)S(1)}, u32[]{:S(2)}, u32[]{:S(2)}) collective-permute-start(bf16[20,1,16,720]{3,2,1,0:T(8,128)(2,1)S(1)} %get-tuple-element.27), channel_id=1, source_target_pairs={{4,0},{8,4},{12,8},{16,12},{20,16},{24,20},{28,24},{0,28},{5,1},{9... | collective-permute-start | bytes 1382408 | tf_op jit(solution)/shard_map/ppermute | solution.py:18
  5.0 13.0 %collective-permute-start = (bf16[20,1,16,720]{3,2,1,0:T(8,128)(2,1)S(1)}, bf16[20,1,16,720]{3,2,1,0:T(8,128)(2,1)S(1)}, u32[]{:S(2)}, u32[]{:S(2)}) collective-permute-start(bf16[20,1,16,720]{3,2,1,0:T(8,128)(2,1)S(1)} %get-tuple-element.28), channel_id=1, source_target_pairs={{0,4},{4,8},{8,12},{12,16},{16,20},{20,24},{24,28},{28,0},{1,5},{5... | collective-permute-start | bytes 1382408 | tf_op jit(solution)/shard_map/ppermute | solution.py:15
  18.0 1.9 %copy-start.3 = (bf16[20,1,16,720]{3,2,1,0:T(8,128)(2,1)}, bf16[20,1,16,720]{3,2,1,0:T(8,128)(2,1)S(1)}, u32[]{:S(2)}) copy-start(bf16[20,1,16,720]{3,2,1,0:T(8,128)(2,1)S(1)} %collective-permute-done.1.high_ref) | copy-start | bytes 1382404
  18.0 1.9 %copy-start.4 = (bf16[20,1,16,720]{3,2,1,0:T(8,128)(2,1)}, bf16[20,1,16,720]{3,2,1,0:T(8,128)(2,1)S(1)}, u32[]{:S(2)}) copy-start(bf16[20,1,16,720]{3,2,1,0:T(8,128)(2,1)S(1)} %collective-permute-done.low_ref) | copy-start | bytes 1382404
  18.2 24.3 %collective-permute-start.3 = (bf16[20,1,16,720]{3,2,1,0:T(8,128)(2,1)S(1)}, bf16[20,1,16,720]{3,2,1,0:T(8,128)(2,1)S(1)}, u32[]{:S(2)}, u32[]{:S(2)}) collective-permute-start(bf16[20,1,16,720]{3,2,1,0:T(8,128)(2,1)S(1)} %get-tuple-element.25), channel_id=1, source_target_pairs={{4,0},{8,4},{12,8},{16,12},{20,16},{24,20},{28,24},{0,28},{5,1},{9... | collective-permute-start | bytes 1382408 | tf_op jit(solution)/shard_map/ppermute | solution.py:18
  19.3 23.2 %collective-permute-start.2 = (bf16[20,1,16,720]{3,2,1,0:T(8,128)(2,1)S(1)}, bf16[20,1,16,720]{3,2,1,0:T(8,128)(2,1)S(1)}, u32[]{:S(2)}, u32[]{:S(2)}) collective-permute-start(bf16[20,1,16,720]{3,2,1,0:T(8,128)(2,1)S(1)} %get-tuple-element.26), channel_id=1, source_target_pairs={{0,4},{4,8},{8,12},{12,16},{16,20},{20,24},{24,28},{28,0},{1,5},{5... | collective-permute-start | bytes 1382408 | tf_op jit(solution)/shard_map/ppermute | solution.py:15
  25.2 5.2 %collective-permute-start.6 = (f32[8,256]{1,0:T(8,128)}, f32[8,256]{1,0:T(8,128)S(1)}, u32[]{:S(2)}, u32[]{:S(2)}) collective-permute-start(f32[8,256]{1,0:T(8,128)} %shard_map.86.refs_0_), channel_id=1, source_target_pairs={{0,3},{1,0},{2,1},{3,2},{4,7},{5,4},{6,5},{7,6},{8,11},{9,8},{10,9... | collective-permute-start | bytes 24584 | tf_op jit(solution)/shard_map/ppermute | solution.py:25
  28.8 4.8 %collective-permute-start.5 = (f32[8,256]{1,0:T(8,128)}, f32[8,256]{1,0:T(8,128)S(1)}, u32[]{:S(2)}, u32[]{:S(2)}) collective-permute-start(f32[8,256]{1,0:T(8,128)} %shard_map.86.refs_0_), channel_id=1, source_target_pairs={{0,2},{1,3},{2,0},{3,1},{4,6},{5,7},{6,4},{7,5},{8,10},{9,11},{10,... | collective-permute-start | bytes 24584 | tf_op jit(solution)/shard_map/ppermute | solution.py:25
  28.8 5.7 %collective-permute-start.4 = (f32[8,256]{1,0:T(8,128)}, f32[8,256]{1,0:T(8,128)S(1)}, u32[]{:S(2)}, u32[]{:S(2)}) collective-permute-start(f32[8,256]{1,0:T(8,128)} %shard_map.86.refs_0_), channel_id=1, source_target_pairs={{0,1},{1,2},{2,3},{3,0},{4,5},{5,6},{6,7},{7,4},{8,9},{9,10},{10,1... | collective-permute-start | bytes 24584 | tf_op jit(solution)/shard_map/ppermute | solution.py:25
  30.4 4.1 %copy-start.7 = (f32[8,256]{1,0:T(8,128)}, f32[8,256]{1,0:T(8,128)S(1)}, u32[]{:S(2)}) copy-start(f32[8,256]{1,0:T(8,128)S(1)} %collective-permute-done.6.refs_3_) | copy-start | bytes 24580
  33.5 0.9 %copy-start.8 = (f32[8,256]{1,0:T(8,128)}, f32[8,256]{1,0:T(8,128)S(1)}, u32[]{:S(2)}) copy-start(f32[8,256]{1,0:T(8,128)S(1)} %collective-permute-done.5.refs_2_) | copy-start | bytes 24580
  34.5 0.6 %copy-start.9 = (f32[8,256]{1,0:T(8,128)}, f32[8,256]{1,0:T(8,128)S(1)}, u32[]{:S(2)}) copy-start(f32[8,256]{1,0:T(8,128)S(1)} %collective-permute-done.4.refs_1_) | copy-start | bytes 24580
  37.7 4.8 %collective-permute-start.7 = (f32[16,720]{1,0:T(8,128)}, f32[16,720]{1,0:T(8,128)S(1)}, u32[]{:S(2)}, u32[]{:S(2)}) collective-permute-start(f32[16,720]{1,0:T(8,128)} %get-tuple-element.23), channel_id=1, source_target_pairs={{0,4},{4,8},{8,12},{12,16},{16,20},{20,24},{24,28},{28,0},{1,5},{5... | collective-permute-start | bytes 138248 | tf_op jit(solution)/shard_map/ppermute | solution.py:340
  37.7 4.8 %collective-permute-start.8 = (f32[16,720]{1,0:T(8,128)}, f32[16,720]{1,0:T(8,128)S(1)}, u32[]{:S(2)}, u32[]{:S(2)}) collective-permute-start(f32[16,720]{1,0:T(8,128)} %get-tuple-element.24), channel_id=1, source_target_pairs={{4,0},{8,4},{12,8},{16,12},{20,16},{24,20},{28,24},{0,28},{5,1},{9... | collective-permute-start | bytes 138248 | tf_op jit(solution)/shard_map/ppermute | solution.py:341
  42.4 0.6 %copy-start.5 = (f32[16,720]{1,0:T(8,128)}, f32[16,720]{1,0:T(8,128)S(1)}, u32[]{:S(2)}) copy-start(f32[16,720]{1,0:T(8,128)S(1)} %collective-permute-done.7) | copy-start | bytes 138244
  42.4 0.6 %copy-start.6 = (f32[16,720]{1,0:T(8,128)}, f32[16,720]{1,0:T(8,128)S(1)}, u32[]{:S(2)}) copy-start(f32[16,720]{1,0:T(8,128)S(1)} %collective-permute-done.8) | copy-start | bytes 138244
  42.4 0.8 %copy-start.1 = (bf16[20,1,16,720]{3,2,1,0:T(8,128)(2,1)}, bf16[20,1,16,720]{3,2,1,0:T(8,128)(2,1)S(1)}, u32[]{:S(2)}) copy-start(bf16[20,1,16,720]{3,2,1,0:T(8,128)(2,1)S(1)} %collective-permute-done.3.phigh_ref) | copy-start | bytes 1382404
  42.5 1.0 %copy-start.2 = (bf16[20,1,16,720]{3,2,1,0:T(8,128)(2,1)}, bf16[20,1,16,720]{3,2,1,0:T(8,128)(2,1)S(1)}, u32[]{:S(2)}) copy-start(bf16[20,1,16,720]{3,2,1,0:T(8,128)(2,1)S(1)} %collective-permute-done.2.plow_ref) | copy-start | bytes 1382404

commit v15 on v14

--- a/solution.py
+++ b/solution.py
@@ -138,8 +138,8 @@
     members, levels, lon_cells, lat_cells = control.shape
     radius = c_low.shape[2]
     padded, ext_cells = band_lon.shape
-    chunk = member_chunk(members)
-    steps = members // chunk
+    chunk = members
+    steps = 1
     _, sources, slots = cells.shape
     parts = -(-lat_cells // 128)
 

time: 49.1 us -> 49.8 us (1.014)
  Pallas kernels: 15.3 us -> 15.9 us
    pallas_call x1, Pallas kernels: 5.31 us -> 5.92 us  [forward_pick(): pl.pallas_call(kernel, grid=(steps,), in_specs=[field, halo, halo, field,...]
  transfers between devices with their start and end apart: 9 -> 9, of which waited for: 4 -> 4; matrix products, arithmetic and copies ran while one was open for 4% -> 4% of each run, Pallas kernels for 20% -> 21%
where the time goes in v15:
time: 49.8 us; the launch traced here: 49.5 us
  Pallas kernels  15.9 us (32%)
  starting transfers between devices  11.8 us (24%)
  blocking collectives  9.75 us (20%)
  waiting for transfers between devices  6.87 us (14%)
  local copies, waits for them, and re-layouts  3.91 us (8%)
  other arithmetic  1.2 us (2%)
    all_to_all x1, blocking collectives, local(): lax.all_to_all(lists, 'tile', split_axis=1, concat_axis=1, tiled=True)  9.75 us
    pallas_call x1, Pallas kernels, forward_pick(): pl.pallas_call(kernel, grid=(steps,), in_specs=[field, halo, halo, field,...  5.92 us
    pallas_call x1, Pallas kernels, backward_grad(): pl.pallas_call(kernel, grid=(levels, members // chunk), in_specs=[field,...  5.41 us
    ppermute x3, waiting for transfers between devices, gather_over(): lax.ppermute(values, axis, [(i, (i + shift) % count) for i in range(count)])  4.64 us
    ppermute x3, starting transfers between devices, gather_over(): lax.ppermute(values, axis, [(i, (i + shift) % count) for i in range(count)])  4.62 us
    ppermute x2, starting transfers between devices, halos(): lax.ppermute(lax.slice_in_dim(block, 0, width, axis=dim), axis, backward)  4.52 us
    ppermute x1, starting transfers between devices, local(): lax.ppermute(high_send, 'tile', [((i + 1) % count, i) for i in range(coun...  2.64 us
    pallas_call x1, Pallas kernels, spread_misfits(): pl.pallas_call(kernel, out_shape=(jax.ShapeDtypeStruct((lon_cells, lat_ce...  2.6 us
  transfers between devices with their start and end apart: 9, of which 4 were waited for; matrix products, arithmetic and copies ran while one was open for 4% of the time, Pallas kernels for 21%

profile of v15, /device:TPU:0, one launch (start us, length us, event | category | flops | bytes accessed | tf_op | source)
XLA Modules:
  0.0 49.5 jit_solution(15840026647303408864)
XLA Ops:
  0.0 0.0 copy-start.12
  0.0 0.0 copy-start
  0.0 1.5 %fusion.1 = (bf16[20,1,16,720]{3,2,1,0:T(8,128)(2,1)S(1)}, bf16[20,1,16,720]{3,2,1,0:T(8,128)(2,1)S(1)}) fusion(bf16[20,1,45,720]{3,2,1,0:T(8,128)(2,1)} %ctrl_ref.3), kind=kLoop, calls=%fused_computation.3 | loop fusion | bytes 1843200 | tf_op jit(solution)/shard_map/slice | solution.py:18
  1.6 3.4 %collective-permute-start.1 = (bf16[20,1,16,720]{3,2,1,0:T(8,128)(2,1)S(1)}, bf16[20,1,16,720]{3,2,1,0:T(8,128)(2,1)S(1)}, u32[]{:S(2)}, u32[]{:S(2)}) collective-permute-start(bf16[20,1,16,720]{3,2,1,0:T(8,128)(2,1)S(1)} %get-tuple-element.27), channel_id=1, source_target_pairs={{4,0},{8,4},{12,8},{16,12},{20,16},{24,20},{28,24},{0,28},{5,1},{9... | collective-permute-start | bytes 1382408 | tf_op jit(solution)/shard_map/ppermute | solution.py:18
  5.0 0.0 collective-permute-start
  5.0 0.0 copy-done.14
  5.0 0.5 %convert_element_type.10.lon_ref = f32[17]{0:T(128)} convert(bf16[17]{0:T(256)(128)(2,1)S(1)} %copy-done.14) | non-fusion elementwise | flops 17 | bytes 102 | tf_op jit(solution)/shard_map/convert_element_type | solution.py:84
  5.5 0.0 copy-done.15
  5.5 0.6 %convert_element_type.11.lat_ref = f32[17]{0:T(128)} convert(bf16[17]{0:T(256)(128)(2,1)S(1)} %copy-done.15) | non-fusion elementwise | flops 17 | bytes 102 | tf_op jit(solution)/shard_map/convert_element_type | solution.py:84
  6.1 0.0 copy-done.10
  6.1 0.0 copy-done.11
  6.2 2.0 %shard_map.85 = (bf16[48,80]{1,0:T(8,128)(2,1)}, bf16[720,720]{1,0:T(8,128)(2,1)}) custom-call(f32[17]{0:T(128)} %convert_element_type.10.lon_ref, f32[17]{0:T(128)} %convert_element_type.11.lat_ref), custom_call_target="tpu_custom_call" | custom-call | tf_op jit(solution)/shard_map/pallas_call | solution.py:77
  8.1 0.0 copy-done.13
  8.1 0.0 copy-done.12
  8.1 0.1 compare_select_fusion
  8.2 9.7 %all_to_all.5 = f32[3,8,256]{2,0,1:T(4,128)S(1)} all-to-all(f32[3,8,256]{2,0,1:T(4,128)S(1)} %pad_maximum_fusion), channel_id=1, replica_groups=mesh['tile'=8,'mem'=4] {'tile'}, dimensions={1} | all-to-all | bytes 49152 | tf_op jit(solution)/shard_map/all_to_all | solution.py:326
  18.0 0.0 collective-permute-done.1.high_ref
  18.0 0.0 collective-permute-done.low_ref
  18.0 0.0 copy-done
  18.0 0.0 copy-start.4
  18.0 0.1 fusion
  18.2 1.1 %collective-permute-start.3 = (bf16[20,1,16,720]{3,2,1,0:T(8,128)(2,1)S(1)}, bf16[20,1,16,720]{3,2,1,0:T(8,128)(2,1)S(1)}, u32[]{:S(2)}, u32[]{:S(2)}) collective-permute-start(bf16[20,1,16,720]{3,2,1,0:T(8,128)(2,1)S(1)} %get-tuple-element.25), channel_id=1, source_target_pairs={{4,0},{8,4},{12,8},{16,12},{20,16},{24,20},{28,24},{0,28},{5,1},{9... | collective-permute-start | bytes 1382408 | tf_op jit(solution)/shard_map/ppermute | solution.py:18
  19.3 0.0 collective-permute-start.2
  19.3 0.6 %copy.12.cells_ref.refs_4_ = f32[3,8,256]{2,1,0:T(8,128)} copy(f32[3,8,256]{2,0,1:T(4,128)S(1)} %all_to_all.5) | data formatting | bytes 49152 | tf_op jit(solution)/shard_map/optimization_barrier | solution.py:329
  19.9 0.0 copy-done.3
  19.9 0.0 copy-done.4
  19.9 5.9 %shard_map.86.refs_0_ = f32[8,256]{1,0:T(8,128)} custom-call(bf16[20,1,45,720]{3,2,1,0:T(8,128)(2,1)} %ctrl_ref.3, bf16[20,1,16,720]{3,2,1,0:T(8,128)(2,1)} %copy-done.4, bf16[20,1,16,720]{3,2,1,0:T(8,128)(2,1)} %copy-done.3, bf16[20,1,45,720]{3,2,1,0:T(8,128)(2,1)} %pert_ref.3, bf16[48,80]{1,0:T(8,128)(2,1)} %get-tuple-element.15.blon_ref, ...), custom_call_target="tpu_custom_call" | custom-call | tf_op jit(solution)/shard_map/pallas_call | solution.py:189
  25.8 3.6 %collective-permute-start.6 = (f32[8,256]{1,0:T(8,128)}, f32[8,256]{1,0:T(8,128)S(1)}, u32[]{:S(2)}, u32[]{:S(2)}) collective-permute-start(f32[8,256]{1,0:T(8,128)} %shard_map.86.refs_0_), channel_id=1, source_target_pairs={{0,3},{1,0},{2,1},{3,2},{4,7},{5,4},{6,5},{7,6},{8,11},{9,8},{10,9... | collective-permute-start | bytes 24584 | tf_op jit(solution)/shard_map/ppermute | solution.py:25
  29.4 0.0 collective-permute-start.5
  29.4 1.0 %collective-permute-start.4 = (f32[8,256]{1,0:T(8,128)}, f32[8,256]{1,0:T(8,128)S(1)}, u32[]{:S(2)}, u32[]{:S(2)}) collective-permute-start(f32[8,256]{1,0:T(8,128)} %shard_map.86.refs_0_), channel_id=1, source_target_pairs={{0,1},{1,2},{2,3},{3,0},{4,5},{5,6},{6,7},{7,4},{8,9},{9,10},{10,1... | collective-permute-start | bytes 24584 | tf_op jit(solution)/shard_map/ppermute | solution.py:25
  30.4 0.6 %collective-permute-done.6.refs_3_ = f32[8,256]{1,0:T(8,128)S(1)} collective-permute-done((f32[8,256]{1,0:T(8,128)}, f32[8,256]{1,0:T(8,128)S(1)}, u32[]{:S(2)}, u32[]{:S(2)}) %collective-permute-start.6) | collective-permute-done | bytes 8224 | tf_op jit(solution)/shard_map/ppermute | solution.py:25
  31.0 3.2 %collective-permute-done.5.refs_2_ = f32[8,256]{1,0:T(8,128)S(1)} collective-permute-done((f32[8,256]{1,0:T(8,128)}, f32[8,256]{1,0:T(8,128)S(1)}, u32[]{:S(2)}, u32[]{:S(2)}) %collective-permute-start.5) | collective-permute-done | bytes 8224 | tf_op jit(solution)/shard_map/ppermute | solution.py:25
  34.2 0.9 %collective-permute-done.4.refs_1_ = f32[8,256]{1,0:T(8,128)S(1)} collective-permute-done((f32[8,256]{1,0:T(8,128)}, f32[8,256]{1,0:T(8,128)S(1)}, u32[]{:S(2)}, u32[]{:S(2)}) %collective-permute-start.4) | collective-permute-done | bytes 8224 | tf_op jit(solution)/shard_map/ppermute | solution.py:25
  35.1 0.0 copy-done.7
  35.1 0.6 %copy-done.9 = f32[8,256]{1,0:T(8,128)} copy-done((f32[8,256]{1,0:T(8,128)}, f32[8,256]{1,0:T(8,128)S(1)}, u32[]{:S(2)}) %copy-start.9) | copy-done | bytes 8216
  35.7 2.6 %shard_map.87 = (f32[45,720]{1,0:T(8,128)}, f32[16,720]{1,0:T(8,128)}, f32[16,720]{1,0:T(8,128)}) custom-call(f32[8,256]{1,0:T(8,128)} %shard_map.86.refs_0_, f32[8,256]{1,0:T(8,128)} %copy-done.9, f32[8,256]{1,0:T(8,128)} %copy-done.8, f32[8,256]{1,0:T(8,128)} %copy-done.7, f32[3,8,256]{2,1,0:T(8,128)} %copy.12.cells_ref.refs_4_), custom_call_target="tpu_custom_call" | custom-call | tf_op jit(solution)/shard_map/pallas_call | solution.py:247
  38.3 0.0 collective-permute-start.7
  38.3 2.6 %collective-permute-start.8 = (f32[16,720]{1,0:T(8,128)}, f32[16,720]{1,0:T(8,128)S(1)}, u32[]{:S(2)}, u32[]{:S(2)}) collective-permute-start(f32[16,720]{1,0:T(8,128)} %get-tuple-element.24), channel_id=1, source_target_pairs={{4,0},{8,4},{12,8},{16,12},{20,16},{24,20},{28,24},{0,28},{5,1},{9... | collective-permute-start | bytes 138248 | tf_op jit(solution)/shard_map/ppermute | solution.py:341
  40.9 2.2 %collective-permute-done.7 = f32[16,720]{1,0:T(8,128)S(1)} collective-permute-done((f32[16,720]{1,0:T(8,128)}, f32[16,720]{1,0:T(8,128)S(1)}, u32[]{:S(2)}, u32[]{:S(2)}) %collective-permute-start.7) | collective-permute-done | bytes 46112 | tf_op jit(solution)/shard_map/ppermute | solution.py:340
  43.1 0.0 collective-permute-done.8
  43.1 0.0 collective-permute-done.3.phigh_ref
  43.1 0.0 collective-permute-done.2.plow_ref
  43.2 0.0 copy-start.2
  43.2 0.6 %copy-done.5 = f32[16,720]{1,0:T(8,128)} copy-done((f32[16,720]{1,0:T(8,128)}, f32[16,720]{1,0:T(8,128)S(1)}, u32[]{:S(2)}) %copy-start.5) | copy-done | bytes 46104
  43.7 0.0 copy-done.6
  43.8 0.2 copy-done.1
  43.9 0.2 copy-done.2
  44.1 5.4 %shard_map.88 = f32[20,45,1,720]{3,2,1,0:T(1,128)} custom-call(bf16[20,1,45,720]{3,2,1,0:T(8,128)(2,1)} %pert_ref.3, bf16[20,1,16,720]{3,2,1,0:T(8,128)(2,1)} %copy-done.2, bf16[20,1,16,720]{3,2,1,0:T(8,128)(2,1)} %copy-done.1, f32[1,45,720]{2,1,0:T(8,128)} %bitcast.5, f32[1,16,720]{2,1,0:T(8,128)} %bitcast.6, f32[1,16,720]{2,1,0:T(8,128)} %bitcast.7, ...), custom_call_target="tpu_custom_call" | custom-call | tf_op jit(solution)/shard_map/pallas_call | solution.py:291
  (17 shorter events, 0.1 us)
Async XLA Ops:
  0.0 5.0 %copy-start.14 = (bf16[17]{0:T(256)(128)(2,1)S(1)}, bf16[17]{0:T(256)(128)(2,1)}, u32[]{:S(2)}) copy-start(bf16[17]{0:T(256)(128)(2,1)} %param.10) | copy-start | bytes 106
  0.0 5.5 %copy-start.15 = (bf16[17]{0:T(256)(128)(2,1)S(1)}, bf16[17]{0:T(256)(128)(2,1)}, u32[]{:S(2)}) copy-start(bf16[17]{0:T(256)(128)(2,1)} %param.11) | copy-start | bytes 106
  0.0 6.1 %copy-start.10 = (f32[1,8,256]{2,1,0:T(8,128)S(1)}, f32[1,8,256]{2,1,0:T(8,128)}, u32[]{:S(2)}) copy-start(f32[1,8,256]{2,1,0:T(8,128)} %param.12) | copy-start | bytes 24580
  0.0 6.1 %copy-start.11 = (s32[1,8,256]{2,1,0:T(8,128)S(1)}, s32[1,8,256]{2,1,0:T(8,128)}, u32[]{:S(2)}) copy-start(s32[1,8,256]{2,1,0:T(8,128)} %param.14) | copy-start | bytes 24580
  0.0 8.1 %copy-start.13 = (s32[1,8]{1,0:T(1,128)S(1)}, s32[1,8]{1,0:T(1,128)}, u32[]{:S(2)}) copy-start(s32[1,8]{1,0:T(1,128)} %param.15) | copy-start | bytes 100
  0.0 8.1 %copy-start.12 = (f32[1,8,256]{2,1,0:T(8,128)S(1)}, f32[1,8,256]{2,1,0:T(8,128)}, u32[]{:S(2)}) copy-start(f32[1,8,256]{2,1,0:T(8,128)} %param.13) | copy-start | bytes 24580
  0.0 18.0 %copy-start = (bf16[20,1,45,720]{3,2,1,0:T(8,128)(2,1)S(1)}, bf16[20,1,45,720]{3,2,1,0:T(8,128)(2,1)}, u32[]{:S(2)}) copy-start(bf16[20,1,45,720]{3,2,1,0:T(8,128)(2,1)} %pert_ref.3) | copy-start | bytes 3888004
  1.6 16.4 %collective-permute-start.1 = (bf16[20,1,16,720]{3,2,1,0:T(8,128)(2,1)S(1)}, bf16[20,1,16,720]{3,2,1,0:T(8,128)(2,1)S(1)}, u32[]{:S(2)}, u32[]{:S(2)}) collective-permute-start(bf16[20,1,16,720]{3,2,1,0:T(8,128)(2,1)S(1)} %get-tuple-element.27), channel_id=1, source_target_pairs={{4,0},{8,4},{12,8},{16,12},{20,16},{24,20},{28,24},{0,28},{5,1},{9... | collective-permute-start | bytes 1382408 | tf_op jit(solution)/shard_map/ppermute | solution.py:18
  5.0 13.0 %collective-permute-start = (bf16[20,1,16,720]{3,2,1,0:T(8,128)(2,1)S(1)}, bf16[20,1,16,720]{3,2,1,0:T(8,128)(2,1)S(1)}, u32[]{:S(2)}, u32[]{:S(2)}) collective-permute-start(bf16[20,1,16,720]{3,2,1,0:T(8,128)(2,1)S(1)} %get-tuple-element.28), channel_id=1, source_target_pairs={{0,4},{4,8},{8,12},{12,16},{16,20},{20,24},{24,28},{28,0},{1,5},{5... | collective-permute-start | bytes 1382408 | tf_op jit(solution)/shard_map/ppermute | solution.py:15
  18.0 1.9 %copy-start.3 = (bf16[20,1,16,720]{3,2,1,0:T(8,128)(2,1)}, bf16[20,1,16,720]{3,2,1,0:T(8,128)(2,1)S(1)}, u32[]{:S(2)}) copy-start(bf16[20,1,16,720]{3,2,1,0:T(8,128)(2,1)S(1)} %collective-permute-done.1.high_ref) | copy-start | bytes 1382404
  18.0 1.9 %copy-start.4 = (bf16[20,1,16,720]{3,2,1,0:T(8,128)(2,1)}, bf16[20,1,16,720]{3,2,1,0:T(8,128)(2,1)S(1)}, u32[]{:S(2)}) copy-start(bf16[20,1,16,720]{3,2,1,0:T(8,128)(2,1)S(1)} %collective-permute-done.low_ref) | copy-start | bytes 1382404
  18.2 25.0 %collective-permute-start.3 = (bf16[20,1,16,720]{3,2,1,0:T(8,128)(2,1)S(1)}, bf16[20,1,16,720]{3,2,1,0:T(8,128)(2,1)S(1)}, u32[]{:S(2)}, u32[]{:S(2)}) collective-permute-start(bf16[20,1,16,720]{3,2,1,0:T(8,128)(2,1)S(1)} %get-tuple-element.25), channel_id=1, source_target_pairs={{4,0},{8,4},{12,8},{16,12},{20,16},{24,20},{28,24},{0,28},{5,1},{9... | collective-permute-start | bytes 1382408 | tf_op jit(solution)/shard_map/ppermute | solution.py:18
  19.3 23.9 %collective-permute-start.2 = (bf16[20,1,16,720]{3,2,1,0:T(8,128)(2,1)S(1)}, bf16[20,1,16,720]{3,2,1,0:T(8,128)(2,1)S(1)}, u32[]{:S(2)}, u32[]{:S(2)}) collective-permute-start(bf16[20,1,16,720]{3,2,1,0:T(8,128)(2,1)S(1)} %get-tuple-element.26), channel_id=1, source_target_pairs={{0,4},{4,8},{8,12},{12,16},{16,20},{20,24},{24,28},{28,0},{1,5},{5... | collective-permute-start | bytes 1382408 | tf_op jit(solution)/shard_map/ppermute | solution.py:15
  25.8 5.2 %collective-permute-start.6 = (f32[8,256]{1,0:T(8,128)}, f32[8,256]{1,0:T(8,128)S(1)}, u32[]{:S(2)}, u32[]{:S(2)}) collective-permute-start(f32[8,256]{1,0:T(8,128)} %shard_map.86.refs_0_), channel_id=1, source_target_pairs={{0,3},{1,0},{2,1},{3,2},{4,7},{5,4},{6,5},{7,6},{8,11},{9,8},{10,9... | collective-permute-start | bytes 24584 | tf_op jit(solution)/shard_map/ppermute | solution.py:25
  29.4 4.8 %collective-permute-start.5 = (f32[8,256]{1,0:T(8,128)}, f32[8,256]{1,0:T(8,128)S(1)}, u32[]{:S(2)}, u32[]{:S(2)}) collective-permute-start(f32[8,256]{1,0:T(8,128)} %shard_map.86.refs_0_), channel_id=1, source_target_pairs={{0,2},{1,3},{2,0},{3,1},{4,6},{5,7},{6,4},{7,5},{8,10},{9,11},{10,... | collective-permute-start | bytes 24584 | tf_op jit(solution)/shard_map/ppermute | solution.py:25
  29.4 5.7 %collective-permute-start.4 = (f32[8,256]{1,0:T(8,128)}, f32[8,256]{1,0:T(8,128)S(1)}, u32[]{:S(2)}, u32[]{:S(2)}) collective-permute-start(f32[8,256]{1,0:T(8,128)} %shard_map.86.refs_0_), channel_id=1, source_target_pairs={{0,1},{1,2},{2,3},{3,0},{4,5},{5,6},{6,7},{7,4},{8,9},{9,10},{10,1... | collective-permute-start | bytes 24584 | tf_op jit(solution)/shard_map/ppermute | solution.py:25
  31.0 4.1 %copy-start.7 = (f32[8,256]{1,0:T(8,128)}, f32[8,256]{1,0:T(8,128)S(1)}, u32[]{:S(2)}) copy-start(f32[8,256]{1,0:T(8,128)S(1)} %collective-permute-done.6.refs_3_) | copy-start | bytes 24580
  34.2 0.9 %copy-start.8 = (f32[8,256]{1,0:T(8,128)}, f32[8,256]{1,0:T(8,128)S(1)}, u32[]{:S(2)}) copy-start(f32[8,256]{1,0:T(8,128)S(1)} %collective-permute-done.5.refs_2_) | copy-start | bytes 24580
  35.1 0.6 %copy-start.9 = (f32[8,256]{1,0:T(8,128)}, f32[8,256]{1,0:T(8,128)S(1)}, u32[]{:S(2)}) copy-start(f32[8,256]{1,0:T(8,128)S(1)} %collective-permute-done.4.refs_1_) | copy-start | bytes 24580
  38.3 4.9 %collective-permute-start.7 = (f32[16,720]{1,0:T(8,128)}, f32[16,720]{1,0:T(8,128)S(1)}, u32[]{:S(2)}, u32[]{:S(2)}) collective-permute-start(f32[16,720]{1,0:T(8,128)} %get-tuple-element.23), channel_id=1, source_target_pairs={{0,4},{4,8},{8,12},{12,16},{16,20},{20,24},{24,28},{28,0},{1,5},{5... | collective-permute-start | bytes 138248 | tf_op jit(solution)/shard_map/ppermute | solution.py:340
  38.3 4.9 %collective-permute-start.8 = (f32[16,720]{1,0:T(8,128)}, f32[16,720]{1,0:T(8,128)S(1)}, u32[]{:S(2)}, u32[]{:S(2)}) collective-permute-start(f32[16,720]{1,0:T(8,128)} %get-tuple-element.24), channel_id=1, source_target_pairs={{4,0},{8,4},{12,8},{16,12},{20,16},{24,20},{28,24},{0,28},{5,1},{9... | collective-permute-start | bytes 138248 | tf_op jit(solution)/shard_map/ppermute | solution.py:341
  43.1 0.6 %copy-start.5 = (f32[16,720]{1,0:T(8,128)}, f32[16,720]{1,0:T(8,128)S(1)}, u32[]{:S(2)}) copy-start(f32[16,720]{1,0:T(8,128)S(1)} %collective-permute-done.7) | copy-start | bytes 138244
  43.1 0.6 %copy-start.6 = (f32[16,720]{1,0:T(8,128)}, f32[16,720]{1,0:T(8,128)S(1)}, u32[]{:S(2)}) copy-start(f32[16,720]{1,0:T(8,128)S(1)} %collective-permute-done.8) | copy-start | bytes 138244
  43.1 0.8 %copy-start.1 = (bf16[20,1,16,720]{3,2,1,0:T(8,128)(2,1)}, bf16[20,1,16,720]{3,2,1,0:T(8,128)(2,1)S(1)}, u32[]{:S(2)}) copy-start(bf16[20,1,16,720]{3,2,1,0:T(8,128)(2,1)S(1)} %collective-permute-done.3.phigh_ref) | copy-start | bytes 1382404
  43.2 1.0 %copy-start.2 = (bf16[20,1,16,720]{3,2,1,0:T(8,128)(2,1)}, bf16[20,1,16,720]{3,2,1,0:T(8,128)(2,1)S(1)}, u32[]{:S(2)}) copy-start(bf16[20,1,16,720]{3,2,1,0:T(8,128)(2,1)S(1)} %collective-permute-done.2.plow_ref) | copy-start | bytes 1382404

commit v16 on v14

--- a/solution.py
+++ b/solution.py
@@ -226,15 +226,25 @@
             misfit = lists_ref[1, row:row + 1, :] * (
                 at_cells[row:row + 1, :] - lists_ref[0, row:row + 1, :]
             )
-            keys, onehot = cell_keys(lists_ref[2, row:row + 1, :], padded, lat_cells)
-            for piece in split3(misfit):
-                weighted = jnp.where(key_ids == keys, piece.astype(jnp.float32), 0.0)
-                folded = folded + lax.dot_general(
-                    weighted.astype(jnp.bfloat16),
-                    onehot,
-                    (((1,), (1,)), ((), ())),
-                    preferred_element_type=jnp.float32,
-                )
+            keys, _ = cell_keys(lists_ref[2, row:row + 1, :], padded, lat_cells)
+            cells_col = jnp.transpose(
+                jnp.broadcast_to(lists_ref[2, row:row + 1, :], (8, slots))
+            )[:, 0:1]
+            rows_col = jnp.floor((cells_col + 0.5) / lat_cells)
+            lanes_col = (cells_col - rows_col * lat_cells).astype(jnp.int32) % 128
+            lane_ids = lax.broadcasted_iota(jnp.int32, (slots, 128), 1)
+            onehot_t = jnp.where(lane_ids == lanes_col, 1.0, 0.0).astype(jnp.bfloat16)
+            weighted = jnp.concatenate(
+                [
+                    jnp.where(key_ids == keys, piece.astype(jnp.float32), 0.0).astype(
+                        jnp.bfloat16
+                    )
+                    for piece in split3(misfit)
+                ],
+                axis=1,
+            )
+            stacked = jnp.concatenate([onehot_t, onehot_t, onehot_t], axis=0)
+            folded = folded + jnp.dot(weighted, stacked, preferred_element_type=jnp.float32)
         for part in range(parts):
             width = min(128, lat_cells - part * 128)
             fold_ref[:, part * 128:part * 128 + width] = folded[

time: 49.1 us -> 49.8 us (1.014)
  Pallas kernels: 15.3 us -> 16 us
    pallas_call x1, Pallas kernels: 2.6 us -> 3.27 us  [spread_misfits(): pl.pallas_call(kernel, out_shape=(jax.ShapeDtypeStruct((lon_cells, lat_ce...]
  transfers between devices with their start and end apart: 9 -> 9, of which waited for: 4 -> 4; matrix products, arithmetic and copies ran while one was open for 4% -> 4% of each run, Pallas kernels for 20% -> 21%
where the time goes in v16:
time: 49.8 us; the launch traced here: 49.5 us
  Pallas kernels  16 us (32%)
  starting transfers between devices  11.8 us (24%)
  blocking collectives  9.75 us (20%)
  waiting for transfers between devices  6.8 us (14%)
  local copies, waits for them, and re-layouts  3.91 us (8%)
  other arithmetic  1.2 us (2%)
    all_to_all x1, blocking collectives, local(): lax.all_to_all(lists, 'tile', split_axis=1, concat_axis=1, tiled=True)  9.75 us
    pallas_call x1, Pallas kernels, backward_grad(): pl.pallas_call(kernel, grid=(levels, members // chunk), in_specs=[field,...  5.4 us
    pallas_call x1, Pallas kernels, forward_pick(): pl.pallas_call(kernel, grid=(steps,), in_specs=[field, halo, halo, field,...  5.31 us
    ppermute x3, waiting for transfers between devices, gather_over(): lax.ppermute(values, axis, [(i, (i + shift) % count) for i in range(count)])  4.64 us
    ppermute x3, starting transfers between devices, gather_over(): lax.ppermute(values, axis, [(i, (i + shift) % count) for i in range(count)])  4.62 us
    ppermute x2, starting transfers between devices, halos(): lax.ppermute(lax.slice_in_dim(block, 0, width, axis=dim), axis, backward)  4.52 us
    pallas_call x1, Pallas kernels, spread_misfits(): pl.pallas_call(kernel, out_shape=(jax.ShapeDtypeStruct((lon_cells, lat_ce...  3.27 us
    ppermute x1, starting transfers between devices, local(): lax.ppermute(high_send, 'tile', [((i + 1) % count, i) for i in range(coun...  2.64 us
  transfers between devices with their start and end apart: 9, of which 4 were waited for; matrix products, arithmetic and copies ran while one was open for 4% of the time, Pallas kernels for 21%

profile of v16, /device:TPU:0, one launch (start us, length us, event | category | flops | bytes accessed | tf_op | source)
XLA Modules:
  0.0 49.5 jit_solution(9170405954795952953)
XLA Ops:
  0.0 0.0 copy-start.12
  0.0 0.0 copy-start
  0.0 1.5 %fusion.1 = (bf16[20,1,16,720]{3,2,1,0:T(8,128)(2,1)S(1)}, bf16[20,1,16,720]{3,2,1,0:T(8,128)(2,1)S(1)}) fusion(bf16[20,1,45,720]{3,2,1,0:T(8,128)(2,1)} %ctrl_ref.3), kind=kLoop, calls=%fused_computation.3 | loop fusion | bytes 1843200 | tf_op jit(solution)/shard_map/slice | solution.py:18
  1.6 3.4 %collective-permute-start.1 = (bf16[20,1,16,720]{3,2,1,0:T(8,128)(2,1)S(1)}, bf16[20,1,16,720]{3,2,1,0:T(8,128)(2,1)S(1)}, u32[]{:S(2)}, u32[]{:S(2)}) collective-permute-start(bf16[20,1,16,720]{3,2,1,0:T(8,128)(2,1)S(1)} %get-tuple-element.27), channel_id=1, source_target_pairs={{4,0},{8,4},{12,8},{16,12},{20,16},{24,20},{28,24},{0,28},{5,1},{9... | collective-permute-start | bytes 1382408 | tf_op jit(solution)/shard_map/ppermute | solution.py:18
  5.0 0.0 collective-permute-start
  5.0 0.0 copy-done.14
  5.0 0.5 %convert_element_type.10.lon_ref = f32[17]{0:T(128)} convert(bf16[17]{0:T(256)(128)(2,1)S(1)} %copy-done.14) | non-fusion elementwise | flops 17 | bytes 102 | tf_op jit(solution)/shard_map/convert_element_type | solution.py:84
  5.5 0.0 copy-done.15
  5.5 0.6 %convert_element_type.11.lat_ref = f32[17]{0:T(128)} convert(bf16[17]{0:T(256)(128)(2,1)S(1)} %copy-done.15) | non-fusion elementwise | flops 17 | bytes 102 | tf_op jit(solution)/shard_map/convert_element_type | solution.py:84
  6.1 0.0 copy-done.10
  6.1 0.0 copy-done.11
  6.2 2.0 %shard_map.85 = (bf16[48,80]{1,0:T(8,128)(2,1)}, bf16[720,720]{1,0:T(8,128)(2,1)}) custom-call(f32[17]{0:T(128)} %convert_element_type.10.lon_ref, f32[17]{0:T(128)} %convert_element_type.11.lat_ref), custom_call_target="tpu_custom_call" | custom-call | tf_op jit(solution)/shard_map/pallas_call | solution.py:77
  8.1 0.0 copy-done.13
  8.1 0.0 copy-done.12
  8.1 0.1 compare_select_fusion
  8.2 9.7 %all_to_all.5 = f32[3,8,256]{2,0,1:T(4,128)S(1)} all-to-all(f32[3,8,256]{2,0,1:T(4,128)S(1)} %pad_maximum_fusion), channel_id=1, replica_groups=mesh['tile'=8,'mem'=4] {'tile'}, dimensions={1} | all-to-all | bytes 49152 | tf_op jit(solution)/shard_map/all_to_all | solution.py:336
  18.0 0.0 collective-permute-done.1.high_ref
  18.0 0.0 collective-permute-done.low_ref
  18.0 0.0 copy-done
  18.0 0.0 copy-start.4
  18.0 0.1 fusion
  18.2 1.1 %collective-permute-start.3 = (bf16[20,1,16,720]{3,2,1,0:T(8,128)(2,1)S(1)}, bf16[20,1,16,720]{3,2,1,0:T(8,128)(2,1)S(1)}, u32[]{:S(2)}, u32[]{:S(2)}) collective-permute-start(bf16[20,1,16,720]{3,2,1,0:T(8,128)(2,1)S(1)} %get-tuple-element.25), channel_id=1, source_target_pairs={{4,0},{8,4},{12,8},{16,12},{20,16},{24,20},{28,24},{0,28},{5,1},{9... | collective-permute-start | bytes 1382408 | tf_op jit(solution)/shard_map/ppermute | solution.py:18
  19.3 0.0 collective-permute-start.2
  19.3 0.6 %copy.12.cells_ref.refs_4_ = f32[3,8,256]{2,1,0:T(8,128)} copy(f32[3,8,256]{2,0,1:T(4,128)S(1)} %all_to_all.5) | data formatting | bytes 49152 | tf_op jit(solution)/shard_map/optimization_barrier | solution.py:339
  19.9 0.0 copy-done.3
  19.9 0.0 copy-done.4
  19.9 5.3 %shard_map.86.refs_0_ = f32[8,256]{1,0:T(8,128)} custom-call(bf16[20,1,45,720]{3,2,1,0:T(8,128)(2,1)} %ctrl_ref.3, bf16[20,1,16,720]{3,2,1,0:T(8,128)(2,1)} %copy-done.4, bf16[20,1,16,720]{3,2,1,0:T(8,128)(2,1)} %copy-done.3, bf16[20,1,45,720]{3,2,1,0:T(8,128)(2,1)} %pert_ref.3, bf16[48,80]{1,0:T(8,128)(2,1)} %get-tuple-element.15.blon_ref, ...), custom_call_target="tpu_custom_call" | custom-call | tf_op jit(solution)/shard_map/pallas_call | solution.py:189
  25.2 3.6 %collective-permute-start.6 = (f32[8,256]{1,0:T(8,128)}, f32[8,256]{1,0:T(8,128)S(1)}, u32[]{:S(2)}, u32[]{:S(2)}) collective-permute-start(f32[8,256]{1,0:T(8,128)} %shard_map.86.refs_0_), channel_id=1, source_target_pairs={{0,3},{1,0},{2,1},{3,2},{4,7},{5,4},{6,5},{7,6},{8,11},{9,8},{10,9... | collective-permute-start | bytes 24584 | tf_op jit(solution)/shard_map/ppermute | solution.py:25
  28.8 0.0 collective-permute-start.5
  28.8 1.0 %collective-permute-start.4 = (f32[8,256]{1,0:T(8,128)}, f32[8,256]{1,0:T(8,128)S(1)}, u32[]{:S(2)}, u32[]{:S(2)}) collective-permute-start(f32[8,256]{1,0:T(8,128)} %shard_map.86.refs_0_), channel_id=1, source_target_pairs={{0,1},{1,2},{2,3},{3,0},{4,5},{5,6},{6,7},{7,4},{8,9},{9,10},{10,1... | collective-permute-start | bytes 24584 | tf_op jit(solution)/shard_map/ppermute | solution.py:25
  29.8 0.6 %collective-permute-done.6.refs_3_ = f32[8,256]{1,0:T(8,128)S(1)} collective-permute-done((f32[8,256]{1,0:T(8,128)}, f32[8,256]{1,0:T(8,128)S(1)}, u32[]{:S(2)}, u32[]{:S(2)}) %collective-permute-start.6) | collective-permute-done | bytes 8224 | tf_op jit(solution)/shard_map/ppermute | solution.py:25
  30.4 3.2 %collective-permute-done.5.refs_2_ = f32[8,256]{1,0:T(8,128)S(1)} collective-permute-done((f32[8,256]{1,0:T(8,128)}, f32[8,256]{1,0:T(8,128)S(1)}, u32[]{:S(2)}, u32[]{:S(2)}) %collective-permute-start.5) | collective-permute-done | bytes 8224 | tf_op jit(solution)/shard_map/ppermute | solution.py:25
  33.6 0.9 %collective-permute-done.4.refs_1_ = f32[8,256]{1,0:T(8,128)S(1)} collective-permute-done((f32[8,256]{1,0:T(8,128)}, f32[8,256]{1,0:T(8,128)S(1)}, u32[]{:S(2)}, u32[]{:S(2)}) %collective-permute-start.4) | collective-permute-done | bytes 8224 | tf_op jit(solution)/shard_map/ppermute | solution.py:25
  34.5 0.0 copy-done.7
  34.5 0.0 copy-done.8
  34.5 0.6 %copy-done.9 = f32[8,256]{1,0:T(8,128)} copy-done((f32[8,256]{1,0:T(8,128)}, f32[8,256]{1,0:T(8,128)S(1)}, u32[]{:S(2)}) %copy-start.9) | copy-done | bytes 8216
  35.1 3.3 %shard_map.87 = (f32[45,720]{1,0:T(8,128)}, f32[16,720]{1,0:T(8,128)}, f32[16,720]{1,0:T(8,128)}) custom-call(f32[8,256]{1,0:T(8,128)} %shard_map.86.refs_0_, f32[8,256]{1,0:T(8,128)} %copy-done.9, f32[8,256]{1,0:T(8,128)} %copy-done.8, f32[8,256]{1,0:T(8,128)} %copy-done.7, f32[3,8,256]{2,1,0:T(8,128)} %copy.12.cells_ref.refs_4_), custom_call_target="tpu_custom_call" | custom-call | tf_op jit(solution)/shard_map/pallas_call | solution.py:257
  38.3 0.0 collective-permute-start.7
  38.3 2.6 %collective-permute-start.8 = (f32[16,720]{1,0:T(8,128)}, f32[16,720]{1,0:T(8,128)S(1)}, u32[]{:S(2)}, u32[]{:S(2)}) collective-permute-start(f32[16,720]{1,0:T(8,128)} %get-tuple-element.24), channel_id=1, source_target_pairs={{4,0},{8,4},{12,8},{16,12},{20,16},{24,20},{28,24},{0,28},{5,1},{9... | collective-permute-start | bytes 138248 | tf_op jit(solution)/shard_map/ppermute | solution.py:351
  41.0 2.1 %collective-permute-done.7 = f32[16,720]{1,0:T(8,128)S(1)} collective-permute-done((f32[16,720]{1,0:T(8,128)}, f32[16,720]{1,0:T(8,128)S(1)}, u32[]{:S(2)}, u32[]{:S(2)}) %collective-permute-start.7) | collective-permute-done | bytes 46112 | tf_op jit(solution)/shard_map/ppermute | solution.py:350
  43.1 0.0 collective-permute-done.8
  43.1 0.0 collective-permute-done.3.phigh_ref
  43.1 0.0 collective-permute-done.2.plow_ref
  43.2 0.6 %copy-done.5 = f32[16,720]{1,0:T(8,128)} copy-done((f32[16,720]{1,0:T(8,128)}, f32[16,720]{1,0:T(8,128)S(1)}, u32[]{:S(2)}) %copy-start.5) | copy-done | bytes 46104
  43.7 0.0 copy-done.6
  43.7 0.2 copy-done.1
  43.9 0.2 copy-done.2
  44.1 5.4 %shard_map.88 = f32[20,45,1,720]{3,2,1,0:T(1,128)} custom-call(bf16[20,1,45,720]{3,2,1,0:T(8,128)(2,1)} %pert_ref.3, bf16[20,1,16,720]{3,2,1,0:T(8,128)(2,1)} %copy-done.2, bf16[20,1,16,720]{3,2,1,0:T(8,128)(2,1)} %copy-done.1, f32[1,45,720]{2,1,0:T(8,128)} %bitcast.5, f32[1,16,720]{2,1,0:T(8,128)} %bitcast.6, f32[1,16,720]{2,1,0:T(8,128)} %bitcast.7, ...), custom_call_target="tpu_custom_call" | custom-call | tf_op jit(solution)/shard_map/pallas_call | solution.py:301
  (17 shorter events, 0.1 us)
Async XLA Ops:
  0.0 5.0 %copy-start.14 = (bf16[17]{0:T(256)(128)(2,1)S(1)}, bf16[17]{0:T(256)(128)(2,1)}, u32[]{:S(2)}) copy-start(bf16[17]{0:T(256)(128)(2,1)} %param.10) | copy-start | bytes 106
  0.0 5.5 %copy-start.15 = (bf16[17]{0:T(256)(128)(2,1)S(1)}, bf16[17]{0:T(256)(128)(2,1)}, u32[]{:S(2)}) copy-start(bf16[17]{0:T(256)(128)(2,1)} %param.11) | copy-start | bytes 106
  0.0 6.1 %copy-start.10 = (f32[1,8,256]{2,1,0:T(8,128)S(1)}, f32[1,8,256]{2,1,0:T(8,128)}, u32[]{:S(2)}) copy-start(f32[1,8,256]{2,1,0:T(8,128)} %param.12) | copy-start | bytes 24580
  0.0 6.1 %copy-start.11 = (s32[1,8,256]{2,1,0:T(8,128)S(1)}, s32[1,8,256]{2,1,0:T(8,128)}, u32[]{:S(2)}) copy-start(s32[1,8,256]{2,1,0:T(8,128)} %param.14) | copy-start | bytes 24580
  0.0 8.1 %copy-start.13 = (s32[1,8]{1,0:T(1,128)S(1)}, s32[1,8]{1,0:T(1,128)}, u32[]{:S(2)}) copy-start(s32[1,8]{1,0:T(1,128)} %param.15) | copy-start | bytes 100
  0.0 8.1 %copy-start.12 = (f32[1,8,256]{2,1,0:T(8,128)S(1)}, f32[1,8,256]{2,1,0:T(8,128)}, u32[]{:S(2)}) copy-start(f32[1,8,256]{2,1,0:T(8,128)} %param.13) | copy-start | bytes 24580
  0.0 18.0 %copy-start = (bf16[20,1,45,720]{3,2,1,0:T(8,128)(2,1)S(1)}, bf16[20,1,45,720]{3,2,1,0:T(8,128)(2,1)}, u32[]{:S(2)}) copy-start(bf16[20,1,45,720]{3,2,1,0:T(8,128)(2,1)} %pert_ref.3) | copy-start | bytes 3888004
  1.6 16.4 %collective-permute-start.1 = (bf16[20,1,16,720]{3,2,1,0:T(8,128)(2,1)S(1)}, bf16[20,1,16,720]{3,2,1,0:T(8,128)(2,1)S(1)}, u32[]{:S(2)}, u32[]{:S(2)}) collective-permute-start(bf16[20,1,16,720]{3,2,1,0:T(8,128)(2,1)S(1)} %get-tuple-element.27), channel_id=1, source_target_pairs={{4,0},{8,4},{12,8},{16,12},{20,16},{24,20},{28,24},{0,28},{5,1},{9... | collective-permute-start | bytes 1382408 | tf_op jit(solution)/shard_map/ppermute | solution.py:18
  5.0 13.0 %collective-permute-start = (bf16[20,1,16,720]{3,2,1,0:T(8,128)(2,1)S(1)}, bf16[20,1,16,720]{3,2,1,0:T(8,128)(2,1)S(1)}, u32[]{:S(2)}, u32[]{:S(2)}) collective-permute-start(bf16[20,1,16,720]{3,2,1,0:T(8,128)(2,1)S(1)} %get-tuple-element.28), channel_id=1, source_target_pairs={{0,4},{4,8},{8,12},{12,16},{16,20},{20,24},{24,28},{28,0},{1,5},{5... | collective-permute-start | bytes 1382408 | tf_op jit(solution)/shard_map/ppermute | solution.py:15
  18.0 1.9 %copy-start.3 = (bf16[20,1,16,720]{3,2,1,0:T(8,128)(2,1)}, bf16[20,1,16,720]{3,2,1,0:T(8,128)(2,1)S(1)}, u32[]{:S(2)}) copy-start(bf16[20,1,16,720]{3,2,1,0:T(8,128)(2,1)S(1)} %collective-permute-done.1.high_ref) | copy-start | bytes 1382404
  18.0 1.9 %copy-start.4 = (bf16[20,1,16,720]{3,2,1,0:T(8,128)(2,1)}, bf16[20,1,16,720]{3,2,1,0:T(8,128)(2,1)S(1)}, u32[]{:S(2)}) copy-start(bf16[20,1,16,720]{3,2,1,0:T(8,128)(2,1)S(1)} %collective-permute-done.low_ref) | copy-start | bytes 1382404
  18.2 25.0 %collective-permute-start.3 = (bf16[20,1,16,720]{3,2,1,0:T(8,128)(2,1)S(1)}, bf16[20,1,16,720]{3,2,1,0:T(8,128)(2,1)S(1)}, u32[]{:S(2)}, u32[]{:S(2)}) collective-permute-start(bf16[20,1,16,720]{3,2,1,0:T(8,128)(2,1)S(1)} %get-tuple-element.25), channel_id=1, source_target_pairs={{4,0},{8,4},{12,8},{16,12},{20,16},{24,20},{28,24},{0,28},{5,1},{9... | collective-permute-start | bytes 1382408 | tf_op jit(solution)/shard_map/ppermute | solution.py:18
  19.3 23.9 %collective-permute-start.2 = (bf16[20,1,16,720]{3,2,1,0:T(8,128)(2,1)S(1)}, bf16[20,1,16,720]{3,2,1,0:T(8,128)(2,1)S(1)}, u32[]{:S(2)}, u32[]{:S(2)}) collective-permute-start(bf16[20,1,16,720]{3,2,1,0:T(8,128)(2,1)S(1)} %get-tuple-element.26), channel_id=1, source_target_pairs={{0,4},{4,8},{8,12},{12,16},{16,20},{20,24},{24,28},{28,0},{1,5},{5... | collective-permute-start | bytes 1382408 | tf_op jit(solution)/shard_map/ppermute | solution.py:15
  25.2 5.2 %collective-permute-start.6 = (f32[8,256]{1,0:T(8,128)}, f32[8,256]{1,0:T(8,128)S(1)}, u32[]{:S(2)}, u32[]{:S(2)}) collective-permute-start(f32[8,256]{1,0:T(8,128)} %shard_map.86.refs_0_), channel_id=1, source_target_pairs={{0,3},{1,0},{2,1},{3,2},{4,7},{5,4},{6,5},{7,6},{8,11},{9,8},{10,9... | collective-permute-start | bytes 24584 | tf_op jit(solution)/shard_map/ppermute | solution.py:25
  28.8 4.8 %collective-permute-start.5 = (f32[8,256]{1,0:T(8,128)}, f32[8,256]{1,0:T(8,128)S(1)}, u32[]{:S(2)}, u32[]{:S(2)}) collective-permute-start(f32[8,256]{1,0:T(8,128)} %shard_map.86.refs_0_), channel_id=1, source_target_pairs={{0,2},{1,3},{2,0},{3,1},{4,6},{5,7},{6,4},{7,5},{8,10},{9,11},{10,... | collective-permute-start | bytes 24584 | tf_op jit(solution)/shard_map/ppermute | solution.py:25
  28.8 5.7 %collective-permute-start.4 = (f32[8,256]{1,0:T(8,128)}, f32[8,256]{1,0:T(8,128)S(1)}, u32[]{:S(2)}, u32[]{:S(2)}) collective-permute-start(f32[8,256]{1,0:T(8,128)} %shard_map.86.refs_0_), channel_id=1, source_target_pairs={{0,1},{1,2},{2,3},{3,0},{4,5},{5,6},{6,7},{7,4},{8,9},{9,10},{10,1... | collective-permute-start | bytes 24584 | tf_op jit(solution)/shard_map/ppermute | solution.py:25
  30.4 4.1 %copy-start.7 = (f32[8,256]{1,0:T(8,128)}, f32[8,256]{1,0:T(8,128)S(1)}, u32[]{:S(2)}) copy-start(f32[8,256]{1,0:T(8,128)S(1)} %collective-permute-done.6.refs_3_) | copy-start | bytes 24580
  33.5 0.9 %copy-start.8 = (f32[8,256]{1,0:T(8,128)}, f32[8,256]{1,0:T(8,128)S(1)}, u32[]{:S(2)}) copy-start(f32[8,256]{1,0:T(8,128)S(1)} %collective-permute-done.5.refs_2_) | copy-start | bytes 24580
  34.5 0.6 %copy-start.9 = (f32[8,256]{1,0:T(8,128)}, f32[8,256]{1,0:T(8,128)S(1)}, u32[]{:S(2)}) copy-start(f32[8,256]{1,0:T(8,128)S(1)} %collective-permute-done.4.refs_1_) | copy-start | bytes 24580
  38.3 4.8 %collective-permute-start.7 = (f32[16,720]{1,0:T(8,128)}, f32[16,720]{1,0:T(8,128)S(1)}, u32[]{:S(2)}, u32[]{:S(2)}) collective-permute-start(f32[16,720]{1,0:T(8,128)} %get-tuple-element.23), channel_id=1, source_target_pairs={{0,4},{4,8},{8,12},{12,16},{16,20},{20,24},{24,28},{28,0},{1,5},{5... | collective-permute-start | bytes 138248 | tf_op jit(solution)/shard_map/ppermute | solution.py:350
  38.3 4.8 %collective-permute-start.8 = (f32[16,720]{1,0:T(8,128)}, f32[16,720]{1,0:T(8,128)S(1)}, u32[]{:S(2)}, u32[]{:S(2)}) collective-permute-start(f32[16,720]{1,0:T(8,128)} %get-tuple-element.24), channel_id=1, source_target_pairs={{4,0},{8,4},{12,8},{16,12},{20,16},{24,20},{28,24},{0,28},{5,1},{9... | collective-permute-start | bytes 138248 | tf_op jit(solution)/shard_map/ppermute | solution.py:351
  43.1 0.6 %copy-start.5 = (f32[16,720]{1,0:T(8,128)}, f32[16,720]{1,0:T(8,128)S(1)}, u32[]{:S(2)}) copy-start(f32[16,720]{1,0:T(8,128)S(1)} %collective-permute-done.7) | copy-start | bytes 138244
  43.1 0.6 %copy-start.6 = (f32[16,720]{1,0:T(8,128)}, f32[16,720]{1,0:T(8,128)S(1)}, u32[]{:S(2)}) copy-start(f32[16,720]{1,0:T(8,128)S(1)} %collective-permute-done.8) | copy-start | bytes 138244
  43.1 0.8 %copy-start.1 = (bf16[20,1,16,720]{3,2,1,0:T(8,128)(2,1)}, bf16[20,1,16,720]{3,2,1,0:T(8,128)(2,1)S(1)}, u32[]{:S(2)}) copy-start(bf16[20,1,16,720]{3,2,1,0:T(8,128)(2,1)S(1)} %collective-permute-done.3.phigh_ref) | copy-start | bytes 1382404
  43.1 1.0 %copy-start.2 = (bf16[20,1,16,720]{3,2,1,0:T(8,128)(2,1)}, bf16[20,1,16,720]{3,2,1,0:T(8,128)(2,1)S(1)}, u32[]{:S(2)}) copy-start(bf16[20,1,16,720]{3,2,1,0:T(8,128)(2,1)S(1)} %collective-permute-done.2.plow_ref) | copy-start | bytes 1382404

commit v17 on v14

--- a/solution.py
+++ b/solution.py
@@ -140,7 +140,7 @@
     padded, ext_cells = band_lon.shape
     chunk = member_chunk(members)
     steps = members // chunk
-    _, sources, slots = cells.shape
+    sources, _, slots = cells.shape
     parts = -(-lat_cells // 128)
 
     def kernel(ctrl_ref, low_ref, high_ref, pert_ref, blon_ref, blat_ref, cells_ref, out_ref,
@@ -175,7 +175,7 @@
             pieces = split3(fold_ref[...])
             key_ids = lax.broadcasted_iota(jnp.int32, (parts * padded, slots), 0)
             for row in range(sources):
-                keys, onehot = cell_keys(cells_ref[2, row:row + 1, :], padded, lat_cells)
+                keys, onehot = cell_keys(cells_ref[row, 2:3, :], padded, lat_cells)
                 at_keys = jnp.dot(pieces[0], onehot, preferred_element_type=jnp.float32)
                 at_keys = at_keys + jnp.dot(pieces[1], onehot, preferred_element_type=jnp.float32)
                 at_keys = at_keys + jnp.dot(pieces[2], onehot, preferred_element_type=jnp.float32)
@@ -211,7 +211,7 @@
 
 
 def spread_misfits(partials, lists, lon_cells, lat_cells, radius, padded):
-    _, sources, slots = lists.shape
+    sources, _, slots = lists.shape
     parts = -(-lat_cells // 128)
 
     def kernel(*refs):
@@ -223,10 +223,10 @@
         key_ids = lax.broadcasted_iota(jnp.int32, (parts * padded, slots), 0)
         folded = jnp.zeros((parts * padded, 128), jnp.float32)
         for row in range(sources):
-            misfit = lists_ref[1, row:row + 1, :] * (
-                at_cells[row:row + 1, :] - lists_ref[0, row:row + 1, :]
+            misfit = lists_ref[row, 1:2, :] * (
+                at_cells[row:row + 1, :] - lists_ref[row, 0:1, :]
             )
-            keys, onehot = cell_keys(lists_ref[2, row:row + 1, :], padded, lat_cells)
+            keys, onehot = cell_keys(lists_ref[row, 2:3, :], padded, lat_cells)
             for piece in split3(misfit):
                 weighted = jnp.where(key_ids == keys, piece.astype(jnp.float32), 0.0)
                 folded = folded + lax.dot_general(
@@ -321,9 +321,9 @@
 
     slot_ids = lax.broadcasted_iota(jnp.int32, innov.shape, 2)
     weights = jnp.where(slot_ids < counts[:, :, None], inv_var, 0.0)
-    lists = jnp.concatenate([innov, weights, cell_index.astype(jnp.float32)])
+    lists = jnp.stack([innov[0], weights[0], cell_index[0].astype(jnp.float32)], axis=1)
     lists = lax.optimization_barrier((lists, band_lon, band_lat))[0]
-    received = lax.all_to_all(lists, "tile", split_axis=1, concat_axis=1, tiled=True)
+    received = lax.all_to_all(lists, "tile", split_axis=0, concat_axis=0, tiled=True)
 
     c_low, c_high = halos(control, "tile", 2, radius)
     c_low, c_high, received = lax.optimization_barrier((c_low, c_high, received))

time: 49.1 us -> 48.6 us (0.990)
  local copies, waits for them, and re-layouts: 3.91 us -> 3.29 us
    optimization_barrier x1 -> x0, local copies, waits for them, and re-layouts: 0.61 us -> none  [local(): lax.optimization_barrier((c_low, c_high, received))]
    unnamed x33 -> x32, local copies, waits for them, and re-layouts: 1.63 us -> 1.61 us
  transfers between devices with their start and end apart: 9 -> 9, of which waited for: 4 -> 4; matrix products, arithmetic and copies ran while one was open for 4% -> 2% of each run, Pallas kernels for 20% -> 21%
where the time goes in v17:
time: 48.6 us; the launch traced here: 48.3 us
  Pallas kernels  15.3 us (31%)
  starting transfers between devices  11.8 us (24%)
  blocking collectives  9.92 us (20%)
  waiting for transfers between devices  6.73 us (14%)
  local copies, waits for them, and re-layouts  3.29 us (7%)
  other arithmetic  1.16 us (2%)
    all_to_all x1, blocking collectives, local(): lax.all_to_all(lists, 'tile', split_axis=0, concat_axis=0, tiled=True)  9.92 us
    pallas_call x1, Pallas kernels, backward_grad(): pl.pallas_call(kernel, grid=(levels, members // chunk), in_specs=[field,...  5.41 us
    pallas_call x1, Pallas kernels, forward_pick(): pl.pallas_call(kernel, grid=(steps,), in_specs=[field, halo, halo, field,...  5.32 us
    ppermute x3, waiting for transfers between devices, gather_over(): lax.ppermute(values, axis, [(i, (i + shift) % count) for i in range(count)])  4.64 us
    ppermute x3, starting transfers between devices, gather_over(): lax.ppermute(values, axis, [(i, (i + shift) % count) for i in range(count)])  4.62 us
    ppermute x2, starting transfers between devices, halos(): lax.ppermute(lax.slice_in_dim(block, 0, width, axis=dim), axis, backward)  4.52 us
    ppermute x1, starting transfers between devices, local(): lax.ppermute(high_send, 'tile', [((i + 1) % count, i) for i in range(coun...  2.64 us
    pallas_call x1, Pallas kernels, spread_misfits(): pl.pallas_call(kernel, out_shape=(jax.ShapeDtypeStruct((lon_cells, lat_ce...  2.63 us
  transfers between devices with their start and end apart: 9, of which 4 were waited for; matrix products, arithmetic and copies ran while one was open for 2% of the time, Pallas kernels for 21%

profile of v17, /device:TPU:0, one launch (start us, length us, event | category | flops | bytes accessed | tf_op | source)
XLA Modules:
  0.0 48.3 jit_solution(14301068484417245196)
XLA Ops:
  0.0 0.0 copy-start.9
  0.0 0.0 copy-start
  0.0 1.5 %fusion.2 = (bf16[20,1,16,720]{3,2,1,0:T(8,128)(2,1)S(1)}, bf16[20,1,16,720]{3,2,1,0:T(8,128)(2,1)S(1)}) fusion(bf16[20,1,45,720]{3,2,1,0:T(8,128)(2,1)} %ctrl_ref.3), kind=kLoop, calls=%fused_computation.5 | loop fusion | bytes 1843200 | tf_op jit(solution)/shard_map/slice | solution.py:18
  1.6 3.4 %collective-permute-start.1 = (bf16[20,1,16,720]{3,2,1,0:T(8,128)(2,1)S(1)}, bf16[20,1,16,720]{3,2,1,0:T(8,128)(2,1)S(1)}, u32[]{:S(2)}, u32[]{:S(2)}) collective-permute-start(bf16[20,1,16,720]{3,2,1,0:T(8,128)(2,1)S(1)} %get-tuple-element.27), channel_id=1, source_target_pairs={{4,0},{8,4},{12,8},{16,12},{20,16},{24,20},{28,24},{0,28},{5,1},{9... | collective-permute-start | bytes 1382408 | tf_op jit(solution)/shard_map/ppermute | solution.py:18
  5.0 0.0 collective-permute-start
  5.0 0.0 copy-done.14
  5.0 0.5 %convert_element_type.21.lon_ref = f32[17]{0:T(128)} convert(bf16[17]{0:T(256)(128)(2,1)S(1)} %copy-done.14) | non-fusion elementwise | flops 17 | bytes 102 | tf_op jit(solution)/shard_map/convert_element_type | solution.py:84
  5.5 0.0 copy-done.15
  5.5 0.5 %convert_element_type.22.lat_ref = f32[17]{0:T(128)} convert(bf16[17]{0:T(256)(128)(2,1)S(1)} %copy-done.15) | non-fusion elementwise | flops 17 | bytes 102 | tf_op jit(solution)/shard_map/convert_element_type | solution.py:84
  6.1 0.0 copy-done.7
  6.1 0.0 copy-done.8
  6.1 2.0 %shard_map.85 = (bf16[48,80]{1,0:T(8,128)(2,1)}, bf16[720,720]{1,0:T(8,128)(2,1)}) custom-call(f32[17]{0:T(128)} %convert_element_type.21.lon_ref, f32[17]{0:T(128)} %convert_element_type.22.lat_ref), custom_call_target="tpu_custom_call" | custom-call | tf_op jit(solution)/shard_map/pallas_call | solution.py:77
  8.1 0.0 copy-done.13
  8.1 0.0 copy-done.9
  8.1 0.1 fusion
  8.2 9.9 %all_to_all.5.cells_ref.refs_4_ = f32[8,3,256]{2,1,0:T(4,128)} all-to-all(f32[8,3,256]{2,1,0:T(4,128)S(1)} %pad_maximum_fusion), channel_id=1, replica_groups=mesh['tile'=8,'mem'=4] {'tile'}, dimensions={0} | all-to-all | bytes 49152 | tf_op jit(solution)/shard_map/all_to_all | solution.py:326
  18.1 0.0 collective-permute-done.1.high_ref
  18.1 0.0 collective-permute-done.low_ref
  18.1 0.0 copy-done
  18.1 0.0 copy-start.4
  18.1 0.1 fusion.1
  18.3 1.1 %collective-permute-start.3 = (bf16[20,1,16,720]{3,2,1,0:T(8,128)(2,1)S(1)}, bf16[20,1,16,720]{3,2,1,0:T(8,128)(2,1)S(1)}, u32[]{:S(2)}, u32[]{:S(2)}) collective-permute-start(bf16[20,1,16,720]{3,2,1,0:T(8,128)(2,1)S(1)} %get-tuple-element.25), channel_id=1, source_target_pairs={{4,0},{8,4},{12,8},{16,12},{20,16},{24,20},{28,24},{0,28},{5,1},{9... | collective-permute-start | bytes 1382408 | tf_op jit(solution)/shard_map/ppermute | solution.py:18
  19.4 0.0 collective-permute-start.2
  19.4 0.0 copy-done.3
  19.4 0.0 copy-done.4
  19.4 5.3 %shard_map.86.refs_0_ = f32[8,256]{1,0:T(8,128)} custom-call(bf16[20,1,45,720]{3,2,1,0:T(8,128)(2,1)} %ctrl_ref.3, bf16[20,1,16,720]{3,2,1,0:T(8,128)(2,1)} %copy-done.4, bf16[20,1,16,720]{3,2,1,0:T(8,128)(2,1)} %copy-done.3, bf16[20,1,45,720]{3,2,1,0:T(8,128)(2,1)} %pert_ref.3, bf16[48,80]{1,0:T(8,128)(2,1)} %get-tuple-element.15.blon_ref, ...), custom_call_target="tpu_custom_call" | custom-call | tf_op jit(solution)/shard_map/pallas_call | solution.py:189
  24.7 3.6 %collective-permute-start.6 = (f32[8,256]{1,0:T(8,128)}, f32[8,256]{1,0:T(8,128)S(1)}, u32[]{:S(2)}, u32[]{:S(2)}) collective-permute-start(f32[8,256]{1,0:T(8,128)} %shard_map.86.refs_0_), channel_id=1, source_target_pairs={{0,3},{1,0},{2,1},{3,2},{4,7},{5,4},{6,5},{7,6},{8,11},{9,8},{10,9... | collective-permute-start | bytes 24584 | tf_op jit(solution)/shard_map/ppermute | solution.py:25
  28.3 0.0 collective-permute-start.5
  28.3 1.0 %collective-permute-start.4 = (f32[8,256]{1,0:T(8,128)}, f32[8,256]{1,0:T(8,128)S(1)}, u32[]{:S(2)}, u32[]{:S(2)}) collective-permute-start(f32[8,256]{1,0:T(8,128)} %shard_map.86.refs_0_), channel_id=1, source_target_pairs={{0,1},{1,2},{2,3},{3,0},{4,5},{5,6},{6,7},{7,4},{8,9},{9,10},{10,1... | collective-permute-start | bytes 24584 | tf_op jit(solution)/shard_map/ppermute | solution.py:25
  29.3 0.6 %collective-permute-done.6.refs_3_ = f32[8,256]{1,0:T(8,128)S(1)} collective-permute-done((f32[8,256]{1,0:T(8,128)}, f32[8,256]{1,0:T(8,128)S(1)}, u32[]{:S(2)}, u32[]{:S(2)}) %collective-permute-start.6) | collective-permute-done | bytes 8224 | tf_op jit(solution)/shard_map/ppermute | solution.py:25
  29.9 3.2 %collective-permute-done.5.refs_2_ = f32[8,256]{1,0:T(8,128)S(1)} collective-permute-done((f32[8,256]{1,0:T(8,128)}, f32[8,256]{1,0:T(8,128)S(1)}, u32[]{:S(2)}, u32[]{:S(2)}) %collective-permute-start.5) | collective-permute-done | bytes 8224 | tf_op jit(solution)/shard_map/ppermute | solution.py:25
  33.1 0.9 %collective-permute-done.4.refs_1_ = f32[8,256]{1,0:T(8,128)S(1)} collective-permute-done((f32[8,256]{1,0:T(8,128)}, f32[8,256]{1,0:T(8,128)S(1)}, u32[]{:S(2)}, u32[]{:S(2)}) %collective-permute-start.4) | collective-permute-done | bytes 8224 | tf_op jit(solution)/shard_map/ppermute | solution.py:25
  34.0 0.0 copy-done.10
  34.0 0.0 copy-done.11
  34.0 0.6 %copy-done.12 = f32[8,256]{1,0:T(8,128)} copy-done((f32[8,256]{1,0:T(8,128)}, f32[8,256]{1,0:T(8,128)S(1)}, u32[]{:S(2)}) %copy-start.12) | copy-done | bytes 8216
  34.6 2.6 %shard_map.87 = (f32[45,720]{1,0:T(8,128)}, f32[16,720]{1,0:T(8,128)}, f32[16,720]{1,0:T(8,128)}) custom-call(f32[8,256]{1,0:T(8,128)} %shard_map.86.refs_0_, f32[8,256]{1,0:T(8,128)} %copy-done.12, f32[8,256]{1,0:T(8,128)} %copy-done.11, f32[8,256]{1,0:T(8,128)} %copy-done.10, f32[8,3,256]{2,1,0:T(4,128)} %all_to_all.5.cells_ref.refs_4_), custom_call_target="tpu_custom_call" | custom-call | tf_op jit(solution)/shard_map/pallas_call | solution.py:247
  37.2 0.0 collective-permute-start.7
  37.2 2.6 %collective-permute-start.8 = (f32[16,720]{1,0:T(8,128)}, f32[16,720]{1,0:T(8,128)S(1)}, u32[]{:S(2)}, u32[]{:S(2)}) collective-permute-start(f32[16,720]{1,0:T(8,128)} %get-tuple-element.24), channel_id=1, source_target_pairs={{4,0},{8,4},{12,8},{16,12},{20,16},{24,20},{28,24},{0,28},{5,1},{9... | collective-permute-start | bytes 138248 | tf_op jit(solution)/shard_map/ppermute | solution.py:341
  39.8 2.1 %collective-permute-done.7 = f32[16,720]{1,0:T(8,128)S(1)} collective-permute-done((f32[16,720]{1,0:T(8,128)}, f32[16,720]{1,0:T(8,128)S(1)}, u32[]{:S(2)}, u32[]{:S(2)}) %collective-permute-start.7) | collective-permute-done | bytes 46112 | tf_op jit(solution)/shard_map/ppermute | solution.py:340
  41.9 0.0 collective-permute-done.8
  41.9 0.0 collective-permute-done.3.phigh_ref
  41.9 0.0 copy-start.1
  41.9 0.0 collective-permute-done.2.plow_ref
  42.0 0.6 %copy-done.5 = f32[16,720]{1,0:T(8,128)} copy-done((f32[16,720]{1,0:T(8,128)}, f32[16,720]{1,0:T(8,128)S(1)}, u32[]{:S(2)}) %copy-start.5) | copy-done | bytes 46104
  42.5 0.0 copy-done.6
  42.6 0.2 copy-done.1
  42.7 0.2 copy-done.2
  42.9 5.4 %shard_map.88 = f32[20,45,1,720]{3,2,1,0:T(1,128)} custom-call(bf16[20,1,45,720]{3,2,1,0:T(8,128)(2,1)} %pert_ref.3, bf16[20,1,16,720]{3,2,1,0:T(8,128)(2,1)} %copy-done.2, bf16[20,1,16,720]{3,2,1,0:T(8,128)(2,1)} %copy-done.1, f32[1,45,720]{2,1,0:T(8,128)} %bitcast.9, f32[1,16,720]{2,1,0:T(8,128)} %bitcast.10, f32[1,16,720]{2,1,0:T(8,128)} %bitcast.11, ...), custom_call_target="tpu_custom_call" | custom-call | tf_op jit(solution)/shard_map/pallas_call | solution.py:291
  (15 shorter events, 0.1 us)
Async XLA Ops:
  0.0 5.0 %copy-start.14 = (bf16[17]{0:T(256)(128)(2,1)S(1)}, bf16[17]{0:T(256)(128)(2,1)}, u32[]{:S(2)}) copy-start(bf16[17]{0:T(256)(128)(2,1)} %param.10) | copy-start | bytes 106
  0.0 5.5 %copy-start.15 = (bf16[17]{0:T(256)(128)(2,1)S(1)}, bf16[17]{0:T(256)(128)(2,1)}, u32[]{:S(2)}) copy-start(bf16[17]{0:T(256)(128)(2,1)} %param.11) | copy-start | bytes 106
  0.0 6.0 %copy-start.7 = (f32[1,8,256]{2,1,0:T(8,128)S(1)}, f32[1,8,256]{2,1,0:T(8,128)}, u32[]{:S(2)}) copy-start(f32[1,8,256]{2,1,0:T(8,128)} %param.12) | copy-start | bytes 24580
  0.0 6.1 %copy-start.8 = (s32[1,8,256]{2,1,0:T(8,128)S(1)}, s32[1,8,256]{2,1,0:T(8,128)}, u32[]{:S(2)}) copy-start(s32[1,8,256]{2,1,0:T(8,128)} %param.14) | copy-start | bytes 24580
  0.0 8.0 %copy-start.13 = (s32[1,8]{1,0:T(1,128)S(1)}, s32[1,8]{1,0:T(1,128)}, u32[]{:S(2)}) copy-start(s32[1,8]{1,0:T(1,128)} %param.15) | copy-start | bytes 100
  0.0 8.0 %copy-start.9 = (f32[1,8,256]{2,1,0:T(8,128)S(1)}, f32[1,8,256]{2,1,0:T(8,128)}, u32[]{:S(2)}) copy-start(f32[1,8,256]{2,1,0:T(8,128)} %param.13) | copy-start | bytes 24580
  0.0 18.1 %copy-start = (bf16[20,1,45,720]{3,2,1,0:T(8,128)(2,1)S(1)}, bf16[20,1,45,720]{3,2,1,0:T(8,128)(2,1)}, u32[]{:S(2)}) copy-start(bf16[20,1,45,720]{3,2,1,0:T(8,128)(2,1)} %pert_ref.3) | copy-start | bytes 3888004
  1.6 16.5 %collective-permute-start.1 = (bf16[20,1,16,720]{3,2,1,0:T(8,128)(2,1)S(1)}, bf16[20,1,16,720]{3,2,1,0:T(8,128)(2,1)S(1)}, u32[]{:S(2)}, u32[]{:S(2)}) collective-permute-start(bf16[20,1,16,720]{3,2,1,0:T(8,128)(2,1)S(1)} %get-tuple-element.27), channel_id=1, source_target_pairs={{4,0},{8,4},{12,8},{16,12},{20,16},{24,20},{28,24},{0,28},{5,1},{9... | collective-permute-start | bytes 1382408 | tf_op jit(solution)/shard_map/ppermute | solution.py:18
  5.0 13.1 %collective-permute-start = (bf16[20,1,16,720]{3,2,1,0:T(8,128)(2,1)S(1)}, bf16[20,1,16,720]{3,2,1,0:T(8,128)(2,1)S(1)}, u32[]{:S(2)}, u32[]{:S(2)}) collective-permute-start(bf16[20,1,16,720]{3,2,1,0:T(8,128)(2,1)S(1)} %get-tuple-element.28), channel_id=1, source_target_pairs={{0,4},{4,8},{8,12},{12,16},{16,20},{20,24},{24,28},{28,0},{1,5},{5... | collective-permute-start | bytes 1382408 | tf_op jit(solution)/shard_map/ppermute | solution.py:15
  18.1 1.3 %copy-start.3 = (bf16[20,1,16,720]{3,2,1,0:T(8,128)(2,1)}, bf16[20,1,16,720]{3,2,1,0:T(8,128)(2,1)S(1)}, u32[]{:S(2)}) copy-start(bf16[20,1,16,720]{3,2,1,0:T(8,128)(2,1)S(1)} %collective-permute-done.1.high_ref) | copy-start | bytes 1382404
  18.1 1.3 %copy-start.4 = (bf16[20,1,16,720]{3,2,1,0:T(8,128)(2,1)}, bf16[20,1,16,720]{3,2,1,0:T(8,128)(2,1)S(1)}, u32[]{:S(2)}) copy-start(bf16[20,1,16,720]{3,2,1,0:T(8,128)(2,1)S(1)} %collective-permute-done.low_ref) | copy-start | bytes 1382404
  18.3 23.6 %collective-permute-start.3 = (bf16[20,1,16,720]{3,2,1,0:T(8,128)(2,1)S(1)}, bf16[20,1,16,720]{3,2,1,0:T(8,128)(2,1)S(1)}, u32[]{:S(2)}, u32[]{:S(2)}) collective-permute-start(bf16[20,1,16,720]{3,2,1,0:T(8,128)(2,1)S(1)} %get-tuple-element.25), channel_id=1, source_target_pairs={{4,0},{8,4},{12,8},{16,12},{20,16},{24,20},{28,24},{0,28},{5,1},{9... | collective-permute-start | bytes 1382408 | tf_op jit(solution)/shard_map/ppermute | solution.py:18
  19.4 22.6 %collective-permute-start.2 = (bf16[20,1,16,720]{3,2,1,0:T(8,128)(2,1)S(1)}, bf16[20,1,16,720]{3,2,1,0:T(8,128)(2,1)S(1)}, u32[]{:S(2)}, u32[]{:S(2)}) collective-permute-start(bf16[20,1,16,720]{3,2,1,0:T(8,128)(2,1)S(1)} %get-tuple-element.26), channel_id=1, source_target_pairs={{0,4},{4,8},{8,12},{12,16},{16,20},{20,24},{24,28},{28,0},{1,5},{5... | collective-permute-start | bytes 1382408 | tf_op jit(solution)/shard_map/ppermute | solution.py:15
  24.7 5.2 %collective-permute-start.6 = (f32[8,256]{1,0:T(8,128)}, f32[8,256]{1,0:T(8,128)S(1)}, u32[]{:S(2)}, u32[]{:S(2)}) collective-permute-start(f32[8,256]{1,0:T(8,128)} %shard_map.86.refs_0_), channel_id=1, source_target_pairs={{0,3},{1,0},{2,1},{3,2},{4,7},{5,4},{6,5},{7,6},{8,11},{9,8},{10,9... | collective-permute-start | bytes 24584 | tf_op jit(solution)/shard_map/ppermute | solution.py:25
  28.3 4.8 %collective-permute-start.5 = (f32[8,256]{1,0:T(8,128)}, f32[8,256]{1,0:T(8,128)S(1)}, u32[]{:S(2)}, u32[]{:S(2)}) collective-permute-start(f32[8,256]{1,0:T(8,128)} %shard_map.86.refs_0_), channel_id=1, source_target_pairs={{0,2},{1,3},{2,0},{3,1},{4,6},{5,7},{6,4},{7,5},{8,10},{9,11},{10,... | collective-permute-start | bytes 24584 | tf_op jit(solution)/shard_map/ppermute | solution.py:25
  28.3 5.7 %collective-permute-start.4 = (f32[8,256]{1,0:T(8,128)}, f32[8,256]{1,0:T(8,128)S(1)}, u32[]{:S(2)}, u32[]{:S(2)}) collective-permute-start(f32[8,256]{1,0:T(8,128)} %shard_map.86.refs_0_), channel_id=1, source_target_pairs={{0,1},{1,2},{2,3},{3,0},{4,5},{5,6},{6,7},{7,4},{8,9},{9,10},{10,1... | collective-permute-start | bytes 24584 | tf_op jit(solution)/shard_map/ppermute | solution.py:25
  29.9 4.1 %copy-start.10 = (f32[8,256]{1,0:T(8,128)}, f32[8,256]{1,0:T(8,128)S(1)}, u32[]{:S(2)}) copy-start(f32[8,256]{1,0:T(8,128)S(1)} %collective-permute-done.6.refs_3_) | copy-start | bytes 24580
  33.1 0.9 %copy-start.11 = (f32[8,256]{1,0:T(8,128)}, f32[8,256]{1,0:T(8,128)S(1)}, u32[]{:S(2)}) copy-start(f32[8,256]{1,0:T(8,128)S(1)} %collective-permute-done.5.refs_2_) | copy-start | bytes 24580
  34.0 0.6 %copy-start.12 = (f32[8,256]{1,0:T(8,128)}, f32[8,256]{1,0:T(8,128)S(1)}, u32[]{:S(2)}) copy-start(f32[8,256]{1,0:T(8,128)S(1)} %collective-permute-done.4.refs_1_) | copy-start | bytes 24580
  37.2 4.7 %collective-permute-start.7 = (f32[16,720]{1,0:T(8,128)}, f32[16,720]{1,0:T(8,128)S(1)}, u32[]{:S(2)}, u32[]{:S(2)}) collective-permute-start(f32[16,720]{1,0:T(8,128)} %get-tuple-element.23), channel_id=1, source_target_pairs={{0,4},{4,8},{8,12},{12,16},{16,20},{20,24},{24,28},{28,0},{1,5},{5... | collective-permute-start | bytes 138248 | tf_op jit(solution)/shard_map/ppermute | solution.py:340
  37.2 4.7 %collective-permute-start.8 = (f32[16,720]{1,0:T(8,128)}, f32[16,720]{1,0:T(8,128)S(1)}, u32[]{:S(2)}, u32[]{:S(2)}) collective-permute-start(f32[16,720]{1,0:T(8,128)} %get-tuple-element.24), channel_id=1, source_target_pairs={{4,0},{8,4},{12,8},{16,12},{20,16},{24,20},{28,24},{0,28},{5,1},{9... | collective-permute-start | bytes 138248 | tf_op jit(solution)/shard_map/ppermute | solution.py:341
  41.9 0.6 %copy-start.5 = (f32[16,720]{1,0:T(8,128)}, f32[16,720]{1,0:T(8,128)S(1)}, u32[]{:S(2)}) copy-start(f32[16,720]{1,0:T(8,128)S(1)} %collective-permute-done.7) | copy-start | bytes 138244
  41.9 0.6 %copy-start.6 = (f32[16,720]{1,0:T(8,128)}, f32[16,720]{1,0:T(8,128)S(1)}, u32[]{:S(2)}) copy-start(f32[16,720]{1,0:T(8,128)S(1)} %collective-permute-done.8) | copy-start | bytes 138244
  41.9 0.8 %copy-start.1 = (bf16[20,1,16,720]{3,2,1,0:T(8,128)(2,1)}, bf16[20,1,16,720]{3,2,1,0:T(8,128)(2,1)S(1)}, u32[]{:S(2)}) copy-start(bf16[20,1,16,720]{3,2,1,0:T(8,128)(2,1)S(1)} %collective-permute-done.3.phigh_ref) | copy-start | bytes 1382404
  41.9 1.0 %copy-start.2 = (bf16[20,1,16,720]{3,2,1,0:T(8,128)(2,1)}, bf16[20,1,16,720]{3,2,1,0:T(8,128)(2,1)S(1)}, u32[]{:S(2)}) copy-start(bf16[20,1,16,720]{3,2,1,0:T(8,128)(2,1)S(1)} %collective-permute-done.2.plow_ref) | copy-start | bytes 1382404

commit v18 on v17

--- a/solution.py
+++ b/solution.py
@@ -1,5 +1,3 @@
-import math
-
 import jax
 import jax.numpy as jnp
 from jax import lax
@@ -135,7 +133,7 @@
 
 
 def forward_pick(control, c_low, c_high, perturb, band_lon, band_lat, cells):
-    members, levels, lon_cells, lat_cells = control.shape
+    members, _, lon_cells, lat_cells = control.shape
     radius = c_low.shape[2]
     padded, ext_cells = band_lon.shape
     chunk = member_chunk(members)
@@ -313,8 +311,8 @@
     return jnp.transpose(out, (0, 2, 1, 3))
 
 
-def local(control, perturb, lon_taps, lat_taps, innov, inv_var, cell_index, counts):
-    members_here, levels, lon_cells, lat_cells = control.shape
+def local_body(control, perturb, lon_taps, lat_taps, innov, inv_var, cell_index, counts):
+    _, _, lon_cells, lat_cells = control.shape
     radius = lon_taps.shape[0] - 1
     padded = -(-lon_cells // 16) * 16
     band_lon, band_lat = build_bands(lon_taps, lat_taps, lon_cells, padded, lat_cells)
@@ -327,12 +325,12 @@
 
     c_low, c_high = halos(control, "tile", 2, radius)
     c_low, c_high, received = lax.optimization_barrier((c_low, c_high, received))
-    late_perturb = lax.optimization_barrier((perturb, c_low, c_high))[0]
-    p_low, p_high = halos(late_perturb, "tile", 2, radius)
     partial = forward_pick(
         control, c_low, c_high, perturb, band_lon, band_lat, received
     )
     partials = gather_over(partial, "mem")
+    late_perturb = lax.optimization_barrier((perturb, partial))[0]
+    p_low, p_high = halos(late_perturb, "tile", 2, radius)
     spread, low_send, high_send = spread_misfits(
         partials, received, lon_cells, lat_cells, radius, padded
     )
@@ -354,7 +352,7 @@
 
 def solution(mesh):
     return jax.shard_map(
-        local,
+        local_body,
         mesh=mesh,
         in_specs=(
             P("mem", None, "tile", None),

time: 48.6 us -> 49.9 us (1.027)
  local copies, waits for them, and re-layouts: 3.29 us -> 4.79 us
    unnamed x32 -> x34, local copies, waits for them, and re-layouts: 1.61 us -> 3.17 us
  transfers between devices with their start and end apart: 9 -> 9, of which waited for: 4 -> 4; matrix products, arithmetic and copies ran while one was open for 2% -> 2% of each run, Pallas kernels for 21% -> 9%
where the time goes in v18:
time: 49.9 us; the launch traced here: 49.6 us
  Pallas kernels  15.3 us (31%)
  starting transfers between devices  11.8 us (24%)
  blocking collectives  9.87 us (20%)
  waiting for transfers between devices  6.57 us (13%)
  local copies, waits for them, and re-layouts  4.79 us (10%)
  other arithmetic  1.2 us (2%)
    all_to_all x1, blocking collectives, local_body(): lax.all_to_all(lists, 'tile', split_axis=0, concat_axis=0, tiled=True)  9.87 us
    pallas_call x1, Pallas kernels, backward_grad(): pl.pallas_call(kernel, grid=(levels, members // chunk), in_specs=[field,...  5.41 us
    pallas_call x1, Pallas kernels, forward_pick(): pl.pallas_call(kernel, grid=(steps,), in_specs=[field, halo, halo, field,...  5.29 us
    ppermute x3, starting transfers between devices, gather_over(): lax.ppermute(values, axis, [(i, (i + shift) % count) for i in range(count)])  4.62 us
    ppermute x2, starting transfers between devices, halos(): lax.ppermute(lax.slice_in_dim(block, 0, width, axis=dim), axis, backward)  4.5 us
    ppermute x3, waiting for transfers between devices, gather_over(): lax.ppermute(values, axis, [(i, (i + shift) % count) for i in range(count)])  4.43 us
    unnamed x34, local copies, waits for them, and re-layouts  3.17 us
    ppermute x1, starting transfers between devices, local_body(): lax.ppermute(high_send, 'tile', [((i + 1) % count, i) for i in range(coun...  2.64 us
  transfers between devices with their start and end apart: 9, of which 4 were waited for; matrix products, arithmetic and copies ran while one was open for 2% of the time, Pallas kernels for 9%

profile of v18, /device:TPU:0, one launch (start us, length us, event | category | flops | bytes accessed | tf_op | source)
XLA Modules:
  0.0 49.6 jit_solution(11903239086722966987)
XLA Ops:
  0.0 0.0 copy-start.10
  0.0 1.5 %fusion.2 = (bf16[20,1,16,720]{3,2,1,0:T(8,128)(2,1)S(1)}, bf16[20,1,16,720]{3,2,1,0:T(8,128)(2,1)S(1)}) fusion(bf16[20,1,45,720]{3,2,1,0:T(8,128)(2,1)} %ctrl_ref.3), kind=kLoop, calls=%fused_computation.5 | loop fusion | bytes 1843200 | tf_op jit(solution)/shard_map/slice | solution.py:16
  1.5 3.4 %collective-permute-start.1 = (bf16[20,1,16,720]{3,2,1,0:T(8,128)(2,1)S(1)}, bf16[20,1,16,720]{3,2,1,0:T(8,128)(2,1)S(1)}, u32[]{:S(2)}, u32[]{:S(2)}) collective-permute-start(bf16[20,1,16,720]{3,2,1,0:T(8,128)(2,1)S(1)} %get-tuple-element.27), channel_id=1, source_target_pairs={{4,0},{8,4},{12,8},{16,12},{20,16},{24,20},{28,24},{0,28},{5,1},{9... | collective-permute-start | bytes 1382408 | tf_op jit(solution)/shard_map/ppermute | solution.py:16
  4.9 0.0 collective-permute-start
  4.9 0.0 copy-done.15
  4.9 0.5 %convert_element_type.21.lon_ref = f32[17]{0:T(128)} convert(bf16[17]{0:T(256)(128)(2,1)S(1)} %copy-done.15) | non-fusion elementwise | flops 17 | bytes 102 | tf_op jit(solution)/shard_map/convert_element_type | solution.py:82
  5.4 0.0 copy-done.16
  5.4 0.6 %convert_element_type.22.lat_ref = f32[17]{0:T(128)} convert(bf16[17]{0:T(256)(128)(2,1)S(1)} %copy-done.16) | non-fusion elementwise | flops 17 | bytes 102 | tf_op jit(solution)/shard_map/convert_element_type | solution.py:82
  6.0 0.0 copy-done.8
  6.0 0.0 copy-done.9
  6.1 2.0 %shard_map.85 = (bf16[48,80]{1,0:T(8,128)(2,1)}, bf16[720,720]{1,0:T(8,128)(2,1)}) custom-call(f32[17]{0:T(128)} %convert_element_type.21.lon_ref, f32[17]{0:T(128)} %convert_element_type.22.lat_ref), custom_call_target="tpu_custom_call" | custom-call | tf_op jit(solution)/shard_map/pallas_call | solution.py:75
  8.0 0.0 copy-done.14
  8.0 0.0 copy-done.10
  8.0 0.1 fusion
  8.1 9.9 %all_to_all.5.cells_ref.refs_4_ = f32[8,3,256]{2,1,0:T(4,128)} all-to-all(f32[8,3,256]{2,1,0:T(4,128)S(1)} %pad_maximum_fusion), channel_id=1, replica_groups=mesh['tile'=8,'mem'=4] {'tile'}, dimensions={0} | all-to-all | bytes 49152 | tf_op jit(solution)/shard_map/all_to_all | solution.py:324
  18.0 0.0 collective-permute-done.1.high_ref
  18.0 0.0 collective-permute-done.low_ref
  18.0 0.8 %copy-done.3 = bf16[20,1,16,720]{3,2,1,0:T(8,128)(2,1)} copy-done((bf16[20,1,16,720]{3,2,1,0:T(8,128)(2,1)}, bf16[20,1,16,720]{3,2,1,0:T(8,128)(2,1)S(1)}, u32[]{:S(2)}) %copy-start.3) | copy-done | bytes 460824
  18.8 0.8 %copy-done.4 = bf16[20,1,16,720]{3,2,1,0:T(8,128)(2,1)} copy-done((bf16[20,1,16,720]{3,2,1,0:T(8,128)(2,1)}, bf16[20,1,16,720]{3,2,1,0:T(8,128)(2,1)S(1)}, u32[]{:S(2)}) %copy-start.4) | copy-done | bytes 460824
  19.6 5.3 %shard_map.86.refs_0_ = f32[8,256]{1,0:T(8,128)} custom-call(bf16[20,1,45,720]{3,2,1,0:T(8,128)(2,1)} %ctrl_ref.3, bf16[20,1,16,720]{3,2,1,0:T(8,128)(2,1)} %copy-done.4, bf16[20,1,16,720]{3,2,1,0:T(8,128)(2,1)} %copy-done.3, bf16[20,1,45,720]{3,2,1,0:T(8,128)(2,1)} %pert_ref.3, bf16[48,80]{1,0:T(8,128)(2,1)} %get-tuple-element.15.blon_ref, ...), custom_call_target="tpu_custom_call" | custom-call | tf_op jit(solution)/shard_map/pallas_call | solution.py:187
  24.9 0.0 copy-done
  24.9 0.1 fusion.1
  25.0 1.1 %collective-permute-start.3 = (bf16[20,1,16,720]{3,2,1,0:T(8,128)(2,1)S(1)}, bf16[20,1,16,720]{3,2,1,0:T(8,128)(2,1)S(1)}, u32[]{:S(2)}, u32[]{:S(2)}) collective-permute-start(bf16[20,1,16,720]{3,2,1,0:T(8,128)(2,1)S(1)} %get-tuple-element.25), channel_id=1, source_target_pairs={{4,0},{8,4},{12,8},{16,12},{20,16},{24,20},{28,24},{0,28},{5,1},{9... | collective-permute-start | bytes 1382408 | tf_op jit(solution)/shard_map/ppermute | solution.py:16
  26.1 0.0 collective-permute-start.2
  26.1 0.0 copy-done.7
  26.1 3.6 %collective-permute-start.6 = (f32[8,256]{1,0:T(8,128)S(1)}, f32[8,256]{1,0:T(8,128)S(1)}, u32[]{:S(2)}, u32[]{:S(2)}) collective-permute-start(f32[8,256]{1,0:T(8,128)S(1)} %copy-done.7), channel_id=1, source_target_pairs={{0,3},{1,0},{2,1},{3,2},{4,7},{5,4},{6,5},{7,6},{8,11},{9,8},{10,9... | collective-permute-start | bytes 24584 | tf_op jit(solution)/shard_map/ppermute | solution.py:23
  29.7 0.0 collective-permute-start.5
  29.7 1.0 %collective-permute-start.4 = (f32[8,256]{1,0:T(8,128)S(1)}, f32[8,256]{1,0:T(8,128)S(1)}, u32[]{:S(2)}, u32[]{:S(2)}) collective-permute-start(f32[8,256]{1,0:T(8,128)S(1)} %copy-done.7), channel_id=1, source_target_pairs={{0,1},{1,2},{2,3},{3,0},{4,5},{5,6},{6,7},{7,4},{8,9},{9,10},{10,1... | collective-permute-start | bytes 24584 | tf_op jit(solution)/shard_map/ppermute | solution.py:23
  30.8 0.3 collective-permute-done.6.refs_3_
  31.1 3.2 %collective-permute-done.5.refs_2_ = f32[8,256]{1,0:T(8,128)S(1)} collective-permute-done((f32[8,256]{1,0:T(8,128)S(1)}, f32[8,256]{1,0:T(8,128)S(1)}, u32[]{:S(2)}, u32[]{:S(2)}) %collective-permute-start.5) | collective-permute-done | bytes 8224 | tf_op jit(solution)/shard_map/ppermute | solution.py:23
  34.3 0.9 %collective-permute-done.4.refs_1_ = f32[8,256]{1,0:T(8,128)S(1)} collective-permute-done((f32[8,256]{1,0:T(8,128)S(1)}, f32[8,256]{1,0:T(8,128)S(1)}, u32[]{:S(2)}, u32[]{:S(2)}) %collective-permute-start.4) | collective-permute-done | bytes 8224 | tf_op jit(solution)/shard_map/ppermute | solution.py:23
  35.2 0.0 copy-done.11
  35.2 0.0 copy-done.12
  35.2 0.6 %copy-done.13 = f32[8,256]{1,0:T(8,128)} copy-done((f32[8,256]{1,0:T(8,128)}, f32[8,256]{1,0:T(8,128)S(1)}, u32[]{:S(2)}) %copy-start.13) | copy-done | bytes 8216
  35.8 2.6 %shard_map.87 = (f32[45,720]{1,0:T(8,128)}, f32[16,720]{1,0:T(8,128)}, f32[16,720]{1,0:T(8,128)}) custom-call(f32[8,256]{1,0:T(8,128)} %shard_map.86.refs_0_, f32[8,256]{1,0:T(8,128)} %copy-done.13, f32[8,256]{1,0:T(8,128)} %copy-done.12, f32[8,256]{1,0:T(8,128)} %copy-done.11, f32[8,3,256]{2,1,0:T(4,128)} %all_to_all.5.cells_ref.refs_4_), custom_call_target="tpu_custom_call" | custom-call | tf_op jit(solution)/shard_map/pallas_call | solution.py:245
  38.4 0.0 collective-permute-start.7
  38.4 2.6 %collective-permute-start.8 = (f32[16,720]{1,0:T(8,128)}, f32[16,720]{1,0:T(8,128)S(1)}, u32[]{:S(2)}, u32[]{:S(2)}) collective-permute-start(f32[16,720]{1,0:T(8,128)} %get-tuple-element.24), channel_id=1, source_target_pairs={{4,0},{8,4},{12,8},{16,12},{20,16},{24,20},{28,24},{0,28},{5,1},{9... | collective-permute-start | bytes 138248 | tf_op jit(solution)/shard_map/ppermute | solution.py:339
  41.1 2.1 %collective-permute-done.7 = f32[16,720]{1,0:T(8,128)S(1)} collective-permute-done((f32[16,720]{1,0:T(8,128)}, f32[16,720]{1,0:T(8,128)S(1)}, u32[]{:S(2)}, u32[]{:S(2)}) %collective-permute-start.7) | collective-permute-done | bytes 46112 | tf_op jit(solution)/shard_map/ppermute | solution.py:338
  43.2 0.0 collective-permute-done.8
  43.2 0.0 collective-permute-done.3.phigh_ref
  43.2 0.0 copy-start.1
  43.2 0.0 collective-permute-done.2.plow_ref
  43.2 0.0 copy-start.2
  43.2 0.6 %copy-done.5 = f32[16,720]{1,0:T(8,128)} copy-done((f32[16,720]{1,0:T(8,128)}, f32[16,720]{1,0:T(8,128)S(1)}, u32[]{:S(2)}) %copy-start.5) | copy-done | bytes 46104
  43.8 0.0 copy-done.6
  43.8 0.2 copy-done.1
  44.0 0.2 copy-done.2
  44.2 5.4 %shard_map.88 = f32[20,45,1,720]{3,2,1,0:T(1,128)} custom-call(bf16[20,1,45,720]{3,2,1,0:T(8,128)(2,1)} %pert_ref.3, bf16[20,1,16,720]{3,2,1,0:T(8,128)(2,1)} %copy-done.2, bf16[20,1,16,720]{3,2,1,0:T(8,128)(2,1)} %copy-done.1, f32[1,45,720]{2,1,0:T(8,128)} %bitcast.9, f32[1,16,720]{2,1,0:T(8,128)} %bitcast.10, f32[1,16,720]{2,1,0:T(8,128)} %bitcast.11, ...), custom_call_target="tpu_custom_call" | custom-call | tf_op jit(solution)/shard_map/pallas_call | solution.py:289
  (17 shorter events, 0.1 us)
Async XLA Ops:
  0.0 4.9 %copy-start.15 = (bf16[17]{0:T(256)(128)(2,1)S(1)}, bf16[17]{0:T(256)(128)(2,1)}, u32[]{:S(2)}) copy-start(bf16[17]{0:T(256)(128)(2,1)} %param.10) | copy-start | bytes 106
  0.0 5.4 %copy-start.16 = (bf16[17]{0:T(256)(128)(2,1)S(1)}, bf16[17]{0:T(256)(128)(2,1)}, u32[]{:S(2)}) copy-start(bf16[17]{0:T(256)(128)(2,1)} %param.11) | copy-start | bytes 106
  0.0 6.0 %copy-start.8 = (f32[1,8,256]{2,1,0:T(8,128)S(1)}, f32[1,8,256]{2,1,0:T(8,128)}, u32[]{:S(2)}) copy-start(f32[1,8,256]{2,1,0:T(8,128)} %param.12) | copy-start | bytes 24580
  0.0 6.0 %copy-start.9 = (s32[1,8,256]{2,1,0:T(8,128)S(1)}, s32[1,8,256]{2,1,0:T(8,128)}, u32[]{:S(2)}) copy-start(s32[1,8,256]{2,1,0:T(8,128)} %param.14) | copy-start | bytes 24580
  0.0 8.0 %copy-start.14 = (s32[1,8]{1,0:T(1,128)S(1)}, s32[1,8]{1,0:T(1,128)}, u32[]{:S(2)}) copy-start(s32[1,8]{1,0:T(1,128)} %param.15) | copy-start | bytes 100
  0.0 8.0 %copy-start.10 = (f32[1,8,256]{2,1,0:T(8,128)S(1)}, f32[1,8,256]{2,1,0:T(8,128)}, u32[]{:S(2)}) copy-start(f32[1,8,256]{2,1,0:T(8,128)} %param.13) | copy-start | bytes 24580
  1.5 16.5 %collective-permute-start.1 = (bf16[20,1,16,720]{3,2,1,0:T(8,128)(2,1)S(1)}, bf16[20,1,16,720]{3,2,1,0:T(8,128)(2,1)S(1)}, u32[]{:S(2)}, u32[]{:S(2)}) collective-permute-start(bf16[20,1,16,720]{3,2,1,0:T(8,128)(2,1)S(1)} %get-tuple-element.27), channel_id=1, source_target_pairs={{4,0},{8,4},{12,8},{16,12},{20,16},{24,20},{28,24},{0,28},{5,1},{9... | collective-permute-start | bytes 1382408 | tf_op jit(solution)/shard_map/ppermute | solution.py:16
  4.9 13.1 %collective-permute-start = (bf16[20,1,16,720]{3,2,1,0:T(8,128)(2,1)S(1)}, bf16[20,1,16,720]{3,2,1,0:T(8,128)(2,1)S(1)}, u32[]{:S(2)}, u32[]{:S(2)}) collective-permute-start(bf16[20,1,16,720]{3,2,1,0:T(8,128)(2,1)S(1)} %get-tuple-element.28), channel_id=1, source_target_pairs={{0,4},{4,8},{8,12},{12,16},{16,20},{20,24},{24,28},{28,0},{1,5},{5... | collective-permute-start | bytes 1382408 | tf_op jit(solution)/shard_map/ppermute | solution.py:13
  18.0 6.9 %copy-start = (bf16[20,1,45,720]{3,2,1,0:T(8,128)(2,1)S(1)}, bf16[20,1,45,720]{3,2,1,0:T(8,128)(2,1)}, u32[]{:S(2)}) copy-start(bf16[20,1,45,720]{3,2,1,0:T(8,128)(2,1)} %pert_ref.3) | copy-start | bytes 3888004
  18.0 0.8 %copy-start.3 = (bf16[20,1,16,720]{3,2,1,0:T(8,128)(2,1)}, bf16[20,1,16,720]{3,2,1,0:T(8,128)(2,1)S(1)}, u32[]{:S(2)}) copy-start(bf16[20,1,16,720]{3,2,1,0:T(8,128)(2,1)S(1)} %collective-permute-done.1.high_ref) | copy-start | bytes 1382404
  18.8 0.8 %copy-start.4 = (bf16[20,1,16,720]{3,2,1,0:T(8,128)(2,1)}, bf16[20,1,16,720]{3,2,1,0:T(8,128)(2,1)S(1)}, u32[]{:S(2)}) copy-start(bf16[20,1,16,720]{3,2,1,0:T(8,128)(2,1)S(1)} %collective-permute-done.low_ref) | copy-start | bytes 1382404
  24.9 1.2 %copy-start.7 = (f32[8,256]{1,0:T(8,128)S(1)}, f32[8,256]{1,0:T(8,128)}, u32[]{:S(2)}) copy-start(f32[8,256]{1,0:T(8,128)} %shard_map.86.refs_0_) | copy-start | bytes 24580
  25.0 18.1 %collective-permute-start.3 = (bf16[20,1,16,720]{3,2,1,0:T(8,128)(2,1)S(1)}, bf16[20,1,16,720]{3,2,1,0:T(8,128)(2,1)S(1)}, u32[]{:S(2)}, u32[]{:S(2)}) collective-permute-start(bf16[20,1,16,720]{3,2,1,0:T(8,128)(2,1)S(1)} %get-tuple-element.25), channel_id=1, source_target_pairs={{4,0},{8,4},{12,8},{16,12},{20,16},{24,20},{28,24},{0,28},{5,1},{9... | collective-permute-start | bytes 1382408 | tf_op jit(solution)/shard_map/ppermute | solution.py:16
  26.1 17.1 %collective-permute-start.2 = (bf16[20,1,16,720]{3,2,1,0:T(8,128)(2,1)S(1)}, bf16[20,1,16,720]{3,2,1,0:T(8,128)(2,1)S(1)}, u32[]{:S(2)}, u32[]{:S(2)}) collective-permute-start(bf16[20,1,16,720]{3,2,1,0:T(8,128)(2,1)S(1)} %get-tuple-element.26), channel_id=1, source_target_pairs={{0,4},{4,8},{8,12},{12,16},{16,20},{20,24},{24,28},{28,0},{1,5},{5... | collective-permute-start | bytes 1382408 | tf_op jit(solution)/shard_map/ppermute | solution.py:13
  26.1 5.0 %collective-permute-start.6 = (f32[8,256]{1,0:T(8,128)S(1)}, f32[8,256]{1,0:T(8,128)S(1)}, u32[]{:S(2)}, u32[]{:S(2)}) collective-permute-start(f32[8,256]{1,0:T(8,128)S(1)} %copy-done.7), channel_id=1, source_target_pairs={{0,3},{1,0},{2,1},{3,2},{4,7},{5,4},{6,5},{7,6},{8,11},{9,8},{10,9... | collective-permute-start | bytes 24584 | tf_op jit(solution)/shard_map/ppermute | solution.py:23
  29.7 4.5 %collective-permute-start.5 = (f32[8,256]{1,0:T(8,128)S(1)}, f32[8,256]{1,0:T(8,128)S(1)}, u32[]{:S(2)}, u32[]{:S(2)}) collective-permute-start(f32[8,256]{1,0:T(8,128)S(1)} %copy-done.7), channel_id=1, source_target_pairs={{0,2},{1,3},{2,0},{3,1},{4,6},{5,7},{6,4},{7,5},{8,10},{9,11},{10,... | collective-permute-start | bytes 24584 | tf_op jit(solution)/shard_map/ppermute | solution.py:23
  29.7 5.4 %collective-permute-start.4 = (f32[8,256]{1,0:T(8,128)S(1)}, f32[8,256]{1,0:T(8,128)S(1)}, u32[]{:S(2)}, u32[]{:S(2)}) collective-permute-start(f32[8,256]{1,0:T(8,128)S(1)} %copy-done.7), channel_id=1, source_target_pairs={{0,1},{1,2},{2,3},{3,0},{4,5},{5,6},{6,7},{7,4},{8,9},{9,10},{10,1... | collective-permute-start | bytes 24584 | tf_op jit(solution)/shard_map/ppermute | solution.py:23
  31.1 4.1 %copy-start.11 = (f32[8,256]{1,0:T(8,128)}, f32[8,256]{1,0:T(8,128)S(1)}, u32[]{:S(2)}) copy-start(f32[8,256]{1,0:T(8,128)S(1)} %collective-permute-done.6.refs_3_) | copy-start | bytes 24580
  34.3 0.9 %copy-start.12 = (f32[8,256]{1,0:T(8,128)}, f32[8,256]{1,0:T(8,128)S(1)}, u32[]{:S(2)}) copy-start(f32[8,256]{1,0:T(8,128)S(1)} %collective-permute-done.5.refs_2_) | copy-start | bytes 24580
  35.2 0.6 %copy-start.13 = (f32[8,256]{1,0:T(8,128)}, f32[8,256]{1,0:T(8,128)S(1)}, u32[]{:S(2)}) copy-start(f32[8,256]{1,0:T(8,128)S(1)} %collective-permute-done.4.refs_1_) | copy-start | bytes 24580
  38.4 4.8 %collective-permute-start.7 = (f32[16,720]{1,0:T(8,128)}, f32[16,720]{1,0:T(8,128)S(1)}, u32[]{:S(2)}, u32[]{:S(2)}) collective-permute-start(f32[16,720]{1,0:T(8,128)} %get-tuple-element.23), channel_id=1, source_target_pairs={{0,4},{4,8},{8,12},{12,16},{16,20},{20,24},{24,28},{28,0},{1,5},{5... | collective-permute-start | bytes 138248 | tf_op jit(solution)/shard_map/ppermute | solution.py:338
  38.4 4.8 %collective-permute-start.8 = (f32[16,720]{1,0:T(8,128)}, f32[16,720]{1,0:T(8,128)S(1)}, u32[]{:S(2)}, u32[]{:S(2)}) collective-permute-start(f32[16,720]{1,0:T(8,128)} %get-tuple-element.24), channel_id=1, source_target_pairs={{4,0},{8,4},{12,8},{16,12},{20,16},{24,20},{28,24},{0,28},{5,1},{9... | collective-permute-start | bytes 138248 | tf_op jit(solution)/shard_map/ppermute | solution.py:339
  43.2 0.6 %copy-start.5 = (f32[16,720]{1,0:T(8,128)}, f32[16,720]{1,0:T(8,128)S(1)}, u32[]{:S(2)}) copy-start(f32[16,720]{1,0:T(8,128)S(1)} %collective-permute-done.7) | copy-start | bytes 138244
  43.2 0.6 %copy-start.6 = (f32[16,720]{1,0:T(8,128)}, f32[16,720]{1,0:T(8,128)S(1)}, u32[]{:S(2)}) copy-start(f32[16,720]{1,0:T(8,128)S(1)} %collective-permute-done.8) | copy-start | bytes 138244
  43.2 0.8 %copy-start.1 = (bf16[20,1,16,720]{3,2,1,0:T(8,128)(2,1)}, bf16[20,1,16,720]{3,2,1,0:T(8,128)(2,1)S(1)}, u32[]{:S(2)}) copy-start(bf16[20,1,16,720]{3,2,1,0:T(8,128)(2,1)S(1)} %collective-permute-done.3.phigh_ref) | copy-start | bytes 1382404
  43.2 1.0 %copy-start.2 = (bf16[20,1,16,720]{3,2,1,0:T(8,128)(2,1)}, bf16[20,1,16,720]{3,2,1,0:T(8,128)(2,1)S(1)}, u32[]{:S(2)}) copy-start(bf16[20,1,16,720]{3,2,1,0:T(8,128)(2,1)S(1)} %collective-permute-done.2.plow_ref) | copy-start | bytes 1382404

commit v19 on v17

--- a/solution.py
+++ b/solution.py
@@ -172,13 +172,15 @@
                 fold_ref[part * padded:(part + 1) * padded, 0:width] = acc_ref[
                     :, part * 128:part * 128 + width
                 ]
-            pieces = split3(fold_ref[...])
+            pieces = jnp.concatenate(split3(fold_ref[...]), axis=1)
             key_ids = lax.broadcasted_iota(jnp.int32, (parts * padded, slots), 0)
             for row in range(sources):
                 keys, onehot = cell_keys(cells_ref[row, 2:3, :], padded, lat_cells)
-                at_keys = jnp.dot(pieces[0], onehot, preferred_element_type=jnp.float32)
-                at_keys = at_keys + jnp.dot(pieces[1], onehot, preferred_element_type=jnp.float32)
-                at_keys = at_keys + jnp.dot(pieces[2], onehot, preferred_element_type=jnp.float32)
+                at_keys = jnp.dot(
+                    pieces,
+                    jnp.concatenate([onehot, onehot, onehot], axis=0),
+                    preferred_element_type=jnp.float32,
+                )
                 out_ref[row:row + 1, :] = jnp.sum(
                     jnp.where(key_ids == keys, at_keys, 0.0), axis=0, keepdims=True
                 )
@@ -227,14 +229,21 @@
                 at_cells[row:row + 1, :] - lists_ref[row, 0:1, :]
             )
             keys, onehot = cell_keys(lists_ref[row, 2:3, :], padded, lat_cells)
-            for piece in split3(misfit):
-                weighted = jnp.where(key_ids == keys, piece.astype(jnp.float32), 0.0)
-                folded = folded + lax.dot_general(
-                    weighted.astype(jnp.bfloat16),
-                    onehot,
-                    (((1,), (1,)), ((), ())),
-                    preferred_element_type=jnp.float32,
-                )
+            hits = key_ids == keys
+            weighted = jnp.concatenate(
+                [
+                    jnp.where(hits, piece.astype(jnp.float32), 0.0).astype(jnp.bfloat16)
+                    for piece in split3(misfit)
+                ],
+                axis=0,
+            )
+            summed = lax.dot_general(
+                weighted, onehot, (((1,), (1,)), ((), ())), preferred_element_type=jnp.float32
+            )
+            rows_here = parts * padded
+            folded = folded + (
+                summed[0:rows_here] + summed[rows_here:2 * rows_here]
+            ) + summed[2 * rows_here:3 * rows_here]
         for part in range(parts):
             width = min(128, lat_cells - part * 128)
             fold_ref[:, part * 128:part * 128 + width] = folded[

time: 48.6 us -> 48.4 us (level)
  transfers between devices with their start and end apart: 9 -> 9, of which waited for: 4 -> 4; matrix products, arithmetic and copies ran while one was open for 2% -> 2% of each run, Pallas kernels for 21% -> 20%
where the time goes in v19:
time: 48.4 us; the launch traced here: 48.2 us
  Pallas kernels  15.2 us (31%)
  starting transfers between devices  11.8 us (24%)
  blocking collectives  9.92 us (20%)
  waiting for transfers between devices  6.72 us (14%)
  local copies, waits for them, and re-layouts  3.29 us (7%)
  other arithmetic  1.16 us (2%)
    all_to_all x1, blocking collectives, local(): lax.all_to_all(lists, 'tile', split_axis=0, concat_axis=0, tiled=True)  9.92 us
    pallas_call x1, Pallas kernels, backward_grad(): pl.pallas_call(kernel, grid=(levels, members // chunk), in_specs=[field,...  5.42 us
    pallas_call x1, Pallas kernels, forward_pick(): pl.pallas_call(kernel, grid=(steps,), in_specs=[field, halo, halo, field,...  5.14 us
    ppermute x3, waiting for transfers between devices, gather_over(): lax.ppermute(values, axis, [(i, (i + shift) % count) for i in range(count)])  4.64 us
    ppermute x3, starting transfers between devices, gather_over(): lax.ppermute(values, axis, [(i, (i + shift) % count) for i in range(count)])  4.62 us
    ppermute x2, starting transfers between devices, halos(): lax.ppermute(lax.slice_in_dim(block, 0, width, axis=dim), axis, backward)  4.52 us
    ppermute x1, starting transfers between devices, local(): lax.ppermute(high_send, 'tile', [((i + 1) % count, i) for i in range(coun...  2.64 us
    pallas_call x1, Pallas kernels, spread_misfits(): pl.pallas_call(kernel, out_shape=(jax.ShapeDtypeStruct((lon_cells, lat_ce...  2.63 us
  transfers between devices with their start and end apart: 9, of which 4 were waited for; matrix products, arithmetic and copies ran while one was open for 2% of the time, Pallas kernels for 20%

profile of v19, /device:TPU:0, one launch (start us, length us, event | category | flops | bytes accessed | tf_op | source)
XLA Modules:
  0.0 48.2 jit_solution(13797821402240963358)
XLA Ops:
  0.0 0.0 copy-start.9
  0.0 0.0 copy-start
  0.0 1.5 %fusion.2 = (bf16[20,1,16,720]{3,2,1,0:T(8,128)(2,1)S(1)}, bf16[20,1,16,720]{3,2,1,0:T(8,128)(2,1)S(1)}) fusion(bf16[20,1,45,720]{3,2,1,0:T(8,128)(2,1)} %ctrl_ref.3), kind=kLoop, calls=%fused_computation.5 | loop fusion | bytes 1843200 | tf_op jit(solution)/shard_map/slice | solution.py:18
  1.6 3.4 %collective-permute-start.1 = (bf16[20,1,16,720]{3,2,1,0:T(8,128)(2,1)S(1)}, bf16[20,1,16,720]{3,2,1,0:T(8,128)(2,1)S(1)}, u32[]{:S(2)}, u32[]{:S(2)}) collective-permute-start(bf16[20,1,16,720]{3,2,1,0:T(8,128)(2,1)S(1)} %get-tuple-element.27), channel_id=1, source_target_pairs={{4,0},{8,4},{12,8},{16,12},{20,16},{24,20},{28,24},{0,28},{5,1},{9... | collective-permute-start | bytes 1382408 | tf_op jit(solution)/shard_map/ppermute | solution.py:18
  5.0 0.0 collective-permute-start
  5.0 0.0 copy-done.14
  5.0 0.5 %convert_element_type.21.lon_ref = f32[17]{0:T(128)} convert(bf16[17]{0:T(256)(128)(2,1)S(1)} %copy-done.14) | non-fusion elementwise | flops 17 | bytes 102 | tf_op jit(solution)/shard_map/convert_element_type | solution.py:84
  5.5 0.0 copy-done.15
  5.5 0.5 %convert_element_type.22.lat_ref = f32[17]{0:T(128)} convert(bf16[17]{0:T(256)(128)(2,1)S(1)} %copy-done.15) | non-fusion elementwise | flops 17 | bytes 102 | tf_op jit(solution)/shard_map/convert_element_type | solution.py:84
  6.1 0.0 copy-done.7
  6.1 0.0 copy-done.8
  6.1 2.0 %shard_map.85 = (bf16[48,80]{1,0:T(8,128)(2,1)}, bf16[720,720]{1,0:T(8,128)(2,1)}) custom-call(f32[17]{0:T(128)} %convert_element_type.21.lon_ref, f32[17]{0:T(128)} %convert_element_type.22.lat_ref), custom_call_target="tpu_custom_call" | custom-call | tf_op jit(solution)/shard_map/pallas_call | solution.py:77
  8.1 0.0 copy-done.13
  8.1 0.0 copy-done.9
  8.1 0.1 fusion
  8.2 9.9 %all_to_all.5.cells_ref.refs_4_ = f32[8,3,256]{2,1,0:T(4,128)} all-to-all(f32[8,3,256]{2,1,0:T(4,128)S(1)} %pad_maximum_fusion), channel_id=1, replica_groups=mesh['tile'=8,'mem'=4] {'tile'}, dimensions={0} | all-to-all | bytes 49152 | tf_op jit(solution)/shard_map/all_to_all | solution.py:335
  18.1 0.0 collective-permute-done.1.high_ref
  18.1 0.0 collective-permute-done.low_ref
  18.1 0.0 copy-done
  18.1 0.0 copy-start.4
  18.1 0.1 fusion.1
  18.3 1.1 %collective-permute-start.3 = (bf16[20,1,16,720]{3,2,1,0:T(8,128)(2,1)S(1)}, bf16[20,1,16,720]{3,2,1,0:T(8,128)(2,1)S(1)}, u32[]{:S(2)}, u32[]{:S(2)}) collective-permute-start(bf16[20,1,16,720]{3,2,1,0:T(8,128)(2,1)S(1)} %get-tuple-element.25), channel_id=1, source_target_pairs={{4,0},{8,4},{12,8},{16,12},{20,16},{24,20},{28,24},{0,28},{5,1},{9... | collective-permute-start | bytes 1382408 | tf_op jit(solution)/shard_map/ppermute | solution.py:18
  19.4 0.0 collective-permute-start.2
  19.4 0.0 copy-done.3
  19.4 0.0 copy-done.4
  19.4 5.1 %shard_map.86.refs_0_ = f32[8,256]{1,0:T(8,128)} custom-call(bf16[20,1,45,720]{3,2,1,0:T(8,128)(2,1)} %ctrl_ref.3, bf16[20,1,16,720]{3,2,1,0:T(8,128)(2,1)} %copy-done.4, bf16[20,1,16,720]{3,2,1,0:T(8,128)(2,1)} %copy-done.3, bf16[20,1,45,720]{3,2,1,0:T(8,128)(2,1)} %pert_ref.3, bf16[48,80]{1,0:T(8,128)(2,1)} %get-tuple-element.15.blon_ref, ...), custom_call_target="tpu_custom_call" | custom-call | tf_op jit(solution)/shard_map/pallas_call | solution.py:191
  24.5 3.6 %collective-permute-start.6 = (f32[8,256]{1,0:T(8,128)}, f32[8,256]{1,0:T(8,128)S(1)}, u32[]{:S(2)}, u32[]{:S(2)}) collective-permute-start(f32[8,256]{1,0:T(8,128)} %shard_map.86.refs_0_), channel_id=1, source_target_pairs={{0,3},{1,0},{2,1},{3,2},{4,7},{5,4},{6,5},{7,6},{8,11},{9,8},{10,9... | collective-permute-start | bytes 24584 | tf_op jit(solution)/shard_map/ppermute | solution.py:25
  28.1 0.0 collective-permute-start.5
  28.1 1.0 %collective-permute-start.4 = (f32[8,256]{1,0:T(8,128)}, f32[8,256]{1,0:T(8,128)S(1)}, u32[]{:S(2)}, u32[]{:S(2)}) collective-permute-start(f32[8,256]{1,0:T(8,128)} %shard_map.86.refs_0_), channel_id=1, source_target_pairs={{0,1},{1,2},{2,3},{3,0},{4,5},{5,6},{6,7},{7,4},{8,9},{9,10},{10,1... | collective-permute-start | bytes 24584 | tf_op jit(solution)/shard_map/ppermute | solution.py:25
  29.1 0.6 %collective-permute-done.6.refs_3_ = f32[8,256]{1,0:T(8,128)S(1)} collective-permute-done((f32[8,256]{1,0:T(8,128)}, f32[8,256]{1,0:T(8,128)S(1)}, u32[]{:S(2)}, u32[]{:S(2)}) %collective-permute-start.6) | collective-permute-done | bytes 8224 | tf_op jit(solution)/shard_map/ppermute | solution.py:25
  29.7 3.2 %collective-permute-done.5.refs_2_ = f32[8,256]{1,0:T(8,128)S(1)} collective-permute-done((f32[8,256]{1,0:T(8,128)}, f32[8,256]{1,0:T(8,128)S(1)}, u32[]{:S(2)}, u32[]{:S(2)}) %collective-permute-start.5) | collective-permute-done | bytes 8224 | tf_op jit(solution)/shard_map/ppermute | solution.py:25
  32.9 0.9 %collective-permute-done.4.refs_1_ = f32[8,256]{1,0:T(8,128)S(1)} collective-permute-done((f32[8,256]{1,0:T(8,128)}, f32[8,256]{1,0:T(8,128)S(1)}, u32[]{:S(2)}, u32[]{:S(2)}) %collective-permute-start.4) | collective-permute-done | bytes 8224 | tf_op jit(solution)/shard_map/ppermute | solution.py:25
  33.8 0.0 copy-done.10
  33.8 0.0 copy-done.11
  33.8 0.6 %copy-done.12 = f32[8,256]{1,0:T(8,128)} copy-done((f32[8,256]{1,0:T(8,128)}, f32[8,256]{1,0:T(8,128)S(1)}, u32[]{:S(2)}) %copy-start.12) | copy-done | bytes 8216
  34.4 2.6 %shard_map.87 = (f32[45,720]{1,0:T(8,128)}, f32[16,720]{1,0:T(8,128)}, f32[16,720]{1,0:T(8,128)}) custom-call(f32[8,256]{1,0:T(8,128)} %shard_map.86.refs_0_, f32[8,256]{1,0:T(8,128)} %copy-done.12, f32[8,256]{1,0:T(8,128)} %copy-done.11, f32[8,256]{1,0:T(8,128)} %copy-done.10, f32[8,3,256]{2,1,0:T(4,128)} %all_to_all.5.cells_ref.refs_4_), custom_call_target="tpu_custom_call" | custom-call | tf_op jit(solution)/shard_map/pallas_call | solution.py:256
  37.0 0.0 collective-permute-start.7
  37.0 2.6 %collective-permute-start.8 = (f32[16,720]{1,0:T(8,128)}, f32[16,720]{1,0:T(8,128)S(1)}, u32[]{:S(2)}, u32[]{:S(2)}) collective-permute-start(f32[16,720]{1,0:T(8,128)} %get-tuple-element.24), channel_id=1, source_target_pairs={{4,0},{8,4},{12,8},{16,12},{20,16},{24,20},{28,24},{0,28},{5,1},{9... | collective-permute-start | bytes 138248 | tf_op jit(solution)/shard_map/ppermute | solution.py:350
  39.7 2.1 %collective-permute-done.7 = f32[16,720]{1,0:T(8,128)S(1)} collective-permute-done((f32[16,720]{1,0:T(8,128)}, f32[16,720]{1,0:T(8,128)S(1)}, u32[]{:S(2)}, u32[]{:S(2)}) %collective-permute-start.7) | collective-permute-done | bytes 46112 | tf_op jit(solution)/shard_map/ppermute | solution.py:349
  41.7 0.0 collective-permute-done.8
  41.7 0.0 collective-permute-done.3.phigh_ref
  41.7 0.0 collective-permute-done.2.plow_ref
  41.8 0.0 copy-start.2
  41.8 0.6 %copy-done.5 = f32[16,720]{1,0:T(8,128)} copy-done((f32[16,720]{1,0:T(8,128)}, f32[16,720]{1,0:T(8,128)S(1)}, u32[]{:S(2)}) %copy-start.5) | copy-done | bytes 46104
  42.3 0.0 copy-done.6
  42.4 0.2 copy-done.1
  42.6 0.2 copy-done.2
  42.7 5.4 %shard_map.88 = f32[20,45,1,720]{3,2,1,0:T(1,128)} custom-call(bf16[20,1,45,720]{3,2,1,0:T(8,128)(2,1)} %pert_ref.3, bf16[20,1,16,720]{3,2,1,0:T(8,128)(2,1)} %copy-done.2, bf16[20,1,16,720]{3,2,1,0:T(8,128)(2,1)} %copy-done.1, f32[1,45,720]{2,1,0:T(8,128)} %bitcast.9, f32[1,16,720]{2,1,0:T(8,128)} %bitcast.10, f32[1,16,720]{2,1,0:T(8,128)} %bitcast.11, ...), custom_call_target="tpu_custom_call" | custom-call | tf_op jit(solution)/shard_map/pallas_call | solution.py:300
  (15 shorter events, 0.1 us)
Async XLA Ops:
  0.0 5.0 %copy-start.14 = (bf16[17]{0:T(256)(128)(2,1)S(1)}, bf16[17]{0:T(256)(128)(2,1)}, u32[]{:S(2)}) copy-start(bf16[17]{0:T(256)(128)(2,1)} %param.10) | copy-start | bytes 106
  0.0 5.5 %copy-start.15 = (bf16[17]{0:T(256)(128)(2,1)S(1)}, bf16[17]{0:T(256)(128)(2,1)}, u32[]{:S(2)}) copy-start(bf16[17]{0:T(256)(128)(2,1)} %param.11) | copy-start | bytes 106
  0.0 6.0 %copy-start.7 = (f32[1,8,256]{2,1,0:T(8,128)S(1)}, f32[1,8,256]{2,1,0:T(8,128)}, u32[]{:S(2)}) copy-start(f32[1,8,256]{2,1,0:T(8,128)} %param.12) | copy-start | bytes 24580
  0.0 6.1 %copy-start.8 = (s32[1,8,256]{2,1,0:T(8,128)S(1)}, s32[1,8,256]{2,1,0:T(8,128)}, u32[]{:S(2)}) copy-start(s32[1,8,256]{2,1,0:T(8,128)} %param.14) | copy-start | bytes 24580
  0.0 8.0 %copy-start.13 = (s32[1,8]{1,0:T(1,128)S(1)}, s32[1,8]{1,0:T(1,128)}, u32[]{:S(2)}) copy-start(s32[1,8]{1,0:T(1,128)} %param.15) | copy-start | bytes 100
  0.0 8.0 %copy-start.9 = (f32[1,8,256]{2,1,0:T(8,128)S(1)}, f32[1,8,256]{2,1,0:T(8,128)}, u32[]{:S(2)}) copy-start(f32[1,8,256]{2,1,0:T(8,128)} %param.13) | copy-start | bytes 24580
  0.0 18.1 %copy-start = (bf16[20,1,45,720]{3,2,1,0:T(8,128)(2,1)S(1)}, bf16[20,1,45,720]{3,2,1,0:T(8,128)(2,1)}, u32[]{:S(2)}) copy-start(bf16[20,1,45,720]{3,2,1,0:T(8,128)(2,1)} %pert_ref.3) | copy-start | bytes 3888004
  1.6 16.5 %collective-permute-start.1 = (bf16[20,1,16,720]{3,2,1,0:T(8,128)(2,1)S(1)}, bf16[20,1,16,720]{3,2,1,0:T(8,128)(2,1)S(1)}, u32[]{:S(2)}, u32[]{:S(2)}) collective-permute-start(bf16[20,1,16,720]{3,2,1,0:T(8,128)(2,1)S(1)} %get-tuple-element.27), channel_id=1, source_target_pairs={{4,0},{8,4},{12,8},{16,12},{20,16},{24,20},{28,24},{0,28},{5,1},{9... | collective-permute-start | bytes 1382408 | tf_op jit(solution)/shard_map/ppermute | solution.py:18
  5.0 13.1 %collective-permute-start = (bf16[20,1,16,720]{3,2,1,0:T(8,128)(2,1)S(1)}, bf16[20,1,16,720]{3,2,1,0:T(8,128)(2,1)S(1)}, u32[]{:S(2)}, u32[]{:S(2)}) collective-permute-start(bf16[20,1,16,720]{3,2,1,0:T(8,128)(2,1)S(1)} %get-tuple-element.28), channel_id=1, source_target_pairs={{0,4},{4,8},{8,12},{12,16},{16,20},{20,24},{24,28},{28,0},{1,5},{5... | collective-permute-start | bytes 1382408 | tf_op jit(solution)/shard_map/ppermute | solution.py:15
  18.1 1.3 %copy-start.3 = (bf16[20,1,16,720]{3,2,1,0:T(8,128)(2,1)}, bf16[20,1,16,720]{3,2,1,0:T(8,128)(2,1)S(1)}, u32[]{:S(2)}) copy-start(bf16[20,1,16,720]{3,2,1,0:T(8,128)(2,1)S(1)} %collective-permute-done.1.high_ref) | copy-start | bytes 1382404
  18.1 1.3 %copy-start.4 = (bf16[20,1,16,720]{3,2,1,0:T(8,128)(2,1)}, bf16[20,1,16,720]{3,2,1,0:T(8,128)(2,1)S(1)}, u32[]{:S(2)}) copy-start(bf16[20,1,16,720]{3,2,1,0:T(8,128)(2,1)S(1)} %collective-permute-done.low_ref) | copy-start | bytes 1382404
  18.3 23.5 %collective-permute-start.3 = (bf16[20,1,16,720]{3,2,1,0:T(8,128)(2,1)S(1)}, bf16[20,1,16,720]{3,2,1,0:T(8,128)(2,1)S(1)}, u32[]{:S(2)}, u32[]{:S(2)}) collective-permute-start(bf16[20,1,16,720]{3,2,1,0:T(8,128)(2,1)S(1)} %get-tuple-element.25), channel_id=1, source_target_pairs={{4,0},{8,4},{12,8},{16,12},{20,16},{24,20},{28,24},{0,28},{5,1},{9... | collective-permute-start | bytes 1382408 | tf_op jit(solution)/shard_map/ppermute | solution.py:18
  19.4 22.4 %collective-permute-start.2 = (bf16[20,1,16,720]{3,2,1,0:T(8,128)(2,1)S(1)}, bf16[20,1,16,720]{3,2,1,0:T(8,128)(2,1)S(1)}, u32[]{:S(2)}, u32[]{:S(2)}) collective-permute-start(bf16[20,1,16,720]{3,2,1,0:T(8,128)(2,1)S(1)} %get-tuple-element.26), channel_id=1, source_target_pairs={{0,4},{4,8},{8,12},{12,16},{16,20},{20,24},{24,28},{28,0},{1,5},{5... | collective-permute-start | bytes 1382408 | tf_op jit(solution)/shard_map/ppermute | solution.py:15
  24.5 5.2 %collective-permute-start.6 = (f32[8,256]{1,0:T(8,128)}, f32[8,256]{1,0:T(8,128)S(1)}, u32[]{:S(2)}, u32[]{:S(2)}) collective-permute-start(f32[8,256]{1,0:T(8,128)} %shard_map.86.refs_0_), channel_id=1, source_target_pairs={{0,3},{1,0},{2,1},{3,2},{4,7},{5,4},{6,5},{7,6},{8,11},{9,8},{10,9... | collective-permute-start | bytes 24584 | tf_op jit(solution)/shard_map/ppermute | solution.py:25
  28.1 4.8 %collective-permute-start.5 = (f32[8,256]{1,0:T(8,128)}, f32[8,256]{1,0:T(8,128)S(1)}, u32[]{:S(2)}, u32[]{:S(2)}) collective-permute-start(f32[8,256]{1,0:T(8,128)} %shard_map.86.refs_0_), channel_id=1, source_target_pairs={{0,2},{1,3},{2,0},{3,1},{4,6},{5,7},{6,4},{7,5},{8,10},{9,11},{10,... | collective-permute-start | bytes 24584 | tf_op jit(solution)/shard_map/ppermute | solution.py:25
  28.1 5.7 %collective-permute-start.4 = (f32[8,256]{1,0:T(8,128)}, f32[8,256]{1,0:T(8,128)S(1)}, u32[]{:S(2)}, u32[]{:S(2)}) collective-permute-start(f32[8,256]{1,0:T(8,128)} %shard_map.86.refs_0_), channel_id=1, source_target_pairs={{0,1},{1,2},{2,3},{3,0},{4,5},{5,6},{6,7},{7,4},{8,9},{9,10},{10,1... | collective-permute-start | bytes 24584 | tf_op jit(solution)/shard_map/ppermute | solution.py:25
  29.7 4.1 %copy-start.10 = (f32[8,256]{1,0:T(8,128)}, f32[8,256]{1,0:T(8,128)S(1)}, u32[]{:S(2)}) copy-start(f32[8,256]{1,0:T(8,128)S(1)} %collective-permute-done.6.refs_3_) | copy-start | bytes 24580
  32.9 0.9 %copy-start.11 = (f32[8,256]{1,0:T(8,128)}, f32[8,256]{1,0:T(8,128)S(1)}, u32[]{:S(2)}) copy-start(f32[8,256]{1,0:T(8,128)S(1)} %collective-permute-done.5.refs_2_) | copy-start | bytes 24580
  33.8 0.6 %copy-start.12 = (f32[8,256]{1,0:T(8,128)}, f32[8,256]{1,0:T(8,128)S(1)}, u32[]{:S(2)}) copy-start(f32[8,256]{1,0:T(8,128)S(1)} %collective-permute-done.4.refs_1_) | copy-start | bytes 24580
  37.0 4.7 %collective-permute-start.7 = (f32[16,720]{1,0:T(8,128)}, f32[16,720]{1,0:T(8,128)S(1)}, u32[]{:S(2)}, u32[]{:S(2)}) collective-permute-start(f32[16,720]{1,0:T(8,128)} %get-tuple-element.23), channel_id=1, source_target_pairs={{0,4},{4,8},{8,12},{12,16},{16,20},{20,24},{24,28},{28,0},{1,5},{5... | collective-permute-start | bytes 138248 | tf_op jit(solution)/shard_map/ppermute | solution.py:349
  37.0 4.7 %collective-permute-start.8 = (f32[16,720]{1,0:T(8,128)}, f32[16,720]{1,0:T(8,128)S(1)}, u32[]{:S(2)}, u32[]{:S(2)}) collective-permute-start(f32[16,720]{1,0:T(8,128)} %get-tuple-element.24), channel_id=1, source_target_pairs={{4,0},{8,4},{12,8},{16,12},{20,16},{24,20},{28,24},{0,28},{5,1},{9... | collective-permute-start | bytes 138248 | tf_op jit(solution)/shard_map/ppermute | solution.py:350
  41.7 0.6 %copy-start.5 = (f32[16,720]{1,0:T(8,128)}, f32[16,720]{1,0:T(8,128)S(1)}, u32[]{:S(2)}) copy-start(f32[16,720]{1,0:T(8,128)S(1)} %collective-permute-done.7) | copy-start | bytes 138244
  41.7 0.6 %copy-start.6 = (f32[16,720]{1,0:T(8,128)}, f32[16,720]{1,0:T(8,128)S(1)}, u32[]{:S(2)}) copy-start(f32[16,720]{1,0:T(8,128)S(1)} %collective-permute-done.8) | copy-start | bytes 138244
  41.7 0.8 %copy-start.1 = (bf16[20,1,16,720]{3,2,1,0:T(8,128)(2,1)}, bf16[20,1,16,720]{3,2,1,0:T(8,128)(2,1)S(1)}, u32[]{:S(2)}) copy-start(bf16[20,1,16,720]{3,2,1,0:T(8,128)(2,1)S(1)} %collective-permute-done.3.phigh_ref) | copy-start | bytes 1382404
  41.8 1.0 %copy-start.2 = (bf16[20,1,16,720]{3,2,1,0:T(8,128)(2,1)}, bf16[20,1,16,720]{3,2,1,0:T(8,128)(2,1)S(1)}, u32[]{:S(2)}) copy-start(bf16[20,1,16,720]{3,2,1,0:T(8,128)(2,1)S(1)} %collective-permute-done.2.plow_ref) | copy-start | bytes 1382404

commit v20 on v17

--- a/solution.py
+++ b/solution.py
@@ -259,7 +259,7 @@
     members, levels, lon_cells, lat_cells = control.shape
     radius = p_low.shape[2]
     padded, ext_cells = band_lon.shape
-    chunk = member_chunk(members)
+    chunk = members
 
     def kernel(pert_ref, plow_ref, phigh_ref, spread_ref, slow_ref, shigh_ref, ctrl_ref,
                blon_ref, blat_ref, out_ref, ext_ref, along_ref):

time: 48.6 us -> 49.4 us (1.016)
  Pallas kernels: 15.3 us -> 16.1 us
    pallas_call x1, Pallas kernels: 5.41 us -> 6.18 us  [backward_grad(): pl.pallas_call(kernel, grid=(levels, members // chunk), in_specs=[field,...]
  transfers between devices with their start and end apart: 9 -> 9, of which waited for: 4 -> 4; matrix products, arithmetic and copies ran while one was open for 2% -> 2% of each run, Pallas kernels for 21% -> 20%
where the time goes in v20:
time: 49.4 us; the launch traced here: 49.1 us
  Pallas kernels  16.1 us (33%)
  starting transfers between devices  11.8 us (24%)
  blocking collectives  9.92 us (20%)
  waiting for transfers between devices  6.73 us (14%)
  local copies, waits for them, and re-layouts  3.29 us (7%)
  other arithmetic  1.16 us (2%)
    all_to_all x1, blocking collectives, local(): lax.all_to_all(lists, 'tile', split_axis=0, concat_axis=0, tiled=True)  9.92 us
    pallas_call x1, Pallas kernels, backward_grad(): pl.pallas_call(kernel, grid=(levels, members // chunk), in_specs=[field,...  6.18 us
    pallas_call x1, Pallas kernels, forward_pick(): pl.pallas_call(kernel, grid=(steps,), in_specs=[field, halo, halo, field,...  5.32 us
    ppermute x3, waiting for transfers between devices, gather_over(): lax.ppermute(values, axis, [(i, (i + shift) % count) for i in range(count)])  4.64 us
    ppermute x3, starting transfers between devices, gather_over(): lax.ppermute(values, axis, [(i, (i + shift) % count) for i in range(count)])  4.62 us
    ppermute x2, starting transfers between devices, halos(): lax.ppermute(lax.slice_in_dim(block, 0, width, axis=dim), axis, backward)  4.52 us
    ppermute x1, starting transfers between devices, local(): lax.ppermute(high_send, 'tile', [((i + 1) % count, i) for i in range(coun...  2.64 us
    pallas_call x1, Pallas kernels, spread_misfits(): pl.pallas_call(kernel, out_shape=(jax.ShapeDtypeStruct((lon_cells, lat_ce...  2.63 us
  transfers between devices with their start and end apart: 9, of which 4 were waited for; matrix products, arithmetic and copies ran while one was open for 2% of the time, Pallas kernels for 20%

profile of v20, /device:TPU:0, one launch (start us, length us, event | category | flops | bytes accessed | tf_op | source)
XLA Modules:
  0.0 49.1 jit_solution(3147159785646506158)
XLA Ops:
  0.0 0.0 copy-start.9
  0.0 0.0 copy-start
  0.0 1.5 %fusion.2 = (bf16[20,1,16,720]{3,2,1,0:T(8,128)(2,1)S(1)}, bf16[20,1,16,720]{3,2,1,0:T(8,128)(2,1)S(1)}) fusion(bf16[20,1,45,720]{3,2,1,0:T(8,128)(2,1)} %ctrl_ref.3), kind=kLoop, calls=%fused_computation.5 | loop fusion | bytes 1843200 | tf_op jit(solution)/shard_map/slice | solution.py:18
  1.6 3.4 %collective-permute-start.1 = (bf16[20,1,16,720]{3,2,1,0:T(8,128)(2,1)S(1)}, bf16[20,1,16,720]{3,2,1,0:T(8,128)(2,1)S(1)}, u32[]{:S(2)}, u32[]{:S(2)}) collective-permute-start(bf16[20,1,16,720]{3,2,1,0:T(8,128)(2,1)S(1)} %get-tuple-element.27), channel_id=1, source_target_pairs={{4,0},{8,4},{12,8},{16,12},{20,16},{24,20},{28,24},{0,28},{5,1},{9... | collective-permute-start | bytes 1382408 | tf_op jit(solution)/shard_map/ppermute | solution.py:18
  5.0 0.0 collective-permute-start
  5.0 0.0 copy-done.14
  5.0 0.5 %convert_element_type.21.lon_ref = f32[17]{0:T(128)} convert(bf16[17]{0:T(256)(128)(2,1)S(1)} %copy-done.14) | non-fusion elementwise | flops 17 | bytes 102 | tf_op jit(solution)/shard_map/convert_element_type | solution.py:84
  5.5 0.0 copy-done.15
  5.5 0.5 %convert_element_type.22.lat_ref = f32[17]{0:T(128)} convert(bf16[17]{0:T(256)(128)(2,1)S(1)} %copy-done.15) | non-fusion elementwise | flops 17 | bytes 102 | tf_op jit(solution)/shard_map/convert_element_type | solution.py:84
  6.1 0.0 copy-done.7
  6.1 0.0 copy-done.8
  6.1 2.0 %shard_map.85 = (bf16[48,80]{1,0:T(8,128)(2,1)}, bf16[720,720]{1,0:T(8,128)(2,1)}) custom-call(f32[17]{0:T(128)} %convert_element_type.21.lon_ref, f32[17]{0:T(128)} %convert_element_type.22.lat_ref), custom_call_target="tpu_custom_call" | custom-call | tf_op jit(solution)/shard_map/pallas_call | solution.py:77
  8.1 0.0 copy-done.13
  8.1 0.0 copy-done.9
  8.1 0.1 fusion
  8.2 9.9 %all_to_all.5.cells_ref.refs_4_ = f32[8,3,256]{2,1,0:T(4,128)} all-to-all(f32[8,3,256]{2,1,0:T(4,128)S(1)} %pad_maximum_fusion), channel_id=1, replica_groups=mesh['tile'=8,'mem'=4] {'tile'}, dimensions={0} | all-to-all | bytes 49152 | tf_op jit(solution)/shard_map/all_to_all | solution.py:326
  18.1 0.0 collective-permute-done.1.high_ref
  18.1 0.0 collective-permute-done.low_ref
  18.1 0.0 copy-done
  18.1 0.0 copy-start.4
  18.1 0.1 fusion.1
  18.3 1.1 %collective-permute-start.3 = (bf16[20,1,16,720]{3,2,1,0:T(8,128)(2,1)S(1)}, bf16[20,1,16,720]{3,2,1,0:T(8,128)(2,1)S(1)}, u32[]{:S(2)}, u32[]{:S(2)}) collective-permute-start(bf16[20,1,16,720]{3,2,1,0:T(8,128)(2,1)S(1)} %get-tuple-element.25), channel_id=1, source_target_pairs={{4,0},{8,4},{12,8},{16,12},{20,16},{24,20},{28,24},{0,28},{5,1},{9... | collective-permute-start | bytes 1382408 | tf_op jit(solution)/shard_map/ppermute | solution.py:18
  19.4 0.0 collective-permute-start.2
  19.4 0.0 copy-done.3
  19.4 0.0 copy-done.4
  19.4 5.3 %shard_map.86.refs_0_ = f32[8,256]{1,0:T(8,128)} custom-call(bf16[20,1,45,720]{3,2,1,0:T(8,128)(2,1)} %ctrl_ref.3, bf16[20,1,16,720]{3,2,1,0:T(8,128)(2,1)} %copy-done.4, bf16[20,1,16,720]{3,2,1,0:T(8,128)(2,1)} %copy-done.3, bf16[20,1,45,720]{3,2,1,0:T(8,128)(2,1)} %pert_ref.3, bf16[48,80]{1,0:T(8,128)(2,1)} %get-tuple-element.15.blon_ref, ...), custom_call_target="tpu_custom_call" | custom-call | tf_op jit(solution)/shard_map/pallas_call | solution.py:189
  24.7 3.6 %collective-permute-start.6 = (f32[8,256]{1,0:T(8,128)}, f32[8,256]{1,0:T(8,128)S(1)}, u32[]{:S(2)}, u32[]{:S(2)}) collective-permute-start(f32[8,256]{1,0:T(8,128)} %shard_map.86.refs_0_), channel_id=1, source_target_pairs={{0,3},{1,0},{2,1},{3,2},{4,7},{5,4},{6,5},{7,6},{8,11},{9,8},{10,9... | collective-permute-start | bytes 24584 | tf_op jit(solution)/shard_map/ppermute | solution.py:25
  28.3 0.0 collective-permute-start.5
  28.3 1.0 %collective-permute-start.4 = (f32[8,256]{1,0:T(8,128)}, f32[8,256]{1,0:T(8,128)S(1)}, u32[]{:S(2)}, u32[]{:S(2)}) collective-permute-start(f32[8,256]{1,0:T(8,128)} %shard_map.86.refs_0_), channel_id=1, source_target_pairs={{0,1},{1,2},{2,3},{3,0},{4,5},{5,6},{6,7},{7,4},{8,9},{9,10},{10,1... | collective-permute-start | bytes 24584 | tf_op jit(solution)/shard_map/ppermute | solution.py:25
  29.3 0.6 %collective-permute-done.6.refs_3_ = f32[8,256]{1,0:T(8,128)S(1)} collective-permute-done((f32[8,256]{1,0:T(8,128)}, f32[8,256]{1,0:T(8,128)S(1)}, u32[]{:S(2)}, u32[]{:S(2)}) %collective-permute-start.6) | collective-permute-done | bytes 8224 | tf_op jit(solution)/shard_map/ppermute | solution.py:25
  29.9 3.2 %collective-permute-done.5.refs_2_ = f32[8,256]{1,0:T(8,128)S(1)} collective-permute-done((f32[8,256]{1,0:T(8,128)}, f32[8,256]{1,0:T(8,128)S(1)}, u32[]{:S(2)}, u32[]{:S(2)}) %collective-permute-start.5) | collective-permute-done | bytes 8224 | tf_op jit(solution)/shard_map/ppermute | solution.py:25
  33.1 0.9 %collective-permute-done.4.refs_1_ = f32[8,256]{1,0:T(8,128)S(1)} collective-permute-done((f32[8,256]{1,0:T(8,128)}, f32[8,256]{1,0:T(8,128)S(1)}, u32[]{:S(2)}, u32[]{:S(2)}) %collective-permute-start.4) | collective-permute-done | bytes 8224 | tf_op jit(solution)/shard_map/ppermute | solution.py:25
  34.0 0.0 copy-done.10
  34.0 0.0 copy-done.11
  34.0 0.6 %copy-done.12 = f32[8,256]{1,0:T(8,128)} copy-done((f32[8,256]{1,0:T(8,128)}, f32[8,256]{1,0:T(8,128)S(1)}, u32[]{:S(2)}) %copy-start.12) | copy-done | bytes 8216
  34.6 2.6 %shard_map.87 = (f32[45,720]{1,0:T(8,128)}, f32[16,720]{1,0:T(8,128)}, f32[16,720]{1,0:T(8,128)}) custom-call(f32[8,256]{1,0:T(8,128)} %shard_map.86.refs_0_, f32[8,256]{1,0:T(8,128)} %copy-done.12, f32[8,256]{1,0:T(8,128)} %copy-done.11, f32[8,256]{1,0:T(8,128)} %copy-done.10, f32[8,3,256]{2,1,0:T(4,128)} %all_to_all.5.cells_ref.refs_4_), custom_call_target="tpu_custom_call" | custom-call | tf_op jit(solution)/shard_map/pallas_call | solution.py:247
  37.2 0.0 collective-permute-start.7
  37.2 2.6 %collective-permute-start.8 = (f32[16,720]{1,0:T(8,128)}, f32[16,720]{1,0:T(8,128)S(1)}, u32[]{:S(2)}, u32[]{:S(2)}) collective-permute-start(f32[16,720]{1,0:T(8,128)} %get-tuple-element.24), channel_id=1, source_target_pairs={{4,0},{8,4},{12,8},{16,12},{20,16},{24,20},{28,24},{0,28},{5,1},{9... | collective-permute-start | bytes 138248 | tf_op jit(solution)/shard_map/ppermute | solution.py:341
  39.8 2.1 %collective-permute-done.7 = f32[16,720]{1,0:T(8,128)S(1)} collective-permute-done((f32[16,720]{1,0:T(8,128)}, f32[16,720]{1,0:T(8,128)S(1)}, u32[]{:S(2)}, u32[]{:S(2)}) %collective-permute-start.7) | collective-permute-done | bytes 46112 | tf_op jit(solution)/shard_map/ppermute | solution.py:340
  41.9 0.0 collective-permute-done.8
  41.9 0.0 collective-permute-done.3.phigh_ref
  41.9 0.0 copy-start.1
  41.9 0.0 collective-permute-done.2.plow_ref
  42.0 0.6 %copy-done.5 = f32[16,720]{1,0:T(8,128)} copy-done((f32[16,720]{1,0:T(8,128)}, f32[16,720]{1,0:T(8,128)S(1)}, u32[]{:S(2)}) %copy-start.5) | copy-done | bytes 46104
  42.5 0.0 copy-done.6
  42.6 0.2 copy-done.1
  42.7 0.2 copy-done.2
  42.9 6.2 %shard_map.88 = f32[20,45,1,720]{3,2,1,0:T(1,128)} custom-call(bf16[20,1,45,720]{3,2,1,0:T(8,128)(2,1)} %pert_ref.3, bf16[20,1,16,720]{3,2,1,0:T(8,128)(2,1)} %copy-done.2, bf16[20,1,16,720]{3,2,1,0:T(8,128)(2,1)} %copy-done.1, f32[1,45,720]{2,1,0:T(8,128)} %bitcast.9, f32[1,16,720]{2,1,0:T(8,128)} %bitcast.10, f32[1,16,720]{2,1,0:T(8,128)} %bitcast.11, ...), custom_call_target="tpu_custom_call" | custom-call | tf_op jit(solution)/shard_map/pallas_call | solution.py:291
  (15 shorter events, 0.1 us)
Async XLA Ops:
  0.0 5.0 %copy-start.14 = (bf16[17]{0:T(256)(128)(2,1)S(1)}, bf16[17]{0:T(256)(128)(2,1)}, u32[]{:S(2)}) copy-start(bf16[17]{0:T(256)(128)(2,1)} %param.10) | copy-start | bytes 106
  0.0 5.5 %copy-start.15 = (bf16[17]{0:T(256)(128)(2,1)S(1)}, bf16[17]{0:T(256)(128)(2,1)}, u32[]{:S(2)}) copy-start(bf16[17]{0:T(256)(128)(2,1)} %param.11) | copy-start | bytes 106
  0.0 6.0 %copy-start.7 = (f32[1,8,256]{2,1,0:T(8,128)S(1)}, f32[1,8,256]{2,1,0:T(8,128)}, u32[]{:S(2)}) copy-start(f32[1,8,256]{2,1,0:T(8,128)} %param.12) | copy-start | bytes 24580
  0.0 6.1 %copy-start.8 = (s32[1,8,256]{2,1,0:T(8,128)S(1)}, s32[1,8,256]{2,1,0:T(8,128)}, u32[]{:S(2)}) copy-start(s32[1,8,256]{2,1,0:T(8,128)} %param.14) | copy-start | bytes 24580
  0.0 8.0 %copy-start.13 = (s32[1,8]{1,0:T(1,128)S(1)}, s32[1,8]{1,0:T(1,128)}, u32[]{:S(2)}) copy-start(s32[1,8]{1,0:T(1,128)} %param.15) | copy-start | bytes 100
  0.0 8.0 %copy-start.9 = (f32[1,8,256]{2,1,0:T(8,128)S(1)}, f32[1,8,256]{2,1,0:T(8,128)}, u32[]{:S(2)}) copy-start(f32[1,8,256]{2,1,0:T(8,128)} %param.13) | copy-start | bytes 24580
  0.0 18.1 %copy-start = (bf16[20,1,45,720]{3,2,1,0:T(8,128)(2,1)S(1)}, bf16[20,1,45,720]{3,2,1,0:T(8,128)(2,1)}, u32[]{:S(2)}) copy-start(bf16[20,1,45,720]{3,2,1,0:T(8,128)(2,1)} %pert_ref.3) | copy-start | bytes 3888004
  1.6 16.5 %collective-permute-start.1 = (bf16[20,1,16,720]{3,2,1,0:T(8,128)(2,1)S(1)}, bf16[20,1,16,720]{3,2,1,0:T(8,128)(2,1)S(1)}, u32[]{:S(2)}, u32[]{:S(2)}) collective-permute-start(bf16[20,1,16,720]{3,2,1,0:T(8,128)(2,1)S(1)} %get-tuple-element.27), channel_id=1, source_target_pairs={{4,0},{8,4},{12,8},{16,12},{20,16},{24,20},{28,24},{0,28},{5,1},{9... | collective-permute-start | bytes 1382408 | tf_op jit(solution)/shard_map/ppermute | solution.py:18
  5.0 13.1 %collective-permute-start = (bf16[20,1,16,720]{3,2,1,0:T(8,128)(2,1)S(1)}, bf16[20,1,16,720]{3,2,1,0:T(8,128)(2,1)S(1)}, u32[]{:S(2)}, u32[]{:S(2)}) collective-permute-start(bf16[20,1,16,720]{3,2,1,0:T(8,128)(2,1)S(1)} %get-tuple-element.28), channel_id=1, source_target_pairs={{0,4},{4,8},{8,12},{12,16},{16,20},{20,24},{24,28},{28,0},{1,5},{5... | collective-permute-start | bytes 1382408 | tf_op jit(solution)/shard_map/ppermute | solution.py:15
  18.1 1.3 %copy-start.3 = (bf16[20,1,16,720]{3,2,1,0:T(8,128)(2,1)}, bf16[20,1,16,720]{3,2,1,0:T(8,128)(2,1)S(1)}, u32[]{:S(2)}) copy-start(bf16[20,1,16,720]{3,2,1,0:T(8,128)(2,1)S(1)} %collective-permute-done.1.high_ref) | copy-start | bytes 1382404
  18.1 1.3 %copy-start.4 = (bf16[20,1,16,720]{3,2,1,0:T(8,128)(2,1)}, bf16[20,1,16,720]{3,2,1,0:T(8,128)(2,1)S(1)}, u32[]{:S(2)}) copy-start(bf16[20,1,16,720]{3,2,1,0:T(8,128)(2,1)S(1)} %collective-permute-done.low_ref) | copy-start | bytes 1382404
  18.3 23.6 %collective-permute-start.3 = (bf16[20,1,16,720]{3,2,1,0:T(8,128)(2,1)S(1)}, bf16[20,1,16,720]{3,2,1,0:T(8,128)(2,1)S(1)}, u32[]{:S(2)}, u32[]{:S(2)}) collective-permute-start(bf16[20,1,16,720]{3,2,1,0:T(8,128)(2,1)S(1)} %get-tuple-element.25), channel_id=1, source_target_pairs={{4,0},{8,4},{12,8},{16,12},{20,16},{24,20},{28,24},{0,28},{5,1},{9... | collective-permute-start | bytes 1382408 | tf_op jit(solution)/shard_map/ppermute | solution.py:18
  19.4 22.6 %collective-permute-start.2 = (bf16[20,1,16,720]{3,2,1,0:T(8,128)(2,1)S(1)}, bf16[20,1,16,720]{3,2,1,0:T(8,128)(2,1)S(1)}, u32[]{:S(2)}, u32[]{:S(2)}) collective-permute-start(bf16[20,1,16,720]{3,2,1,0:T(8,128)(2,1)S(1)} %get-tuple-element.26), channel_id=1, source_target_pairs={{0,4},{4,8},{8,12},{12,16},{16,20},{20,24},{24,28},{28,0},{1,5},{5... | collective-permute-start | bytes 1382408 | tf_op jit(solution)/shard_map/ppermute | solution.py:15
  24.7 5.2 %collective-permute-start.6 = (f32[8,256]{1,0:T(8,128)}, f32[8,256]{1,0:T(8,128)S(1)}, u32[]{:S(2)}, u32[]{:S(2)}) collective-permute-start(f32[8,256]{1,0:T(8,128)} %shard_map.86.refs_0_), channel_id=1, source_target_pairs={{0,3},{1,0},{2,1},{3,2},{4,7},{5,4},{6,5},{7,6},{8,11},{9,8},{10,9... | collective-permute-start | bytes 24584 | tf_op jit(solution)/shard_map/ppermute | solution.py:25
  28.3 4.8 %collective-permute-start.5 = (f32[8,256]{1,0:T(8,128)}, f32[8,256]{1,0:T(8,128)S(1)}, u32[]{:S(2)}, u32[]{:S(2)}) collective-permute-start(f32[8,256]{1,0:T(8,128)} %shard_map.86.refs_0_), channel_id=1, source_target_pairs={{0,2},{1,3},{2,0},{3,1},{4,6},{5,7},{6,4},{7,5},{8,10},{9,11},{10,... | collective-permute-start | bytes 24584 | tf_op jit(solution)/shard_map/ppermute | solution.py:25
  28.3 5.7 %collective-permute-start.4 = (f32[8,256]{1,0:T(8,128)}, f32[8,256]{1,0:T(8,128)S(1)}, u32[]{:S(2)}, u32[]{:S(2)}) collective-permute-start(f32[8,256]{1,0:T(8,128)} %shard_map.86.refs_0_), channel_id=1, source_target_pairs={{0,1},{1,2},{2,3},{3,0},{4,5},{5,6},{6,7},{7,4},{8,9},{9,10},{10,1... | collective-permute-start | bytes 24584 | tf_op jit(solution)/shard_map/ppermute | solution.py:25
  29.9 4.1 %copy-start.10 = (f32[8,256]{1,0:T(8,128)}, f32[8,256]{1,0:T(8,128)S(1)}, u32[]{:S(2)}) copy-start(f32[8,256]{1,0:T(8,128)S(1)} %collective-permute-done.6.refs_3_) | copy-start | bytes 24580
  33.1 0.9 %copy-start.11 = (f32[8,256]{1,0:T(8,128)}, f32[8,256]{1,0:T(8,128)S(1)}, u32[]{:S(2)}) copy-start(f32[8,256]{1,0:T(8,128)S(1)} %collective-permute-done.5.refs_2_) | copy-start | bytes 24580
  34.0 0.6 %copy-start.12 = (f32[8,256]{1,0:T(8,128)}, f32[8,256]{1,0:T(8,128)S(1)}, u32[]{:S(2)}) copy-start(f32[8,256]{1,0:T(8,128)S(1)} %collective-permute-done.4.refs_1_) | copy-start | bytes 24580
  37.2 4.7 %collective-permute-start.7 = (f32[16,720]{1,0:T(8,128)}, f32[16,720]{1,0:T(8,128)S(1)}, u32[]{:S(2)}, u32[]{:S(2)}) collective-permute-start(f32[16,720]{1,0:T(8,128)} %get-tuple-element.23), channel_id=1, source_target_pairs={{0,4},{4,8},{8,12},{12,16},{16,20},{20,24},{24,28},{28,0},{1,5},{5... | collective-permute-start | bytes 138248 | tf_op jit(solution)/shard_map/ppermute | solution.py:340
  37.2 4.7 %collective-permute-start.8 = (f32[16,720]{1,0:T(8,128)}, f32[16,720]{1,0:T(8,128)S(1)}, u32[]{:S(2)}, u32[]{:S(2)}) collective-permute-start(f32[16,720]{1,0:T(8,128)} %get-tuple-element.24), channel_id=1, source_target_pairs={{4,0},{8,4},{12,8},{16,12},{20,16},{24,20},{28,24},{0,28},{5,1},{9... | collective-permute-start | bytes 138248 | tf_op jit(solution)/shard_map/ppermute | solution.py:341
  41.9 0.6 %copy-start.5 = (f32[16,720]{1,0:T(8,128)}, f32[16,720]{1,0:T(8,128)S(1)}, u32[]{:S(2)}) copy-start(f32[16,720]{1,0:T(8,128)S(1)} %collective-permute-done.7) | copy-start | bytes 138244
  41.9 0.6 %copy-start.6 = (f32[16,720]{1,0:T(8,128)}, f32[16,720]{1,0:T(8,128)S(1)}, u32[]{:S(2)}) copy-start(f32[16,720]{1,0:T(8,128)S(1)} %collective-permute-done.8) | copy-start | bytes 138244
  41.9 0.8 %copy-start.1 = (bf16[20,1,16,720]{3,2,1,0:T(8,128)(2,1)}, bf16[20,1,16,720]{3,2,1,0:T(8,128)(2,1)S(1)}, u32[]{:S(2)}) copy-start(bf16[20,1,16,720]{3,2,1,0:T(8,128)(2,1)S(1)} %collective-permute-done.3.phigh_ref) | copy-start | bytes 1382404
  41.9 1.0 %copy-start.2 = (bf16[20,1,16,720]{3,2,1,0:T(8,128)(2,1)}, bf16[20,1,16,720]{3,2,1,0:T(8,128)(2,1)S(1)}, u32[]{:S(2)}) copy-start(bf16[20,1,16,720]{3,2,1,0:T(8,128)(2,1)S(1)} %collective-permute-done.2.plow_ref) | copy-start | bytes 1382404

commit v21 on v17

--- a/solution.py
+++ b/solution.py
@@ -74,7 +74,7 @@
                 ]
 
     smem = pl.BlockSpec(memory_space=pltpu.SMEM)
-    return pl.pallas_call(
+    band_lon, band_lat = pl.pallas_call(
         kernel,
         in_specs=[smem, smem],
         out_shape=(
@@ -82,6 +82,20 @@
             jax.ShapeDtypeStruct((lat_cells, lat_cells), jnp.bfloat16),
         ),
     )(lon_taps.astype(jnp.float32), lat_taps.astype(jnp.float32))
+    windows = tuple(
+        band_lat[low:high, start:stop] for start, stop, low, high in lat_windows(lat_cells, radius)
+    )
+    return band_lon, windows
+
+
+def lat_windows(lat_cells, radius):
+    out = []
+    for start in range(0, lat_cells, 256):
+        stop = min(lat_cells, start + 256)
+        low = max(0, (start - radius) // 128 * 128)
+        high = min(lat_cells, -(-(stop + radius) // 128) * 128)
+        out.append((start, stop, low, high))
+    return out
 
 
 def member_chunk(members):
@@ -91,20 +105,12 @@
     return 1
 
 
-def lat_conv(along_ref, blat_ref, radius):
-    lat_cells = blat_ref.shape[0]
-    blocks = []
-    for start in range(0, lat_cells, 256):
-        stop = min(lat_cells, start + 256)
-        low = max(0, (start - radius) // 128 * 128)
-        high = min(lat_cells, -(-(stop + radius) // 128) * 128)
-        blocks.append(
-            jnp.dot(
-                along_ref[:, low:high],
-                blat_ref[low:high, start:stop],
-                preferred_element_type=jnp.float32,
-            )
-        )
+def lat_conv(along_ref, window_refs, radius):
+    lat_cells = along_ref.shape[1]
+    blocks = [
+        jnp.dot(along_ref[:, low:high], ref[...], preferred_element_type=jnp.float32)
+        for (start, stop, low, high), ref in zip(lat_windows(lat_cells, radius), window_refs)
+    ]
     return jnp.concatenate(blocks, axis=1) if len(blocks) > 1 else blocks[0]
 
 
@@ -143,15 +149,18 @@
     sources, _, slots = cells.shape
     parts = -(-lat_cells // 128)
 
-    def kernel(ctrl_ref, low_ref, high_ref, pert_ref, blon_ref, blat_ref, cells_ref, out_ref,
-               ext_ref, along_ref, acc_ref, fold_ref):
+    count = len(band_lat)
+
+    def kernel(ctrl_ref, low_ref, high_ref, pert_ref, blon_ref, *refs):
+        blat_refs = refs[:count]
+        cells_ref, out_ref, ext_ref, along_ref, acc_ref, fold_ref = refs[count:]
         step = pl.program_id(0)
         blon = blon_ref[...]
         for m in range(chunk):
             fill_ext(ext_ref, ctrl_ref[m], low_ref[m], high_ref[m], lon_cells, padded)
             along = jnp.dot(blon, ext_ref[...], preferred_element_type=jnp.float32)
             along_ref[m * padded:(m + 1) * padded, :] = along.astype(jnp.bfloat16)
-        smoothed = lat_conv(along_ref, blat_ref, radius)
+        smoothed = lat_conv(along_ref, blat_refs, radius)
         total = pert_ref[0].astype(jnp.float32) * smoothed[0:lon_cells]
         for m in range(1, chunk):
             total = total + pert_ref[m].astype(jnp.float32) * smoothed[
@@ -195,7 +204,8 @@
             halo,
             field,
             whole(band_lon.shape),
-            whole(band_lat.shape),
+        ] + [whole(w.shape) for w in band_lat] + [
+
             whole(cells.shape),
         ],
         out_specs=whole((sources, slots)),
@@ -207,7 +217,7 @@
             pltpu.VMEM((parts * padded, 128), jnp.float32),
         ],
         compiler_params=pltpu.CompilerParams(dimension_semantics=("arbitrary",)),
-    )(control, c_low, c_high, perturb, band_lon, band_lat, cells)
+    )(control, c_low, c_high, perturb, band_lon, *band_lat, cells)
 
 
 def spread_misfits(partials, lists, lon_cells, lat_cells, radius, padded):
@@ -261,8 +271,12 @@
     padded, ext_cells = band_lon.shape
     chunk = member_chunk(members)
 
+    count = len(band_lat)
+
     def kernel(pert_ref, plow_ref, phigh_ref, spread_ref, slow_ref, shigh_ref, ctrl_ref,
-               blon_ref, blat_ref, out_ref, ext_ref, along_ref):
+               blon_ref, *refs):
+        blat_refs = refs[:count]
+        out_ref, ext_ref, along_ref = refs[count:]
         blon = blon_ref[...]
         spread = spread_ref[...]
         s_lo = slow_ref[...]
@@ -278,7 +292,7 @@
             )
             along = jnp.dot(blon, ext_ref[...], preferred_element_type=jnp.float32)
             along_ref[m * padded:(m + 1) * padded, :] = along.astype(jnp.bfloat16)
-        smoothed = lat_conv(along_ref, blat_ref, radius)
+        smoothed = lat_conv(along_ref, blat_refs, radius)
         for m in range(chunk):
             out_ref[m] = ctrl_ref[m].astype(jnp.float32) + smoothed[
                 m * padded:m * padded + lon_cells
@@ -300,7 +314,7 @@
             level_halo,
             field,
             pl.BlockSpec(band_lon.shape, lambda l, g: (0, 0)),
-            pl.BlockSpec(band_lat.shape, lambda l, g: (0, 0)),
+        ] + [pl.BlockSpec(w.shape, lambda l, g: (0, 0)) for w in band_lat] + [
         ],
         out_specs=pl.BlockSpec((chunk, lon_cells, None, lat_cells), lambda l, g: (g, 0, l, 0)),
         out_shape=jax.ShapeDtypeStruct((members, lon_cells, levels, lat_cells), jnp.float32),
@@ -309,7 +323,7 @@
             pltpu.VMEM((chunk * padded, lat_cells), jnp.bfloat16),
         ],
         compiler_params=pltpu.CompilerParams(dimension_semantics=("arbitrary", "arbitrary")),
-    )(perturb, p_low, p_high, spread, s_low, s_high, control, band_lon, band_lat)
+    )(perturb, p_low, p_high, spread, s_low, s_high, control, band_lon, *band_lat)
     return jnp.transpose(out, (0, 2, 1, 3))
 
 

time: 48.6 us -> 51.8 us (1.066)
  local copies, waits for them, and re-layouts: 3.29 us -> 8.36 us
  blocking collectives: 9.92 us -> 8.66 us
    slice x0 -> x3, local copies, waits for them, and re-layouts: none -> 4.87 us  [build_bands(): band_lat[low:high, start:stop]]
    all_to_all x1, blocking collectives: 9.92 us -> 8.66 us  [local(): lax.all_to_all(lists, 'tile', split_axis=0, concat_axis=0, tiled=True)]
    ppermute x2, starting transfers between devices: 4.52 us -> 3.68 us  [halos(): lax.ppermute(lax.slice_in_dim(block, 0, width, axis=dim), axis, backward)]
  transfers between devices with their start and end apart: 9 -> 9, of which waited for: 4 -> 4; matrix products, arithmetic and copies ran while one was open for 2% -> 12% of each run, Pallas kernels for 21% -> 19%
where the time goes in v21:
time: 51.8 us; the launch traced here: 51.4 us
  Pallas kernels  15 us (29%)
  starting transfers between devices  11.3 us (22%)
  blocking collectives  8.66 us (17%)
  local copies, waits for them, and re-layouts  8.36 us (16%)
  waiting for transfers between devices  6.82 us (13%)
  other arithmetic  1.19 us (2%)
    all_to_all x1, blocking collectives, local(): lax.all_to_all(lists, 'tile', split_axis=0, concat_axis=0, tiled=True)  8.66 us
    pallas_call x1, Pallas kernels, backward_grad(): pl.pallas_call(kernel, grid=(levels, members // chunk), in_specs=[field,...  5.26 us
    pallas_call x1, Pallas kernels, forward_pick(): pl.pallas_call(kernel, grid=(steps,), in_specs=[field, halo, halo, field,...  5.19 us
    slice x3, local copies, waits for them, and re-layouts, build_bands(): band_lat[low:high, start:stop]  4.87 us
    ppermute x3, waiting for transfers between devices, gather_over(): lax.ppermute(values, axis, [(i, (i + shift) % count) for i in range(count)])  4.64 us
    ppermute x3, starting transfers between devices, gather_over(): lax.ppermute(values, axis, [(i, (i + shift) % count) for i in range(count)])  4.61 us
    ppermute x2, starting transfers between devices, halos(): lax.ppermute(lax.slice_in_dim(block, 0, width, axis=dim), axis, backward)  3.68 us
    ppermute x1, starting transfers between devices, local(): lax.ppermute(high_send, 'tile', [((i + 1) % count, i) for i in range(coun...  2.64 us
  transfers between devices with their start and end apart: 9, of which 4 were waited for; matrix products, arithmetic and copies ran while one was open for 12% of the time, Pallas kernels for 19%

profile of v21, /device:TPU:0, one launch (start us, length us, event | category | flops | bytes accessed | tf_op | source)
XLA Modules:
  0.0 51.4 jit_solution(6479707248658198453)
XLA Ops:
  0.0 0.0 copy-start.9
  0.0 0.0 copy-start
  0.0 1.5 %fusion.2 = (bf16[20,1,16,720]{3,2,1,0:T(8,128)(2,1)S(1)}, bf16[20,1,16,720]{3,2,1,0:T(8,128)(2,1)S(1)}) fusion(bf16[20,1,45,720]{3,2,1,0:T(8,128)(2,1)} %ctrl_ref.3), kind=kLoop, calls=%fused_computation.5 | loop fusion | bytes 1843200 | tf_op jit(solution)/shard_map/slice | solution.py:18
  1.6 3.4 %collective-permute-start.1 = (bf16[20,1,16,720]{3,2,1,0:T(8,128)(2,1)S(1)}, bf16[20,1,16,720]{3,2,1,0:T(8,128)(2,1)S(1)}, u32[]{:S(2)}, u32[]{:S(2)}) collective-permute-start(bf16[20,1,16,720]{3,2,1,0:T(8,128)(2,1)S(1)} %get-tuple-element.27), channel_id=1, source_target_pairs={{4,0},{8,4},{12,8},{16,12},{20,16},{24,20},{28,24},{0,28},{5,1},{9... | collective-permute-start | bytes 1382408 | tf_op jit(solution)/shard_map/ppermute | solution.py:18
  5.0 0.0 collective-permute-start
  5.0 0.0 copy-done.14
  5.0 0.5 %convert_element_type.21.lon_ref = f32[17]{0:T(128)} convert(bf16[17]{0:T(256)(128)(2,1)S(1)} %copy-done.14) | non-fusion elementwise | flops 17 | bytes 102 | tf_op jit(solution)/shard_map/convert_element_type | solution.py:84
  5.5 0.0 copy-done.15
  5.5 0.5 %convert_element_type.22.lat_ref = f32[17]{0:T(128)} convert(bf16[17]{0:T(256)(128)(2,1)S(1)} %copy-done.15) | non-fusion elementwise | flops 17 | bytes 102 | tf_op jit(solution)/shard_map/convert_element_type | solution.py:84
  6.1 1.9 %shard_map.85 = (bf16[48,80]{1,0:T(8,128)(2,1)}, bf16[720,720]{1,0:T(8,128)(2,1)}) custom-call(f32[17]{0:T(128)} %convert_element_type.21.lon_ref, f32[17]{0:T(128)} %convert_element_type.22.lat_ref), custom_call_target="tpu_custom_call" | custom-call | tf_op jit(solution)/shard_map/pallas_call | solution.py:77
  8.0 1.6 %slice.25.refs_2_ = bf16[336,208]{1,0:T(8,128)(2,1)} slice(bf16[720,720]{1,0:T(8,128)(2,1)} %get-tuple-element.16), slice={[384:720], [512:720]} | slice | bytes 279552 | tf_op jit(solution)/shard_map/slice | solution.py:86
  9.6 1.6 %slice.23.refs_0_ = bf16[384,256]{1,0:T(8,128)(2,1)} slice(bf16[720,720]{1,0:T(8,128)(2,1)} %get-tuple-element.16), slice={[0:384], [0:256]} | slice | bytes 393216 | tf_op jit(solution)/shard_map/slice | solution.py:86
  11.2 1.7 %slice.24.refs_1_ = bf16[512,256]{1,0:T(8,128)(2,1)} slice(bf16[720,720]{1,0:T(8,128)(2,1)} %get-tuple-element.16), slice={[128:640], [256:512]} | slice | bytes 524288 | tf_op jit(solution)/shard_map/slice | solution.py:86
  12.9 0.0 copy-done.7
  12.9 0.0 copy-done.8
  12.9 0.0 copy-done.13
  12.9 0.0 copy-done.9
  13.0 0.1 fusion
  13.1 8.7 %all_to_all.5.refs_3_.refs_4_ = f32[8,3,256]{2,1,0:T(4,128)} all-to-all(f32[8,3,256]{2,1,0:T(4,128)S(1)} %pad_maximum_fusion), channel_id=1, replica_groups=mesh['tile'=8,'mem'=4] {'tile'}, dimensions={0} | all-to-all | bytes 49152 | tf_op jit(solution)/shard_map/all_to_all | solution.py:340
  21.7 0.0 collective-permute-done.1.high_ref
  21.7 0.0 collective-permute-done.low_ref
  21.7 0.0 copy-done
  21.8 0.0 copy-start.2
  21.8 0.1 fusion.1
  21.9 0.2 collective-permute-start.3
  22.2 0.3 collective-permute-start.2
  22.5 0.1 copy-done.1
  22.5 0.1 copy-done.2
  22.7 5.2 %shard_map.86.refs_0_ = f32[8,256]{1,0:T(8,128)} custom-call(bf16[20,1,45,720]{3,2,1,0:T(8,128)(2,1)} %ctrl_ref.3, bf16[20,1,16,720]{3,2,1,0:T(8,128)(2,1)} %copy-done.2, bf16[20,1,16,720]{3,2,1,0:T(8,128)(2,1)} %copy-done.1, bf16[20,1,45,720]{3,2,1,0:T(8,128)(2,1)} %pert_ref.3, bf16[48,80]{1,0:T(8,128)(2,1)} %get-tuple-element.15.blon_ref, ...), custom_call_target="tpu_custom_call" | custom-call | tf_op jit(solution)/shard_map/pallas_call | solution.py:198
  27.9 3.6 %collective-permute-start.6 = (f32[8,256]{1,0:T(8,128)}, f32[8,256]{1,0:T(8,128)S(1)}, u32[]{:S(2)}, u32[]{:S(2)}) collective-permute-start(f32[8,256]{1,0:T(8,128)} %shard_map.86.refs_0_), channel_id=1, source_target_pairs={{0,3},{1,0},{2,1},{3,2},{4,7},{5,4},{6,5},{7,6},{8,11},{9,8},{10,9... | collective-permute-start | bytes 24584 | tf_op jit(solution)/shard_map/ppermute | solution.py:25
  31.5 0.0 collective-permute-start.5
  31.5 1.0 %collective-permute-start.4 = (f32[8,256]{1,0:T(8,128)}, f32[8,256]{1,0:T(8,128)S(1)}, u32[]{:S(2)}, u32[]{:S(2)}) collective-permute-start(f32[8,256]{1,0:T(8,128)} %shard_map.86.refs_0_), channel_id=1, source_target_pairs={{0,1},{1,2},{2,3},{3,0},{4,5},{5,6},{6,7},{7,4},{8,9},{9,10},{10,1... | collective-permute-start | bytes 24584 | tf_op jit(solution)/shard_map/ppermute | solution.py:25
  32.5 0.6 %collective-permute-done.6.refs_3_ = f32[8,256]{1,0:T(8,128)S(1)} collective-permute-done((f32[8,256]{1,0:T(8,128)}, f32[8,256]{1,0:T(8,128)S(1)}, u32[]{:S(2)}, u32[]{:S(2)}) %collective-permute-start.6) | collective-permute-done | bytes 8224 | tf_op jit(solution)/shard_map/ppermute | solution.py:25
  33.1 3.2 %collective-permute-done.5.refs_2_ = f32[8,256]{1,0:T(8,128)S(1)} collective-permute-done((f32[8,256]{1,0:T(8,128)}, f32[8,256]{1,0:T(8,128)S(1)}, u32[]{:S(2)}, u32[]{:S(2)}) %collective-permute-start.5) | collective-permute-done | bytes 8224 | tf_op jit(solution)/shard_map/ppermute | solution.py:25
  36.2 0.9 %collective-permute-done.4.refs_1_ = f32[8,256]{1,0:T(8,128)S(1)} collective-permute-done((f32[8,256]{1,0:T(8,128)}, f32[8,256]{1,0:T(8,128)S(1)}, u32[]{:S(2)}, u32[]{:S(2)}) %collective-permute-start.4) | collective-permute-done | bytes 8224 | tf_op jit(solution)/shard_map/ppermute | solution.py:25
  37.1 0.6 %copy-done.12 = f32[8,256]{1,0:T(8,128)} copy-done((f32[8,256]{1,0:T(8,128)}, f32[8,256]{1,0:T(8,128)S(1)}, u32[]{:S(2)}) %copy-start.12) | copy-done | bytes 8216
  37.7 2.6 %shard_map.87 = (f32[45,720]{1,0:T(8,128)}, f32[16,720]{1,0:T(8,128)}, f32[16,720]{1,0:T(8,128)}) custom-call(f32[8,256]{1,0:T(8,128)} %shard_map.86.refs_0_, f32[8,256]{1,0:T(8,128)} %copy-done.12, f32[8,256]{1,0:T(8,128)} %copy-done.11, f32[8,256]{1,0:T(8,128)} %copy-done.10, f32[8,3,256]{2,1,0:T(4,128)} %all_to_all.5.refs_3_.refs_4_), custom_call_target="tpu_custom_call" | custom-call | tf_op jit(solution)/shard_map/pallas_call | solution.py:257
  40.4 0.0 collective-permute-start.7
  40.4 2.6 %collective-permute-start.8 = (f32[16,720]{1,0:T(8,128)}, f32[16,720]{1,0:T(8,128)S(1)}, u32[]{:S(2)}, u32[]{:S(2)}) collective-permute-start(f32[16,720]{1,0:T(8,128)} %get-tuple-element.24), channel_id=1, source_target_pairs={{4,0},{8,4},{12,8},{16,12},{20,16},{24,20},{28,24},{0,28},{5,1},{9... | collective-permute-start | bytes 138248 | tf_op jit(solution)/shard_map/ppermute | solution.py:355
  43.0 2.2 %collective-permute-done.7 = f32[16,720]{1,0:T(8,128)S(1)} collective-permute-done((f32[16,720]{1,0:T(8,128)}, f32[16,720]{1,0:T(8,128)S(1)}, u32[]{:S(2)}, u32[]{:S(2)}) %collective-permute-start.7) | collective-permute-done | bytes 46112 | tf_op jit(solution)/shard_map/ppermute | solution.py:354
  45.2 0.0 collective-permute-done.8
  45.2 0.0 collective-permute-done.3.phigh_ref
  45.2 0.0 collective-permute-done.2.plow_ref
  45.2 0.6 %copy-done.5 = f32[16,720]{1,0:T(8,128)} copy-done((f32[16,720]{1,0:T(8,128)}, f32[16,720]{1,0:T(8,128)S(1)}, u32[]{:S(2)}) %copy-start.5) | copy-done | bytes 46104
  45.8 0.0 copy-done.6
  45.8 0.2 copy-done.3
  46.0 0.2 copy-done.4
  46.2 5.3 %shard_map.88 = f32[20,45,1,720]{3,2,1,0:T(1,128)} custom-call(bf16[20,1,45,720]{3,2,1,0:T(8,128)(2,1)} %pert_ref.3, bf16[20,1,16,720]{3,2,1,0:T(8,128)(2,1)} %copy-done.4, bf16[20,1,16,720]{3,2,1,0:T(8,128)(2,1)} %copy-done.3, f32[1,45,720]{2,1,0:T(8,128)} %bitcast.9, f32[1,16,720]{2,1,0:T(8,128)} %bitcast.10, f32[1,16,720]{2,1,0:T(8,128)} %bitcast.11, ...), custom_call_target="tpu_custom_call" | custom-call | tf_op jit(solution)/shard_map/pallas_call | solution.py:305
  (18 shorter events, 0.1 us)
Async XLA Ops:
  0.0 5.0 %copy-start.14 = (bf16[17]{0:T(256)(128)(2,1)S(1)}, bf16[17]{0:T(256)(128)(2,1)}, u32[]{:S(2)}) copy-start(bf16[17]{0:T(256)(128)(2,1)} %param.10) | copy-start | bytes 106
  0.0 5.5 %copy-start.15 = (bf16[17]{0:T(256)(128)(2,1)S(1)}, bf16[17]{0:T(256)(128)(2,1)}, u32[]{:S(2)}) copy-start(bf16[17]{0:T(256)(128)(2,1)} %param.11) | copy-start | bytes 106
  0.0 12.9 %copy-start.7 = (f32[1,8,256]{2,1,0:T(8,128)S(1)}, f32[1,8,256]{2,1,0:T(8,128)}, u32[]{:S(2)}) copy-start(f32[1,8,256]{2,1,0:T(8,128)} %param.12) | copy-start | bytes 24580
  0.0 12.9 %copy-start.8 = (s32[1,8,256]{2,1,0:T(8,128)S(1)}, s32[1,8,256]{2,1,0:T(8,128)}, u32[]{:S(2)}) copy-start(s32[1,8,256]{2,1,0:T(8,128)} %param.14) | copy-start | bytes 24580
  0.0 12.9 %copy-start.13 = (s32[1,8]{1,0:T(1,128)S(1)}, s32[1,8]{1,0:T(1,128)}, u32[]{:S(2)}) copy-start(s32[1,8]{1,0:T(1,128)} %param.15) | copy-start | bytes 100
  0.0 12.9 %copy-start.9 = (f32[1,8,256]{2,1,0:T(8,128)S(1)}, f32[1,8,256]{2,1,0:T(8,128)}, u32[]{:S(2)}) copy-start(f32[1,8,256]{2,1,0:T(8,128)} %param.13) | copy-start | bytes 24580
  0.0 21.7 %copy-start = (bf16[20,1,45,720]{3,2,1,0:T(8,128)(2,1)S(1)}, bf16[20,1,45,720]{3,2,1,0:T(8,128)(2,1)}, u32[]{:S(2)}) copy-start(bf16[20,1,45,720]{3,2,1,0:T(8,128)(2,1)} %pert_ref.3) | copy-start | bytes 3888004
  1.6 20.2 %collective-permute-start.1 = (bf16[20,1,16,720]{3,2,1,0:T(8,128)(2,1)S(1)}, bf16[20,1,16,720]{3,2,1,0:T(8,128)(2,1)S(1)}, u32[]{:S(2)}, u32[]{:S(2)}) collective-permute-start(bf16[20,1,16,720]{3,2,1,0:T(8,128)(2,1)S(1)} %get-tuple-element.27), channel_id=1, source_target_pairs={{4,0},{8,4},{12,8},{16,12},{20,16},{24,20},{28,24},{0,28},{5,1},{9... | collective-permute-start | bytes 1382408 | tf_op jit(solution)/shard_map/ppermute | solution.py:18
  5.0 16.7 %collective-permute-start = (bf16[20,1,16,720]{3,2,1,0:T(8,128)(2,1)S(1)}, bf16[20,1,16,720]{3,2,1,0:T(8,128)(2,1)S(1)}, u32[]{:S(2)}, u32[]{:S(2)}) collective-permute-start(bf16[20,1,16,720]{3,2,1,0:T(8,128)(2,1)S(1)} %get-tuple-element.28), channel_id=1, source_target_pairs={{0,4},{4,8},{8,12},{12,16},{16,20},{20,24},{24,28},{28,0},{1,5},{5... | collective-permute-start | bytes 1382408 | tf_op jit(solution)/shard_map/ppermute | solution.py:15
  21.7 0.8 %copy-start.1 = (bf16[20,1,16,720]{3,2,1,0:T(8,128)(2,1)}, bf16[20,1,16,720]{3,2,1,0:T(8,128)(2,1)S(1)}, u32[]{:S(2)}) copy-start(bf16[20,1,16,720]{3,2,1,0:T(8,128)(2,1)S(1)} %collective-permute-done.1.high_ref) | copy-start | bytes 1382404
  21.8 0.9 %copy-start.2 = (bf16[20,1,16,720]{3,2,1,0:T(8,128)(2,1)}, bf16[20,1,16,720]{3,2,1,0:T(8,128)(2,1)S(1)}, u32[]{:S(2)}) copy-start(bf16[20,1,16,720]{3,2,1,0:T(8,128)(2,1)S(1)} %collective-permute-done.low_ref) | copy-start | bytes 1382404
  21.9 23.3 %collective-permute-start.3 = (bf16[20,1,16,720]{3,2,1,0:T(8,128)(2,1)S(1)}, bf16[20,1,16,720]{3,2,1,0:T(8,128)(2,1)S(1)}, u32[]{:S(2)}, u32[]{:S(2)}) collective-permute-start(bf16[20,1,16,720]{3,2,1,0:T(8,128)(2,1)S(1)} %get-tuple-element.25), channel_id=1, source_target_pairs={{4,0},{8,4},{12,8},{16,12},{20,16},{24,20},{28,24},{0,28},{5,1},{9... | collective-permute-start | bytes 1382408 | tf_op jit(solution)/shard_map/ppermute | solution.py:18
  22.2 23.0 %collective-permute-start.2 = (bf16[20,1,16,720]{3,2,1,0:T(8,128)(2,1)S(1)}, bf16[20,1,16,720]{3,2,1,0:T(8,128)(2,1)S(1)}, u32[]{:S(2)}, u32[]{:S(2)}) collective-permute-start(bf16[20,1,16,720]{3,2,1,0:T(8,128)(2,1)S(1)} %get-tuple-element.26), channel_id=1, source_target_pairs={{0,4},{4,8},{8,12},{12,16},{16,20},{20,24},{24,28},{28,0},{1,5},{5... | collective-permute-start | bytes 1382408 | tf_op jit(solution)/shard_map/ppermute | solution.py:15
  27.9 5.2 %collective-permute-start.6 = (f32[8,256]{1,0:T(8,128)}, f32[8,256]{1,0:T(8,128)S(1)}, u32[]{:S(2)}, u32[]{:S(2)}) collective-permute-start(f32[8,256]{1,0:T(8,128)} %shard_map.86.refs_0_), channel_id=1, source_target_pairs={{0,3},{1,0},{2,1},{3,2},{4,7},{5,4},{6,5},{7,6},{8,11},{9,8},{10,9... | collective-permute-start | bytes 24584 | tf_op jit(solution)/shard_map/ppermute | solution.py:25
  31.5 4.8 %collective-permute-start.5 = (f32[8,256]{1,0:T(8,128)}, f32[8,256]{1,0:T(8,128)S(1)}, u32[]{:S(2)}, u32[]{:S(2)}) collective-permute-start(f32[8,256]{1,0:T(8,128)} %shard_map.86.refs_0_), channel_id=1, source_target_pairs={{0,2},{1,3},{2,0},{3,1},{4,6},{5,7},{6,4},{7,5},{8,10},{9,11},{10,... | collective-permute-start | bytes 24584 | tf_op jit(solution)/shard_map/ppermute | solution.py:25
  31.5 5.7 %collective-permute-start.4 = (f32[8,256]{1,0:T(8,128)}, f32[8,256]{1,0:T(8,128)S(1)}, u32[]{:S(2)}, u32[]{:S(2)}) collective-permute-start(f32[8,256]{1,0:T(8,128)} %shard_map.86.refs_0_), channel_id=1, source_target_pairs={{0,1},{1,2},{2,3},{3,0},{4,5},{5,6},{6,7},{7,4},{8,9},{9,10},{10,1... | collective-permute-start | bytes 24584 | tf_op jit(solution)/shard_map/ppermute | solution.py:25
  33.0 4.1 %copy-start.10 = (f32[8,256]{1,0:T(8,128)}, f32[8,256]{1,0:T(8,128)S(1)}, u32[]{:S(2)}) copy-start(f32[8,256]{1,0:T(8,128)S(1)} %collective-permute-done.6.refs_3_) | copy-start | bytes 24580
  36.2 0.9 %copy-start.11 = (f32[8,256]{1,0:T(8,128)}, f32[8,256]{1,0:T(8,128)S(1)}, u32[]{:S(2)}) copy-start(f32[8,256]{1,0:T(8,128)S(1)} %collective-permute-done.5.refs_2_) | copy-start | bytes 24580
  37.1 0.6 %copy-start.12 = (f32[8,256]{1,0:T(8,128)}, f32[8,256]{1,0:T(8,128)S(1)}, u32[]{:S(2)}) copy-start(f32[8,256]{1,0:T(8,128)S(1)} %collective-permute-done.4.refs_1_) | copy-start | bytes 24580
  40.4 4.8 %collective-permute-start.7 = (f32[16,720]{1,0:T(8,128)}, f32[16,720]{1,0:T(8,128)S(1)}, u32[]{:S(2)}, u32[]{:S(2)}) collective-permute-start(f32[16,720]{1,0:T(8,128)} %get-tuple-element.23), channel_id=1, source_target_pairs={{0,4},{4,8},{8,12},{12,16},{16,20},{20,24},{24,28},{28,0},{1,5},{5... | collective-permute-start | bytes 138248 | tf_op jit(solution)/shard_map/ppermute | solution.py:354
  40.4 4.8 %collective-permute-start.8 = (f32[16,720]{1,0:T(8,128)}, f32[16,720]{1,0:T(8,128)S(1)}, u32[]{:S(2)}, u32[]{:S(2)}) collective-permute-start(f32[16,720]{1,0:T(8,128)} %get-tuple-element.24), channel_id=1, source_target_pairs={{4,0},{8,4},{12,8},{16,12},{20,16},{24,20},{28,24},{0,28},{5,1},{9... | collective-permute-start | bytes 138248 | tf_op jit(solution)/shard_map/ppermute | solution.py:355
  45.2 0.6 %copy-start.5 = (f32[16,720]{1,0:T(8,128)}, f32[16,720]{1,0:T(8,128)S(1)}, u32[]{:S(2)}) copy-start(f32[16,720]{1,0:T(8,128)S(1)} %collective-permute-done.7) | copy-start | bytes 138244
  45.2 0.6 %copy-start.6 = (f32[16,720]{1,0:T(8,128)}, f32[16,720]{1,0:T(8,128)S(1)}, u32[]{:S(2)}) copy-start(f32[16,720]{1,0:T(8,128)S(1)} %collective-permute-done.8) | copy-start | bytes 138244
  45.2 0.8 %copy-start.3 = (bf16[20,1,16,720]{3,2,1,0:T(8,128)(2,1)}, bf16[20,1,16,720]{3,2,1,0:T(8,128)(2,1)S(1)}, u32[]{:S(2)}) copy-start(bf16[20,1,16,720]{3,2,1,0:T(8,128)(2,1)S(1)} %collective-permute-done.3.phigh_ref) | copy-start | bytes 1382404
  45.2 1.0 %copy-start.4 = (bf16[20,1,16,720]{3,2,1,0:T(8,128)(2,1)}, bf16[20,1,16,720]{3,2,1,0:T(8,128)(2,1)S(1)}, u32[]{:S(2)}) copy-start(bf16[20,1,16,720]{3,2,1,0:T(8,128)(2,1)S(1)} %collective-permute-done.2.plow_ref) | copy-start | bytes 1382404
